TPU v7x, 512 devices: a whole 4x8x8 slice. The times are simulated.
512 devices in a mesh: chan: 128 (over x, z_hi, y, core), seg: 4 (over z_lo).
Axes of the slice: x: 4, y: 8, z: 8 (z_hi: 2, z_lo: 4; z = z_hi * 4 + z_lo), core: 2. Of those that a mesh axis runs over, the one named last changes fastest.
Arguments:
- spectra: bfloat16 [2, 32, 4096, 512], P(None, 'seg', 'chan'), may hold values from -6 to 6
- sources: int32 [8, 4], replicated, may hold values from 0 to 4095, as said below
Outputs:
- correlations: float32 [32, 4096, 512], P(None, ('chan', 'seg'))
Inputs may be any that keep to these rules, and one draw needn't show every extreme that they name: `sources`: each entry names a channel of the array; entries may repeat and may crowd onto the channels of a few devices of chan.
All inputs are finite; a program needn't handle non-finite values.
Results may differ from a plain program's by a relative error of at most 0.004.
Values may be sent and summed in bfloat16 or wider, within the bound.
No kernel may reach another device: no remote copies, remote signals or barrier semaphores. Data moves between devices by JAX's collectives and lax.ppermute only.
A program may use at most 128 MiB of HBM per device.

v0:
```python
import math

import jax
import jax.numpy as jnp
from jax import lax
from jax.sharding import PartitionSpec as P

LAGS = 256


def whiten(spectra):
    values = spectra.astype(jnp.float32)
    power_mean = jnp.mean(values[0] * values[0] + values[1] * values[1], axis=-1)
    inv_scale = lax.rsqrt(power_mean + 1e-06)
    return (values * inv_scale[None, :, :, None]).astype(jnp.bfloat16)


def lag_matrix(freqs, half_lags):
    period = 2 * freqs
    rows = jnp.arange(freqs, dtype=jnp.int32)
    shifts = jnp.arange(2 * half_lags, dtype=jnp.int32) - half_lags
    phase = jnp.mod(rows[:, None] * shifts[None, :], period)
    angles = phase.astype(jnp.float32) * (2.0 * math.pi / period)
    return jnp.concatenate([jnp.cos(angles), -jnp.sin(angles)], axis=0)


def correlate(source_spec, receiver_spec, lag_table):
    segs = receiver_spec.shape[1]
    freqs = receiver_spec.shape[3]
    real_part = jnp.einsum(
        "pkf,krf->prf", source_spec[0], receiver_spec[0], preferred_element_type=jnp.float32
    ) + jnp.einsum(
        "pkf,krf->prf", source_spec[1], receiver_spec[1], preferred_element_type=jnp.float32
    )
    imag_part = jnp.einsum(
        "pkf,krf->prf", source_spec[0], receiver_spec[1], preferred_element_type=jnp.float32
    ) - jnp.einsum(
        "pkf,krf->prf", source_spec[1], receiver_spec[0], preferred_element_type=jnp.float32
    )
    stacked = jnp.concatenate([real_part, imag_part], axis=-1) * (1.0 / math.sqrt(segs))
    flat = stacked.reshape(-1, 2 * freqs)
    result = jnp.dot(
        flat, lag_table, precision=lax.Precision.HIGHEST, preferred_element_type=jnp.float32
    ) * (1.0 / math.sqrt(freqs))
    return result.reshape(stacked.shape[0], stacked.shape[1], -1)


def shards(spectra, sources):
    whitened = whiten(spectra)
    regrouped = lax.all_to_all(whitened, "seg", split_axis=2, concat_axis=1, tiled=True)
    ch_dev = spectra.shape[2]
    freqs = spectra.shape[3]
    first_row = lax.axis_index("chan") * ch_dev
    lag_table = lag_matrix(freqs, LAGS)
    batches = sources.shape[0]
    results = []
    for batch_no in range(batches):
        local_row = sources[batch_no] - first_row
        onehot = (local_row[:, None] == jnp.arange(ch_dev, dtype=jnp.int32)[None, :]).astype(
            jnp.bfloat16
        )
        local_spec = lax.psum(
            jnp.einsum("pc,xscf->xpsf", onehot, whitened, preferred_element_type=jnp.float32),
            "chan",
        ).astype(jnp.bfloat16)
        source_spec = lax.all_gather(local_spec, "seg", axis=2, tiled=True)
        results.append(correlate(source_spec, regrouped, lag_table))
    return jnp.concatenate(results, axis=0)


def solution(mesh):
    placed = (P(None, "seg", "chan", None), P())
    return jax.shard_map(
        shards,
        mesh=mesh,
        in_specs=placed,
        out_specs=P(None, ("chan", "seg"), None),
        check_vma=False,
    )
```

profile of v0, /device:TPU:64, one launch (start us, length us, event | category | flops | bytes accessed | tf_op | source)
XLA Modules:
  0.0 1094.6 jit_solution(12847016964361997581)
XLA Ops:
  2.7 8.5 all-to-all-start
  23.0 814.0 %all-reduce.2 = (bf16[2,4,8,512]{3,1,2,0:T(4,128)(2,1)S(1)}, bf16[2,4,8,512]{3,1,2,0:T(4,128)(2,1)S(1)}, bf16[2,4,8,512]{3,1,2,0:T(4,128)(2,1)S(1)}, bf16[2,4,8,...) all-reduce(f32[2,4,8,512]{3,1,2,0:T(4,128)S(1)} %convolution_bitcas, ...), channel_id=1, replica_groups=mesh['chan'=128,'seg'=4] {'chan'}, use_global_device_ids=true, to_apply=%region_1.2 | all-reduce | flops 262144 | bytes 1572864 | tf_op jit(solution)/shard_map/psum | solution.py:62
  837.0 14.2 %all_gather.26 = bf16[2,4,32,512]{3,1,2,0:T(4,128)(2,1)S(1)} all-gather(bf16[2,4,8,512]{3,1,2,0:T(4,128)(2,1)S(1)} %get-tuple-element.15), channel_id=1, replica_groups=mesh['chan'=128,'seg'=4] {'seg'}, dimensions={2}, use_global_device_ids=true | all-gather | bytes 327680 | tf_op jit(solution)/shard_map/all_gather | solution.py:66
  851.3 14.5 %all_gather.25 = bf16[2,4,32,512]{3,1,2,0:T(4,128)(2,1)S(1)} all-gather(bf16[2,4,8,512]{3,1,2,0:T(4,128)(2,1)S(1)} %get-tuple-element.14), channel_id=1, replica_groups=mesh['chan'=128,'seg'=4] {'seg'}, dimensions={2}, use_global_device_ids=true | all-gather | bytes 327680 | tf_op jit(solution)/shard_map/all_gather | solution.py:66
  865.9 14.4 %all_gather.24 = bf16[2,4,32,512]{3,1,2,0:T(4,128)(2,1)S(1)} all-gather(bf16[2,4,8,512]{3,1,2,0:T(4,128)(2,1)S(1)} %get-tuple-element.13), channel_id=1, replica_groups=mesh['chan'=128,'seg'=4] {'seg'}, dimensions={2}, use_global_device_ids=true | all-gather | bytes 327680 | tf_op jit(solution)/shard_map/all_gather | solution.py:66
  880.3 14.2 %all_gather.27 = bf16[2,4,32,512]{3,1,2,0:T(4,128)(2,1)S(1)} all-gather(bf16[2,4,8,512]{3,1,2,0:T(4,128)(2,1)S(1)} %get-tuple-element.16), channel_id=1, replica_groups=mesh['chan'=128,'seg'=4] {'seg'}, dimensions={2}, use_global_device_ids=true | all-gather | bytes 327680 | tf_op jit(solution)/shard_map/all_gather | solution.py:66
  894.6 14.3 %all_gather.28 = bf16[2,4,32,512]{3,1,2,0:T(4,128)(2,1)S(1)} all-gather(bf16[2,4,8,512]{3,1,2,0:T(4,128)(2,1)S(1)} %get-tuple-element.17), channel_id=1, replica_groups=mesh['chan'=128,'seg'=4] {'seg'}, dimensions={2}, use_global_device_ids=true | all-gather | bytes 327680 | tf_op jit(solution)/shard_map/all_gather | solution.py:66
  909.0 13.9 %all_gather.29 = bf16[2,4,32,512]{3,1,2,0:T(4,128)(2,1)S(1)} all-gather(bf16[2,4,8,512]{3,1,2,0:T(4,128)(2,1)S(1)} %get-tuple-element.18), channel_id=1, replica_groups=mesh['chan'=128,'seg'=4] {'seg'}, dimensions={2}, use_global_device_ids=true | all-gather | bytes 327680 | tf_op jit(solution)/shard_map/all_gather | solution.py:66
  923.0 14.5 %all_gather.30 = bf16[2,4,32,512]{3,1,2,0:T(4,128)(2,1)S(1)} all-gather(bf16[2,4,8,512]{3,1,2,0:T(4,128)(2,1)S(1)} %get-tuple-element.19), channel_id=1, replica_groups=mesh['chan'=128,'seg'=4] {'seg'}, dimensions={2}, use_global_device_ids=true | all-gather | bytes 327680 | tf_op jit(solution)/shard_map/all_gather | solution.py:66
  952.9 13.9 %all_gather.31 = bf16[2,4,32,512]{3,1,2,0:T(4,128)(2,1)S(1)} all-gather(bf16[2,4,8,512]{3,1,2,0:T(4,128)(2,1)S(1)} %get-tuple-element.20), channel_id=1, replica_groups=mesh['chan'=128,'seg'=4] {'seg'}, dimensions={2}, use_global_device_ids=true | all-gather | bytes 327680 | tf_op jit(solution)/shard_map/all_gather | solution.py:66
  969.1 5.8 fusion.40
  1007.9 3.1 fusion.10
  1012.5 3.1 fusion.13
  1017.1 3.1 fusion.12
  1021.7 3.1 fusion.15
  1026.4 3.1 fusion.14
  1031.6 3.1 fusion.9
  1036.2 3.1 fusion.8
  1041.4 3.1 fusion.7
  1046.7 3.1 fusion.6
  1052.0 3.1 fusion.5
  1057.2 3.1 fusion.4
  1067.6 3.1 fusion.2
  1072.9 3.3 fusion.1
  (132 shorter events, 111.5 us)
Async XLA Ops:
  0.0 1.6 copy-start.11
  1.6 9.6 copy-start.20
  2.7 972.2 %all-to-all-start = ((bf16[2,8,32,512]{3,1,0,2:T(8,128)(2,1)}), bf16[2,8,32,512]{3,1,0,2:T(8,128)(2,1)S(1)}, u32[]{:S(2)}, u32[]{:S(2)}) async-start(bf16[2,8,32,512]{3,1,0,2:T(8,128)(2,1)} %multiply_convert_fusion), calls=%async_computation | async-start | bytes 1048576 | tf_op jit(solution)/shard_map/all_to_all | solution.py:50
  977.0 1.8 copy-start.3
  978.8 1.7 copy-start.4
  982.3 1.7 copy-start.5
  985.7 1.7 copy-start.6
  989.1 1.7 copy-start.7
  992.6 1.7 copy-start.8
  996.0 1.7 copy-start.9
  999.4 1.7 copy-start.10
  1002.9 1.9 copy-start.2
  1076.2 1.6 copy-start.1
  1080.7 1.6 copy-start
  1080.7 1.6 copy-start.14
  1085.0 1.3 copy-start.12
  1086.3 1.3 copy-start.13
  1086.3 1.3 copy-start.15
  1087.7 1.3 copy-start.16
  1087.7 1.3 copy-start.17
  1089.0 1.3 copy-start.18
  1089.0 1.3 copy-start.19
  1091.7 0.8 copy-start.21
where the time goes:
time: 1100 us; the launch traced here: 1090 us
  blocking collectives  928 us (84%)
  matrix products  98.2 us (9%)
  local copies, waits for them, and re-layouts  50.7 us (5%)
    psum x1, blocking collectives, shards(): lax.psum(jnp.einsum('pc,xscf->xpsf', onehot, whitened, preferred_element_...  814 us
    all_gather x8, blocking collectives, shards(): source_spec = lax.all_gather(local_spec, 'seg', axis=2, tiled=True)  114 us
    dot_general x8, matrix products, correlate(): jnp.einsum('pkf,krf->prf', source_spec[1], receiver_spec[0], preferred_el...  24.5 us
    dot_general x8, matrix products, correlate(): jnp.einsum('pkf,krf->prf', source_spec[1], receiver_spec[1], preferred_el...  23.5 us
  transfers between devices with their start and end apart: 1, of which 0 were waited for; matrix products, arithmetic and copies ran while one was open for 3% of the time, Pallas kernels for 0%

commit v1 on v0

--- a/solution.py
+++ b/solution.py
@@ -3,9 +3,12 @@
 import jax
 import jax.numpy as jnp
 from jax import lax
-from jax.sharding import PartitionSpec as P
+from jax.sharding import Mesh, PartitionSpec as P
 
 LAGS = 256
+CHAN_FACTORS = (("x", 4), ("zh", 2), ("y", 8), ("c", 2))
+CHAN_AXES = tuple(name for name, _ in CHAN_FACTORS)
+REDUCE_ORDER = ("c", "y", "zh", "x")
 
 
 def whiten(spectra):
@@ -45,35 +48,44 @@
     return result.reshape(stacked.shape[0], stacked.shape[1], -1)
 
 
-def shards(spectra, sources):
-    whitened = whiten(spectra)
-    regrouped = lax.all_to_all(whitened, "seg", split_axis=2, concat_axis=1, tiled=True)
-    ch_dev = spectra.shape[2]
-    freqs = spectra.shape[3]
-    first_row = lax.axis_index("chan") * ch_dev
-    lag_table = lag_matrix(freqs, LAGS)
-    batches = sources.shape[0]
-    results = []
-    for batch_no in range(batches):
-        local_row = sources[batch_no] - first_row
+def make_shards(chan_axes, reduce_order):
+    def shards(spectra, sources):
+        whitened = whiten(spectra)
+        regrouped = lax.all_to_all(whitened, "seg", split_axis=2, concat_axis=1, tiled=True)
+        ch_dev = spectra.shape[2]
+        freqs = spectra.shape[3]
+        first_row = lax.axis_index(chan_axes) * ch_dev
+        lag_table = lag_matrix(freqs, LAGS)
+        local_row = sources.reshape(-1) - first_row
         onehot = (local_row[:, None] == jnp.arange(ch_dev, dtype=jnp.int32)[None, :]).astype(
             jnp.bfloat16
         )
-        local_spec = lax.psum(
-            jnp.einsum("pc,xscf->xpsf", onehot, whitened, preferred_element_type=jnp.float32),
-            "chan",
+        local_spec = jnp.einsum(
+            "pc,xscf->xpsf", onehot, whitened, preferred_element_type=jnp.float32
         ).astype(jnp.bfloat16)
+        for axis in reduce_order:
+            local_spec = lax.psum(local_spec, axis)
         source_spec = lax.all_gather(local_spec, "seg", axis=2, tiled=True)
-        results.append(correlate(source_spec, regrouped, lag_table))
-    return jnp.concatenate(results, axis=0)
+        return correlate(source_spec, regrouped, lag_table)
+
+    return shards
 
 
 def solution(mesh):
-    placed = (P(None, "seg", "chan", None), P())
+    chan = mesh.shape["chan"]
+    sizes = tuple(size for _, size in CHAN_FACTORS)
+    if math.prod(sizes) == chan:
+        devices = mesh.devices.reshape(sizes + (mesh.shape["seg"],))
+        fine = Mesh(devices, CHAN_AXES + ("seg",))
+        chan_axes, reduce_order = CHAN_AXES, REDUCE_ORDER
+    else:
+        fine = mesh
+        chan_axes, reduce_order = "chan", ("chan",)
+    placed = (P(None, "seg", chan_axes, None), P())
     return jax.shard_map(
-        shards,
-        mesh=mesh,
+        make_shards(chan_axes, reduce_order),
+        mesh=fine,
         in_specs=placed,
-        out_specs=P(None, ("chan", "seg"), None),
+        out_specs=P(None, tuple(chan_axes) + ("seg",) if isinstance(chan_axes, tuple) else ("chan", "seg"), None),
         check_vma=False,
     )

time: 1100 us -> 358 us (0.33)
  the two profiles are of different devices: /device:TPU:64 before, /device:TPU:1 now
where the time goes in v1:
time: 358 us
  waiting for transfers between devices  282 us (79%)
  local copies, waits for them, and re-layouts  26.2 us (7%)
  matrix products  22.6 us (6%)
  between operations  13.2 us (4%)
  other arithmetic  8.44 us (2%)
  starting transfers between devices  5.1 us (1%)
    psum x4, waiting for transfers between devices, shards(): local_spec = lax.psum(local_spec, axis)  236 us
    all_gather x1, waiting for transfers between devices, shards(): source_spec = lax.all_gather(local_spec, 'seg', axis=2, tiled=True)  39.8 us
    squeeze x2, local copies, waits for them, and re-layouts, correlate(): source_spec[1]  9.56 us
    squeeze x1, local copies, waits for them, and re-layouts, correlate(): source_spec[0]  8.57 us
  transfers between devices with their start and end apart: 6, of which 6 were waited for; matrix products, arithmetic and copies ran while one was open for 2% of the time, Pallas kernels for 0%

profile of v1, /device:TPU:1, one launch (start us, length us, event | category | flops | bytes accessed | tf_op | source)
XLA Modules:
  0.0 358.0 jit_solution(14407823031726481966)
XLA Ops:
  6.5 0.7 broadcast_subtract_fusion
  7.4 1.4 copy_convert_fusion
  9.0 1.1 multiply_convert_fusion
  10.1 2.3 fusion.4
  12.4 42.2 %all-reduce.5.cloned.1.call-done = bf16[2,32,8,512]{3,1,2,0:T(8,128)(2,1)} async-done(((bf16[2,32,8,512]{3,1,2,0:T(8,128)(2,1)}), bf16[2,32,8,512]{3,1,2,0:T(8,128)(2,1)}) %all-reduce.5.cloned.1.call-update) | async-done | bytes 524304 | tf_op jit(solution)/shard_map/psum | solution.py:67
  54.7 76.2 %all-reduce.7.cloned.1.call-done = bf16[2,32,8,512]{3,1,2,0:T(8,128)(2,1)} async-done(((bf16[2,32,8,512]{3,1,2,0:T(8,128)(2,1)}), bf16[2,32,8,512]{3,1,2,0:T(8,128)(2,1)}) %all-reduce.7.cloned.1.call-update) | async-done | bytes 524304 | tf_op jit(solution)/shard_map/psum | solution.py:67
  130.9 67.8 %all-reduce.9.cloned.1.call-done = bf16[2,32,8,512]{3,1,2,0:T(8,128)(2,1)} async-done(((bf16[2,32,8,512]{3,1,2,0:T(8,128)(2,1)}), bf16[2,32,8,512]{3,1,2,0:T(8,128)(2,1)}) %all-reduce.9.cloned.1.call-update) | async-done | bytes 524304 | tf_op jit(solution)/shard_map/psum | solution.py:67
  198.9 50.2 %all-reduce.11.cloned.1.call-done = bf16[2,32,8,512]{3,1,2,0:T(8,128)(2,1)} async-done(((bf16[2,32,8,512]{3,1,2,0:T(8,128)(2,1)}), bf16[2,32,8,512]{3,1,2,0:T(8,128)(2,1)}) %all-reduce.11.cloned.1.call-update) | async-done | bytes 524304 | tf_op jit(solution)/shard_map/psum | solution.py:67
  249.0 4.9 %all-to-all-start = ((bf16[2,8,32,512]{3,1,0,2:T(8,128)(2,1)}), bf16[2,8,32,512]{3,1,0,2:T(8,128)(2,1)S(1)}, u32[]{:S(2)}, u32[]{:S(2)}) async-start(bf16[2,8,32,512]{3,1,0,2:T(8,128)(2,1)} %multiply_convert_fusion), calls=%async_computation | async-start | bytes 1048576 | tf_op jit(solution)/shard_map/all_to_all | solution.py:54
  254.0 5.1 %fusion.22 = (f32[512,512]{1,0:T(8,128)}, f32[512,512]{1,0:T(8,128)}) fusion(s32[512]{0:T(512)S(1)} %iota_add_fusion), kind=kLoop, calls=%fused_computation.33 | loop fusion | flops 3932160 | bytes 2099200 | tf_op jit(solution)/shard_map/cos | solution.py:27
  259.1 6.2 %all-to-all-done = bf16[2,8,32,512]{3,1,0,2:T(8,128)(2,1)S(1)} async-done(((bf16[2,8,32,512]{3,1,0,2:T(8,128)(2,1)}), bf16[2,8,32,512]{3,1,0,2:T(8,128)(2,1)S(1)}, u32[]{:S(2)}, u32[]{:S(2)}) %all-to-all-start) | async-done | bytes 524320 | tf_op jit(solution)/shard_map/all_to_all | solution.py:54
  265.6 0.8 copy.38
  266.5 0.8 copy.41
  267.4 39.8 %all-gather.2.cloned.1.call-done = bf16[2,32,32,512]{3,1,2,0:T(8,128)(2,1)} async-done(((bf16[2,32,8,512]{3,1,2,0:T(8,128)(2,1)}), bf16[2,32,32,512]{3,1,2,0:T(8,128)(2,1)}) %all-gather.2.cloned.1.call-update) | async-done | bytes 2097168 | tf_op jit(solution)/shard_map/all_gather | solution.py:68
  307.2 2.7 slice_bitcast_fusion
  309.9 8.6 %copy.39 = bf16[32,32,512]{1,0,2:T(8,128)(2,1)} copy(bf16[32,32,512]{2,0,1:T(8,128)(2,1)} %get-tuple-element.6) | data formatting | bytes 2097152 | tf_op jit(solution)/shard_map/squeeze | solution.py:34
  318.5 6.8 %copy.42 = bf16[32,32,512]{1,0,2:T(8,128)(2,1)} copy(bf16[32,32,512]{2,0,1:T(8,128)(2,1)S(1)} %get-tuple-element.5) | data formatting | bytes 2097152 | tf_op jit(solution)/shard_map/squeeze | solution.py:36
  325.3 4.6 %fusion.30 = f32[512,8,32]{2,1,0:T(8,128)S(1)} fusion(bf16[32,8,512]{0,1,2:T(8,128)(2,1)S(1)} %copy.38, bf16[32,32,512]{1,0,2:T(8,128)(2,1)} %copy.39), kind=kOutput, calls=%fused_computation.44 | convolution fusion | flops 8388608 | bytes 1835008 | tf_op jit(solution)/shard_map/pkf,krf->prf/dot_general | solution.py:33
  329.9 3.6 %fusion.31 = f32[512,8,32]{2,1,0:T(8,128)} fusion(bf16[32,8,512]{0,1,2:T(8,128)(2,1)S(1)} %copy.41, bf16[32,32,512]{1,0,2:T(8,128)(2,1)S(1)} %copy-done.1), kind=kOutput, calls=%fused_computation.45 | convolution fusion | flops 8388608 | bytes 1835008 | tf_op jit(solution)/shard_map/pkf,krf->prf/dot_general | solution.py:38
  333.5 3.6 %add_bitcast_fusion = f32[32,8,512]{0,1,2:T(8,128)} fusion(f32[512,8,32]{2,1,0:T(8,128)S(1)} %fusion.30, bf16[32,8,512]{0,1,2:T(8,128)(2,1)S(1)} %copy.41, bf16[32,32,512]{1,0,2:T(8,128)(2,1)S(1)} %copy-done), kind=kOutput, calls=%fused_computation.5 | convolution fusion | flops 8519680 | bytes 2359296 | tf_op jit(solution)/shard_map/pkf,krf->prf/dot_general | solution.py:35
  337.1 3.3 copy.43
  340.4 5.8 %subtract_bitcast_fusion = f32[32,8,512]{0,1,2:T(8,128)} fusion(f32[512,8,32]{2,1,0:T(8,128)S(1)} %copy-done.2, bf16[32,8,512]{0,1,2:T(8,128)(2,1)S(1)} %copy.38, bf16[32,32,512]{1,0,2:T(8,128)(2,1)} %copy.42), kind=kOutput, calls=%fused_computation.4 | convolution fusion | flops 8519680 | bytes 2359296 | tf_op jit(solution)/shard_map/pkf,krf->prf/dot_general | solution.py:40
  346.2 2.5 copy.48
  348.8 2.8 fusion.8
  (33 shorter events, 1.0 us)
Async XLA Ops:
  6.5 2.4 copy-start.6
  6.5 48.1 %all-reduce.5.cloned.1.call-start = ((), (), s32[]{:S(2)}) async-start(), calls=%async_computation.1 | async-start | bytes 1048576 | tf_op jit(solution)/shard_map/psum | solution.py:67
  12.4 118.5 %all-reduce.7.cloned.1.call-start = ((), (), s32[]{:S(2)}) async-start(), calls=%async_computation.2 | async-start | bytes 1048576 | tf_op jit(solution)/shard_map/psum | solution.py:67
  54.6 144.2 %all-reduce.9.cloned.1.call-start = ((), (), s32[]{:S(2)}) async-start(), calls=%async_computation.3 | async-start | bytes 1048576 | tf_op jit(solution)/shard_map/psum | solution.py:67
  130.9 118.1 %all-reduce.11.cloned.1.call-start = ((), (), s32[]{:S(2)}) async-start(), calls=%async_computation.4 | async-start | bytes 1048576 | tf_op jit(solution)/shard_map/psum | solution.py:67
  198.8 108.4 %all-gather.2.cloned.1.call-start = ((), (), s32[]{:S(2)}) async-start(), calls=%async_computation.5 | async-start | bytes 2621440 | tf_op jit(solution)/shard_map/all_gather | solution.py:68
  249.0 16.2 %all-to-all-start = ((bf16[2,8,32,512]{3,1,0,2:T(8,128)(2,1)}), bf16[2,8,32,512]{3,1,0,2:T(8,128)(2,1)S(1)}, u32[]{:S(2)}, u32[]{:S(2)}) async-start(bf16[2,8,32,512]{3,1,0,2:T(8,128)(2,1)} %multiply_convert_fusion), calls=%async_computation | async-start | bytes 1048576 | tf_op jit(solution)/shard_map/all_to_all | solution.py:54
  325.3 4.6 %copy-start.1 = (bf16[32,32,512]{1,0,2:T(8,128)(2,1)S(1)}, bf16[32,32,512]{1,0,2:T(8,128)(2,1)}, u32[]{:S(2)}) copy-start(bf16[32,32,512]{1,0,2:T(8,128)(2,1)} %copy.39) | copy-start | bytes 3145732
  329.9 3.6 %copy-start = (bf16[32,32,512]{1,0,2:T(8,128)(2,1)S(1)}, bf16[32,32,512]{1,0,2:T(8,128)(2,1)}, u32[]{:S(2)}) copy-start(bf16[32,32,512]{1,0,2:T(8,128)(2,1)} %copy.42) | copy-start | bytes 3145732
  337.1 3.3 copy-start.2
  346.2 2.6 copy-start.3
  346.2 2.6 copy-start.4
  346.2 2.6 copy-start.5
Sparse Core Ops, SparseCore 0:
  12.5 42.0 all-reduce.4
  57.0 73.7 all-reduce.6
  133.8 64.9 all-reduce.8
  201.1 47.8 all-reduce.10
  251.2 55.9 all-gather.1

commit v2 on v1

--- a/solution.py
+++ b/solution.py
@@ -8,7 +8,7 @@
 LAGS = 256
 CHAN_FACTORS = (("x", 4), ("zh", 2), ("y", 8), ("c", 2))
 CHAN_AXES = tuple(name for name, _ in CHAN_FACTORS)
-REDUCE_ORDER = ("c", "y", "zh", "x")
+REDUCE_ORDER = (("c", 2), ("y", 8), ("zh", 2), ("x", 4))
 
 
 def whiten(spectra):
@@ -48,6 +48,17 @@
     return result.reshape(stacked.shape[0], stacked.shape[1], -1)
 
 
+def exchange_sum(value, axis, size):
+    if size & (size - 1):
+        return lax.psum(value, axis)
+    step = 1
+    while step < size:
+        pairs = [(i, i ^ step) for i in range(size)]
+        value = value + lax.ppermute(value, axis, pairs)
+        step *= 2
+    return value
+
+
 def make_shards(chan_axes, reduce_order):
     def shards(spectra, sources):
         whitened = whiten(spectra)
@@ -63,8 +74,8 @@
         local_spec = jnp.einsum(
             "pc,xscf->xpsf", onehot, whitened, preferred_element_type=jnp.float32
         ).astype(jnp.bfloat16)
-        for axis in reduce_order:
-            local_spec = lax.psum(local_spec, axis)
+        for axis, size in reduce_order:
+            local_spec = exchange_sum(local_spec, axis, size)
         source_spec = lax.all_gather(local_spec, "seg", axis=2, tiled=True)
         return correlate(source_spec, regrouped, lag_table)
 
@@ -80,7 +91,7 @@
         chan_axes, reduce_order = CHAN_AXES, REDUCE_ORDER
     else:
         fine = mesh
-        chan_axes, reduce_order = "chan", ("chan",)
+        chan_axes, reduce_order = "chan", (("chan", chan),)
     placed = (P(None, "seg", chan_axes, None), P())
     return jax.shard_map(
         make_shards(chan_axes, reduce_order),

time: 358 us -> 261 us (0.73)
  waiting for transfers between devices: 282 us -> 139 us
  starting transfers between devices: 5.1 us -> 49.8 us
    psum x4 -> x0, waiting for transfers between devices: 236 us -> none  [shards(): local_spec = lax.psum(local_spec, axis)]
    ppermute x0 -> x7, waiting for transfers between devices: none -> 96 us  [exchange_sum(): value = value + lax.ppermute(value, axis, pairs)]
    ppermute x0 -> x7, starting transfers between devices: none -> 30.8 us  [exchange_sum(): value = value + lax.ppermute(value, axis, pairs)]
    all_to_all x1, starting transfers between devices: 4.95 us -> 19 us  [shards(): lax.all_to_all(whitened, 'seg', split_axis=2, concat_axis=1, tiled=True)]
  transfers between devices with their start and end apart: 6 -> 9, of which waited for: 6 -> 9; matrix products, arithmetic and copies ran while one was open for 2% -> 3% of each run, Pallas kernels for 0% -> 0%
where the time goes in v2:
time: 261 us
  waiting for transfers between devices  139 us (53%)
  starting transfers between devices  49.8 us (19%)
  local copies, waits for them, and re-layouts  26.2 us (10%)
  matrix products  21.9 us (8%)
  between operations  13.6 us (5%)
  other arithmetic  10.4 us (4%)
    ppermute x7, waiting for transfers between devices, exchange_sum(): value = value + lax.ppermute(value, axis, pairs)  96 us
    all_gather x1, waiting for transfers between devices, shards(): source_spec = lax.all_gather(local_spec, 'seg', axis=2, tiled=True)  36.4 us
    ppermute x7, starting transfers between devices, exchange_sum(): value = value + lax.ppermute(value, axis, pairs)  30.8 us
    all_to_all x1, starting transfers between devices, shards(): lax.all_to_all(whitened, 'seg', split_axis=2, concat_axis=1, tiled=True)  19 us
    squeeze x2, local copies, waits for them, and re-layouts, correlate(): source_spec[1]  9.54 us
    squeeze x1, local copies, waits for them, and re-layouts, correlate(): source_spec[0]  8.6 us
    all_to_all x1, waiting for transfers between devices, shards(): lax.all_to_all(whitened, 'seg', split_axis=2, concat_axis=1, tiled=True)  6.48 us
    dot_general x1, matrix products, correlate(): jnp.einsum('pkf,krf->prf', source_spec[1], receiver_spec[0], preferred_el...  5.82 us
  transfers between devices with their start and end apart: 9, of which 9 were waited for; matrix products, arithmetic and copies ran while one was open for 3% of the time, Pallas kernels for 0%

profile of v2, /device:TPU:1, one launch (start us, length us, event | category | flops | bytes accessed | tf_op | source)
XLA Modules:
  0.0 260.8 jit_solution(5652770719042452872)
XLA Ops:
  11.6 8.8 %collective-permute-start = (bf16[2,32,8,512]{3,1,2,0:T(8,128)(2,1)S(1)}, bf16[2,32,8,512]{3,1,2,0:T(8,128)(2,1)S(1)}, u32[]{:S(2)}, u32[]{:S(2)}) collective-permute-start(bf16[2,32,8,512]{3,1,2,0:T(8,128)(2,1)S(1)} %fusion.4), channel_id=1, source_target_pairs={{0,4},{4,0},{1,5},{5,1},{2,6},{6,2},{3,7},{7,3},{8,12},{12,8},{9,1... | collective-permute-start | bytes 1572872 | tf_op jit(solution)/shard_map/ppermute | solution.py:57
  24.0 13.1 %collective-permute-done.1 = bf16[2,32,8,512]{3,1,2,0:T(8,128)(2,1)S(1)} collective-permute-done((bf16[2,32,8,512]{3,1,2,0:T(8,128)(2,1)S(1)}, bf16[2,32,8,512]{3,1,2,0:T(8,128)(2,1)S(1)}, u32[]{:S(2)}, u32[]{:S(2)}) %collective-permute-start.1) | collective-permute-done | bytes 524320 | tf_op jit(solution)/shard_map/ppermute | solution.py:57
  39.2 25.9 %collective-permute-done.2 = bf16[2,32,8,512]{3,1,2,0:T(8,128)(2,1)S(1)} collective-permute-done((bf16[2,32,8,512]{3,1,2,0:T(8,128)(2,1)S(1)}, bf16[2,32,8,512]{3,1,2,0:T(8,128)(2,1)S(1)}, u32[]{:S(2)}, u32[]{:S(2)}) %collective-permute-start.2) | collective-permute-done | bytes 524320 | tf_op jit(solution)/shard_map/ppermute | solution.py:57
  67.2 25.2 %collective-permute-done.3 = bf16[2,32,8,512]{3,1,2,0:T(8,128)(2,1)S(1)} collective-permute-done((bf16[2,32,8,512]{3,1,2,0:T(8,128)(2,1)S(1)}, bf16[2,32,8,512]{3,1,2,0:T(8,128)(2,1)S(1)}, u32[]{:S(2)}, u32[]{:S(2)}) %collective-permute-start.3) | collective-permute-done | bytes 524320 | tf_op jit(solution)/shard_map/ppermute | solution.py:57
  92.6 8.4 %collective-permute-start.4 = (bf16[2,32,8,512]{3,1,2,0:T(8,128)(2,1)S(1)}, bf16[2,32,8,512]{3,1,2,0:T(8,128)(2,1)S(1)}, u32[]{:S(2)}, u32[]{:S(2)}) collective-permute-start(bf16[2,32,8,512]{3,1,2,0:T(8,128)(2,1)S(1)} %add.72), channel_id=1, source_target_pairs={{0,64},{64,0},{1,65},{65,1},{2,66},{66,2},{3,67},{67,3},{4,68},{68... | collective-permute-start | bytes 1572872 | tf_op jit(solution)/shard_map/ppermute | solution.py:57
  101.0 11.0 %collective-permute-done.4 = bf16[2,32,8,512]{3,1,2,0:T(8,128)(2,1)S(1)} collective-permute-done((bf16[2,32,8,512]{3,1,2,0:T(8,128)(2,1)S(1)}, bf16[2,32,8,512]{3,1,2,0:T(8,128)(2,1)S(1)}, u32[]{:S(2)}, u32[]{:S(2)}) %collective-permute-start.4) | collective-permute-done | bytes 524320 | tf_op jit(solution)/shard_map/ppermute | solution.py:57
  112.1 3.1 %collective-permute-start.5 = (bf16[2,32,8,512]{3,1,2,0:T(8,128)(2,1)S(1)}, bf16[2,32,8,512]{3,1,2,0:T(8,128)(2,1)S(1)}, u32[]{:S(2)}, u32[]{:S(2)}) collective-permute-start(bf16[2,32,8,512]{3,1,2,0:T(8,128)(2,1)S(1)} %add.73), channel_id=1, source_target_pairs={{0,128},{128,0},{256,384},{384,256},{1,129},{129,1},{257,385},{385... | collective-permute-start | bytes 1572872 | tf_op jit(solution)/shard_map/ppermute | solution.py:57
  115.3 10.1 %collective-permute-done.5 = bf16[2,32,8,512]{3,1,2,0:T(8,128)(2,1)S(1)} collective-permute-done((bf16[2,32,8,512]{3,1,2,0:T(8,128)(2,1)S(1)}, bf16[2,32,8,512]{3,1,2,0:T(8,128)(2,1)S(1)}, u32[]{:S(2)}, u32[]{:S(2)}) %collective-permute-start.5) | collective-permute-done | bytes 524320 | tf_op jit(solution)/shard_map/ppermute | solution.py:57
  125.6 4.7 %collective-permute-start.6 = (bf16[2,32,8,512]{3,1,2,0:T(8,128)(2,1)S(1)}, bf16[2,32,8,512]{3,1,2,0:T(8,128)(2,1)S(1)}, u32[]{:S(2)}, u32[]{:S(2)}) collective-permute-start(bf16[2,32,8,512]{3,1,2,0:T(8,128)(2,1)S(1)} %add.74), channel_id=1, source_target_pairs={{0,256},{128,384},{256,0},{384,128},{1,257},{129,385},{257,1},{385... | collective-permute-start | bytes 1572872 | tf_op jit(solution)/shard_map/ppermute | solution.py:57
  130.3 9.2 %collective-permute-done.6 = bf16[2,32,8,512]{3,1,2,0:T(8,128)(2,1)S(1)} collective-permute-done((bf16[2,32,8,512]{3,1,2,0:T(8,128)(2,1)S(1)}, bf16[2,32,8,512]{3,1,2,0:T(8,128)(2,1)S(1)}, u32[]{:S(2)}, u32[]{:S(2)}) %collective-permute-start.6) | collective-permute-done | bytes 524320 | tf_op jit(solution)/shard_map/ppermute | solution.py:57
  140.4 19.0 %all-to-all-start = ((bf16[2,8,32,512]{3,1,0,2:T(8,128)(2,1)}), bf16[2,8,32,512]{3,1,0,2:T(8,128)(2,1)S(1)}, u32[]{:S(2)}, u32[]{:S(2)}) async-start(bf16[2,8,32,512]{3,1,0,2:T(8,128)(2,1)} %multiply_convert_fusion), calls=%async_computation | async-start | bytes 1048576 | tf_op jit(solution)/shard_map/all_to_all | solution.py:65
  159.4 5.1 %fusion.22 = (f32[512,512]{1,0:T(8,128)}, f32[512,512]{1,0:T(8,128)}) fusion(s32[512]{0:T(512)S(1)} %iota_add_fusion), kind=kLoop, calls=%fused_computation.33 | loop fusion | flops 3932160 | bytes 2099200 | tf_op jit(solution)/shard_map/cos | solution.py:27
  164.5 6.5 %all-to-all-done = bf16[2,8,32,512]{3,1,0,2:T(8,128)(2,1)S(1)} async-done(((bf16[2,8,32,512]{3,1,0,2:T(8,128)(2,1)}), bf16[2,8,32,512]{3,1,0,2:T(8,128)(2,1)S(1)}, u32[]{:S(2)}, u32[]{:S(2)}) %all-to-all-start) | async-done | bytes 524320 | tf_op jit(solution)/shard_map/all_to_all | solution.py:65
  173.1 36.4 %all-gather.2.cloned.1.call-done = bf16[2,32,32,512]{3,1,2,0:T(8,128)(2,1)} async-done(((bf16[2,32,8,512]{3,1,2,0:T(8,128)(2,1)}), bf16[2,32,32,512]{3,1,2,0:T(8,128)(2,1)}) %all-gather.2.cloned.1.call-update) | async-done | bytes 2097168 | tf_op jit(solution)/shard_map/all_gather | solution.py:79
  209.5 2.7 %slice_bitcast_fusion = (bf16[32,32,512]{2,0,1:T(8,128)(2,1)S(1)}, bf16[32,32,512]{2,0,1:T(8,128)(2,1)}) fusion(bf16[2,32,32,512]{3,1,2,0:T(8,128)(2,1)} %all-gather.2.cloned.1.call-done), kind=kLoop, calls=%fused_computation.16 | loop fusion | bytes 4194304 | tf_op jit(solution)/shard_map/squeeze | solution.py:36
  212.2 8.6 %copy.39 = bf16[32,32,512]{1,0,2:T(8,128)(2,1)} copy(bf16[32,32,512]{2,0,1:T(8,128)(2,1)} %get-tuple-element.6) | data formatting | bytes 2097152 | tf_op jit(solution)/shard_map/squeeze | solution.py:34
  220.8 6.8 %copy.42 = bf16[32,32,512]{1,0,2:T(8,128)(2,1)} copy(bf16[32,32,512]{2,0,1:T(8,128)(2,1)S(1)} %get-tuple-element.5) | data formatting | bytes 2097152 | tf_op jit(solution)/shard_map/squeeze | solution.py:36
  227.6 4.6 %fusion.30 = f32[512,8,32]{2,1,0:T(8,128)S(1)} fusion(bf16[32,8,512]{0,1,2:T(8,128)(2,1)S(1)} %copy.38, bf16[32,32,512]{1,0,2:T(8,128)(2,1)} %copy.39), kind=kOutput, calls=%fused_computation.44 | convolution fusion | flops 8388608 | bytes 1835008 | tf_op jit(solution)/shard_map/pkf,krf->prf/dot_general | solution.py:33
  232.2 3.7 %fusion.31 = f32[512,8,32]{2,1,0:T(8,128)} fusion(bf16[32,8,512]{0,1,2:T(8,128)(2,1)S(1)} %copy.41, bf16[32,32,512]{1,0,2:T(8,128)(2,1)S(1)} %copy-done.1), kind=kOutput, calls=%fused_computation.45 | convolution fusion | flops 8388608 | bytes 1835008 | tf_op jit(solution)/shard_map/pkf,krf->prf/dot_general | solution.py:38
  235.9 3.6 %add_bitcast_fusion = f32[32,8,512]{0,1,2:T(8,128)} fusion(f32[512,8,32]{2,1,0:T(8,128)S(1)} %fusion.30, bf16[32,8,512]{0,1,2:T(8,128)(2,1)S(1)} %copy.41, bf16[32,32,512]{1,0,2:T(8,128)(2,1)S(1)} %copy-done), kind=kOutput, calls=%fused_computation.5 | convolution fusion | flops 8519680 | bytes 2359296 | tf_op jit(solution)/shard_map/pkf,krf->prf/dot_general | solution.py:35
  239.5 3.3 %copy.43 = f32[32,8,512]{2,1,0:T(8,128)} copy(f32[32,8,512]{0,1,2:T(8,128)} %add_bitcast_fusion) | data formatting | bytes 1048576 | tf_op jit(solution)/shard_map/add | solution.py:33
  242.8 5.8 %subtract_bitcast_fusion = f32[32,8,512]{0,1,2:T(8,128)} fusion(f32[512,8,32]{2,1,0:T(8,128)S(1)} %copy-done.2, bf16[32,8,512]{0,1,2:T(8,128)(2,1)S(1)} %copy.38, bf16[32,32,512]{1,0,2:T(8,128)(2,1)} %copy.42), kind=kOutput, calls=%fused_computation.4 | convolution fusion | flops 8519680 | bytes 2359296 | tf_op jit(solution)/shard_map/pkf,krf->prf/dot_general | solution.py:40
  248.6 2.5 copy.48
  251.2 2.8 %fusion.8 = f32[32,8,512]{2,1,0:T(8,128)} fusion(f32[512,512]{1,0:T(8,128)S(1)} %copy-done.4, f32[512,512]{1,0:T(8,128)S(1)} %copy-done.3, f32[256,512]{1,0:T(8,128)S(1)} %bitcast.35, f32[256,512]{1,0:T(8,128)S(1)} %bitcast.34), kind=kOutput, calls=%fused_computation.12 | convolution fusion | flops 1611792384 | bytes 3670016 | tf_op jit(solution)/shard_map/dot_general | solution.py:45
  (42 shorter events, 16.4 us)
Async XLA Ops:
  6.5 2.4 copy-start.6
  6.5 202.9 %all-gather.2.cloned.1.call-start = ((), (), s32[]{:S(2)}) async-start(), calls=%async_computation.1 | async-start | bytes 2621440 | tf_op jit(solution)/shard_map/all_gather | solution.py:79
  11.6 10.3 %collective-permute-start = (bf16[2,32,8,512]{3,1,2,0:T(8,128)(2,1)S(1)}, bf16[2,32,8,512]{3,1,2,0:T(8,128)(2,1)S(1)}, u32[]{:S(2)}, u32[]{:S(2)}) collective-permute-start(bf16[2,32,8,512]{3,1,2,0:T(8,128)(2,1)S(1)} %fusion.4), channel_id=1, source_target_pairs={{0,4},{4,0},{1,5},{5,1},{2,6},{6,2},{3,7},{7,3},{8,12},{12,8},{9,1... | collective-permute-start | bytes 1572872 | tf_op jit(solution)/shard_map/ppermute | solution.py:57
  22.0 15.0 %collective-permute-start.1 = (bf16[2,32,8,512]{3,1,2,0:T(8,128)(2,1)S(1)}, bf16[2,32,8,512]{3,1,2,0:T(8,128)(2,1)S(1)}, u32[]{:S(2)}, u32[]{:S(2)}) collective-permute-start(bf16[2,32,8,512]{3,1,2,0:T(8,128)(2,1)S(1)} %add.69), channel_id=1, source_target_pairs={{0,8},{8,0},{16,24},{24,16},{32,40},{40,32},{48,56},{56,48},{1,9},... | collective-permute-start | bytes 1572872 | tf_op jit(solution)/shard_map/ppermute | solution.py:57
  37.2 27.8 %collective-permute-start.2 = (bf16[2,32,8,512]{3,1,2,0:T(8,128)(2,1)S(1)}, bf16[2,32,8,512]{3,1,2,0:T(8,128)(2,1)S(1)}, u32[]{:S(2)}, u32[]{:S(2)}) collective-permute-start(bf16[2,32,8,512]{3,1,2,0:T(8,128)(2,1)S(1)} %add.70), channel_id=1, source_target_pairs={{0,16},{8,24},{16,0},{24,8},{32,48},{40,56},{48,32},{56,40},{1,17}... | collective-permute-start | bytes 1572872 | tf_op jit(solution)/shard_map/ppermute | solution.py:57
  65.2 27.2 %collective-permute-start.3 = (bf16[2,32,8,512]{3,1,2,0:T(8,128)(2,1)S(1)}, bf16[2,32,8,512]{3,1,2,0:T(8,128)(2,1)S(1)}, u32[]{:S(2)}, u32[]{:S(2)}) collective-permute-start(bf16[2,32,8,512]{3,1,2,0:T(8,128)(2,1)S(1)} %add.71), channel_id=1, source_target_pairs={{0,32},{8,40},{16,48},{24,56},{32,0},{40,8},{48,16},{56,24},{1,33}... | collective-permute-start | bytes 1572872 | tf_op jit(solution)/shard_map/ppermute | solution.py:57
  92.6 19.4 %collective-permute-start.4 = (bf16[2,32,8,512]{3,1,2,0:T(8,128)(2,1)S(1)}, bf16[2,32,8,512]{3,1,2,0:T(8,128)(2,1)S(1)}, u32[]{:S(2)}, u32[]{:S(2)}) collective-permute-start(bf16[2,32,8,512]{3,1,2,0:T(8,128)(2,1)S(1)} %add.72), channel_id=1, source_target_pairs={{0,64},{64,0},{1,65},{65,1},{2,66},{66,2},{3,67},{67,3},{4,68},{68... | collective-permute-start | bytes 1572872 | tf_op jit(solution)/shard_map/ppermute | solution.py:57
  112.1 13.3 %collective-permute-start.5 = (bf16[2,32,8,512]{3,1,2,0:T(8,128)(2,1)S(1)}, bf16[2,32,8,512]{3,1,2,0:T(8,128)(2,1)S(1)}, u32[]{:S(2)}, u32[]{:S(2)}) collective-permute-start(bf16[2,32,8,512]{3,1,2,0:T(8,128)(2,1)S(1)} %add.73), channel_id=1, source_target_pairs={{0,128},{128,0},{256,384},{384,256},{1,129},{129,1},{257,385},{385... | collective-permute-start | bytes 1572872 | tf_op jit(solution)/shard_map/ppermute | solution.py:57
  125.6 13.9 %collective-permute-start.6 = (bf16[2,32,8,512]{3,1,2,0:T(8,128)(2,1)S(1)}, bf16[2,32,8,512]{3,1,2,0:T(8,128)(2,1)S(1)}, u32[]{:S(2)}, u32[]{:S(2)}) collective-permute-start(bf16[2,32,8,512]{3,1,2,0:T(8,128)(2,1)S(1)} %add.74), channel_id=1, source_target_pairs={{0,256},{128,384},{256,0},{384,128},{1,257},{129,385},{257,1},{385... | collective-permute-start | bytes 1572872 | tf_op jit(solution)/shard_map/ppermute | solution.py:57
  140.4 30.5 %all-to-all-start = ((bf16[2,8,32,512]{3,1,0,2:T(8,128)(2,1)}), bf16[2,8,32,512]{3,1,0,2:T(8,128)(2,1)S(1)}, u32[]{:S(2)}, u32[]{:S(2)}) async-start(bf16[2,8,32,512]{3,1,0,2:T(8,128)(2,1)} %multiply_convert_fusion), calls=%async_computation | async-start | bytes 1048576 | tf_op jit(solution)/shard_map/all_to_all | solution.py:65
  227.6 4.6 %copy-start.1 = (bf16[32,32,512]{1,0,2:T(8,128)(2,1)S(1)}, bf16[32,32,512]{1,0,2:T(8,128)(2,1)}, u32[]{:S(2)}) copy-start(bf16[32,32,512]{1,0,2:T(8,128)(2,1)} %copy.39) | copy-start | bytes 3145732
  232.2 3.7 %copy-start = (bf16[32,32,512]{1,0,2:T(8,128)(2,1)S(1)}, bf16[32,32,512]{1,0,2:T(8,128)(2,1)}, u32[]{:S(2)}) copy-start(bf16[32,32,512]{1,0,2:T(8,128)(2,1)} %copy.42) | copy-start | bytes 3145732
  239.5 3.3 %copy-start.2 = (f32[512,8,32]{2,1,0:T(8,128)S(1)}, f32[512,8,32]{2,1,0:T(8,128)}, u32[]{:S(2)}) copy-start(f32[512,8,32]{2,1,0:T(8,128)} %fusion.31) | copy-start | bytes 1572868
  248.6 2.6 copy-start.3
  248.6 2.6 copy-start.4
  248.6 2.6 copy-start.5
Sparse Core Ops, SparseCore 0:
  140.5 68.8 all-gather.1

commit v3 on v1

--- a/solution.py
+++ b/solution.py
@@ -8,7 +8,7 @@
 LAGS = 256
 CHAN_FACTORS = (("x", 4), ("zh", 2), ("y", 8), ("c", 2))
 CHAN_AXES = tuple(name for name, _ in CHAN_FACTORS)
-REDUCE_ORDER = ("c", "y", "zh", "x")
+REDUCE_STEPS = (("c", 2, 1), ("y", 8, 1), ("x", 4, 1), ("y", 8, 2), ("x", 4, 2), ("zh", 2, 1), ("y", 8, 4))
 
 
 def whiten(spectra):
@@ -48,6 +48,38 @@
     return result.reshape(stacked.shape[0], stacked.shape[1], -1)
 
 
+def halving_steps(chan_order):
+    steps = []
+    for axis, size in chan_order:
+        bit = 1
+        while bit < size:
+            steps.append((axis, size, bit))
+            bit *= 2
+    return steps
+
+
+def chan_allreduce(value, steps):
+    rows = value.shape[0]
+    pieces = []
+    for axis, size, bit in steps:
+        mine = (lax.axis_index(axis) // bit) % 2 == 1
+        half = value.shape[0] // 2
+        low, high = value[:half], value[half:]
+        keep = jnp.where(mine, high, low)
+        send = jnp.where(mine, low, high)
+        pairs = [(i, i ^ bit) for i in range(size)]
+        value = keep + lax.ppermute(send, axis, pairs)
+        pieces.append((axis, size, bit, mine))
+    for axis, size, bit, mine in reversed(pieces):
+        pairs = [(i, i ^ bit) for i in range(size)]
+        other = lax.ppermute(value, axis, pairs)
+        value = jnp.concatenate(
+            [jnp.where(mine, other, value), jnp.where(mine, value, other)], axis=0
+        )
+    assert value.shape[0] == rows
+    return value
+
+
 def make_shards(chan_axes, reduce_order):
     def shards(spectra, sources):
         whitened = whiten(spectra)
@@ -63,8 +95,9 @@
         local_spec = jnp.einsum(
             "pc,xscf->xpsf", onehot, whitened, preferred_element_type=jnp.float32
         ).astype(jnp.bfloat16)
-        for axis in reduce_order:
-            local_spec = lax.psum(local_spec, axis)
+        shape = local_spec.shape
+        steps = reduce_order
+        local_spec = chan_allreduce(local_spec.reshape(-1, shape[-1]), steps).reshape(shape)
         source_spec = lax.all_gather(local_spec, "seg", axis=2, tiled=True)
         return correlate(source_spec, regrouped, lag_table)
 
@@ -77,10 +110,10 @@
     if math.prod(sizes) == chan:
         devices = mesh.devices.reshape(sizes + (mesh.shape["seg"],))
         fine = Mesh(devices, CHAN_AXES + ("seg",))
-        chan_axes, reduce_order = CHAN_AXES, REDUCE_ORDER
+        chan_axes, reduce_order = CHAN_AXES, REDUCE_STEPS
     else:
         fine = mesh
-        chan_axes, reduce_order = "chan", ("chan",)
+        chan_axes, reduce_order = "chan", halving_steps((("chan", chan),))
     placed = (P(None, "seg", chan_axes, None), P())
     return jax.shard_map(
         make_shards(chan_axes, reduce_order),

time: 358 us -> 224 us (0.63)
  waiting for transfers between devices: 282 us -> 85.7 us
  starting transfers between devices: 5.1 us -> 65.3 us
    psum x4 -> x0, waiting for transfers between devices: 236 us -> none  [shards(): local_spec = lax.psum(local_spec, axis)]
    ppermute x0 -> x14, starting transfers between devices: none -> 61.8 us  [the longest x7 34.9 us: chan_allreduce(): other = lax.ppermute(value, axis, pairs)]
    ppermute x0 -> x14, waiting for transfers between devices: none -> 43.7 us  [the longest x7 23 us: chan_allreduce(): value = keep + lax.ppermute(send, axis, pairs)]
    squeeze x3 -> x0, local copies, waits for them, and re-layouts: 18.1 us -> none  [the longest x2 9.56 us: correlate(): source_spec[1]]
    unnamed x14 -> x16, local copies, waits for them, and re-layouts: 0.03 us -> 15.5 us
    all_gather x1, waiting for transfers between devices: 39.8 us -> 32.9 us  [shards(): source_spec = lax.all_gather(local_spec, 'seg', axis=2, tiled=True)]
  transfers between devices with their start and end apart: 6 -> 16, of which waited for: 6 -> 16; matrix products, arithmetic and copies ran while one was open for 2% -> 3% of each run, Pallas kernels for 0% -> 0%
where the time goes in v3:
time: 224 us; the launch traced here: 223 us
  waiting for transfers between devices  85.7 us (38%)
  starting transfers between devices  65.3 us (29%)
  local copies, waits for them, and re-layouts  27.4 us (12%)
  matrix products  22 us (10%)
  between operations  13.9 us (6%)
  other arithmetic  9.1 us (4%)
    ppermute x7, starting transfers between devices, chan_allreduce(): other = lax.ppermute(value, axis, pairs)  34.9 us
    all_gather x1, waiting for transfers between devices, shards(): source_spec = lax.all_gather(local_spec, 'seg', axis=2, tiled=True)  32.9 us
    ppermute x7, starting transfers between devices, chan_allreduce(): value = keep + lax.ppermute(send, axis, pairs)  26.8 us
    ppermute x7, waiting for transfers between devices, chan_allreduce(): value = keep + lax.ppermute(send, axis, pairs)  23 us
    ppermute x7, waiting for transfers between devices, chan_allreduce(): other = lax.ppermute(value, axis, pairs)  20.7 us
    unnamed x16, local copies, waits for them, and re-layouts  15.5 us
    all_to_all x1, waiting for transfers between devices, shards(): lax.all_to_all(whitened, 'seg', split_axis=2, concat_axis=1, tiled=True)  9.09 us
    dot_general x1, matrix products, correlate(): jnp.einsum('pkf,krf->prf', source_spec[0], receiver_spec[1], preferred_el...  5.84 us
  transfers between devices with their start and end apart: 16, of which 16 were waited for; matrix products, arithmetic and copies ran while one was open for 3% of the time, Pallas kernels for 0%

profile of v3, /device:TPU:1, one launch (start us, length us, event | category | flops | bytes accessed | tf_op | source)
XLA Modules:
  0.0 223.3 jit_solution(11426825025840136855)
XLA Ops:
  11.8 8.8 %collective-permute-start = (bf16[256,512]{1,0:T(8,128)(2,1)S(1)}, bf16[256,512]{1,0:T(8,128)(2,1)S(1)}, u32[]{:S(2)}, u32[]{:S(2)}) collective-permute-start(bf16[256,512]{1,0:T(8,128)(2,1)S(1)} %bitcast.52), channel_id=1, source_target_pairs={{0,4},{4,0},{1,5},{5,1},{2,6},{6,2},{3,7},{7,3},{8,12},{12,8},{9,1... | collective-permute-start | bytes 786440 | tf_op jit(solution)/shard_map/ppermute | solution.py:71
  23.8 4.7 %collective-permute-done.1 = bf16[128,512]{1,0:T(8,128)(2,1)S(1)} collective-permute-done((bf16[128,512]{1,0:T(8,128)(2,1)S(1)}, bf16[128,512]{1,0:T(8,128)(2,1)S(1)}, u32[]{:S(2)}, u32[]{:S(2)}) %collective-permute-start.1) | collective-permute-done | bytes 131104 | tf_op jit(solution)/shard_map/ppermute | solution.py:71
  35.5 3.9 %collective-permute-done.3 = bf16[32,512]{1,0:T(8,128)(2,1)S(1)} collective-permute-done((bf16[32,512]{1,0:T(8,128)(2,1)S(1)}, bf16[32,512]{1,0:T(8,128)(2,1)S(1)}, u32[]{:S(2)}, u32[]{:S(2)}) %collective-permute-start.3) | collective-permute-done | bytes 32800 | tf_op jit(solution)/shard_map/ppermute | solution.py:71
  41.5 4.0 %collective-permute-done.4 = bf16[16,512]{1,0:T(8,128)(2,1)S(1)} collective-permute-done((bf16[16,512]{1,0:T(8,128)(2,1)S(1)}, bf16[16,512]{1,0:T(8,128)(2,1)S(1)}, u32[]{:S(2)}, u32[]{:S(2)}) %collective-permute-start.4) | collective-permute-done | bytes 16416 | tf_op jit(solution)/shard_map/ppermute | solution.py:71
  45.5 4.9 %collective-permute-start.5 = (bf16[8,512]{1,0:T(8,128)(2,1)S(1)}, bf16[8,512]{1,0:T(8,128)(2,1)S(1)}, u32[]{:S(2)}, u32[]{:S(2)}) collective-permute-start(bf16[8,512]{1,0:T(8,128)(2,1)S(1)} %broadcast_select_fusion.18), channel_id=1, source_target_pairs={{0,64},{64,0},{1,65},{65,1},{2,66},{66,2},{3,67},{67,3},{4,68},{68... | collective-permute-start | bytes 24584 | tf_op jit(solution)/shard_map/ppermute | solution.py:71
  50.5 3.4 %collective-permute-done.5 = bf16[8,512]{1,0:T(8,128)(2,1)S(1)} collective-permute-done((bf16[8,512]{1,0:T(8,128)(2,1)S(1)}, bf16[8,512]{1,0:T(8,128)(2,1)S(1)}, u32[]{:S(2)}, u32[]{:S(2)}) %collective-permute-start.5) | collective-permute-done | bytes 8224 | tf_op jit(solution)/shard_map/ppermute | solution.py:71
  53.8 5.4 %collective-permute-start.6 = (bf16[4,512]{1,0:T(4,128)(2,1)S(1)}, bf16[4,512]{1,0:T(4,128)(2,1)S(1)}, u32[]{:S(2)}, u32[]{:S(2)}) collective-permute-start(bf16[4,512]{1,0:T(4,128)(2,1)S(1)} %broadcast_select_fusion.21), channel_id=1, source_target_pairs={{0,32},{8,40},{16,48},{24,56},{32,0},{40,8},{48,16},{56,24},{1,33}... | collective-permute-start | bytes 12296 | tf_op jit(solution)/shard_map/ppermute | solution.py:71
  62.1 5.4 %collective-permute-start.7 = (bf16[4,512]{1,0:T(4,128)(2,1)S(1)}, bf16[4,512]{1,0:T(4,128)(2,1)S(1)}, u32[]{:S(2)}, u32[]{:S(2)}) collective-permute-start(bf16[4,512]{1,0:T(4,128)(2,1)S(1)} %select_add_fusion.5), channel_id=1, source_target_pairs={{0,32},{8,40},{16,48},{24,56},{32,0},{40,8},{48,16},{56,24},{1,33}... | collective-permute-start | bytes 12296 | tf_op jit(solution)/shard_map/ppermute | solution.py:75
  70.4 5.4 %collective-permute-start.8 = (bf16[8,512]{1,0:T(8,128)(2,1)S(1)}, bf16[8,512]{1,0:T(8,128)(2,1)S(1)}, u32[]{:S(2)}, u32[]{:S(2)}) collective-permute-start(bf16[8,512]{1,0:T(8,128)(2,1)S(1)} %pad_maximum_fusion.6), channel_id=1, source_target_pairs={{0,64},{64,0},{1,65},{65,1},{2,66},{66,2},{3,67},{67,3},{4,68},{68... | collective-permute-start | bytes 24584 | tf_op jit(solution)/shard_map/ppermute | solution.py:75
  81.6 3.1 %collective-permute-done.9 = bf16[16,512]{1,0:T(8,128)(2,1)S(1)} collective-permute-done((bf16[16,512]{1,0:T(8,128)(2,1)S(1)}, bf16[16,512]{1,0:T(8,128)(2,1)S(1)}, u32[]{:S(2)}, u32[]{:S(2)}) %collective-permute-start.9) | collective-permute-done | bytes 16416 | tf_op jit(solution)/shard_map/ppermute | solution.py:75
  86.7 3.8 %collective-permute-done.10 = bf16[32,512]{1,0:T(8,128)(2,1)S(1)} collective-permute-done((bf16[32,512]{1,0:T(8,128)(2,1)S(1)}, bf16[32,512]{1,0:T(8,128)(2,1)S(1)}, u32[]{:S(2)}, u32[]{:S(2)}) %collective-permute-start.10) | collective-permute-done | bytes 32800 | tf_op jit(solution)/shard_map/ppermute | solution.py:75
  97.5 4.1 %collective-permute-done.12 = bf16[128,512]{1,0:T(8,128)(2,1)S(1)} collective-permute-done((bf16[128,512]{1,0:T(8,128)(2,1)S(1)}, bf16[128,512]{1,0:T(8,128)(2,1)S(1)}, u32[]{:S(2)}, u32[]{:S(2)}) %collective-permute-start.12) | collective-permute-done | bytes 131104 | tf_op jit(solution)/shard_map/ppermute | solution.py:75
  101.7 15.2 %collective-permute-start.13 = (bf16[256,512]{1,0:T(8,128)(2,1)S(1)}, bf16[256,512]{1,0:T(8,128)(2,1)S(1)}, u32[]{:S(2)}, u32[]{:S(2)}) collective-permute-start(bf16[256,512]{1,0:T(8,128)(2,1)S(1)} %pad_maximum_fusion.1), channel_id=1, source_target_pairs={{0,4},{4,0},{1,5},{5,1},{2,6},{6,2},{3,7},{7,3},{8,12},{12,8},{9,1... | collective-permute-start | bytes 786440 | tf_op jit(solution)/shard_map/ppermute | solution.py:75
  119.2 3.5 %all-to-all-start = ((bf16[2,8,32,512]{3,1,0,2:T(8,128)(2,1)}), bf16[2,8,32,512]{3,1,0,2:T(8,128)(2,1)S(1)}, u32[]{:S(2)}, u32[]{:S(2)}) async-start(bf16[2,8,32,512]{3,1,0,2:T(8,128)(2,1)} %multiply_convert_fusion), calls=%async_computation | async-start | bytes 1048576 | tf_op jit(solution)/shard_map/all_to_all | solution.py:86
  122.7 5.1 %fusion.34 = (f32[512,512]{1,0:T(8,128)}, f32[512,512]{1,0:T(8,128)}) fusion(s32[512]{0:T(512)S(1)} %iota_add_fusion), kind=kLoop, calls=%fused_computation.40 | loop fusion | flops 3932160 | bytes 2099200 | tf_op jit(solution)/shard_map/cos | solution.py:27
  127.8 9.1 %all-to-all-done = bf16[2,8,32,512]{3,1,0,2:T(8,128)(2,1)S(1)} async-done(((bf16[2,8,32,512]{3,1,0,2:T(8,128)(2,1)}), bf16[2,8,32,512]{3,1,0,2:T(8,128)(2,1)S(1)}, u32[]{:S(2)}, u32[]{:S(2)}) %all-to-all-start) | async-done | bytes 524320 | tf_op jit(solution)/shard_map/all_to_all | solution.py:86
  139.0 32.9 %all-gather.2.cloned.1.call-done = bf16[2,32,32,512]{3,1,0,2:T(8,128)(2,1)} async-done(((bf16[2,32,8,512]{3,1,0,2:T(8,128)(2,1)}), bf16[2,32,32,512]{3,1,0,2:T(8,128)(2,1)}) %all-gather.2.cloned.1.call-update) | async-done | bytes 2097168 | tf_op jit(solution)/shard_map/all_gather | solution.py:101
  174.6 8.6 %copy.46 = bf16[1,32,32,512]{2,1,3,0:T(8,128)(2,1)} copy(bf16[1,32,32,512]{3,1,0,2:T(8,128)(2,1)} %get-tuple-element.6) | data formatting | bytes 2097152
  183.3 6.8 %copy.45 = bf16[1,32,32,512]{2,1,3,0:T(8,128)(2,1)} copy(bf16[1,32,32,512]{3,1,0,2:T(8,128)(2,1)S(1)} %get-tuple-element.5) | data formatting | bytes 2097152
  190.1 4.6 %fusion.2 = f32[512,8,32]{2,1,0:T(8,128)S(1)} fusion(bf16[32,8,512]{0,1,2:T(8,128)(2,1)S(1)} %copy.39, bf16[1,32,32,512]{2,1,3,0:T(8,128)(2,1)} %copy.46), kind=kOutput, calls=%fused_computation.2 | convolution fusion | flops 8388608 | bytes 1835008 | tf_op jit(solution)/shard_map/pkf,krf->prf/dot_general | solution.py:35
  194.7 3.7 %fusion = f32[512,8,32]{2,1,0:T(8,128)} fusion(bf16[32,8,512]{0,1,2:T(8,128)(2,1)S(1)} %copy.36, bf16[1,32,32,512]{2,1,3,0:T(8,128)(2,1)S(1)} %copy-done.1), kind=kOutput, calls=%fused_computation | convolution fusion | flops 8388608 | bytes 1835008 | tf_op jit(solution)/shard_map/pkf,krf->prf/dot_general | solution.py:40
  198.4 3.7 %add_bitcast_fusion = f32[32,8,512]{0,1,2:T(8,128)} fusion(f32[512,8,32]{2,1,0:T(8,128)S(1)} %fusion.2, bf16[32,8,512]{0,1,2:T(8,128)(2,1)S(1)} %copy.36, bf16[1,32,32,512]{2,1,3,0:T(8,128)(2,1)S(1)} %copy-done), kind=kOutput, calls=%fused_computation.13 | convolution fusion | flops 8519680 | bytes 2359296 | tf_op jit(solution)/shard_map/pkf,krf->prf/dot_general | solution.py:33
  202.0 3.3 %copy.40 = f32[32,8,512]{2,1,0:T(8,128)} copy(f32[32,8,512]{0,1,2:T(8,128)} %add_bitcast_fusion) | data formatting | bytes 1048576 | tf_op jit(solution)/shard_map/add | solution.py:33
  205.3 5.8 %subtract_bitcast_fusion = f32[32,8,512]{0,1,2:T(8,128)} fusion(f32[512,8,32]{2,1,0:T(8,128)S(1)} %copy-done.2, bf16[32,8,512]{0,1,2:T(8,128)(2,1)S(1)} %copy.39, bf16[1,32,32,512]{2,1,3,0:T(8,128)(2,1)} %copy.45), kind=kOutput, calls=%fused_computation.12 | convolution fusion | flops 8519680 | bytes 2359296 | tf_op jit(solution)/shard_map/pkf,krf->prf/dot_general | solution.py:38
  (79 shorter events, 50.0 us)
Async XLA Ops:
  6.5 2.4 %copy-start.6 = (bf16[2,8,32,512]{3,2,1,0:T(8,128)(2,1)S(1)}, bf16[2,8,32,512]{3,2,1,0:T(8,128)(2,1)}, u32[]{:S(2)}) copy-start(bf16[2,8,32,512]{3,2,1,0:T(8,128)(2,1)} %param.2) | copy-start | bytes 1572868
  6.5 165.3 %all-gather.2.cloned.1.call-start = ((), (), s32[]{:S(2)}) async-start(), calls=%async_computation.1 | async-start | bytes 2621440 | tf_op jit(solution)/shard_map/all_gather | solution.py:101
  11.8 9.9 %collective-permute-start = (bf16[256,512]{1,0:T(8,128)(2,1)S(1)}, bf16[256,512]{1,0:T(8,128)(2,1)S(1)}, u32[]{:S(2)}, u32[]{:S(2)}) collective-permute-start(bf16[256,512]{1,0:T(8,128)(2,1)S(1)} %bitcast.52), channel_id=1, source_target_pairs={{0,4},{4,0},{1,5},{5,1},{2,6},{6,2},{3,7},{7,3},{8,12},{12,8},{9,1... | collective-permute-start | bytes 786440 | tf_op jit(solution)/shard_map/ppermute | solution.py:71
  21.9 6.6 %collective-permute-start.1 = (bf16[128,512]{1,0:T(8,128)(2,1)S(1)}, bf16[128,512]{1,0:T(8,128)(2,1)S(1)}, u32[]{:S(2)}, u32[]{:S(2)}) collective-permute-start(bf16[128,512]{1,0:T(8,128)(2,1)S(1)} %broadcast_select_fusion.6), channel_id=1, source_target_pairs={{0,8},{8,0},{16,24},{24,16},{32,40},{40,32},{48,56},{56,48},{1,9},... | collective-permute-start | bytes 393224 | tf_op jit(solution)/shard_map/ppermute | solution.py:71
  28.5 5.0 %collective-permute-start.2 = (bf16[64,512]{1,0:T(8,128)(2,1)S(1)}, bf16[64,512]{1,0:T(8,128)(2,1)S(1)}, u32[]{:S(2)}, u32[]{:S(2)}) collective-permute-start(bf16[64,512]{1,0:T(8,128)(2,1)S(1)} %broadcast_select_fusion.9), channel_id=1, source_target_pairs={{0,128},{128,0},{256,384},{384,256},{1,129},{129,1},{257,385},{385... | collective-permute-start | bytes 196616 | tf_op jit(solution)/shard_map/ppermute | solution.py:71
  33.6 5.9 %collective-permute-start.3 = (bf16[32,512]{1,0:T(8,128)(2,1)S(1)}, bf16[32,512]{1,0:T(8,128)(2,1)S(1)}, u32[]{:S(2)}, u32[]{:S(2)}) collective-permute-start(bf16[32,512]{1,0:T(8,128)(2,1)S(1)} %broadcast_select_fusion.12), channel_id=1, source_target_pairs={{0,16},{8,24},{16,0},{24,8},{32,48},{40,56},{48,32},{56,40},{1,17}... | collective-permute-start | bytes 98312 | tf_op jit(solution)/shard_map/ppermute | solution.py:71
  39.5 6.0 %collective-permute-start.4 = (bf16[16,512]{1,0:T(8,128)(2,1)S(1)}, bf16[16,512]{1,0:T(8,128)(2,1)S(1)}, u32[]{:S(2)}, u32[]{:S(2)}) collective-permute-start(bf16[16,512]{1,0:T(8,128)(2,1)S(1)} %broadcast_select_fusion.15), channel_id=1, source_target_pairs={{0,256},{128,384},{256,0},{384,128},{1,257},{129,385},{257,1},{385... | collective-permute-start | bytes 49160 | tf_op jit(solution)/shard_map/ppermute | solution.py:71
  45.5 8.3 %collective-permute-start.5 = (bf16[8,512]{1,0:T(8,128)(2,1)S(1)}, bf16[8,512]{1,0:T(8,128)(2,1)S(1)}, u32[]{:S(2)}, u32[]{:S(2)}) collective-permute-start(bf16[8,512]{1,0:T(8,128)(2,1)S(1)} %broadcast_select_fusion.18), channel_id=1, source_target_pairs={{0,64},{64,0},{1,65},{65,1},{2,66},{66,2},{3,67},{67,3},{4,68},{68... | collective-permute-start | bytes 24584 | tf_op jit(solution)/shard_map/ppermute | solution.py:71
  53.8 8.3 %collective-permute-start.6 = (bf16[4,512]{1,0:T(4,128)(2,1)S(1)}, bf16[4,512]{1,0:T(4,128)(2,1)S(1)}, u32[]{:S(2)}, u32[]{:S(2)}) collective-permute-start(bf16[4,512]{1,0:T(4,128)(2,1)S(1)} %broadcast_select_fusion.21), channel_id=1, source_target_pairs={{0,32},{8,40},{16,48},{24,56},{32,0},{40,8},{48,16},{56,24},{1,33}... | collective-permute-start | bytes 12296 | tf_op jit(solution)/shard_map/ppermute | solution.py:71
  62.1 8.3 %collective-permute-start.7 = (bf16[4,512]{1,0:T(4,128)(2,1)S(1)}, bf16[4,512]{1,0:T(4,128)(2,1)S(1)}, u32[]{:S(2)}, u32[]{:S(2)}) collective-permute-start(bf16[4,512]{1,0:T(4,128)(2,1)S(1)} %select_add_fusion.5), channel_id=1, source_target_pairs={{0,32},{8,40},{16,48},{24,56},{32,0},{40,8},{48,16},{56,24},{1,33}... | collective-permute-start | bytes 12296 | tf_op jit(solution)/shard_map/ppermute | solution.py:75
  70.4 8.3 %collective-permute-start.8 = (bf16[8,512]{1,0:T(8,128)(2,1)S(1)}, bf16[8,512]{1,0:T(8,128)(2,1)S(1)}, u32[]{:S(2)}, u32[]{:S(2)}) collective-permute-start(bf16[8,512]{1,0:T(8,128)(2,1)S(1)} %pad_maximum_fusion.6), channel_id=1, source_target_pairs={{0,64},{64,0},{1,65},{65,1},{2,66},{66,2},{3,67},{67,3},{4,68},{68... | collective-permute-start | bytes 24584 | tf_op jit(solution)/shard_map/ppermute | solution.py:75
  78.7 6.0 %collective-permute-start.9 = (bf16[16,512]{1,0:T(8,128)(2,1)S(1)}, bf16[16,512]{1,0:T(8,128)(2,1)S(1)}, u32[]{:S(2)}, u32[]{:S(2)}) collective-permute-start(bf16[16,512]{1,0:T(8,128)(2,1)S(1)} %pad_maximum_fusion.5), channel_id=1, source_target_pairs={{0,256},{128,384},{256,0},{384,128},{1,257},{129,385},{257,1},{385... | collective-permute-start | bytes 49160 | tf_op jit(solution)/shard_map/ppermute | solution.py:75
  84.7 5.7 %collective-permute-start.10 = (bf16[32,512]{1,0:T(8,128)(2,1)S(1)}, bf16[32,512]{1,0:T(8,128)(2,1)S(1)}, u32[]{:S(2)}, u32[]{:S(2)}) collective-permute-start(bf16[32,512]{1,0:T(8,128)(2,1)S(1)} %pad_maximum_fusion.4), channel_id=1, source_target_pairs={{0,16},{8,24},{16,0},{24,8},{32,48},{40,56},{48,32},{56,40},{1,17}... | collective-permute-start | bytes 98312 | tf_op jit(solution)/shard_map/ppermute | solution.py:75
  90.5 5.0 %collective-permute-start.11 = (bf16[64,512]{1,0:T(8,128)(2,1)S(1)}, bf16[64,512]{1,0:T(8,128)(2,1)S(1)}, u32[]{:S(2)}, u32[]{:S(2)}) collective-permute-start(bf16[64,512]{1,0:T(8,128)(2,1)S(1)} %pad_maximum_fusion.3), channel_id=1, source_target_pairs={{0,128},{128,0},{256,384},{384,256},{1,129},{129,1},{257,385},{385... | collective-permute-start | bytes 196616 | tf_op jit(solution)/shard_map/ppermute | solution.py:75
  95.5 6.1 %collective-permute-start.12 = (bf16[128,512]{1,0:T(8,128)(2,1)S(1)}, bf16[128,512]{1,0:T(8,128)(2,1)S(1)}, u32[]{:S(2)}, u32[]{:S(2)}) collective-permute-start(bf16[128,512]{1,0:T(8,128)(2,1)S(1)} %pad_maximum_fusion.2), channel_id=1, source_target_pairs={{0,8},{8,0},{16,24},{24,16},{32,40},{40,32},{48,56},{56,48},{1,9},... | collective-permute-start | bytes 393224 | tf_op jit(solution)/shard_map/ppermute | solution.py:75
  101.7 16.4 %collective-permute-start.13 = (bf16[256,512]{1,0:T(8,128)(2,1)S(1)}, bf16[256,512]{1,0:T(8,128)(2,1)S(1)}, u32[]{:S(2)}, u32[]{:S(2)}) collective-permute-start(bf16[256,512]{1,0:T(8,128)(2,1)S(1)} %pad_maximum_fusion.1), channel_id=1, source_target_pairs={{0,4},{4,0},{1,5},{5,1},{2,6},{6,2},{3,7},{7,3},{8,12},{12,8},{9,1... | collective-permute-start | bytes 786440 | tf_op jit(solution)/shard_map/ppermute | solution.py:75
  119.2 17.7 %all-to-all-start = ((bf16[2,8,32,512]{3,1,0,2:T(8,128)(2,1)}), bf16[2,8,32,512]{3,1,0,2:T(8,128)(2,1)S(1)}, u32[]{:S(2)}, u32[]{:S(2)}) async-start(bf16[2,8,32,512]{3,1,0,2:T(8,128)(2,1)} %multiply_convert_fusion), calls=%async_computation | async-start | bytes 1048576 | tf_op jit(solution)/shard_map/all_to_all | solution.py:86
  190.1 4.6 %copy-start.1 = (bf16[1,32,32,512]{2,1,3,0:T(8,128)(2,1)S(1)}, bf16[1,32,32,512]{2,1,3,0:T(8,128)(2,1)}, u32[]{:S(2)}) copy-start(bf16[1,32,32,512]{2,1,3,0:T(8,128)(2,1)} %copy.46) | copy-start | bytes 3145732
  194.7 3.7 %copy-start = (bf16[1,32,32,512]{2,1,3,0:T(8,128)(2,1)S(1)}, bf16[1,32,32,512]{2,1,3,0:T(8,128)(2,1)}, u32[]{:S(2)}) copy-start(bf16[1,32,32,512]{2,1,3,0:T(8,128)(2,1)} %copy.45) | copy-start | bytes 3145732
  202.0 3.3 %copy-start.2 = (f32[512,8,32]{2,1,0:T(8,128)S(1)}, f32[512,8,32]{2,1,0:T(8,128)}, u32[]{:S(2)}) copy-start(f32[512,8,32]{2,1,0:T(8,128)} %fusion) | copy-start | bytes 1572868
  211.1 2.6 %copy-start.3 = (f32[512,512]{1,0:T(8,128)S(1)}, f32[512,512]{1,0:T(8,128)}, u32[]{:S(2)}) copy-start(f32[512,512]{1,0:T(8,128)} %get-tuple-element.25) | copy-start | bytes 3145732
  211.1 2.6 %copy-start.4 = (f32[512,512]{1,0:T(8,128)S(1)}, f32[512,512]{1,0:T(8,128)}, u32[]{:S(2)}) copy-start(f32[512,512]{1,0:T(8,128)} %get-tuple-element.26) | copy-start | bytes 3145732
  211.1 2.6 %copy-start.5 = (f32[32,8,512]{2,1,0:T(8,128)S(1)}, f32[32,8,512]{2,1,0:T(8,128)}, u32[]{:S(2)}) copy-start(f32[32,8,512]{2,1,0:T(8,128)} %copy.40) | copy-start | bytes 1572868
Sparse Core Ops, SparseCore 0:
  119.3 52.5 all-gather.1

commit v4 on v3

--- a/solution.py
+++ b/solution.py
@@ -80,6 +80,14 @@
     return value
 
 
+def chan_exchange(value, axes):
+    count = lax.psum(1, axes)
+    chunks = value.reshape((count, -1) + value.shape[1:])
+    mine = lax.all_to_all(chunks, axes, 0, 0).sum(axis=0, dtype=value.dtype)
+    spread = jnp.broadcast_to(mine[None], chunks.shape)
+    return lax.all_to_all(spread, axes, 0, 0).reshape(value.shape)
+
+
 def make_shards(chan_axes, reduce_order):
     def shards(spectra, sources):
         whitened = whiten(spectra)
@@ -96,8 +104,7 @@
             "pc,xscf->xpsf", onehot, whitened, preferred_element_type=jnp.float32
         ).astype(jnp.bfloat16)
         shape = local_spec.shape
-        steps = reduce_order
-        local_spec = chan_allreduce(local_spec.reshape(-1, shape[-1]), steps).reshape(shape)
+        local_spec = chan_exchange(local_spec.reshape(-1, shape[-1]), chan_axes).reshape(shape)
         source_spec = lax.all_gather(local_spec, "seg", axis=2, tiled=True)
         return correlate(source_spec, regrouped, lag_table)
 

time: 224 us -> 189 us (0.84)
  blocking collectives: 0 us -> 73.4 us
  starting transfers between devices: 65.3 us -> 4.27 us
  waiting for transfers between devices: 85.7 us -> 39 us
    all_to_all x0 -> x2, blocking collectives: none -> 73.4 us  [the longest x1 44.5 us: chan_exchange(): mine = lax.all_to_all(chunks, axes, 0, 0).sum(axis=0, dtype=value.dtype)]
    ppermute x14 -> x0, starting transfers between devices: 61.8 us -> none  [the longest x7 34.9 us: chan_allreduce(): other = lax.ppermute(value, axis, pairs)]
    ppermute x14 -> x0, waiting for transfers between devices: 43.7 us -> none  [the longest x7 23 us: chan_allreduce(): value = keep + lax.ppermute(send, axis, pairs)]
    all_gather x1, waiting for transfers between devices: 32.9 us -> 19.6 us  [shards(): source_spec = lax.all_gather(local_spec, 'seg', axis=2, tiled=True)]
    all_to_all x1, waiting for transfers between devices: 9.09 us -> 19.4 us  [shards(): lax.all_to_all(whitened, 'seg', split_axis=2, concat_axis=1, tiled=True)]
  transfers between devices with their start and end apart: 16 -> 2, of which waited for: 16 -> 2; matrix products, arithmetic and copies ran while one was open for 3% -> 4% of each run, Pallas kernels for 0% -> 0%
where the time goes in v4:
time: 189 us
  blocking collectives  73.4 us (39%)
  waiting for transfers between devices  39 us (21%)
  local copies, waits for them, and re-layouts  27.8 us (15%)
  matrix products  21.8 us (12%)
  between operations  13.5 us (7%)
  other arithmetic  8.74 us (5%)
  starting transfers between devices  4.27 us (2%)
    all_to_all x1, blocking collectives, chan_exchange(): mine = lax.all_to_all(chunks, axes, 0, 0).sum(axis=0, dtype=value.dtype)  44.5 us
    all_to_all x1, blocking collectives, chan_exchange(): return lax.all_to_all(spread, axes, 0, 0).reshape(value.shape)  28.9 us
    all_gather x1, waiting for transfers between devices, shards(): source_spec = lax.all_gather(local_spec, 'seg', axis=2, tiled=True)  19.6 us
    all_to_all x1, waiting for transfers between devices, shards(): lax.all_to_all(whitened, 'seg', split_axis=2, concat_axis=1, tiled=True)  19.4 us
    unnamed x16, local copies, waits for them, and re-layouts  15.4 us
    dot_general x1, matrix products, correlate(): jnp.einsum('pkf,krf->prf', source_spec[0], receiver_spec[1], preferred_el...  5.78 us
    cos x1, other arithmetic, lag_matrix(): return jnp.concatenate([jnp.cos(angles), -jnp.sin(angles)], axis=0)  5.09 us
    dot_general x1, matrix products, correlate(): jnp.einsum('pkf,krf->prf', source_spec[1], receiver_spec[1], preferred_el...  4.58 us
  transfers between devices with their start and end apart: 2, of which 2 were waited for; matrix products, arithmetic and copies ran while one was open for 4% of the time, Pallas kernels for 0%

profile of v4, /device:TPU:1, one launch (start us, length us, event | category | flops | bytes accessed | tf_op | source)
XLA Modules:
  0.0 188.7 jit_solution(7100129230515258505)
XLA Ops:
  6.5 0.7 broadcast_subtract_fusion
  7.4 1.4 copy_convert_fusion
  9.0 1.1 multiply_convert_fusion
  10.1 1.5 fusion.16
  11.6 0.3 copy.30
  12.0 44.5 %all_to_all.25 = bf16[128,4,512]{2,1,0:T(4,128)(2,1)S(1)} all-to-all(bf16[128,4,512]{2,1,0:T(4,128)(2,1)S(1)} %reshape_reshape.6), channel_id=1, replica_groups=mesh['x'=4,'zh'=2,'y'=8,'c'=2,'seg'=4] {'x','zh','y','c'}, dimensions={0} | all-to-all | bytes 1048576 | tf_op jit(solution)/shard_map/all_to_all | solution.py:86
  57.0 28.9 %all_to_all.26 = bf16[128,4,512]{2,1,0:T(4,128)(2,1)S(1)} all-to-all(bf16[128,4,512]{2,1,0:T(4,128)(2,1)S(1)} %broadcast_in_dim.2), channel_id=1, replica_groups=mesh['x'=4,'zh'=2,'y'=8,'c'=2,'seg'=4] {'x','zh','y','c'}, dimensions={0} | all-to-all | bytes 1048576 | tf_op jit(solution)/shard_map/all_to_all | solution.py:88
  86.0 1.0 copy.31
  87.0 4.3 %all-to-all-start = ((bf16[2,8,32,512]{3,1,0,2:T(8,128)(2,1)}), bf16[2,8,32,512]{3,1,0,2:T(8,128)(2,1)S(1)}, u32[]{:S(2)}, u32[]{:S(2)}) async-start(bf16[2,8,32,512]{3,1,0,2:T(8,128)(2,1)} %multiply_convert_fusion), calls=%async_computation | async-start | bytes 1048576 | tf_op jit(solution)/shard_map/all_to_all | solution.py:94
  91.2 5.1 %fusion.34 = (f32[512,512]{1,0:T(8,128)}, f32[512,512]{1,0:T(8,128)}) fusion(s32[512]{0:T(512)S(1)} %iota_add_fusion), kind=kLoop, calls=%fused_computation.39 | loop fusion | flops 3932160 | bytes 2099200 | tf_op jit(solution)/shard_map/cos | solution.py:27
  96.3 19.4 %all-to-all-done = bf16[2,8,32,512]{3,1,0,2:T(8,128)(2,1)S(1)} async-done(((bf16[2,8,32,512]{3,1,0,2:T(8,128)(2,1)}), bf16[2,8,32,512]{3,1,0,2:T(8,128)(2,1)S(1)}, u32[]{:S(2)}, u32[]{:S(2)}) %all-to-all-start) | async-done | bytes 524320 | tf_op jit(solution)/shard_map/all_to_all | solution.py:94
  116.2 0.8 copy.36
  117.0 0.8 copy.33
  117.9 19.6 %all-gather.2.cloned.1.call-done = bf16[2,32,32,512]{3,1,0,2:T(8,128)(2,1)} async-done(((bf16[2,32,8,512]{3,1,0,2:T(8,128)(2,1)}), bf16[2,32,32,512]{3,1,0,2:T(8,128)(2,1)}) %all-gather.2.cloned.1.call-update) | async-done | bytes 2097168 | tf_op jit(solution)/shard_map/all_gather | solution.py:108
  137.5 2.7 %fusion.41 = (bf16[1,32,32,512]{3,1,0,2:T(8,128)(2,1)S(1)}, bf16[1,32,32,512]{3,1,0,2:T(8,128)(2,1)}) fusion(bf16[2,32,32,512]{3,1,0,2:T(8,128)(2,1)} %all-gather.2.cloned.1.call-done), kind=kLoop, calls=%fused_computation.49 | loop fusion | bytes 4194304 | tf_op jit(solution)/shard_map/slice | solution.py:34
  140.2 8.6 %copy.43 = bf16[1,32,32,512]{2,1,3,0:T(8,128)(2,1)} copy(bf16[1,32,32,512]{3,1,0,2:T(8,128)(2,1)} %get-tuple-element.6) | data formatting | bytes 2097152
  148.7 6.8 %copy.42 = bf16[1,32,32,512]{2,1,3,0:T(8,128)(2,1)} copy(bf16[1,32,32,512]{3,1,0,2:T(8,128)(2,1)S(1)} %get-tuple-element.5) | data formatting | bytes 2097152
  155.6 4.6 %fusion.2 = f32[512,8,32]{2,1,0:T(8,128)S(1)} fusion(bf16[32,8,512]{0,1,2:T(8,128)(2,1)S(1)} %copy.36, bf16[1,32,32,512]{2,1,3,0:T(8,128)(2,1)} %copy.43), kind=kOutput, calls=%fused_computation.2 | convolution fusion | flops 8388608 | bytes 1835008 | tf_op jit(solution)/shard_map/pkf,krf->prf/dot_general | solution.py:35
  160.2 3.6 %fusion = f32[512,8,32]{2,1,0:T(8,128)} fusion(bf16[32,8,512]{0,1,2:T(8,128)(2,1)S(1)} %copy.33, bf16[1,32,32,512]{2,1,3,0:T(8,128)(2,1)S(1)} %copy-done.1), kind=kOutput, calls=%fused_computation | convolution fusion | flops 8388608 | bytes 1835008 | tf_op jit(solution)/shard_map/pkf,krf->prf/dot_general | solution.py:40
  163.8 3.6 %add_bitcast_fusion = f32[32,8,512]{0,1,2:T(8,128)} fusion(f32[512,8,32]{2,1,0:T(8,128)S(1)} %fusion.2, bf16[32,8,512]{0,1,2:T(8,128)(2,1)S(1)} %copy.33, bf16[1,32,32,512]{2,1,3,0:T(8,128)(2,1)S(1)} %copy-done), kind=kOutput, calls=%fused_computation.13 | convolution fusion | flops 8519680 | bytes 2359296 | tf_op jit(solution)/shard_map/pkf,krf->prf/dot_general | solution.py:33
  167.4 3.3 %copy.37 = f32[32,8,512]{2,1,0:T(8,128)} copy(f32[32,8,512]{0,1,2:T(8,128)} %add_bitcast_fusion) | data formatting | bytes 1048576 | tf_op jit(solution)/shard_map/add | solution.py:33
  170.7 5.8 %subtract_bitcast_fusion = f32[32,8,512]{0,1,2:T(8,128)} fusion(f32[512,8,32]{2,1,0:T(8,128)S(1)} %copy-done.2, bf16[32,8,512]{0,1,2:T(8,128)(2,1)S(1)} %copy.36, bf16[1,32,32,512]{2,1,3,0:T(8,128)(2,1)} %copy.42), kind=kOutput, calls=%fused_computation.12 | convolution fusion | flops 8519680 | bytes 2359296 | tf_op jit(solution)/shard_map/pkf,krf->prf/dot_general | solution.py:38
  176.5 2.5 %copy.40 = f32[32,8,512]{2,1,0:T(8,128)S(1)} copy(f32[32,8,512]{0,1,2:T(8,128)} %subtract_bitcast_fusion) | data formatting | bytes 1048576 | tf_op jit(solution)/shard_map/sub | solution.py:38
  179.1 2.8 %fusion.20 = f32[32,8,512]{2,1,0:T(8,128)} fusion(f32[512,512]{1,0:T(8,128)S(1)} %copy-done.4, f32[512,512]{1,0:T(8,128)S(1)} %copy-done.3, f32[256,512]{1,0:T(8,128)S(1)} %bitcast.43, f32[256,512]{1,0:T(8,128)S(1)} %bitcast.42), kind=kOutput, calls=%fused_computation.20 | convolution fusion | flops 1611792384 | bytes 3670016 | tf_op jit(solution)/shard_map/dot_general | solution.py:45
  (29 shorter events, 1.4 us)
Async XLA Ops:
  6.5 2.4 %copy-start.6 = (bf16[2,8,32,512]{3,2,1,0:T(8,128)(2,1)S(1)}, bf16[2,8,32,512]{3,2,1,0:T(8,128)(2,1)}, u32[]{:S(2)}) copy-start(bf16[2,8,32,512]{3,2,1,0:T(8,128)(2,1)} %param.2) | copy-start | bytes 1572868
  6.5 130.9 %all-gather.2.cloned.1.call-start = ((), (), s32[]{:S(2)}) async-start(), calls=%async_computation.3 | async-start | bytes 2621440 | tf_op jit(solution)/shard_map/all_gather | solution.py:108
  87.0 28.8 %all-to-all-start = ((bf16[2,8,32,512]{3,1,0,2:T(8,128)(2,1)}), bf16[2,8,32,512]{3,1,0,2:T(8,128)(2,1)S(1)}, u32[]{:S(2)}, u32[]{:S(2)}) async-start(bf16[2,8,32,512]{3,1,0,2:T(8,128)(2,1)} %multiply_convert_fusion), calls=%async_computation | async-start | bytes 1048576 | tf_op jit(solution)/shard_map/all_to_all | solution.py:94
  155.6 4.6 %copy-start.1 = (bf16[1,32,32,512]{2,1,3,0:T(8,128)(2,1)S(1)}, bf16[1,32,32,512]{2,1,3,0:T(8,128)(2,1)}, u32[]{:S(2)}) copy-start(bf16[1,32,32,512]{2,1,3,0:T(8,128)(2,1)} %copy.43) | copy-start | bytes 3145732
  160.2 3.6 %copy-start = (bf16[1,32,32,512]{2,1,3,0:T(8,128)(2,1)S(1)}, bf16[1,32,32,512]{2,1,3,0:T(8,128)(2,1)}, u32[]{:S(2)}) copy-start(bf16[1,32,32,512]{2,1,3,0:T(8,128)(2,1)} %copy.42) | copy-start | bytes 3145732
  167.4 3.3 %copy-start.2 = (f32[512,8,32]{2,1,0:T(8,128)S(1)}, f32[512,8,32]{2,1,0:T(8,128)}, u32[]{:S(2)}) copy-start(f32[512,8,32]{2,1,0:T(8,128)} %fusion) | copy-start | bytes 1572868
  176.5 2.6 %copy-start.3 = (f32[512,512]{1,0:T(8,128)S(1)}, f32[512,512]{1,0:T(8,128)}, u32[]{:S(2)}) copy-start(f32[512,512]{1,0:T(8,128)} %get-tuple-element.9) | copy-start | bytes 3145732
  176.5 2.6 %copy-start.4 = (f32[512,512]{1,0:T(8,128)S(1)}, f32[512,512]{1,0:T(8,128)}, u32[]{:S(2)}) copy-start(f32[512,512]{1,0:T(8,128)} %get-tuple-element.10) | copy-start | bytes 3145732
  176.5 2.6 %copy-start.5 = (f32[32,8,512]{2,1,0:T(8,128)S(1)}, f32[32,8,512]{2,1,0:T(8,128)}, u32[]{:S(2)}) copy-start(f32[32,8,512]{2,1,0:T(8,128)} %copy.37) | copy-start | bytes 1572868
Sparse Core Ops, SparseCore 0:
  87.1 50.3 all-gather.1

commit v5 on v1

--- a/solution.py
+++ b/solution.py
@@ -8,7 +8,6 @@
 LAGS = 256
 CHAN_FACTORS = (("x", 4), ("zh", 2), ("y", 8), ("c", 2))
 CHAN_AXES = tuple(name for name, _ in CHAN_FACTORS)
-REDUCE_ORDER = ("c", "y", "zh", "x")
 
 
 def whiten(spectra):
@@ -48,7 +47,21 @@
     return result.reshape(stacked.shape[0], stacked.shape[1], -1)
 
 
-def make_shards(chan_axes, reduce_order):
+def gather_sources(value, chan_axes, seg_axis):
+    parts, sources, local_segs, freqs = value.shape
+    count = lax.psum(1, chan_axes)
+    segs = lax.psum(1, seg_axis)
+    chunks = value.reshape(count, -1, freqs)
+    rows = chunks.shape[1]
+    mine = lax.all_to_all(chunks, chan_axes, 0, 0).sum(axis=0, dtype=value.dtype)
+    spread = jnp.broadcast_to(mine[None], (count * segs, rows, freqs))
+    got = lax.all_to_all(spread, chan_axes + (seg_axis,), 0, 0)
+    split = local_segs // rows
+    got = got.reshape(parts, sources, split, segs, rows, freqs).transpose(0, 1, 3, 2, 4, 5)
+    return got.reshape(parts, sources, segs * local_segs, freqs)
+
+
+def make_shards(chan_axes):
     def shards(spectra, sources):
         whitened = whiten(spectra)
         regrouped = lax.all_to_all(whitened, "seg", split_axis=2, concat_axis=1, tiled=True)
@@ -63,9 +76,7 @@
         local_spec = jnp.einsum(
             "pc,xscf->xpsf", onehot, whitened, preferred_element_type=jnp.float32
         ).astype(jnp.bfloat16)
-        for axis in reduce_order:
-            local_spec = lax.psum(local_spec, axis)
-        source_spec = lax.all_gather(local_spec, "seg", axis=2, tiled=True)
+        source_spec = gather_sources(local_spec, chan_axes, "seg")
         return correlate(source_spec, regrouped, lag_table)
 
     return shards
@@ -77,15 +88,15 @@
     if math.prod(sizes) == chan:
         devices = mesh.devices.reshape(sizes + (mesh.shape["seg"],))
         fine = Mesh(devices, CHAN_AXES + ("seg",))
-        chan_axes, reduce_order = CHAN_AXES, REDUCE_ORDER
+        chan_axes = CHAN_AXES
     else:
         fine = mesh
-        chan_axes, reduce_order = "chan", ("chan",)
+        chan_axes = ("chan",)
     placed = (P(None, "seg", chan_axes, None), P())
     return jax.shard_map(
-        make_shards(chan_axes, reduce_order),
+        make_shards(chan_axes),
         mesh=fine,
         in_specs=placed,
-        out_specs=P(None, tuple(chan_axes) + ("seg",) if isinstance(chan_axes, tuple) else ("chan", "seg"), None),
+        out_specs=P(None, chan_axes + ("seg",), None),
         check_vma=False,
     )

time: 358 us -> 181 us (0.51)
  waiting for transfers between devices: 282 us -> 58.7 us
  blocking collectives: 0 us -> 44.5 us
  between operations: 13.2 us -> 0.14 us
  starting transfers between devices: 5.1 us -> 15.9 us
  local copies, waits for them, and re-layouts: 26.2 us -> 30.2 us
    psum x4 -> x0, waiting for transfers between devices: 236 us -> none  [shards(): local_spec = lax.psum(local_spec, axis)]
    all_to_all x0 -> x1, blocking collectives: none -> 44.5 us  [gather_sources(): lax.all_to_all(chunks, chan_axes, 0, 0).sum(axis=0, dtype=value.dtype)]
    all_to_all x0 -> x1, waiting for transfers between devices: none -> 44.2 us  [gather_sources(): got = lax.all_to_all(spread, chan_axes + (seg_axis,), 0, 0)]
    all_gather x1 -> x0, waiting for transfers between devices: 39.8 us -> none  [shards(): source_spec = lax.all_gather(local_spec, 'seg', axis=2, tiled=True)]
    all_to_all x0 -> x1, starting transfers between devices: none -> 11.6 us  [gather_sources(): got = lax.all_to_all(spread, chan_axes + (seg_axis,), 0, 0)]
    all_to_all x1, waiting for transfers between devices: 6.19 us -> 14.4 us  [shards(): lax.all_to_all(whitened, 'seg', split_axis=2, concat_axis=1, tiled=True)]
    slice x0 -> x3, local copies, waits for them, and re-layouts: none -> 6.19 us  [the longest x2 5.61 us: correlate(): source_spec[1]]
    squeeze x2 -> x1, local copies, waits for them, and re-layouts: 9.56 us -> 6.84 us  [correlate(): source_spec[1]]
  transfers between devices with their start and end apart: 6 -> 2, of which waited for: 6 -> 2; matrix products, arithmetic and copies ran while one was open for 2% -> 4% of each run, Pallas kernels for 0% -> 0%
where the time goes in v5:
time: 181 us; the launch traced here: 180 us
  waiting for transfers between devices  58.7 us (32%)
  blocking collectives  44.5 us (25%)
  local copies, waits for them, and re-layouts  30.2 us (17%)
  matrix products  21.8 us (12%)
  starting transfers between devices  15.9 us (9%)
  other arithmetic  8.75 us (5%)
    all_to_all x1, blocking collectives, gather_sources(): lax.all_to_all(chunks, chan_axes, 0, 0).sum(axis=0, dtype=value.dtype)  44.5 us
    all_to_all x1, waiting for transfers between devices, gather_sources(): got = lax.all_to_all(spread, chan_axes + (seg_axis,), 0, 0)  44.2 us
    all_to_all x1, waiting for transfers between devices, shards(): lax.all_to_all(whitened, 'seg', split_axis=2, concat_axis=1, tiled=True)  14.4 us
    all_to_all x1, starting transfers between devices, gather_sources(): got = lax.all_to_all(spread, chan_axes + (seg_axis,), 0, 0)  11.6 us
    squeeze x1, local copies, waits for them, and re-layouts, correlate(): source_spec[0]  6.87 us
    squeeze x1, local copies, waits for them, and re-layouts, correlate(): source_spec[1]  6.84 us
    dot_general x1, matrix products, correlate(): jnp.einsum('pkf,krf->prf', source_spec[1], receiver_spec[0], preferred_el...  5.78 us
    slice x2, local copies, waits for them, and re-layouts, correlate(): source_spec[1]  5.61 us
  transfers between devices with their start and end apart: 2, of which 2 were waited for; matrix products, arithmetic and copies ran while one was open for 4% of the time, Pallas kernels for 0%

profile of v5, /device:TPU:1, one launch (start us, length us, event | category | flops | bytes accessed | tf_op | source)
XLA Modules:
  0.0 180.1 jit_solution(13133652657839099811)
XLA Ops:
  0.0 0.7 broadcast_subtract_fusion
  0.9 1.4 copy_convert_fusion
  2.4 1.1 multiply_convert_fusion
  3.6 1.5 fusion.4
  5.5 44.5 %all_to_all.25 = bf16[128,4,512]{2,1,0:T(4,128)(2,1)S(1)} all-to-all(bf16[128,4,512]{2,1,0:T(4,128)(2,1)S(1)} %reshape.42), channel_id=1, replica_groups=mesh['x'=4,'zh'=2,'y'=8,'c'=2,'seg'=4] {'x','zh','y','c'}, dimensions={0} | all-to-all | bytes 1048576 | tf_op jit(solution)/shard_map/all_to_all | solution.py:56
  50.0 4.3 %all-to-all-start = ((bf16[2,8,32,512]{3,1,0,2:T(8,128)(2,1)}), bf16[2,8,32,512]{3,1,0,2:T(8,128)(2,1)S(1)}, u32[]{:S(2)}, u32[]{:S(2)}) async-start(bf16[2,8,32,512]{3,1,0,2:T(8,128)(2,1)} %multiply_convert_fusion), calls=%async_computation | async-start | bytes 1048576 | tf_op jit(solution)/shard_map/all_to_all | solution.py:67
  54.5 14.4 %all-to-all-done = bf16[2,8,32,512]{3,1,0,2:T(8,128)(2,1)S(1)} async-done(((bf16[2,8,32,512]{3,1,0,2:T(8,128)(2,1)}), bf16[2,8,32,512]{3,1,0,2:T(8,128)(2,1)S(1)}, u32[]{:S(2)}, u32[]{:S(2)}) %all-to-all-start) | async-done | bytes 524320 | tf_op jit(solution)/shard_map/all_to_all | solution.py:67
  69.0 1.8 %broadcast_in_dim.2 = bf16[512,4,512]{2,1,0:T(4,128)(2,1)} broadcast(bf16[4,512]{1,0:T(4,128)(2,1)S(1)} %reduce_sum.19), dimensions={1,2} | broadcast | bytes 2101248 | tf_op jit(solution)/shard_map/broadcast_in_dim | solution.py:57
  70.8 11.6 %all-to-all-start.2 = ((bf16[512,4,512]{2,1,0:T(4,128)(2,1)}), bf16[512,4,512]{2,1,0:T(4,128)(2,1)}, u32[]{:S(2)}, u32[]{:S(2)}) async-start(bf16[512,4,512]{2,1,0:T(4,128)(2,1)} %broadcast_in_dim.2), calls=%async_computation.2 | async-start | bytes 4194304 | tf_op jit(solution)/shard_map/all_to_all | solution.py:58
  82.5 5.1 %fusion.22 = (f32[512,512]{1,0:T(8,128)}, f32[512,512]{1,0:T(8,128)}) fusion(s32[512]{0:T(512)S(1)} %iota_add_fusion), kind=kLoop, calls=%fused_computation.31 | loop fusion | flops 3932160 | bytes 2099200 | tf_op jit(solution)/shard_map/cos | solution.py:26
  88.0 0.8 copy.42
  88.8 0.8 copy.46
  89.7 44.2 %all-to-all-done.2 = bf16[512,4,512]{2,1,0:T(4,128)(2,1)} async-done(((bf16[512,4,512]{2,1,0:T(4,128)(2,1)}), bf16[512,4,512]{2,1,0:T(4,128)(2,1)}, u32[]{:S(2)}, u32[]{:S(2)}) %all-to-all-start.2) | async-done | bytes 2097184 | tf_op jit(solution)/shard_map/all_to_all | solution.py:58
  133.9 3.8 %fusion.29 = (bf16[1,32,4,2,4,512]{5,4,2,3,1,0:T(4,128)(2,1)}, bf16[1,32,4,2,4,512]{5,4,2,3,1,0:T(4,128)(2,1)S(1)}) fusion(bf16[2,32,4,2,4,512]{5,4,2,3,1,0:T(4,128)(2,1)} %bitcast.7), kind=kLoop, calls=%fused_computation.41 | loop fusion | bytes 4194304 | tf_op jit(solution)/shard_map/slice | solution.py:35
  138.3 6.9 %copy.43 = bf16[32,32,512]{1,0,2:T(8,128)(2,1)} copy(bf16[32,32,512]{2,0,1:T(8,128)(2,1)S(1)} %bitcast.37) | data formatting | bytes 2097152 | tf_op jit(solution)/shard_map/squeeze | solution.py:33
  145.2 1.8 %copy.45 = bf16[1,32,4,2,4,512]{5,1,4,3,2,0:T(8,128)(2,1)S(1)} copy(bf16[1,32,4,2,4,512]{5,4,2,3,1,0:T(4,128)(2,1)} %get-tuple-element.5) | data formatting | bytes 2097152 | tf_op jit(solution)/shard_map/slice | solution.py:35
  147.0 6.8 %copy.47 = bf16[32,32,512]{1,0,2:T(8,128)(2,1)} copy(bf16[32,32,512]{2,0,1:T(8,128)(2,1)S(1)} %bitcast.38) | data formatting | bytes 2097152 | tf_op jit(solution)/shard_map/squeeze | solution.py:35
  153.8 4.6 %fusion.31 = f32[512,8,32]{2,1,0:T(8,128)S(1)} fusion(bf16[32,8,512]{0,1,2:T(8,128)(2,1)S(1)} %copy.42, bf16[32,32,512]{1,0,2:T(8,128)(2,1)} %copy.43), kind=kOutput, calls=%fused_computation.43 | convolution fusion | flops 8388608 | bytes 1835008 | tf_op jit(solution)/shard_map/pkf,krf->prf/dot_general | solution.py:32
  158.4 3.6 %fusion.32 = f32[512,8,32]{2,1,0:T(8,128)} fusion(bf16[32,8,512]{0,1,2:T(8,128)(2,1)S(1)} %copy.46, bf16[32,32,512]{1,0,2:T(8,128)(2,1)S(1)} %copy-done.1), kind=kOutput, calls=%fused_computation.44 | convolution fusion | flops 8388608 | bytes 1835008 | tf_op jit(solution)/shard_map/pkf,krf->prf/dot_general | solution.py:37
  162.0 3.6 %add_bitcast_fusion = f32[32,8,512]{0,1,2:T(8,128)} fusion(f32[512,8,32]{2,1,0:T(8,128)S(1)} %fusion.31, bf16[32,8,512]{0,1,2:T(8,128)(2,1)S(1)} %copy.46, bf16[32,32,512]{1,0,2:T(8,128)(2,1)S(1)} %copy-done), kind=kOutput, calls=%fused_computation.5 | convolution fusion | flops 8519680 | bytes 2359296 | tf_op jit(solution)/shard_map/pkf,krf->prf/dot_general | solution.py:34
  165.7 3.3 %copy.48 = f32[32,8,512]{2,1,0:T(8,128)} copy(f32[32,8,512]{0,1,2:T(8,128)} %add_bitcast_fusion) | data formatting | bytes 1048576 | tf_op jit(solution)/shard_map/add | solution.py:32
  168.9 5.8 %subtract_bitcast_fusion = f32[32,8,512]{0,1,2:T(8,128)} fusion(f32[512,8,32]{2,1,0:T(8,128)S(1)} %copy-done.2, bf16[32,8,512]{0,1,2:T(8,128)(2,1)S(1)} %copy.42, bf16[32,32,512]{1,0,2:T(8,128)(2,1)} %copy.47), kind=kOutput, calls=%fused_computation.4 | convolution fusion | flops 8519680 | bytes 2359296 | tf_op jit(solution)/shard_map/pkf,krf->prf/dot_general | solution.py:39
  174.7 2.5 %copy.53 = f32[32,8,512]{2,1,0:T(8,128)S(1)} copy(f32[32,8,512]{0,1,2:T(8,128)} %subtract_bitcast_fusion) | data formatting | bytes 1048576 | tf_op jit(solution)/shard_map/sub | solution.py:37
  177.3 2.8 %fusion.8 = f32[32,8,512]{2,1,0:T(8,128)} fusion(f32[512,512]{1,0:T(8,128)S(1)} %copy-done.4, f32[512,512]{1,0:T(8,128)S(1)} %copy-done.3, f32[256,512]{1,0:T(8,128)S(1)} %bitcast.40, f32[256,512]{1,0:T(8,128)S(1)} %bitcast.39), kind=kOutput, calls=%fused_computation.12 | convolution fusion | flops 1611792384 | bytes 3670016 | tf_op jit(solution)/shard_map/dot_general | solution.py:44
  (27 shorter events, 2.0 us)
Async XLA Ops:
  0.0 2.4 %copy-start.6 = (bf16[2,8,32,512]{3,2,1,0:T(8,128)(2,1)S(1)}, bf16[2,8,32,512]{3,2,1,0:T(8,128)(2,1)}, u32[]{:S(2)}) copy-start(bf16[2,8,32,512]{3,2,1,0:T(8,128)(2,1)} %param.2) | copy-start | bytes 1572868
  50.0 19.0 %all-to-all-start = ((bf16[2,8,32,512]{3,1,0,2:T(8,128)(2,1)}), bf16[2,8,32,512]{3,1,0,2:T(8,128)(2,1)S(1)}, u32[]{:S(2)}, u32[]{:S(2)}) async-start(bf16[2,8,32,512]{3,1,0,2:T(8,128)(2,1)} %multiply_convert_fusion), calls=%async_computation | async-start | bytes 1048576 | tf_op jit(solution)/shard_map/all_to_all | solution.py:67
  70.8 63.1 %all-to-all-start.2 = ((bf16[512,4,512]{2,1,0:T(4,128)(2,1)}), bf16[512,4,512]{2,1,0:T(4,128)(2,1)}, u32[]{:S(2)}, u32[]{:S(2)}) async-start(bf16[512,4,512]{2,1,0:T(4,128)(2,1)} %broadcast_in_dim.2), calls=%async_computation.2 | async-start | bytes 4194304 | tf_op jit(solution)/shard_map/all_to_all | solution.py:58
  153.8 4.6 %copy-start.1 = (bf16[32,32,512]{1,0,2:T(8,128)(2,1)S(1)}, bf16[32,32,512]{1,0,2:T(8,128)(2,1)}, u32[]{:S(2)}) copy-start(bf16[32,32,512]{1,0,2:T(8,128)(2,1)} %copy.43) | copy-start | bytes 3145732
  158.4 3.6 %copy-start = (bf16[32,32,512]{1,0,2:T(8,128)(2,1)S(1)}, bf16[32,32,512]{1,0,2:T(8,128)(2,1)}, u32[]{:S(2)}) copy-start(bf16[32,32,512]{1,0,2:T(8,128)(2,1)} %copy.47) | copy-start | bytes 3145732
  165.7 3.3 %copy-start.2 = (f32[512,8,32]{2,1,0:T(8,128)S(1)}, f32[512,8,32]{2,1,0:T(8,128)}, u32[]{:S(2)}) copy-start(f32[512,8,32]{2,1,0:T(8,128)} %fusion.32) | copy-start | bytes 1572868
  174.7 2.6 %copy-start.3 = (f32[512,512]{1,0:T(8,128)S(1)}, f32[512,512]{1,0:T(8,128)}, u32[]{:S(2)}) copy-start(f32[512,512]{1,0:T(8,128)} %get-tuple-element.9) | copy-start | bytes 3145732
  174.7 2.6 %copy-start.4 = (f32[512,512]{1,0:T(8,128)S(1)}, f32[512,512]{1,0:T(8,128)}, u32[]{:S(2)}) copy-start(f32[512,512]{1,0:T(8,128)} %get-tuple-element.10) | copy-start | bytes 3145732
  174.7 2.6 %copy-start.5 = (f32[32,8,512]{2,1,0:T(8,128)S(1)}, f32[32,8,512]{2,1,0:T(8,128)}, u32[]{:S(2)}) copy-start(f32[32,8,512]{2,1,0:T(8,128)} %copy.48) | copy-start | bytes 1572868

commit v6 on v5

--- a/solution.py
+++ b/solution.py
@@ -29,16 +29,12 @@
 def correlate(source_spec, receiver_spec, lag_table):
     segs = receiver_spec.shape[1]
     freqs = receiver_spec.shape[3]
-    real_part = jnp.einsum(
-        "pkf,krf->prf", source_spec[0], receiver_spec[0], preferred_element_type=jnp.float32
-    ) + jnp.einsum(
-        "pkf,krf->prf", source_spec[1], receiver_spec[1], preferred_element_type=jnp.float32
-    )
-    imag_part = jnp.einsum(
-        "pkf,krf->prf", source_spec[0], receiver_spec[1], preferred_element_type=jnp.float32
-    ) - jnp.einsum(
-        "pkf,krf->prf", source_spec[1], receiver_spec[0], preferred_element_type=jnp.float32
-    )
+    a = source_spec[0].astype(jnp.float32)[:, :, None, :]
+    b = source_spec[1].astype(jnp.float32)[:, :, None, :]
+    c = receiver_spec[0].astype(jnp.float32)[:, None, :, :]
+    d = receiver_spec[1].astype(jnp.float32)[:, None, :, :]
+    real_part = jnp.sum(a * c + b * d, axis=0)
+    imag_part = jnp.sum(a * d - b * c, axis=0)
     stacked = jnp.concatenate([real_part, imag_part], axis=-1) * (1.0 / math.sqrt(segs))
     flat = stacked.reshape(-1, 2 * freqs)
     result = jnp.dot(
@@ -57,8 +53,8 @@
     spread = jnp.broadcast_to(mine[None], (count * segs, rows, freqs))
     got = lax.all_to_all(spread, chan_axes + (seg_axis,), 0, 0)
     split = local_segs // rows
-    got = got.reshape(parts, sources, split, segs, rows, freqs).transpose(0, 1, 3, 2, 4, 5)
-    return got.reshape(parts, sources, segs * local_segs, freqs)
+    got = got.reshape(parts, sources, split, segs, rows, freqs).transpose(0, 3, 2, 4, 1, 5)
+    return got.reshape(parts, segs * local_segs, sources, freqs)
 
 
 def make_shards(chan_axes):

time: 181 us -> 146 us (0.81)
  local copies, waits for them, and re-layouts: 30.2 us -> 6.31 us
  matrix products: 21.8 us -> 4.22 us
  other arithmetic: 8.75 us -> 16.6 us
  starting transfers between devices: 15.9 us -> 13.2 us
    dot_general x4 -> x0, matrix products: 17.6 us -> none  [the longest x1 5.78 us: correlate(): jnp.einsum('pkf,krf->prf', source_spec[1], receiver_spec[0], preferred_el...]
    squeeze x4 -> x0, local copies, waits for them, and re-layouts: 15.4 us -> none  [the longest x1 6.87 us: correlate(): source_spec[0]]
    reduce_sum x0 -> x1, other arithmetic: none -> 6.72 us  [correlate(): real_part = jnp.sum(a * c + b * d, axis=0)]
    slice x6 -> x1, local copies, waits for them, and re-layouts: 6.26 us -> 0.24 us  [correlate(): a = source_spec[0].astype(jnp.float32)[:, :, None, :]]
    add x1 -> x0, local copies, waits for them, and re-layouts: 3.27 us -> none  [correlate(): jnp.einsum('pkf,krf->prf', source_spec[0], receiver_spec[0], preferred_el...]
    all_to_all x1, starting transfers between devices: 11.6 us -> 8.96 us  [gather_sources(): got = lax.all_to_all(spread, chan_axes + (seg_axis,), 0, 0)]
    sub x1 -> x0, local copies, waits for them, and re-layouts: 2.54 us -> none  [correlate(): jnp.einsum('pkf,krf->prf', source_spec[0], receiver_spec[1], preferred_el...]
  transfers between devices with their start and end apart: 2 -> 2, of which waited for: 2 -> 2; matrix products, arithmetic and copies ran while one was open for 4% -> 5% of each run, Pallas kernels for 0% -> 0%
where the time goes in v6:
time: 146 us; the launch traced here: 145 us
  waiting for transfers between devices  60.3 us (41%)
  blocking collectives  44.5 us (30%)
  other arithmetic  16.6 us (11%)
  starting transfers between devices  13.2 us (9%)
  local copies, waits for them, and re-layouts  6.31 us (4%)
  matrix products  4.22 us (3%)
    all_to_all x1, waiting for transfers between devices, gather_sources(): got = lax.all_to_all(spread, chan_axes + (seg_axis,), 0, 0)  45.9 us
    all_to_all x1, blocking collectives, gather_sources(): lax.all_to_all(chunks, chan_axes, 0, 0).sum(axis=0, dtype=value.dtype)  44.5 us
    all_to_all x1, waiting for transfers between devices, shards(): lax.all_to_all(whitened, 'seg', split_axis=2, concat_axis=1, tiled=True)  14.4 us
    all_to_all x1, starting transfers between devices, gather_sources(): got = lax.all_to_all(spread, chan_axes + (seg_axis,), 0, 0)  8.96 us
    reduce_sum x1, other arithmetic, correlate(): real_part = jnp.sum(a * c + b * d, axis=0)  6.72 us
    cos x1, other arithmetic, lag_matrix(): return jnp.concatenate([jnp.cos(angles), -jnp.sin(angles)], axis=0)  5.41 us
    all_to_all x1, starting transfers between devices, shards(): lax.all_to_all(whitened, 'seg', split_axis=2, concat_axis=1, tiled=True)  4.27 us
  transfers between devices with their start and end apart: 2, of which 2 were waited for; matrix products, arithmetic and copies ran while one was open for 5% of the time, Pallas kernels for 0%

profile of v6, /device:TPU:1, one launch (start us, length us, event | category | flops | bytes accessed | tf_op | source)
XLA Modules:
  0.0 145.4 jit_solution(4544809350816190297)
XLA Ops:
  0.0 0.7 broadcast_subtract_fusion
  0.9 1.4 copy_convert_fusion
  2.3 0.1 fusion.20
  2.4 1.1 multiply_convert_fusion
  3.6 1.5 %fusion.4 = bf16[2,32,8,512]{3,1,2,0:T(8,128)(2,1)S(1)} fusion(bf16[2,8,32,512]{3,1,0,2:T(8,128)(2,1)} %multiply_convert_fusion, s32[32]{0:T(128)S(1)} %sub.24), kind=kOutput, calls=%fused_computation.11 | convolution fusion | flops 17040384 | bytes 1048704 | tf_op jit(solution)/shard_map/pc,xscf->xpsf/dot_general | solution.py:72
  5.0 0.3 copy.33
  5.5 44.5 %all_to_all.25 = bf16[128,4,512]{2,1,0:T(4,128)(2,1)S(1)} all-to-all(bf16[128,4,512]{2,1,0:T(4,128)(2,1)S(1)} %reshape.70), channel_id=1, replica_groups=mesh['x'=4,'zh'=2,'y'=8,'c'=2,'seg'=4] {'x','zh','y','c'}, dimensions={0} | all-to-all | bytes 1048576 | tf_op jit(solution)/shard_map/all_to_all | solution.py:52
  50.0 4.3 %all-to-all-start.2 = ((bf16[2,8,32,512]{3,1,0,2:T(8,128)(2,1)}), bf16[2,8,32,512]{3,1,0,2:T(8,128)(2,1)S(1)}, u32[]{:S(2)}, u32[]{:S(2)}) async-start(bf16[2,8,32,512]{3,1,0,2:T(8,128)(2,1)} %multiply_convert_fusion), calls=%async_computation.2 | async-start | bytes 1048576 | tf_op jit(solution)/shard_map/all_to_all | solution.py:63
  54.3 0.3 reduce_sum.37
  54.5 14.4 %all-to-all-done.2 = bf16[2,8,32,512]{3,1,0,2:T(8,128)(2,1)S(1)} async-done(((bf16[2,8,32,512]{3,1,0,2:T(8,128)(2,1)}), bf16[2,8,32,512]{3,1,0,2:T(8,128)(2,1)S(1)}, u32[]{:S(2)}, u32[]{:S(2)}) %all-to-all-start.2) | async-done | bytes 524320 | tf_op jit(solution)/shard_map/all_to_all | solution.py:63
  69.0 1.9 %broadcast_in_dim.2 = bf16[512,4,512]{2,1,0:T(4,128)(2,1)} broadcast(bf16[4,512]{1,0:T(4,128)(2,1)S(1)} %reduce_sum.37), dimensions={1,2} | broadcast | bytes 2101248 | tf_op jit(solution)/shard_map/broadcast_in_dim | solution.py:53
  70.9 9.0 %all-to-all-start.1 = ((bf16[512,4,512]{2,1,0:T(4,128)(2,1)}), bf16[512,4,512]{2,1,0:T(4,128)(2,1)S(1)}, u32[]{:S(2)}, u32[]{:S(2)}) async-start(bf16[512,4,512]{2,1,0:T(4,128)(2,1)} %broadcast_in_dim.2), calls=%async_computation.1 | async-start | bytes 4194304 | tf_op jit(solution)/shard_map/all_to_all | solution.py:54
  79.9 5.4 %fusion.22 = (f32[512,512]{1,0:T(8,128)S(1)}, f32[512,512]{1,0:T(8,128)}) fusion(s32[512]{0:T(512)S(1)} %iota_add_fusion), kind=kLoop, calls=%fused_computation.34 | loop fusion | flops 3932160 | bytes 2099200 | tf_op jit(solution)/shard_map/cos | solution.py:26
  85.3 0.3 copy.47
  85.7 0.8 copy.37
  86.5 0.8 copy.36
  87.4 45.9 %all-to-all-done.1 = bf16[512,4,512]{2,1,0:T(4,128)(2,1)S(1)} async-done(((bf16[512,4,512]{2,1,0:T(4,128)(2,1)}), bf16[512,4,512]{2,1,0:T(4,128)(2,1)S(1)}, u32[]{:S(2)}, u32[]{:S(2)}) %all-to-all-start.1) | async-done | bytes 2097184 | tf_op jit(solution)/shard_map/all_to_all | solution.py:54
  133.2 1.2 copy.46
  134.4 0.2 fusion.29
  134.7 0.7 bitcast_convert_fusion
  135.4 0.3 copy-done.2
  135.7 0.2 copy-done.3
  135.9 6.7 %add_reduce_fusion = (f32[32,8,512]{2,1,0:T(8,128)S(1)}, f32[32,8,512]{2,1,0:T(8,128)S(1)}) fusion(f32[32,8,512]{2,1,0:T(8,128)S(1)} %bitcast.34, f32[32,32,512]{2,1,0:T(8,128)S(1)} %get-tuple-element.13, f32[32,8,512]{2,1,0:T(8,128)S(1)} %bitcast.35, f32[32,32,512]{2,1,0:T(8,128)S(1)} %get-tuple-element.14), kind=kLoop, calls=%fused_computation.1 | loop fusion | flops 33292288 | bytes 6291456 | tf_op jit(solution)/shard_map/reduce_sum | solution.py:36
  142.6 2.8 %fusion.8 = f32[32,8,512]{2,1,0:T(8,128)} fusion(f32[512,512]{1,0:T(8,128)S(1)} %copy-done, f32[512,512]{1,0:T(8,128)S(1)} %get-tuple-element.11, f32[256,512]{1,0:T(8,128)S(1)} %bitcast.33, f32[256,512]{1,0:T(8,128)S(1)} %bitcast.32), kind=kOutput, calls=%fused_computation.13 | convolution fusion | flops 1611792384 | bytes 3670016 | tf_op jit(solution)/shard_map/dot_general | solution.py:40
  (16 shorter events, 0.5 us)
Async XLA Ops:
  0.0 2.4 %copy-start.1 = (bf16[2,8,32,512]{3,2,1,0:T(8,128)(2,1)S(1)}, bf16[2,8,32,512]{3,2,1,0:T(8,128)(2,1)}, u32[]{:S(2)}) copy-start(bf16[2,8,32,512]{3,2,1,0:T(8,128)(2,1)} %param.2) | copy-start | bytes 1572868
  50.0 19.0 %all-to-all-start.2 = ((bf16[2,8,32,512]{3,1,0,2:T(8,128)(2,1)}), bf16[2,8,32,512]{3,1,0,2:T(8,128)(2,1)S(1)}, u32[]{:S(2)}, u32[]{:S(2)}) async-start(bf16[2,8,32,512]{3,1,0,2:T(8,128)(2,1)} %multiply_convert_fusion), calls=%async_computation.2 | async-start | bytes 1048576 | tf_op jit(solution)/shard_map/all_to_all | solution.py:63
  69.0 1.9 %copy-start.4 = (bf16[2,8,32,512]{3,1,0,2:T(8,128)(2,1)}, bf16[2,8,32,512]{3,1,0,2:T(8,128)(2,1)S(1)}, u32[]{:S(2)}) copy-start(bf16[2,8,32,512]{3,1,0,2:T(8,128)(2,1)S(1)} %all-to-all-done.2) | copy-start | bytes 1572868
  70.9 62.4 %all-to-all-start.1 = ((bf16[512,4,512]{2,1,0:T(4,128)(2,1)}), bf16[512,4,512]{2,1,0:T(4,128)(2,1)S(1)}, u32[]{:S(2)}, u32[]{:S(2)}) async-start(bf16[512,4,512]{2,1,0:T(4,128)(2,1)} %broadcast_in_dim.2), calls=%async_computation.1 | async-start | bytes 4194304 | tf_op jit(solution)/shard_map/all_to_all | solution.py:54
  79.8 5.4 %copy-start.5 = (bf16[2,8,32,512]{3,1,0,2:T(8,128)(2,1)S(1)}, bf16[2,8,32,512]{3,1,0,2:T(8,128)(2,1)}, u32[]{:S(2)}) copy-start(bf16[2,8,32,512]{3,1,0,2:T(8,128)(2,1)} %copy-done.4) | copy-start | bytes 1572868
  134.6 1.0 copy-start.2
  134.7 1.2 copy-start.3
  135.9 6.7 %copy-start = (f32[512,512]{1,0:T(8,128)S(1)}, f32[512,512]{1,0:T(8,128)}, u32[]{:S(2)}) copy-start(f32[512,512]{1,0:T(8,128)} %get-tuple-element.12) | copy-start | bytes 3145732

commit v7 on v6

--- a/solution.py
+++ b/solution.py
@@ -49,9 +49,19 @@
     segs = lax.psum(1, seg_axis)
     chunks = value.reshape(count, -1, freqs)
     rows = chunks.shape[1]
-    mine = lax.all_to_all(chunks, chan_axes, 0, 0).sum(axis=0, dtype=value.dtype)
+    if chan_axes == CHAN_AXES:
+        inner = lax.psum(1, ("y", "c"))
+        outer = count // inner
+        part = value.reshape(inner, -1, freqs)
+        part = lax.all_to_all(part, ("y", "c"), 0, 0).sum(axis=0, dtype=value.dtype)
+        part = part.reshape(outer, rows, freqs)
+        mine = lax.all_to_all(part, ("x", "zh"), 0, 0).sum(axis=0, dtype=value.dtype)
+    else:
+        mine = lax.all_to_all(chunks, chan_axes, 0, 0).sum(axis=0, dtype=value.dtype)
     spread = jnp.broadcast_to(mine[None], (count * segs, rows, freqs))
     got = lax.all_to_all(spread, chan_axes + (seg_axis,), 0, 0)
+    if chan_axes == CHAN_AXES:
+        got = got.reshape(outer, inner, segs, rows, freqs).transpose(1, 0, 2, 3, 4)
     split = local_segs // rows
     got = got.reshape(parts, sources, split, segs, rows, freqs).transpose(0, 3, 2, 4, 1, 5)
     return got.reshape(parts, segs * local_segs, sources, freqs)

time: 146 us -> 150 us (1.027)
  blocking collectives: 44.5 us -> 47 us
    all_to_all x1 -> x2, blocking collectives: 44.5 us -> 47 us  [the longest x1 26.7 us: gather_sources(): part = lax.all_to_all(part, ('y', 'c'), 0, 0).sum(axis=0, dtype=value.dtype)]
where the time goes in v7:
time: 150 us; the launch traced here: 149 us
  waiting for transfers between devices  59.9 us (40%)
  blocking collectives  47 us (31%)
  other arithmetic  16.4 us (11%)
  starting transfers between devices  13.9 us (9%)
  local copies, waits for them, and re-layouts  7.6 us (5%)
  matrix products  4.22 us (3%)
    all_to_all x1, waiting for transfers between devices, gather_sources(): got = lax.all_to_all(spread, chan_axes + (seg_axis,), 0, 0)  45.9 us
    all_to_all x1, blocking collectives, gather_sources(): part = lax.all_to_all(part, ('y', 'c'), 0, 0).sum(axis=0, dtype=value.dtype)  26.7 us
    all_to_all x1, blocking collectives, gather_sources(): lax.all_to_all(part, ('x', 'zh'), 0, 0).sum(axis=0, dtype=value.dtype)  20.3 us
    all_to_all x1, waiting for transfers between devices, shards(): lax.all_to_all(whitened, 'seg', split_axis=2, concat_axis=1, tiled=True)  14.1 us
    all_to_all x1, starting transfers between devices, gather_sources(): got = lax.all_to_all(spread, chan_axes + (seg_axis,), 0, 0)  9.58 us
    reduce_sum x1, other arithmetic, correlate(): real_part = jnp.sum(a * c + b * d, axis=0)  6.72 us
    cos x1, other arithmetic, lag_matrix(): return jnp.concatenate([jnp.cos(angles), -jnp.sin(angles)], axis=0)  5.41 us
    all_to_all x1, starting transfers between devices, shards(): lax.all_to_all(whitened, 'seg', split_axis=2, concat_axis=1, tiled=True)  4.28 us
  transfers between devices with their start and end apart: 2, of which 2 were waited for; matrix products, arithmetic and copies ran while one was open for 5% of the time, Pallas kernels for 0%

profile of v7, /device:TPU:1, one launch (start us, length us, event | category | flops | bytes accessed | tf_op | source)
XLA Modules:
  0.0 149.2 jit_solution(12099203867394705971)
XLA Ops:
  0.0 0.7 broadcast_subtract_fusion
  0.9 1.4 copy_convert_fusion
  2.4 1.1 multiply_convert_fusion
  3.6 1.5 fusion.4
  5.0 0.3 copy.49
  5.3 26.7 %all_to_all.30 = bf16[16,32,512]{2,1,0:T(8,128)(2,1)S(1)} all-to-all(bf16[16,32,512]{2,1,0:T(8,128)(2,1)S(1)} %bitcast.40), channel_id=1, replica_groups=mesh['x'=4,'zh'=2,'y'=8,'c'=2,'seg'=4] {'y','c'}, dimensions={0} | all-to-all | bytes 1048576 | tf_op jit(solution)/shard_map/all_to_all | solution.py:56
  32.1 20.3 %all_to_all.31 = bf16[8,4,512]{2,1,0:T(4,128)(2,1)S(1)} all-to-all(bf16[8,4,512]{2,1,0:T(4,128)(2,1)S(1)} %reshape.77), channel_id=1, replica_groups=mesh['x'=4,'zh'=2,'y'=8,'c'=2,'seg'=4] {'x','zh'}, dimensions={0} | all-to-all | bytes 65536 | tf_op jit(solution)/shard_map/all_to_all | solution.py:58
  52.4 4.3 %all-to-all-start.3 = ((bf16[2,8,32,512]{3,1,0,2:T(8,128)(2,1)}), bf16[2,8,32,512]{3,1,0,2:T(8,128)(2,1)S(1)}, u32[]{:S(2)}, u32[]{:S(2)}) async-start(bf16[2,8,32,512]{3,1,0,2:T(8,128)(2,1)} %multiply_convert_fusion), calls=%async_computation.3 | async-start | bytes 1048576 | tf_op jit(solution)/shard_map/all_to_all | solution.py:73
  56.7 14.1 %all-to-all-done.3 = bf16[2,8,32,512]{3,1,0,2:T(8,128)(2,1)S(1)} async-done(((bf16[2,8,32,512]{3,1,0,2:T(8,128)(2,1)}), bf16[2,8,32,512]{3,1,0,2:T(8,128)(2,1)S(1)}, u32[]{:S(2)}, u32[]{:S(2)}) %all-to-all-start.3) | async-done | bytes 524320 | tf_op jit(solution)/shard_map/all_to_all | solution.py:73
  70.8 1.9 %broadcast_in_dim.2 = bf16[512,4,512]{2,1,0:T(4,128)(2,1)} broadcast(bf16[4,512]{1,0:T(4,128)(2,1)S(1)} %reduce_sum.47), dimensions={1,2} | broadcast | bytes 2101248 | tf_op jit(solution)/shard_map/broadcast_in_dim | solution.py:61
  72.7 9.6 %all-to-all-start.2 = ((bf16[512,4,512]{2,1,0:T(4,128)(2,1)}), bf16[512,4,512]{2,1,0:T(4,128)(2,1)S(1)}, u32[]{:S(2)}, u32[]{:S(2)}) async-start(bf16[512,4,512]{2,1,0:T(4,128)(2,1)} %broadcast_in_dim.2), calls=%async_computation.2 | async-start | bytes 4194304 | tf_op jit(solution)/shard_map/all_to_all | solution.py:62
  82.3 5.4 %fusion.22 = (f32[512,512]{1,0:T(8,128)S(1)}, f32[512,512]{1,0:T(8,128)}) fusion(s32[512]{0:T(512)S(1)} %iota_add_fusion), kind=kLoop, calls=%fused_computation.34 | loop fusion | flops 3932160 | bytes 2099200 | tf_op jit(solution)/shard_map/cos | solution.py:26
  87.7 0.3 copy.66
  88.2 0.8 copy.54
  89.0 0.8 copy.55
  89.8 45.9 %all-to-all-done.2 = bf16[512,4,512]{2,1,0:T(4,128)(2,1)S(1)} async-done(((bf16[512,4,512]{2,1,0:T(4,128)(2,1)}), bf16[512,4,512]{2,1,0:T(4,128)(2,1)S(1)}, u32[]{:S(2)}, u32[]{:S(2)}) %all-to-all-start.2) | async-done | bytes 2097184 | tf_op jit(solution)/shard_map/all_to_all | solution.py:62
  135.7 1.4 copy.51
  137.1 1.2 copy.65
  138.3 0.2 fusion.29
  138.5 0.7 bitcast_convert_fusion
  139.2 0.3 copy-done.2
  139.5 0.2 copy-done.3
  139.7 6.7 %add_reduce_fusion = (f32[32,8,512]{2,1,0:T(8,128)S(1)}, f32[32,8,512]{2,1,0:T(8,128)S(1)}) fusion(f32[32,8,512]{2,1,0:T(8,128)S(1)} %bitcast.38, f32[32,32,512]{2,1,0:T(8,128)S(1)} %get-tuple-element.13, f32[32,8,512]{2,1,0:T(8,128)S(1)} %bitcast.37, f32[32,32,512]{2,1,0:T(8,128)S(1)} %get-tuple-element.14), kind=kLoop, calls=%fused_computation.1 | loop fusion | flops 33292288 | bytes 6291456 | tf_op jit(solution)/shard_map/reduce_sum | solution.py:36
  146.4 2.8 %fusion.8 = f32[32,8,512]{2,1,0:T(8,128)} fusion(f32[512,512]{1,0:T(8,128)S(1)} %copy-done, f32[512,512]{1,0:T(8,128)S(1)} %get-tuple-element.11, f32[256,512]{1,0:T(8,128)S(1)} %bitcast.36, f32[256,512]{1,0:T(8,128)S(1)} %bitcast.35), kind=kOutput, calls=%fused_computation.13 | convolution fusion | flops 1611792384 | bytes 3670016 | tf_op jit(solution)/shard_map/dot_general | solution.py:40
  (19 shorter events, 0.6 us)
Async XLA Ops:
  0.0 2.4 %copy-start.1 = (bf16[2,8,32,512]{3,2,1,0:T(8,128)(2,1)S(1)}, bf16[2,8,32,512]{3,2,1,0:T(8,128)(2,1)}, u32[]{:S(2)}) copy-start(bf16[2,8,32,512]{3,2,1,0:T(8,128)(2,1)} %param.2) | copy-start | bytes 1572868
  52.4 18.4 %all-to-all-start.3 = ((bf16[2,8,32,512]{3,1,0,2:T(8,128)(2,1)}), bf16[2,8,32,512]{3,1,0,2:T(8,128)(2,1)S(1)}, u32[]{:S(2)}, u32[]{:S(2)}) async-start(bf16[2,8,32,512]{3,1,0,2:T(8,128)(2,1)} %multiply_convert_fusion), calls=%async_computation.3 | async-start | bytes 1048576 | tf_op jit(solution)/shard_map/all_to_all | solution.py:73
  70.8 1.9 %copy-start.4 = (bf16[2,8,32,512]{3,1,0,2:T(8,128)(2,1)}, bf16[2,8,32,512]{3,1,0,2:T(8,128)(2,1)S(1)}, u32[]{:S(2)}) copy-start(bf16[2,8,32,512]{3,1,0,2:T(8,128)(2,1)S(1)} %all-to-all-done.3) | copy-start | bytes 1572868
  72.7 63.0 %all-to-all-start.2 = ((bf16[512,4,512]{2,1,0:T(4,128)(2,1)}), bf16[512,4,512]{2,1,0:T(4,128)(2,1)S(1)}, u32[]{:S(2)}, u32[]{:S(2)}) async-start(bf16[512,4,512]{2,1,0:T(4,128)(2,1)} %broadcast_in_dim.2), calls=%async_computation.2 | async-start | bytes 4194304 | tf_op jit(solution)/shard_map/all_to_all | solution.py:62
  82.3 5.4 %copy-start.5 = (bf16[2,8,32,512]{3,1,0,2:T(8,128)(2,1)S(1)}, bf16[2,8,32,512]{3,1,0,2:T(8,128)(2,1)}, u32[]{:S(2)}) copy-start(bf16[2,8,32,512]{3,1,0,2:T(8,128)(2,1)} %copy-done.4) | copy-start | bytes 1572868
  138.5 1.0 copy-start.2
  138.5 1.2 copy-start.3
  139.7 6.7 %copy-start = (f32[512,512]{1,0:T(8,128)S(1)}, f32[512,512]{1,0:T(8,128)}, u32[]{:S(2)}) copy-start(f32[512,512]{1,0:T(8,128)} %get-tuple-element.12) | copy-start | bytes 3145732

commit v8 on v6

--- a/solution.py
+++ b/solution.py
@@ -50,8 +50,7 @@
     chunks = value.reshape(count, -1, freqs)
     rows = chunks.shape[1]
     mine = lax.all_to_all(chunks, chan_axes, 0, 0).sum(axis=0, dtype=value.dtype)
-    spread = jnp.broadcast_to(mine[None], (count * segs, rows, freqs))
-    got = lax.all_to_all(spread, chan_axes + (seg_axis,), 0, 0)
+    got = lax.all_gather(mine, chan_axes + (seg_axis,), axis=0)
     split = local_segs // rows
     got = got.reshape(parts, sources, split, segs, rows, freqs).transpose(0, 3, 2, 4, 1, 5)
     return got.reshape(parts, segs * local_segs, sources, freqs)

time: 146 us -> 1120 us (7.67)
  waiting for transfers between devices: 60.3 us -> 1040 us
  between operations: 0.13 us -> 13.5 us
    all_gather x0 -> x1, waiting for transfers between devices: none -> 1030 us  [gather_sources(): got = lax.all_gather(mine, chan_axes + (seg_axis,), axis=0)]
    all_to_all x1 -> x0, waiting for transfers between devices: 45.9 us -> none  [gather_sources(): got = lax.all_to_all(spread, chan_axes + (seg_axis,), 0, 0)]
  transfers between devices with their start and end apart: 2 -> 2, of which waited for: 2 -> 2; matrix products, arithmetic and copies ran while one was open for 5% -> 0% of each run, Pallas kernels for 0% -> 0%
where the time goes in v8:
time: 1120 us
  waiting for transfers between devices  1040 us (93%)
  blocking collectives  44.5 us (4%)
  other arithmetic  15.9 us (1%)
  between operations  13.5 us (1%)
    all_gather x1, waiting for transfers between devices, gather_sources(): got = lax.all_gather(mine, chan_axes + (seg_axis,), axis=0)  1030 us
    all_to_all x1, blocking collectives, gather_sources(): lax.all_to_all(chunks, chan_axes, 0, 0).sum(axis=0, dtype=value.dtype)  44.5 us
  transfers between devices with their start and end apart: 2, of which 2 were waited for; matrix products, arithmetic and copies ran while one was open for 0% of the time, Pallas kernels for 0%

profile of v8, /device:TPU:1, one launch (start us, length us, event | category | flops | bytes accessed | tf_op | source)
XLA Modules:
  0.0 1123.9 jit_solution(16742791527962785791)
XLA Ops:
  6.5 0.0 all-gather.4.cloned.1.call-start
  6.5 0.7 broadcast_subtract_fusion
  7.3 0.1 copy.31
  7.4 0.1 sub.24
  7.4 1.4 copy_convert_fusion
  8.8 0.1 fusion.20
  9.0 1.1 multiply_convert_fusion
  10.1 1.5 fusion.4
  11.6 0.3 copy.33
  11.9 0.1 reshape.69
  12.0 44.5 %all_to_all.20 = bf16[128,4,512]{2,1,0:T(4,128)(2,1)S(1)} all-to-all(bf16[128,4,512]{2,1,0:T(4,128)(2,1)S(1)} %reshape.69), channel_id=1, replica_groups=mesh['x'=4,'zh'=2,'y'=8,'c'=2,'seg'=4] {'x','zh','y','c'}, dimensions={0} | all-to-all | bytes 1048576 | tf_op jit(solution)/shard_map/all_to_all | solution.py:52
  56.5 0.9 reduce_sum.37
  57.4 0.0 all-gather.4.cloned.1.call-update
  57.4 4.3 all-to-all-start.1
  61.7 4.1 fusion.22
  65.8 10.7 all-to-all-done.1
  76.5 0.3 copy.47
  76.8 0.1 slice_convert_fusion.1
  77.0 1026.8 %all-gather.4.cloned.1.call-done = bf16[512,4,512]{2,1,0:T(4,128)(2,1)} async-done(((bf16[1,4,512]{2,1,0:T(4,128)(2,1)}), bf16[512,4,512]{2,1,0:T(4,128)(2,1)}) %all-gather.4.cloned.1.call-update) | async-done | bytes 2097168 | tf_op jit(solution)/shard_map/all_gather | solution.py:53
  1103.9 2.7 copy.46
  1106.6 0.2 fusion.29
  1106.8 0.7 bitcast_convert_fusion
  1107.6 6.7 add_reduce_fusion
  1114.3 2.8 fusion.8
  (6 shorter events, 0.1 us)
Async XLA Ops:
  6.5 2.4 copy-start
  6.5 1097.3 %all-gather.4.cloned.1.call-start = ((), (), s32[]{:S(2)}) async-start(), calls=%async_computation.2 | async-start | bytes 2101248 | tf_op jit(solution)/shard_map/all_gather | solution.py:53
  57.4 19.1 %all-to-all-start.1 = ((bf16[2,8,32,512]{3,1,0,2:T(8,128)(2,1)}), bf16[2,8,32,512]{3,1,0,2:T(8,128)(2,1)S(1)}, u32[]{:S(2)}, u32[]{:S(2)}) async-start(bf16[2,8,32,512]{3,1,0,2:T(8,128)(2,1)} %multiply_convert_fusion), calls=%async_computation.1 | async-start | bytes 1048576 | tf_op jit(solution)/shard_map/all_to_all | solution.py:62
Sparse Core Ops, SparseCore 0:
  57.5 1046.2 all-gather.3

commit v9 on v6

--- a/solution.py
+++ b/solution.py
@@ -57,10 +57,34 @@
     return got.reshape(parts, segs * local_segs, sources, freqs)
 
 
+def regroup_receivers(whitened, seg_axis):
+    segs = lax.psum(1, seg_axis)
+    me = lax.axis_index(seg_axis)
+    parts, local_segs, ch_dev, freqs = whitened.shape
+    groups = whitened.reshape(parts, local_segs, segs, ch_dev // segs, freqs)
+
+    def group(index):
+        return lax.dynamic_index_in_dim(groups, index, axis=2, keepdims=False)
+
+    blocks = [group(me)]
+    for shift in range(1, segs):
+        pairs = [(i, (i + shift) % segs) for i in range(segs)]
+        blocks.append(lax.ppermute(group((me + shift) % segs), seg_axis, pairs))
+    return jnp.concatenate(blocks[::-1], axis=1)
+
+
+def rotate_segments(source_spec, seg_axis):
+    segs = lax.psum(1, seg_axis)
+    me = lax.axis_index(seg_axis)
+    parts, all_segs, sources, freqs = source_spec.shape
+    doubled = jnp.concatenate([source_spec, source_spec], axis=1)
+    return lax.dynamic_slice_in_dim(doubled, ((me + 1) % segs) * (all_segs // segs), all_segs, axis=1)
+
+
 def make_shards(chan_axes):
     def shards(spectra, sources):
         whitened = whiten(spectra)
-        regrouped = lax.all_to_all(whitened, "seg", split_axis=2, concat_axis=1, tiled=True)
+        regrouped = regroup_receivers(whitened, "seg")
         ch_dev = spectra.shape[2]
         freqs = spectra.shape[3]
         first_row = lax.axis_index(chan_axes) * ch_dev
@@ -72,7 +96,7 @@
         local_spec = jnp.einsum(
             "pc,xscf->xpsf", onehot, whitened, preferred_element_type=jnp.float32
         ).astype(jnp.bfloat16)
-        source_spec = gather_sources(local_spec, chan_axes, "seg")
+        source_spec = rotate_segments(gather_sources(local_spec, chan_axes, "seg"), "seg")
         return correlate(source_spec, regrouped, lag_table)
 
     return shards

time: 146 us -> 132 us (0.904)
  waiting for transfers between devices: 60.3 us -> 40.8 us
  starting transfers between devices: 13.2 us -> 19.7 us
  other arithmetic: 16.6 us -> 18.2 us
    all_to_all x1, waiting for transfers between devices: 45.9 us -> 0.01 us  [gather_sources(): got = lax.all_to_all(spread, chan_axes + (seg_axis,), 0, 0)]
    ppermute x0 -> x3, waiting for transfers between devices: none -> 40.8 us  [regroup_receivers(): blocks.append(lax.ppermute(group((me + shift) % segs), seg_axis, pairs))]
    all_to_all x1 -> x0, waiting for transfers between devices: 14.4 us -> none  [shards(): lax.all_to_all(whitened, 'seg', split_axis=2, concat_axis=1, tiled=True)]
    ppermute x0 -> x3, starting transfers between devices: none -> 10.8 us  [regroup_receivers(): blocks.append(lax.ppermute(group((me + shift) % segs), seg_axis, pairs))]
    all_to_all x1 -> x0, starting transfers between devices: 4.27 us -> none  [shards(): lax.all_to_all(whitened, 'seg', split_axis=2, concat_axis=1, tiled=True)]
    concatenate x0 -> x2, other arithmetic: none -> 1.9 us  [the longest x1 1.1 us: regroup_receivers(): return jnp.concatenate(blocks[::-1], axis=1)]
    convert_element_type x2 -> x0, local copies, waits for them, and re-layouts: 1.67 us -> none  [the longest x1 0.84 us: correlate(): d = receiver_spec[1].astype(jnp.float32)[:, None, :, :]]
  transfers between devices with their start and end apart: 2 -> 4, of which waited for: 2 -> 2; matrix products, arithmetic and copies ran while one was open for 5% -> 6% of each run, Pallas kernels for 0% -> 0%
where the time goes in v9:
time: 132 us
  blocking collectives  44.5 us (34%)
  waiting for transfers between devices  40.8 us (31%)
  starting transfers between devices  19.7 us (15%)
  other arithmetic  18.2 us (14%)
  local copies, waits for them, and re-layouts  4.94 us (4%)
  matrix products  3.14 us (2%)
    all_to_all x1, blocking collectives, gather_sources(): lax.all_to_all(chunks, chan_axes, 0, 0).sum(axis=0, dtype=value.dtype)  44.5 us
    ppermute x3, waiting for transfers between devices, regroup_receivers(): blocks.append(lax.ppermute(group((me + shift) % segs), seg_axis, pairs))  40.8 us
    ppermute x3, starting transfers between devices, regroup_receivers(): blocks.append(lax.ppermute(group((me + shift) % segs), seg_axis, pairs))  10.8 us
    all_to_all x1, starting transfers between devices, gather_sources(): got = lax.all_to_all(spread, chan_axes + (seg_axis,), 0, 0)  8.89 us
    reduce_sum x1, other arithmetic, correlate(): real_part = jnp.sum(a * c + b * d, axis=0)  6.72 us
    cos x1, other arithmetic, lag_matrix(): return jnp.concatenate([jnp.cos(angles), -jnp.sin(angles)], axis=0)  5.41 us
    dot_general x1, matrix products, correlate(): jnp.dot(flat, lag_table, precision=lax.Precision.HIGHEST, preferred_eleme...  2.76 us
  transfers between devices with their start and end apart: 4, of which 2 were waited for; matrix products, arithmetic and copies ran while one was open for 6% of the time, Pallas kernels for 0%

profile of v9, /device:TPU:1, one launch (start us, length us, event | category | flops | bytes accessed | tf_op | source)
XLA Modules:
  0.0 131.5 jit_solution(15002162888171040022)
XLA Ops:
  0.0 0.7 broadcast_subtract_fusion
  0.9 1.2 convert_element_type.58
  2.3 0.4 fusion.5
  2.7 0.3 copy.10
  3.1 44.5 %all_to_all.10 = bf16[128,4,512]{2,1,0:T(4,128)(2,1)S(1)} all-to-all(bf16[128,4,512]{2,1,0:T(4,128)(2,1)S(1)} %reshape.67), channel_id=1, replica_groups=mesh['x'=4,'zh'=2,'y'=8,'c'=2,'seg'=4] {'x','zh','y','c'}, dimensions={0} | all-to-all | bytes 1048576 | tf_op jit(solution)/shard_map/all_to_all | solution.py:52
  47.6 0.3 reduce_sum.37
  47.9 1.9 %broadcast_in_dim.2 = bf16[512,4,512]{2,1,0:T(4,128)(2,1)} broadcast(bf16[4,512]{1,0:T(4,128)(2,1)S(1)} %reduce_sum.37), dimensions={1,2} | broadcast | bytes 2101248 | tf_op jit(solution)/shard_map/broadcast_in_dim | solution.py:53
  49.8 8.9 %all-to-all-start.1 = ((bf16[512,4,512]{2,1,0:T(4,128)(2,1)}), bf16[512,4,512]{2,1,0:T(4,128)(2,1)S(1)}, u32[]{:S(2)}, u32[]{:S(2)}) async-start(bf16[512,4,512]{2,1,0:T(4,128)(2,1)} %broadcast_in_dim.2), calls=%async_computation.1 | async-start | bytes 4194304 | tf_op jit(solution)/shard_map/all_to_all | solution.py:54
  58.9 0.7 dynamic-slice_bitcast_fusion.3
  59.6 6.5 %collective-permute-start = (bf16[2,8,8,512]{3,2,1,0:T(8,128)(2,1)}, bf16[2,8,8,512]{3,2,1,0:T(8,128)(2,1)}, u32[]{:S(2)}, u32[]{:S(2)}) collective-permute-start(bf16[2,8,8,512]{3,2,1,0:T(8,128)(2,1)} %get-tuple-element.11), channel_id=1, source_target_pairs={{0,3},{1,0},{2,1},{3,2},{4,7},{5,4},{6,5},{7,6},{8,11},{9,8},{10,9... | collective-permute-start | bytes 393224 | tf_op jit(solution)/shard_map/ppermute | solution.py:72
  66.1 1.9 %collective-permute-start.1 = (bf16[2,8,8,512]{3,2,1,0:T(8,128)(2,1)S(1)}, bf16[2,8,8,512]{3,2,1,0:T(8,128)(2,1)}, u32[]{:S(2)}, u32[]{:S(2)}) collective-permute-start(bf16[2,8,8,512]{3,2,1,0:T(8,128)(2,1)S(1)} %get-tuple-element.14), channel_id=1, source_target_pairs={{0,2},{1,3},{2,0},{3,1},{4,6},{5,7},{6,4},{7,5},{8,10},{9,11},{10,... | collective-permute-start | bytes 393224 | tf_op jit(solution)/shard_map/ppermute | solution.py:72
  68.1 2.4 %collective-permute-start.2 = (bf16[2,8,8,512]{3,2,1,0:T(8,128)(2,1)S(1)}, bf16[2,8,8,512]{3,2,1,0:T(8,128)(2,1)}, u32[]{:S(2)}, u32[]{:S(2)}) collective-permute-start(bf16[2,8,8,512]{3,2,1,0:T(8,128)(2,1)S(1)} %get-tuple-element.13), channel_id=1, source_target_pairs={{0,1},{1,2},{2,3},{3,0},{4,5},{5,6},{6,7},{7,4},{8,9},{9,10},{10,1... | collective-permute-start | bytes 393224 | tf_op jit(solution)/shard_map/ppermute | solution.py:72
  70.5 5.4 %fusion.24 = (f32[512,512]{1,0:T(8,128)S(1)}, f32[512,512]{1,0:T(8,128)}) fusion(s32[512]{0:T(512)S(1)} %iota_add_fusion), kind=kLoop, calls=%fused_computation.36 | loop fusion | flops 3932160 | bytes 2099200 | tf_op jit(solution)/shard_map/cos | solution.py:26
  75.9 29.3 %collective-permute-done = bf16[2,8,8,512]{3,2,1,0:T(8,128)(2,1)} collective-permute-done((bf16[2,8,8,512]{3,2,1,0:T(8,128)(2,1)}, bf16[2,8,8,512]{3,2,1,0:T(8,128)(2,1)}, u32[]{:S(2)}, u32[]{:S(2)}) %collective-permute-start) | collective-permute-done | bytes 131104 | tf_op jit(solution)/shard_map/ppermute | solution.py:72
  105.1 11.5 %collective-permute-done.1 = bf16[2,8,8,512]{3,2,1,0:T(8,128)(2,1)} collective-permute-done((bf16[2,8,8,512]{3,2,1,0:T(8,128)(2,1)S(1)}, bf16[2,8,8,512]{3,2,1,0:T(8,128)(2,1)}, u32[]{:S(2)}, u32[]{:S(2)}) %collective-permute-start.1) | collective-permute-done | bytes 131104 | tf_op jit(solution)/shard_map/ppermute | solution.py:72
  116.6 1.1 pad_maximum_fusion
  117.7 1.1 fusion.27
  118.9 1.2 copy.11
  120.0 0.8 fusion
  120.8 0.6 fusion.16
  121.4 0.4 copy-done.2
  121.9 0.2 copy-done.3
  122.0 6.7 %add_reduce_fusion = (f32[32,8,512]{2,1,0:T(8,128)S(1)}, f32[32,8,512]{2,1,0:T(8,128)S(1)}) fusion(f32[32,8,512]{2,1,0:T(8,128)S(1)} %copy-done.3, f32[32,32,512]{2,1,0:T(8,128)S(1)} %get-tuple-element.8, f32[32,8,512]{2,1,0:T(8,128)S(1)} %copy-done.2, f32[32,32,512]{2,1,0:T(8,128)S(1)} %get-tuple-element.7), kind=kLoop, calls=%fused_computation.1 | loop fusion | flops 33292288 | bytes 6291456 | tf_op jit(solution)/shard_map/reduce_sum | solution.py:36
  128.8 2.8 %fusion.9 = f32[32,8,512]{2,1,0:T(8,128)} fusion(f32[512,512]{1,0:T(8,128)S(1)} %copy-done.1, f32[512,512]{1,0:T(8,128)S(1)} %get-tuple-element.15, f32[256,512]{1,0:T(8,128)S(1)} %bitcast.50, f32[256,512]{1,0:T(8,128)S(1)} %bitcast.49), kind=kOutput, calls=%fused_computation.15 | convolution fusion | flops 1611792384 | bytes 3670016 | tf_op jit(solution)/shard_map/dot_general | solution.py:40
  (15 shorter events, 0.6 us)
Async XLA Ops:
  0.0 2.2 %copy-start = (bf16[2,8,32,512]{3,2,1,0:T(8,128)(2,1)S(1)}, bf16[2,8,32,512]{3,2,1,0:T(8,128)(2,1)}, u32[]{:S(2)}) copy-start(bf16[2,8,32,512]{3,2,1,0:T(8,128)(2,1)} %param.2) | copy-start | bytes 1572868
  49.8 69.1 %all-to-all-start.1 = ((bf16[512,4,512]{2,1,0:T(4,128)(2,1)}), bf16[512,4,512]{2,1,0:T(4,128)(2,1)S(1)}, u32[]{:S(2)}, u32[]{:S(2)}) async-start(bf16[512,4,512]{2,1,0:T(4,128)(2,1)} %broadcast_in_dim.2), calls=%async_computation.1 | async-start | bytes 4194304 | tf_op jit(solution)/shard_map/all_to_all | solution.py:54
  59.6 45.6 %collective-permute-start = (bf16[2,8,8,512]{3,2,1,0:T(8,128)(2,1)}, bf16[2,8,8,512]{3,2,1,0:T(8,128)(2,1)}, u32[]{:S(2)}, u32[]{:S(2)}) collective-permute-start(bf16[2,8,8,512]{3,2,1,0:T(8,128)(2,1)} %get-tuple-element.11), channel_id=1, source_target_pairs={{0,3},{1,0},{2,1},{3,2},{4,7},{5,4},{6,5},{7,6},{8,11},{9,8},{10,9... | collective-permute-start | bytes 393224 | tf_op jit(solution)/shard_map/ppermute | solution.py:72
  66.1 50.5 %collective-permute-start.1 = (bf16[2,8,8,512]{3,2,1,0:T(8,128)(2,1)S(1)}, bf16[2,8,8,512]{3,2,1,0:T(8,128)(2,1)}, u32[]{:S(2)}, u32[]{:S(2)}) collective-permute-start(bf16[2,8,8,512]{3,2,1,0:T(8,128)(2,1)S(1)} %get-tuple-element.14), channel_id=1, source_target_pairs={{0,2},{1,3},{2,0},{3,1},{4,6},{5,7},{6,4},{7,5},{8,10},{9,11},{10,... | collective-permute-start | bytes 393224 | tf_op jit(solution)/shard_map/ppermute | solution.py:72
  68.1 48.6 %collective-permute-start.2 = (bf16[2,8,8,512]{3,2,1,0:T(8,128)(2,1)S(1)}, bf16[2,8,8,512]{3,2,1,0:T(8,128)(2,1)}, u32[]{:S(2)}, u32[]{:S(2)}) collective-permute-start(bf16[2,8,8,512]{3,2,1,0:T(8,128)(2,1)S(1)} %get-tuple-element.13), channel_id=1, source_target_pairs={{0,1},{1,2},{2,3},{3,0},{4,5},{5,6},{6,7},{7,4},{8,9},{9,10},{10,1... | collective-permute-start | bytes 393224 | tf_op jit(solution)/shard_map/ppermute | solution.py:72
  120.8 1.0 copy-start.2
  120.8 1.2 copy-start.3
  122.0 6.7 %copy-start.1 = (f32[512,512]{1,0:T(8,128)S(1)}, f32[512,512]{1,0:T(8,128)}, u32[]{:S(2)}) copy-start(f32[512,512]{1,0:T(8,128)} %get-tuple-element.16) | copy-start | bytes 3145732

commit v10 on v8

--- a/solution.py
+++ b/solution.py
@@ -43,23 +43,40 @@
     return result.reshape(stacked.shape[0], stacked.shape[1], -1)
 
 
-def gather_sources(value, chan_axes, seg_axis):
+def gather_sources(value, chan_axes):
     parts, sources, local_segs, freqs = value.shape
     count = lax.psum(1, chan_axes)
+    chunks = value.reshape(count, -1, freqs)
+    mine = lax.all_to_all(chunks, chan_axes, 0, 0).sum(axis=0, dtype=value.dtype)
+    spread = jnp.broadcast_to(mine[None], chunks.shape)
+    got = lax.all_to_all(spread, chan_axes, 0, 0).reshape(value.shape)
+    return got.transpose(0, 2, 1, 3)
+
+
+def regroup(whitened, source_spec, seg_axis):
     segs = lax.psum(1, seg_axis)
-    chunks = value.reshape(count, -1, freqs)
-    rows = chunks.shape[1]
-    mine = lax.all_to_all(chunks, chan_axes, 0, 0).sum(axis=0, dtype=value.dtype)
-    got = lax.all_gather(mine, chan_axes + (seg_axis,), axis=0)
-    split = local_segs // rows
-    got = got.reshape(parts, sources, split, segs, rows, freqs).transpose(0, 3, 2, 4, 1, 5)
-    return got.reshape(parts, segs * local_segs, sources, freqs)
+    me = lax.axis_index(seg_axis)
+    parts, local_segs, ch_dev, freqs = whitened.shape
+    groups = whitened.reshape(parts, local_segs, segs, ch_dev // segs, freqs)
+
+    def group(index):
+        return lax.dynamic_index_in_dim(groups, index, axis=2, keepdims=False)
+
+    receivers = [group(me)]
+    sources = [source_spec]
+    width = ch_dev // segs
+    for shift in range(1, segs):
+        pairs = [(i, (i + shift) % segs) for i in range(segs)]
+        payload = jnp.concatenate([group((me + shift) % segs), source_spec], axis=2)
+        got = lax.ppermute(payload, seg_axis, pairs)
+        receivers.append(got[:, :, :width])
+        sources.append(got[:, :, width:])
+    return jnp.concatenate(sources, axis=1), jnp.concatenate(receivers, axis=1)
 
 
 def make_shards(chan_axes):
     def shards(spectra, sources):
         whitened = whiten(spectra)
-        regrouped = lax.all_to_all(whitened, "seg", split_axis=2, concat_axis=1, tiled=True)
         ch_dev = spectra.shape[2]
         freqs = spectra.shape[3]
         first_row = lax.axis_index(chan_axes) * ch_dev
@@ -71,7 +88,7 @@
         local_spec = jnp.einsum(
             "pc,xscf->xpsf", onehot, whitened, preferred_element_type=jnp.float32
         ).astype(jnp.bfloat16)
-        source_spec = gather_sources(local_spec, chan_axes, "seg")
+        source_spec, regrouped = regroup(whitened, gather_sources(local_spec, chan_axes), "seg")
         return correlate(source_spec, regrouped, lag_table)
 
     return shards

time: 1120 us -> 152 us (0.14)
  the two profiles are of different devices: /device:TPU:1 before, /device:TPU:65 now
where the time goes in v10:
time: 152 us; the launch traced here: 151 us
  waiting for transfers between devices  71.3 us (47%)
  blocking collectives  42.8 us (28%)
  starting transfers between devices  14.8 us (10%)
  other arithmetic  14.1 us (9%)
  local copies, waits for them, and re-layouts  5.06 us (3%)
  matrix products  3.15 us (2%)
    ppermute x3, waiting for transfers between devices, regroup(): got = lax.ppermute(payload, seg_axis, pairs)  47.9 us
    all_to_all x1, blocking collectives, gather_sources(): lax.all_to_all(chunks, chan_axes, 0, 0).sum(axis=0, dtype=value.dtype)  42.8 us
    all_to_all x1, waiting for transfers between devices, gather_sources(): got = lax.all_to_all(spread, chan_axes, 0, 0).reshape(value.shape)  23.4 us
    ppermute x3, starting transfers between devices, regroup(): got = lax.ppermute(payload, seg_axis, pairs)  9.47 us
    reduce_sum x1, other arithmetic, correlate(): real_part = jnp.sum(a * c + b * d, axis=0)  6.94 us
    all_to_all x1, starting transfers between devices, gather_sources(): got = lax.all_to_all(spread, chan_axes, 0, 0).reshape(value.shape)  5.31 us
    cos x1, other arithmetic, lag_matrix(): return jnp.concatenate([jnp.cos(angles), -jnp.sin(angles)], axis=0)  4.12 us
  transfers between devices with their start and end apart: 4, of which 4 were waited for; matrix products, arithmetic and copies ran while one was open for 3% of the time, Pallas kernels for 0%

profile of v10, /device:TPU:65, one launch (start us, length us, event | category | flops | bytes accessed | tf_op | source)
XLA Modules:
  0.0 151.5 jit_solution(9992587047028563747)
XLA Ops:
  0.0 1.2 convert_element_type.58
  1.6 0.4 fusion.4
  2.0 0.3 copy.15
  2.4 42.8 %all_to_all.10 = bf16[128,4,512]{2,1,0:T(4,128)(2,1)S(1)} all-to-all(bf16[128,4,512]{2,1,0:T(4,128)(2,1)S(1)} %reshape.64), channel_id=1, replica_groups=mesh['x'=4,'zh'=2,'y'=8,'c'=2,'seg'=4] {'x','zh','y','c'}, dimensions={0} | all-to-all | bytes 1048576 | tf_op jit(solution)/shard_map/all_to_all | solution.py:50
  45.2 0.3 reduce_sum.37
  45.5 0.9 broadcast_in_dim.2
  46.4 5.3 %all-to-all-start.1 = ((bf16[128,4,512]{2,1,0:T(4,128)(2,1)}), bf16[128,4,512]{2,1,0:T(4,128)(2,1)S(1)}, u32[]{:S(2)}, u32[]{:S(2)}) async-start(bf16[128,4,512]{2,1,0:T(4,128)(2,1)} %broadcast_in_dim.2), calls=%async_computation.1 | async-start | bytes 1048576 | tf_op jit(solution)/shard_map/all_to_all | solution.py:52
  51.8 0.2 fusion.27
  52.2 23.4 %all-to-all-done.1 = bf16[128,4,512]{2,1,0:T(4,128)(2,1)S(1)} async-done(((bf16[128,4,512]{2,1,0:T(4,128)(2,1)}), bf16[128,4,512]{2,1,0:T(4,128)(2,1)S(1)}, u32[]{:S(2)}, u32[]{:S(2)}) %all-to-all-start.1) | async-done | bytes 524320 | tf_op jit(solution)/shard_map/all_to_all | solution.py:52
  75.8 3.2 %collective-permute-start = (bf16[2,8,40,512]{3,1,2,0:T(8,128)(2,1)S(1)}, bf16[2,8,40,512]{3,1,2,0:T(8,128)(2,1)S(1)}, u32[]{:S(2)}, u32[]{:S(2)}) collective-permute-start(bf16[2,8,40,512]{3,1,2,0:T(8,128)(2,1)S(1)} %get-tuple-element.15), channel_id=1, source_target_pairs={{0,1},{1,2},{2,3},{3,0},{4,5},{5,6},{6,7},{7,4},{8,9},{9,10},{10,1... | collective-permute-start | bytes 1966088 | tf_op jit(solution)/shard_map/ppermute | solution.py:71
  79.0 3.0 %collective-permute-start.1 = (bf16[2,8,40,512]{3,1,2,0:T(8,128)(2,1)S(1)}, bf16[2,8,40,512]{3,1,2,0:T(8,128)(2,1)S(1)}, u32[]{:S(2)}, u32[]{:S(2)}) collective-permute-start(bf16[2,8,40,512]{3,1,2,0:T(8,128)(2,1)S(1)} %get-tuple-element.16), channel_id=1, source_target_pairs={{0,2},{1,3},{2,0},{3,1},{4,6},{5,7},{6,4},{7,5},{8,10},{9,11},{10,... | collective-permute-start | bytes 1966088 | tf_op jit(solution)/shard_map/ppermute | solution.py:71
  82.0 3.3 %collective-permute-start.2 = (bf16[2,8,40,512]{3,1,2,0:T(8,128)(2,1)S(1)}, bf16[2,8,40,512]{3,1,2,0:T(8,128)(2,1)S(1)}, u32[]{:S(2)}, u32[]{:S(2)}) collective-permute-start(bf16[2,8,40,512]{3,1,2,0:T(8,128)(2,1)S(1)} %get-tuple-element.17), channel_id=1, source_target_pairs={{0,3},{1,0},{2,1},{3,2},{4,7},{5,4},{6,5},{7,6},{8,11},{9,8},{10,9... | collective-permute-start | bytes 1966088 | tf_op jit(solution)/shard_map/ppermute | solution.py:71
  85.4 4.1 %fusion.23 = (f32[512,512]{1,0:T(8,128)S(1)}, f32[512,512]{1,0:T(8,128)S(1)}) fusion(s32[512]{0:T(512)S(1)} %iota_add_fusion), kind=kLoop, calls=%fused_computation.37 | loop fusion | flops 3932160 | bytes 2099200 | tf_op jit(solution)/shard_map/cos | solution.py:26
  89.5 4.9 %collective-permute-done = bf16[2,8,40,512]{3,1,2,0:T(8,128)(2,1)S(1)} collective-permute-done((bf16[2,8,40,512]{3,1,2,0:T(8,128)(2,1)S(1)}, bf16[2,8,40,512]{3,1,2,0:T(8,128)(2,1)S(1)}, u32[]{:S(2)}, u32[]{:S(2)}) %collective-permute-start) | collective-permute-done | bytes 655392 | tf_op jit(solution)/shard_map/ppermute | solution.py:71
  94.4 41.1 %collective-permute-done.1 = bf16[2,8,40,512]{3,1,2,0:T(8,128)(2,1)S(1)} collective-permute-done((bf16[2,8,40,512]{3,1,2,0:T(8,128)(2,1)S(1)}, bf16[2,8,40,512]{3,1,2,0:T(8,128)(2,1)S(1)}, u32[]{:S(2)}, u32[]{:S(2)}) %collective-permute-start.1) | collective-permute-done | bytes 655392 | tf_op jit(solution)/shard_map/ppermute | solution.py:71
  135.6 1.9 %collective-permute-done.2 = bf16[2,8,40,512]{3,1,2,0:T(8,128)(2,1)S(1)} collective-permute-done((bf16[2,8,40,512]{3,1,2,0:T(8,128)(2,1)S(1)}, bf16[2,8,40,512]{3,1,2,0:T(8,128)(2,1)S(1)}, u32[]{:S(2)}, u32[]{:S(2)}) %collective-permute-start.2) | collective-permute-done | bytes 655392 | tf_op jit(solution)/shard_map/ppermute | solution.py:71
  137.5 0.3 pad_maximum_fusion
  137.9 0.6 fusion.15
  138.4 1.2 copy.19
  139.7 1.2 copy.22
  141.1 0.3 copy.21
  141.4 0.3 copy.23
  141.8 6.9 %add_reduce_fusion = (f32[32,8,512]{2,1,0:T(8,128)S(1)}, f32[32,8,512]{2,1,0:T(8,128)S(1)}) fusion(f32[32,8,512]{2,1,0:T(8,128)S(1)} %copy.23, f32[32,32,512]{2,1,0:T(8,128)S(1)} %copy.22, f32[32,8,512]{2,1,0:T(8,128)S(1)} %copy.21, f32[32,32,512]{2,1,0:T(8,128)S(1)} %copy.19), kind=kLoop, calls=%fused_computation.1 | loop fusion | flops 33292288 | bytes 6291456 | tf_op jit(solution)/shard_map/reduce_sum | solution.py:36
  148.7 2.8 %fusion.8 = f32[32,8,512]{2,1,0:T(8,128)} fusion(f32[512,512]{1,0:T(8,128)S(1)} %get-tuple-element.19, f32[512,512]{1,0:T(8,128)S(1)} %get-tuple-element.18, f32[256,512]{1,0:T(8,128)S(1)} %bitcast.49, f32[256,512]{1,0:T(8,128)S(1)} %bitcast.48), kind=kOutput, calls=%fused_computation.13 | convolution fusion | flops 1611792384 | bytes 3670016 | tf_op jit(solution)/shard_map/dot_general | solution.py:40
  (25 shorter events, 1.2 us)
Async XLA Ops:
  0.0 1.6 %copy-start = (bf16[2,8,32,512]{3,2,1,0:T(8,128)(2,1)S(1)}, bf16[2,8,32,512]{3,2,1,0:T(8,128)(2,1)}, u32[]{:S(2)}) copy-start(bf16[2,8,32,512]{3,2,1,0:T(8,128)(2,1)} %param.2) | copy-start | bytes 1572868
  0.0 1.4 copy-start.1
  46.4 29.1 %all-to-all-start.1 = ((bf16[128,4,512]{2,1,0:T(4,128)(2,1)}), bf16[128,4,512]{2,1,0:T(4,128)(2,1)S(1)}, u32[]{:S(2)}, u32[]{:S(2)}) async-start(bf16[128,4,512]{2,1,0:T(4,128)(2,1)} %broadcast_in_dim.2), calls=%async_computation.1 | async-start | bytes 1048576 | tf_op jit(solution)/shard_map/all_to_all | solution.py:52
  75.8 18.6 %collective-permute-start = (bf16[2,8,40,512]{3,1,2,0:T(8,128)(2,1)S(1)}, bf16[2,8,40,512]{3,1,2,0:T(8,128)(2,1)S(1)}, u32[]{:S(2)}, u32[]{:S(2)}) collective-permute-start(bf16[2,8,40,512]{3,1,2,0:T(8,128)(2,1)S(1)} %get-tuple-element.15), channel_id=1, source_target_pairs={{0,1},{1,2},{2,3},{3,0},{4,5},{5,6},{6,7},{7,4},{8,9},{9,10},{10,1... | collective-permute-start | bytes 1966088 | tf_op jit(solution)/shard_map/ppermute | solution.py:71
  79.0 56.6 %collective-permute-start.1 = (bf16[2,8,40,512]{3,1,2,0:T(8,128)(2,1)S(1)}, bf16[2,8,40,512]{3,1,2,0:T(8,128)(2,1)S(1)}, u32[]{:S(2)}, u32[]{:S(2)}) collective-permute-start(bf16[2,8,40,512]{3,1,2,0:T(8,128)(2,1)S(1)} %get-tuple-element.16), channel_id=1, source_target_pairs={{0,2},{1,3},{2,0},{3,1},{4,6},{5,7},{6,4},{7,5},{8,10},{9,11},{10,... | collective-permute-start | bytes 1966088 | tf_op jit(solution)/shard_map/ppermute | solution.py:71
  82.0 55.5 %collective-permute-start.2 = (bf16[2,8,40,512]{3,1,2,0:T(8,128)(2,1)S(1)}, bf16[2,8,40,512]{3,1,2,0:T(8,128)(2,1)S(1)}, u32[]{:S(2)}, u32[]{:S(2)}) collective-permute-start(bf16[2,8,40,512]{3,1,2,0:T(8,128)(2,1)S(1)} %get-tuple-element.17), channel_id=1, source_target_pairs={{0,3},{1,0},{2,1},{3,2},{4,7},{5,4},{6,5},{7,6},{8,11},{9,8},{10,9... | collective-permute-start | bytes 1966088 | tf_op jit(solution)/shard_map/ppermute | solution.py:71

commit v11 on v9

--- a/solution.py
+++ b/solution.py
@@ -49,9 +49,22 @@
     segs = lax.psum(1, seg_axis)
     chunks = value.reshape(count, -1, freqs)
     rows = chunks.shape[1]
-    mine = lax.all_to_all(chunks, chan_axes, 0, 0).sum(axis=0, dtype=value.dtype)
+    if chan_axes == CHAN_AXES:
+        pair = lax.psum(1, "c")
+        rest = ("x", "zh", "y")
+        upper = lax.axis_index("c") == 1
+        flat = value.reshape(pair, -1, freqs)
+        keep = jnp.where(upper, flat[1], flat[0])
+        send = jnp.where(upper, flat[0], flat[1])
+        half = keep + lax.ppermute(send, "c", [(0, 1), (1, 0)])
+        part = half.reshape(count // pair, rows, freqs)
+        mine = lax.all_to_all(part, rest, 0, 0).sum(axis=0, dtype=value.dtype)
+    else:
+        mine = lax.all_to_all(chunks, chan_axes, 0, 0).sum(axis=0, dtype=value.dtype)
     spread = jnp.broadcast_to(mine[None], (count * segs, rows, freqs))
     got = lax.all_to_all(spread, chan_axes + (seg_axis,), 0, 0)
+    if chan_axes == CHAN_AXES:
+        got = got.reshape(count // pair, pair, segs, rows, freqs).transpose(1, 0, 2, 3, 4)
     split = local_segs // rows
     got = got.reshape(parts, sources, split, segs, rows, freqs).transpose(0, 3, 2, 4, 1, 5)
     return got.reshape(parts, segs * local_segs, sources, freqs)

time: 132 us -> 129 us (0.977)
  blocking collectives: 44.5 us -> 29 us
  starting transfers between devices: 19.7 us -> 31.1 us
    all_to_all x1, blocking collectives: 44.5 us -> 29 us  [gather_sources(): mine = lax.all_to_all(part, rest, 0, 0).sum(axis=0, dtype=value.dtype)]
    ppermute x0 -> x1, starting transfers between devices: none -> 8.79 us  [gather_sources(): half = keep + lax.ppermute(send, 'c', [(0, 1), (1, 0)])]
    all_to_all x1, starting transfers between devices: 8.89 us -> 11.5 us  [gather_sources(): got = lax.all_to_all(spread, chan_axes + (seg_axis,), 0, 0)]
  transfers between devices with their start and end apart: 4 -> 5, of which waited for: 2 -> 3; matrix products, arithmetic and copies ran while one was open for 6% -> 7% of each run, Pallas kernels for 0% -> 0%
where the time goes in v11:
time: 129 us; the launch traced here: 128 us
  waiting for transfers between devices  41.9 us (32%)
  starting transfers between devices  31.1 us (24%)
  blocking collectives  29 us (22%)
  other arithmetic  18.2 us (14%)
  local copies, waits for them, and re-layouts  4.73 us (4%)
  matrix products  3.14 us (2%)
    ppermute x3, waiting for transfers between devices, regroup_receivers(): blocks.append(lax.ppermute(group((me + shift) % segs), seg_axis, pairs))  40.8 us
    all_to_all x1, blocking collectives, gather_sources(): mine = lax.all_to_all(part, rest, 0, 0).sum(axis=0, dtype=value.dtype)  29 us
    all_to_all x1, starting transfers between devices, gather_sources(): got = lax.all_to_all(spread, chan_axes + (seg_axis,), 0, 0)  11.5 us
    ppermute x3, starting transfers between devices, regroup_receivers(): blocks.append(lax.ppermute(group((me + shift) % segs), seg_axis, pairs))  10.8 us
    ppermute x1, starting transfers between devices, gather_sources(): half = keep + lax.ppermute(send, 'c', [(0, 1), (1, 0)])  8.79 us
    reduce_sum x1, other arithmetic, correlate(): real_part = jnp.sum(a * c + b * d, axis=0)  6.72 us
    cos x1, other arithmetic, lag_matrix(): return jnp.concatenate([jnp.cos(angles), -jnp.sin(angles)], axis=0)  5.41 us
    dot_general x1, matrix products, correlate(): jnp.dot(flat, lag_table, precision=lax.Precision.HIGHEST, preferred_eleme...  2.75 us
  transfers between devices with their start and end apart: 5, of which 3 were waited for; matrix products, arithmetic and copies ran while one was open for 7% of the time, Pallas kernels for 0%

profile of v11, /device:TPU:1, one launch (start us, length us, event | category | flops | bytes accessed | tf_op | source)
XLA Modules:
  0.0 128.4 jit_solution(1591639333086780705)
XLA Ops:
  0.0 0.7 broadcast_subtract_fusion
  0.9 1.2 convert_element_type.58
  2.3 0.4 fusion.5
  2.8 8.8 %collective-permute-start = (bf16[256,512]{1,0:T(8,128)(2,1)S(1)}, bf16[256,512]{1,0:T(8,128)(2,1)S(1)}, u32[]{:S(2)}, u32[]{:S(2)}) collective-permute-start(bf16[256,512]{1,0:T(8,128)(2,1)S(1)} %bitcast.58), channel_id=1, source_target_pairs={{0,4},{4,0},{1,5},{5,1},{2,6},{6,2},{3,7},{7,3},{8,12},{12,8},{9,1... | collective-permute-start | bytes 786440 | tf_op jit(solution)/shard_map/ppermute | solution.py:59
  11.6 1.1 collective-permute-done
  13.0 29.0 %all_to_all.10 = bf16[64,4,512]{2,1,0:T(4,128)(2,1)S(1)} all-to-all(bf16[64,4,512]{2,1,0:T(4,128)(2,1)S(1)} %reshape.79), channel_id=1, replica_groups=mesh['x'=4,'zh'=2,'y'=8,'c'=2,'seg'=4] {'x','zh','y'}, dimensions={0} | all-to-all | bytes 524288 | tf_op jit(solution)/shard_map/all_to_all | solution.py:61
  42.1 1.9 %broadcast_in_dim.2 = bf16[512,4,512]{2,1,0:T(4,128)(2,1)} broadcast(bf16[4,512]{1,0:T(4,128)(2,1)S(1)} %reduce_sum.37), dimensions={1,2} | broadcast | bytes 2101248 | tf_op jit(solution)/shard_map/broadcast_in_dim | solution.py:64
  44.0 11.5 %all-to-all-start.1 = ((bf16[512,4,512]{2,1,0:T(4,128)(2,1)}), bf16[512,4,512]{2,1,0:T(4,128)(2,1)S(1)}, u32[]{:S(2)}, u32[]{:S(2)}) async-start(bf16[512,4,512]{2,1,0:T(4,128)(2,1)} %broadcast_in_dim.2), calls=%async_computation.1 | async-start | bytes 4194304 | tf_op jit(solution)/shard_map/all_to_all | solution.py:65
  55.7 0.7 dynamic-slice_bitcast_fusion.3
  56.4 6.5 %collective-permute-start.1 = (bf16[2,8,8,512]{3,2,1,0:T(8,128)(2,1)}, bf16[2,8,8,512]{3,2,1,0:T(8,128)(2,1)}, u32[]{:S(2)}, u32[]{:S(2)}) collective-permute-start(bf16[2,8,8,512]{3,2,1,0:T(8,128)(2,1)} %get-tuple-element.13), channel_id=1, source_target_pairs={{0,3},{1,0},{2,1},{3,2},{4,7},{5,4},{6,5},{7,6},{8,11},{9,8},{10,9... | collective-permute-start | bytes 393224 | tf_op jit(solution)/shard_map/ppermute | solution.py:85
  63.0 1.9 %collective-permute-start.2 = (bf16[2,8,8,512]{3,2,1,0:T(8,128)(2,1)S(1)}, bf16[2,8,8,512]{3,2,1,0:T(8,128)(2,1)}, u32[]{:S(2)}, u32[]{:S(2)}) collective-permute-start(bf16[2,8,8,512]{3,2,1,0:T(8,128)(2,1)S(1)} %get-tuple-element.16), channel_id=1, source_target_pairs={{0,2},{1,3},{2,0},{3,1},{4,6},{5,7},{6,4},{7,5},{8,10},{9,11},{10,... | collective-permute-start | bytes 393224 | tf_op jit(solution)/shard_map/ppermute | solution.py:85
  64.9 2.4 %collective-permute-start.3 = (bf16[2,8,8,512]{3,2,1,0:T(8,128)(2,1)S(1)}, bf16[2,8,8,512]{3,2,1,0:T(8,128)(2,1)}, u32[]{:S(2)}, u32[]{:S(2)}) collective-permute-start(bf16[2,8,8,512]{3,2,1,0:T(8,128)(2,1)S(1)} %get-tuple-element.15), channel_id=1, source_target_pairs={{0,1},{1,2},{2,3},{3,0},{4,5},{5,6},{6,7},{7,4},{8,9},{9,10},{10,1... | collective-permute-start | bytes 393224 | tf_op jit(solution)/shard_map/ppermute | solution.py:85
  67.3 5.4 %fusion.24 = (f32[512,512]{1,0:T(8,128)S(1)}, f32[512,512]{1,0:T(8,128)}) fusion(s32[512]{0:T(512)S(1)} %iota_add_fusion), kind=kLoop, calls=%fused_computation.36 | loop fusion | flops 3932160 | bytes 2099200 | tf_op jit(solution)/shard_map/cos | solution.py:26
  72.7 29.3 %collective-permute-done.1 = bf16[2,8,8,512]{3,2,1,0:T(8,128)(2,1)} collective-permute-done((bf16[2,8,8,512]{3,2,1,0:T(8,128)(2,1)}, bf16[2,8,8,512]{3,2,1,0:T(8,128)(2,1)}, u32[]{:S(2)}, u32[]{:S(2)}) %collective-permute-start.1) | collective-permute-done | bytes 131104 | tf_op jit(solution)/shard_map/ppermute | solution.py:85
  102.0 11.5 %collective-permute-done.2 = bf16[2,8,8,512]{3,2,1,0:T(8,128)(2,1)} collective-permute-done((bf16[2,8,8,512]{3,2,1,0:T(8,128)(2,1)S(1)}, bf16[2,8,8,512]{3,2,1,0:T(8,128)(2,1)}, u32[]{:S(2)}, u32[]{:S(2)}) %collective-permute-start.2) | collective-permute-done | bytes 131104 | tf_op jit(solution)/shard_map/ppermute | solution.py:85
  113.5 1.1 pad_maximum_fusion
  114.6 1.1 fusion.27
  115.7 1.2 copy.20
  116.8 0.8 fusion
  117.7 0.6 fusion.16
  118.3 0.4 copy-done.2
  118.7 0.2 copy-done.3
  118.9 6.7 %add_reduce_fusion = (f32[32,8,512]{2,1,0:T(8,128)S(1)}, f32[32,8,512]{2,1,0:T(8,128)S(1)}) fusion(f32[32,8,512]{2,1,0:T(8,128)S(1)} %copy-done.3, f32[32,32,512]{2,1,0:T(8,128)S(1)} %get-tuple-element.8, f32[32,8,512]{2,1,0:T(8,128)S(1)} %copy-done.2, f32[32,32,512]{2,1,0:T(8,128)S(1)} %get-tuple-element.7), kind=kLoop, calls=%fused_computation.1 | loop fusion | flops 33292288 | bytes 6291456 | tf_op jit(solution)/shard_map/reduce_sum | solution.py:36
  125.6 2.8 %fusion.9 = f32[32,8,512]{2,1,0:T(8,128)} fusion(f32[512,512]{1,0:T(8,128)S(1)} %copy-done.1, f32[512,512]{1,0:T(8,128)S(1)} %get-tuple-element.17, f32[256,512]{1,0:T(8,128)S(1)} %bitcast.57, f32[256,512]{1,0:T(8,128)S(1)} %bitcast.56), kind=kOutput, calls=%fused_computation.15 | convolution fusion | flops 1611792384 | bytes 3670016 | tf_op jit(solution)/shard_map/dot_general | solution.py:40
  (19 shorter events, 1.1 us)
Async XLA Ops:
  0.0 2.2 %copy-start = (bf16[2,8,32,512]{3,2,1,0:T(8,128)(2,1)S(1)}, bf16[2,8,32,512]{3,2,1,0:T(8,128)(2,1)}, u32[]{:S(2)}) copy-start(bf16[2,8,32,512]{3,2,1,0:T(8,128)(2,1)} %param.2) | copy-start | bytes 1572868
  2.8 9.9 %collective-permute-start = (bf16[256,512]{1,0:T(8,128)(2,1)S(1)}, bf16[256,512]{1,0:T(8,128)(2,1)S(1)}, u32[]{:S(2)}, u32[]{:S(2)}) collective-permute-start(bf16[256,512]{1,0:T(8,128)(2,1)S(1)} %bitcast.58), channel_id=1, source_target_pairs={{0,4},{4,0},{1,5},{5,1},{2,6},{6,2},{3,7},{7,3},{8,12},{12,8},{9,1... | collective-permute-start | bytes 786440 | tf_op jit(solution)/shard_map/ppermute | solution.py:59
  44.0 71.7 %all-to-all-start.1 = ((bf16[512,4,512]{2,1,0:T(4,128)(2,1)}), bf16[512,4,512]{2,1,0:T(4,128)(2,1)S(1)}, u32[]{:S(2)}, u32[]{:S(2)}) async-start(bf16[512,4,512]{2,1,0:T(4,128)(2,1)} %broadcast_in_dim.2), calls=%async_computation.1 | async-start | bytes 4194304 | tf_op jit(solution)/shard_map/all_to_all | solution.py:65
  56.4 45.6 %collective-permute-start.1 = (bf16[2,8,8,512]{3,2,1,0:T(8,128)(2,1)}, bf16[2,8,8,512]{3,2,1,0:T(8,128)(2,1)}, u32[]{:S(2)}, u32[]{:S(2)}) collective-permute-start(bf16[2,8,8,512]{3,2,1,0:T(8,128)(2,1)} %get-tuple-element.13), channel_id=1, source_target_pairs={{0,3},{1,0},{2,1},{3,2},{4,7},{5,4},{6,5},{7,6},{8,11},{9,8},{10,9... | collective-permute-start | bytes 393224 | tf_op jit(solution)/shard_map/ppermute | solution.py:85
  63.0 50.5 %collective-permute-start.2 = (bf16[2,8,8,512]{3,2,1,0:T(8,128)(2,1)S(1)}, bf16[2,8,8,512]{3,2,1,0:T(8,128)(2,1)}, u32[]{:S(2)}, u32[]{:S(2)}) collective-permute-start(bf16[2,8,8,512]{3,2,1,0:T(8,128)(2,1)S(1)} %get-tuple-element.16), channel_id=1, source_target_pairs={{0,2},{1,3},{2,0},{3,1},{4,6},{5,7},{6,4},{7,5},{8,10},{9,11},{10,... | collective-permute-start | bytes 393224 | tf_op jit(solution)/shard_map/ppermute | solution.py:85
  64.9 48.6 %collective-permute-start.3 = (bf16[2,8,8,512]{3,2,1,0:T(8,128)(2,1)S(1)}, bf16[2,8,8,512]{3,2,1,0:T(8,128)(2,1)}, u32[]{:S(2)}, u32[]{:S(2)}) collective-permute-start(bf16[2,8,8,512]{3,2,1,0:T(8,128)(2,1)S(1)} %get-tuple-element.15), channel_id=1, source_target_pairs={{0,1},{1,2},{2,3},{3,0},{4,5},{5,6},{6,7},{7,4},{8,9},{9,10},{10,1... | collective-permute-start | bytes 393224 | tf_op jit(solution)/shard_map/ppermute | solution.py:85
  117.6 1.0 copy-start.2
  117.7 1.2 copy-start.3
  118.9 6.7 %copy-start.1 = (f32[512,512]{1,0:T(8,128)S(1)}, f32[512,512]{1,0:T(8,128)}, u32[]{:S(2)}) copy-start(f32[512,512]{1,0:T(8,128)} %get-tuple-element.18) | copy-start | bytes 3145732

commit v12 on v8

--- a/solution.py
+++ b/solution.py
@@ -26,8 +26,7 @@
     return jnp.concatenate([jnp.cos(angles), -jnp.sin(angles)], axis=0)
 
 
-def correlate(source_spec, receiver_spec, lag_table):
-    segs = receiver_spec.shape[1]
+def correlate(source_spec, receiver_spec, lag_table, segs):
     freqs = receiver_spec.shape[3]
     a = source_spec[0].astype(jnp.float32)[:, :, None, :]
     b = source_spec[1].astype(jnp.float32)[:, :, None, :]
@@ -43,23 +42,49 @@
     return result.reshape(stacked.shape[0], stacked.shape[1], -1)
 
 
-def gather_sources(value, chan_axes, seg_axis):
+def gather_sources(value, chan_axes):
     parts, sources, local_segs, freqs = value.shape
     count = lax.psum(1, chan_axes)
+    rows = value.size // (count * freqs)
+    if chan_axes == CHAN_AXES:
+        pair = lax.psum(1, "c")
+        rest = ("x", "zh", "y")
+        upper = lax.axis_index("c") == 1
+        flat = value.reshape(pair, -1, freqs)
+        keep = jnp.where(upper, flat[1], flat[0])
+        send = jnp.where(upper, flat[0], flat[1])
+        half = keep + lax.ppermute(send, "c", [(0, 1), (1, 0)])
+        part = half.reshape(count // pair, rows, freqs)
+        mine = lax.all_to_all(part, rest, 0, 0).sum(axis=0, dtype=value.dtype)
+        spread = jnp.broadcast_to(mine[None], (count, rows, freqs))
+        got = lax.all_to_all(spread, chan_axes, 0, 0)
+        got = got.reshape(count // pair, pair, rows, freqs).transpose(1, 0, 2, 3)
+    else:
+        chunks = value.reshape(count, rows, freqs)
+        mine = lax.all_to_all(chunks, chan_axes, 0, 0).sum(axis=0, dtype=value.dtype)
+        spread = jnp.broadcast_to(mine[None], chunks.shape)
+        got = lax.all_to_all(spread, chan_axes, 0, 0)
+    return got.reshape(value.shape).transpose(0, 2, 1, 3)
+
+
+def sum_over_seg(partial, seg_axis):
     segs = lax.psum(1, seg_axis)
-    chunks = value.reshape(count, -1, freqs)
-    rows = chunks.shape[1]
-    mine = lax.all_to_all(chunks, chan_axes, 0, 0).sum(axis=0, dtype=value.dtype)
-    got = lax.all_gather(mine, chan_axes + (seg_axis,), axis=0)
-    split = local_segs // rows
-    got = got.reshape(parts, sources, split, segs, rows, freqs).transpose(0, 3, 2, 4, 1, 5)
-    return got.reshape(parts, segs * local_segs, sources, freqs)
+    me = lax.axis_index(seg_axis)
+    width = partial.shape[1] // segs
+
+    def share(index):
+        return lax.dynamic_slice_in_dim(partial, index * width, width, axis=1)
+
+    total = share(me)
+    for shift in range(1, segs):
+        pairs = [(i, (i + shift) % segs) for i in range(segs)]
+        total = total + lax.ppermute(share((me + shift) % segs), seg_axis, pairs)
+    return total
 
 
 def make_shards(chan_axes):
     def shards(spectra, sources):
         whitened = whiten(spectra)
-        regrouped = lax.all_to_all(whitened, "seg", split_axis=2, concat_axis=1, tiled=True)
         ch_dev = spectra.shape[2]
         freqs = spectra.shape[3]
         first_row = lax.axis_index(chan_axes) * ch_dev
@@ -71,8 +96,9 @@
         local_spec = jnp.einsum(
             "pc,xscf->xpsf", onehot, whitened, preferred_element_type=jnp.float32
         ).astype(jnp.bfloat16)
-        source_spec = gather_sources(local_spec, chan_axes, "seg")
-        return correlate(source_spec, regrouped, lag_table)
+        source_spec = gather_sources(local_spec, chan_axes)
+        partial = correlate(source_spec, whitened, lag_table, lax.psum(whitened.shape[1], "seg"))
+        return sum_over_seg(partial, "seg")
 
     return shards
 

time: 1120 us -> 143 us (0.13)
  the two profiles are of different devices: /device:TPU:1 before, /device:TPU:65 now
where the time goes in v12:
time: 143 us
  waiting for transfers between devices  61 us (43%)
  blocking collectives  33.5 us (23%)
  starting transfers between devices  19.7 us (14%)
  other arithmetic  18.1 us (13%)
  matrix products  7.07 us (5%)
  local copies, waits for them, and re-layouts  3.33 us (2%)
    ppermute x3, waiting for transfers between devices, sum_over_seg(): total = total + lax.ppermute(share((me + shift) % segs), seg_axis, pairs)  41.4 us
    all_to_all x1, blocking collectives, gather_sources(): mine = lax.all_to_all(part, rest, 0, 0).sum(axis=0, dtype=value.dtype)  33.5 us
    all_to_all x1, waiting for transfers between devices, gather_sources(): got = lax.all_to_all(spread, chan_axes, 0, 0)  18.4 us
    ppermute x3, starting transfers between devices, sum_over_seg(): total = total + lax.ppermute(share((me + shift) % segs), seg_axis, pairs)  9.28 us
    all_to_all x1, starting transfers between devices, gather_sources(): got = lax.all_to_all(spread, chan_axes, 0, 0)  7.82 us
    dot_general x1, matrix products, correlate(): jnp.dot(flat, lag_table, precision=lax.Precision.HIGHEST, preferred_eleme...  6.71 us
    reduce_sum x1, other arithmetic, correlate(): real_part = jnp.sum(a * c + b * d, axis=0)  6.43 us
    cos x1, other arithmetic, lag_matrix(): return jnp.concatenate([jnp.cos(angles), -jnp.sin(angles)], axis=0)  5.4 us
  transfers between devices with their start and end apart: 5, of which 5 were waited for; matrix products, arithmetic and copies ran while one was open for 4% of the time, Pallas kernels for 0%

profile of v12, /device:TPU:65, one launch (start us, length us, event | category | flops | bytes accessed | tf_op | source)
XLA Modules:
  0.0 142.8 jit_solution(16730851448719772946)
XLA Ops:
  0.0 0.7 broadcast_subtract_fusion
  0.9 1.2 convert_element_type.58
  2.4 0.4 fusion.7
  3.0 2.6 %collective-permute-start = (bf16[256,512]{1,0:T(8,128)(2,1)S(1)}, bf16[256,512]{1,0:T(8,128)(2,1)S(1)}, u32[]{:S(2)}, u32[]{:S(2)}) collective-permute-start(bf16[256,512]{1,0:T(8,128)(2,1)S(1)} %bitcast.42), channel_id=1, source_target_pairs={{0,4},{4,0},{1,5},{5,1},{2,6},{6,2},{3,7},{7,3},{8,12},{12,8},{9,1... | collective-permute-start | bytes 786440 | tf_op jit(solution)/shard_map/ppermute | solution.py:56
  5.6 1.1 collective-permute-done
  6.7 0.2 bitcast_add_fusion
  6.9 33.5 %all_to_all.10 = bf16[64,4,512]{2,1,0:T(4,128)(2,1)S(1)} all-to-all(bf16[64,4,512]{2,1,0:T(4,128)(2,1)S(1)} %reshape.73), channel_id=1, replica_groups=mesh['x'=4,'zh'=2,'y'=8,'c'=2,'seg'=4] {'x','zh','y'}, dimensions={0} | all-to-all | bytes 524288 | tf_op jit(solution)/shard_map/all_to_all | solution.py:58
  40.5 0.9 broadcast_in_dim.2
  41.5 7.8 %all-to-all-start.1 = ((bf16[128,4,512]{2,1,0:T(4,128)(2,1)}), bf16[128,4,512]{2,1,0:T(4,128)(2,1)S(1)}, u32[]{:S(2)}, u32[]{:S(2)}) async-start(bf16[128,4,512]{2,1,0:T(4,128)(2,1)} %broadcast_in_dim.2), calls=%async_computation.1 | async-start | bytes 1048576 | tf_op jit(solution)/shard_map/all_to_all | solution.py:60
  49.5 5.4 %fusion.18 = (f32[512,512]{1,0:T(8,128)S(1)}, f32[512,512]{1,0:T(8,128)}) fusion(s32[512]{0:T(512)S(1)} %iota_add_fusion), kind=kLoop, calls=%fused_computation.33 | loop fusion | flops 3932160 | bytes 2099200 | tf_op jit(solution)/shard_map/cos | solution.py:26
  54.9 18.4 %all-to-all-done.1 = bf16[128,4,512]{2,1,0:T(4,128)(2,1)S(1)} async-done(((bf16[128,4,512]{2,1,0:T(4,128)(2,1)}), bf16[128,4,512]{2,1,0:T(4,128)(2,1)S(1)}, u32[]{:S(2)}, u32[]{:S(2)}) %all-to-all-start.1) | async-done | bytes 524320 | tf_op jit(solution)/shard_map/all_to_all | solution.py:60
  73.3 0.4 copy.20
  73.7 1.2 slice_convert_fusion.1
  74.9 0.6 copy_bitcast_fusion
  75.6 6.4 %add_reduce_fusion = (f32[32,32,512]{2,1,0:T(8,128)S(1)}, f32[32,32,512]{2,1,0:T(8,128)S(1)}) fusion(f32[8,32,512]{2,1,0:T(8,128)S(1)} %get-tuple-element.13, f32[8,32,512]{2,1,0:T(8,128)S(1)} %get-tuple-element.18, f32[8,32,512]{2,1,0:T(8,128)S(1)} %get-tuple-element.12, f32[8,32,512]{2,1,0:T(8,128)S(1)} %get-tuple-element.19), kind=kLoop, calls=%fused_computation.1 | loop fusion | flops 32505856 | bytes 6291456 | tf_op jit(solution)/shard_map/reduce_sum | solution.py:35
  82.0 6.7 %broadcast_multiply_fusion = f32[1024,512]{1,0:T(8,128)S(1)} fusion(f32[512,512]{1,0:T(8,128)S(1)} %copy-done.1, f32[512,512]{1,0:T(8,128)S(1)} %get-tuple-element.16, f32[1024,512]{1,0:T(8,128)S(1)} %bitcast.38, f32[1024,512]{1,0:T(8,128)S(1)} %bitcast.37), kind=kOutput, calls=%fused_computation.18 | convolution fusion | flops 6445596672 | bytes 8388608 | tf_op jit(solution)/shard_map/dot_general | solution.py:39
  88.7 1.0 constant_dynamic-slice_fusion.2
  89.7 3.1 %collective-permute-start.1 = (f32[32,8,512]{2,1,0:T(8,128)}, f32[32,8,512]{2,1,0:T(8,128)}, u32[]{:S(2)}, u32[]{:S(2)}) collective-permute-start(f32[32,8,512]{2,1,0:T(8,128)} %get-tuple-element.7), channel_id=1, source_target_pairs={{0,1},{1,2},{2,3},{3,0},{4,5},{5,6},{6,7},{7,4},{8,9},{9,10},{10,1... | collective-permute-start | bytes 1572872 | tf_op jit(solution)/shard_map/ppermute | solution.py:81
  92.8 3.1 %collective-permute-start.2 = (f32[32,8,512]{2,1,0:T(8,128)S(1)}, f32[32,8,512]{2,1,0:T(8,128)}, u32[]{:S(2)}, u32[]{:S(2)}) collective-permute-start(f32[32,8,512]{2,1,0:T(8,128)S(1)} %get-tuple-element.9), channel_id=1, source_target_pairs={{0,2},{1,3},{2,0},{3,1},{4,6},{5,7},{6,4},{7,5},{8,10},{9,11},{10,... | collective-permute-start | bytes 1572872 | tf_op jit(solution)/shard_map/ppermute | solution.py:81
  95.9 3.1 %collective-permute-start.3 = (f32[32,8,512]{2,1,0:T(8,128)S(1)}, f32[32,8,512]{2,1,0:T(8,128)}, u32[]{:S(2)}, u32[]{:S(2)}) collective-permute-start(f32[32,8,512]{2,1,0:T(8,128)S(1)} %get-tuple-element.8), channel_id=1, source_target_pairs={{0,3},{1,0},{2,1},{3,2},{4,7},{5,4},{6,5},{7,6},{8,11},{9,8},{10,9... | collective-permute-start | bytes 1572872 | tf_op jit(solution)/shard_map/ppermute | solution.py:81
  99.0 6.8 %collective-permute-done.1 = f32[32,8,512]{2,1,0:T(8,128)} collective-permute-done((f32[32,8,512]{2,1,0:T(8,128)}, f32[32,8,512]{2,1,0:T(8,128)}, u32[]{:S(2)}, u32[]{:S(2)}) %collective-permute-start.1) | collective-permute-done | bytes 524320 | tf_op jit(solution)/shard_map/ppermute | solution.py:81
  105.8 32.6 %collective-permute-done.2 = f32[32,8,512]{2,1,0:T(8,128)} collective-permute-done((f32[32,8,512]{2,1,0:T(8,128)S(1)}, f32[32,8,512]{2,1,0:T(8,128)}, u32[]{:S(2)}, u32[]{:S(2)}) %collective-permute-start.2) | collective-permute-done | bytes 524320 | tf_op jit(solution)/shard_map/ppermute | solution.py:81
  138.4 2.1 %collective-permute-done.3 = f32[32,8,512]{2,1,0:T(8,128)} collective-permute-done((f32[32,8,512]{2,1,0:T(8,128)S(1)}, f32[32,8,512]{2,1,0:T(8,128)}, u32[]{:S(2)}, u32[]{:S(2)}) %collective-permute-start.3) | collective-permute-done | bytes 524320 | tf_op jit(solution)/shard_map/ppermute | solution.py:81
  140.4 2.4 %add_add_fusion = f32[32,8,512]{2,1,0:T(8,128)} fusion(f32[32,8,512]{2,1,0:T(8,128)} %collective-permute-done.3, f32[32,8,512]{2,1,0:T(8,128)} %collective-permute-done.2, f32[32,8,512]{2,1,0:T(8,128)} %collective-permute-done.1, f32[32,32,512]{2,1,0:T(8,128)S(1)} %bitcast.40, s32[]{:T(128)S(6)} %select_n.59), kind=kLoop, calls=%fused_computation.32 | loop fusion | flops 393216 | bytes 2621444 | tf_op jit(solution)/shard_map/add | solution.py:81
  (15 shorter events, 1.0 us)
Async XLA Ops:
  0.0 2.2 %copy-start = (bf16[2,8,32,512]{3,2,1,0:T(8,128)(2,1)S(1)}, bf16[2,8,32,512]{3,2,1,0:T(8,128)(2,1)}, u32[]{:S(2)}) copy-start(bf16[2,8,32,512]{3,2,1,0:T(8,128)(2,1)} %param.2) | copy-start | bytes 1572868
  3.0 3.7 %collective-permute-start = (bf16[256,512]{1,0:T(8,128)(2,1)S(1)}, bf16[256,512]{1,0:T(8,128)(2,1)S(1)}, u32[]{:S(2)}, u32[]{:S(2)}) collective-permute-start(bf16[256,512]{1,0:T(8,128)(2,1)S(1)} %bitcast.42), channel_id=1, source_target_pairs={{0,4},{4,0},{1,5},{5,1},{2,6},{6,2},{3,7},{7,3},{8,12},{12,8},{9,1... | collective-permute-start | bytes 786440 | tf_op jit(solution)/shard_map/ppermute | solution.py:56
  41.5 31.8 %all-to-all-start.1 = ((bf16[128,4,512]{2,1,0:T(4,128)(2,1)}), bf16[128,4,512]{2,1,0:T(4,128)(2,1)S(1)}, u32[]{:S(2)}, u32[]{:S(2)}) async-start(bf16[128,4,512]{2,1,0:T(4,128)(2,1)} %broadcast_in_dim.2), calls=%async_computation.1 | async-start | bytes 1048576 | tf_op jit(solution)/shard_map/all_to_all | solution.py:60
  75.5 6.4 %copy-start.1 = (f32[512,512]{1,0:T(8,128)S(1)}, f32[512,512]{1,0:T(8,128)}, u32[]{:S(2)}) copy-start(f32[512,512]{1,0:T(8,128)} %get-tuple-element.17) | copy-start | bytes 3145732
  89.7 16.1 %collective-permute-start.1 = (f32[32,8,512]{2,1,0:T(8,128)}, f32[32,8,512]{2,1,0:T(8,128)}, u32[]{:S(2)}, u32[]{:S(2)}) collective-permute-start(f32[32,8,512]{2,1,0:T(8,128)} %get-tuple-element.7), channel_id=1, source_target_pairs={{0,1},{1,2},{2,3},{3,0},{4,5},{5,6},{6,7},{7,4},{8,9},{9,10},{10,1... | collective-permute-start | bytes 1572872 | tf_op jit(solution)/shard_map/ppermute | solution.py:81
  92.8 45.6 %collective-permute-start.2 = (f32[32,8,512]{2,1,0:T(8,128)S(1)}, f32[32,8,512]{2,1,0:T(8,128)}, u32[]{:S(2)}, u32[]{:S(2)}) collective-permute-start(f32[32,8,512]{2,1,0:T(8,128)S(1)} %get-tuple-element.9), channel_id=1, source_target_pairs={{0,2},{1,3},{2,0},{3,1},{4,6},{5,7},{6,4},{7,5},{8,10},{9,11},{10,... | collective-permute-start | bytes 1572872 | tf_op jit(solution)/shard_map/ppermute | solution.py:81
  95.9 44.6 %collective-permute-start.3 = (f32[32,8,512]{2,1,0:T(8,128)S(1)}, f32[32,8,512]{2,1,0:T(8,128)}, u32[]{:S(2)}, u32[]{:S(2)}) collective-permute-start(f32[32,8,512]{2,1,0:T(8,128)S(1)} %get-tuple-element.8), channel_id=1, source_target_pairs={{0,3},{1,0},{2,1},{3,2},{4,7},{5,4},{6,5},{7,6},{8,11},{9,8},{10,9... | collective-permute-start | bytes 1572872 | tf_op jit(solution)/shard_map/ppermute | solution.py:81

commit v13 on v11

--- a/solution.py
+++ b/solution.py
@@ -109,6 +109,7 @@
         local_spec = jnp.einsum(
             "pc,xscf->xpsf", onehot, whitened, preferred_element_type=jnp.float32
         ).astype(jnp.bfloat16)
+        regrouped, local_spec = lax.optimization_barrier((regrouped, local_spec))
         source_spec = rotate_segments(gather_sources(local_spec, chan_axes, "seg"), "seg")
         return correlate(source_spec, regrouped, lag_table)
 

time: 129 us -> 139 us (1.078)
  waiting for transfers between devices: 41.9 us -> 53.4 us
  starting transfers between devices: 31.1 us -> 27.2 us
  blocking collectives: 29 us -> 31.8 us
    all_to_all x1, waiting for transfers between devices: 0.01 us -> 45.8 us  [gather_sources(): got = lax.all_to_all(spread, chan_axes + (seg_axis,), 0, 0)]
    ppermute x3, waiting for transfers between devices: 40.8 us -> 6.39 us  [regroup_receivers(): blocks.append(lax.ppermute(group((me + shift) % segs), seg_axis, pairs))]
    ppermute x1, starting transfers between devices: 8.79 us -> 3.72 us  [gather_sources(): half = keep + lax.ppermute(send, 'c', [(0, 1), (1, 0)])]
    all_to_all x1, blocking collectives: 29 us -> 31.8 us  [gather_sources(): mine = lax.all_to_all(part, rest, 0, 0).sum(axis=0, dtype=value.dtype)]
    ppermute x3, starting transfers between devices: 10.8 us -> 12.6 us  [regroup_receivers(): blocks.append(lax.ppermute(group((me + shift) % segs), seg_axis, pairs))]
  transfers between devices with their start and end apart: 5 -> 5, of which waited for: 3 -> 4; matrix products, arithmetic and copies ran while one was open for 7% -> 6% of each run, Pallas kernels for 0% -> 0%
where the time goes in v13:
time: 139 us; the launch traced here: 138 us
  waiting for transfers between devices  53.4 us (38%)
  blocking collectives  31.8 us (23%)
  starting transfers between devices  27.2 us (20%)
  other arithmetic  18.4 us (13%)
  local copies, waits for them, and re-layouts  4.09 us (3%)
  matrix products  3.14 us (2%)
    all_to_all x1, waiting for transfers between devices, gather_sources(): got = lax.all_to_all(spread, chan_axes + (seg_axis,), 0, 0)  45.8 us
    all_to_all x1, blocking collectives, gather_sources(): mine = lax.all_to_all(part, rest, 0, 0).sum(axis=0, dtype=value.dtype)  31.8 us
    ppermute x3, starting transfers between devices, regroup_receivers(): blocks.append(lax.ppermute(group((me + shift) % segs), seg_axis, pairs))  12.6 us
    all_to_all x1, starting transfers between devices, gather_sources(): got = lax.all_to_all(spread, chan_axes + (seg_axis,), 0, 0)  10.9 us
    reduce_sum x1, other arithmetic, correlate(): real_part = jnp.sum(a * c + b * d, axis=0)  6.72 us
    ppermute x3, waiting for transfers between devices, regroup_receivers(): blocks.append(lax.ppermute(group((me + shift) % segs), seg_axis, pairs))  6.39 us
    cos x1, other arithmetic, lag_matrix(): return jnp.concatenate([jnp.cos(angles), -jnp.sin(angles)], axis=0)  5.41 us
    ppermute x1, starting transfers between devices, gather_sources(): half = keep + lax.ppermute(send, 'c', [(0, 1), (1, 0)])  3.72 us
  transfers between devices with their start and end apart: 5, of which 4 were waited for; matrix products, arithmetic and copies ran while one was open for 6% of the time, Pallas kernels for 0%

profile of v13, /device:TPU:1, one launch (start us, length us, event | category | flops | bytes accessed | tf_op | source)
XLA Modules:
  0.0 138.2 jit_solution(6879541939940843078)
XLA Ops:
  0.0 1.2 convert_element_type.58
  1.6 8.4 %collective-permute-start = (bf16[2,8,8,512]{3,2,1,0:T(8,128)(2,1)S(1)}, bf16[2,8,8,512]{3,2,1,0:T(8,128)(2,1)S(1)}, u32[]{:S(2)}, u32[]{:S(2)}) collective-permute-start(bf16[2,8,8,512]{3,2,1,0:T(8,128)(2,1)S(1)} %get-tuple-element.17), channel_id=1, source_target_pairs={{0,3},{1,0},{2,1},{3,2},{4,7},{5,4},{6,5},{7,6},{8,11},{9,8},{10,9... | collective-permute-start | bytes 393224 | tf_op jit(solution)/shard_map/ppermute | solution.py:85
  10.1 1.9 %collective-permute-start.1 = (bf16[2,8,8,512]{3,2,1,0:T(8,128)(2,1)S(1)}, bf16[2,8,8,512]{3,2,1,0:T(8,128)(2,1)S(1)}, u32[]{:S(2)}, u32[]{:S(2)}) collective-permute-start(bf16[2,8,8,512]{3,2,1,0:T(8,128)(2,1)S(1)} %get-tuple-element.20), channel_id=1, source_target_pairs={{0,2},{1,3},{2,0},{3,1},{4,6},{5,7},{6,4},{7,5},{8,10},{9,11},{10,... | collective-permute-start | bytes 393224 | tf_op jit(solution)/shard_map/ppermute | solution.py:85
  12.0 2.2 %collective-permute-start.2 = (bf16[2,8,8,512]{3,2,1,0:T(8,128)(2,1)S(1)}, bf16[2,8,8,512]{3,2,1,0:T(8,128)(2,1)S(1)}, u32[]{:S(2)}, u32[]{:S(2)}) collective-permute-start(bf16[2,8,8,512]{3,2,1,0:T(8,128)(2,1)S(1)} %get-tuple-element.19), channel_id=1, source_target_pairs={{0,1},{1,2},{2,3},{3,0},{4,5},{5,6},{6,7},{7,4},{8,9},{9,10},{10,1... | collective-permute-start | bytes 393224 | tf_op jit(solution)/shard_map/ppermute | solution.py:85
  14.4 0.4 fusion.5
  14.8 1.9 %collective-permute-done.1 = bf16[2,8,8,512]{3,2,1,0:T(8,128)(2,1)S(1)} collective-permute-done((bf16[2,8,8,512]{3,2,1,0:T(8,128)(2,1)S(1)}, bf16[2,8,8,512]{3,2,1,0:T(8,128)(2,1)S(1)}, u32[]{:S(2)}, u32[]{:S(2)}) %collective-permute-start.1) | collective-permute-done | bytes 131104 | tf_op jit(solution)/shard_map/ppermute | solution.py:85
  16.7 4.5 %collective-permute-done.2 = bf16[2,8,8,512]{3,2,1,0:T(8,128)(2,1)S(1)} collective-permute-done((bf16[2,8,8,512]{3,2,1,0:T(8,128)(2,1)S(1)}, bf16[2,8,8,512]{3,2,1,0:T(8,128)(2,1)S(1)}, u32[]{:S(2)}, u32[]{:S(2)}) %collective-permute-start.2) | collective-permute-done | bytes 131104 | tf_op jit(solution)/shard_map/ppermute | solution.py:85
  21.2 0.9 pad_maximum_fusion
  22.3 3.7 %collective-permute-start.3 = (bf16[256,512]{1,0:T(8,128)(2,1)S(1)}, bf16[256,512]{1,0:T(8,128)(2,1)S(1)}, u32[]{:S(2)}, u32[]{:S(2)}) collective-permute-start(bf16[256,512]{1,0:T(8,128)(2,1)S(1)} %bitcast.54), channel_id=1, source_target_pairs={{0,4},{4,0},{1,5},{5,1},{2,6},{6,2},{3,7},{7,3},{8,12},{12,8},{9,1... | collective-permute-start | bytes 786440 | tf_op jit(solution)/shard_map/ppermute | solution.py:59
  26.0 1.1 collective-permute-done.3
  27.1 0.2 bitcast_add_fusion
  27.4 31.8 %all_to_all.10 = bf16[64,4,512]{2,1,0:T(4,128)(2,1)S(1)} all-to-all(bf16[64,4,512]{2,1,0:T(4,128)(2,1)S(1)} %reshape.80), channel_id=1, replica_groups=mesh['x'=4,'zh'=2,'y'=8,'c'=2,'seg'=4] {'x','zh','y'}, dimensions={0} | all-to-all | bytes 524288 | tf_op jit(solution)/shard_map/all_to_all | solution.py:61
  59.4 1.9 %broadcast_in_dim.2 = bf16[512,4,512]{2,1,0:T(4,128)(2,1)} broadcast(bf16[4,512]{1,0:T(4,128)(2,1)S(1)} %reduce_sum.37), dimensions={1,2} | broadcast | bytes 2101248 | tf_op jit(solution)/shard_map/broadcast_in_dim | solution.py:64
  61.2 10.9 %all-to-all-start.1 = ((bf16[512,4,512]{2,1,0:T(4,128)(2,1)}), bf16[512,4,512]{2,1,0:T(4,128)(2,1)S(1)}, u32[]{:S(2)}, u32[]{:S(2)}) async-start(bf16[512,4,512]{2,1,0:T(4,128)(2,1)} %broadcast_in_dim.2), calls=%async_computation.1 | async-start | bytes 4194304 | tf_op jit(solution)/shard_map/all_to_all | solution.py:65
  72.2 5.4 %fusion.24 = (f32[512,512]{1,0:T(8,128)S(1)}, f32[512,512]{1,0:T(8,128)}) fusion(s32[512]{0:T(512)S(1)} %iota_add_fusion), kind=kLoop, calls=%fused_computation.36 | loop fusion | flops 3932160 | bytes 2099200 | tf_op jit(solution)/shard_map/cos | solution.py:26
  77.6 2.1 %bitcast_convert_fusion.1 = (f32[32,8,512]{2,1,0:T(8,128)}, f32[32,8,512]{2,1,0:T(8,128)}) fusion(bf16[2,32,8,512]{3,2,1,0:T(8,128)(2,1)} %pad_maximum_fusion), kind=kLoop, calls=%fused_computation.39 | loop fusion | flops 262144 | bytes 1572864 | tf_op jit(solution)/shard_map/convert_element_type | solution.py:34
  79.7 45.8 %all-to-all-done.1 = bf16[512,4,512]{2,1,0:T(4,128)(2,1)S(1)} async-done(((bf16[512,4,512]{2,1,0:T(4,128)(2,1)}), bf16[512,4,512]{2,1,0:T(4,128)(2,1)S(1)}, u32[]{:S(2)}, u32[]{:S(2)}) %all-to-all-start.1) | async-done | bytes 2097184 | tf_op jit(solution)/shard_map/all_to_all | solution.py:65
  125.6 1.2 copy.20
  126.7 0.8 fusion
  127.5 0.6 fusion.16
  128.1 0.4 copy-done.2
  128.6 0.2 copy-done.3
  128.7 6.7 %add_reduce_fusion = (f32[32,8,512]{2,1,0:T(8,128)S(1)}, f32[32,8,512]{2,1,0:T(8,128)S(1)}) fusion(f32[32,8,512]{2,1,0:T(8,128)S(1)} %copy-done.3, f32[32,32,512]{2,1,0:T(8,128)S(1)} %get-tuple-element.12, f32[32,8,512]{2,1,0:T(8,128)S(1)} %copy-done.2, f32[32,32,512]{2,1,0:T(8,128)S(1)} %get-tuple-element.11), kind=kLoop, calls=%fused_computation.1 | loop fusion | flops 33292288 | bytes 6291456 | tf_op jit(solution)/shard_map/reduce_sum | solution.py:36
  135.5 2.8 %fusion.9 = f32[32,8,512]{2,1,0:T(8,128)} fusion(f32[512,512]{1,0:T(8,128)S(1)} %copy-done.1, f32[512,512]{1,0:T(8,128)S(1)} %get-tuple-element.21, f32[256,512]{1,0:T(8,128)S(1)} %bitcast.53, f32[256,512]{1,0:T(8,128)S(1)} %bitcast.52), kind=kOutput, calls=%fused_computation.15 | convolution fusion | flops 1611792384 | bytes 3670016 | tf_op jit(solution)/shard_map/dot_general | solution.py:40
  (21 shorter events, 0.9 us)
Async XLA Ops:
  0.0 1.4 %copy-start = (bf16[2,8,32,512]{3,2,1,0:T(8,128)(2,1)S(1)}, bf16[2,8,32,512]{3,2,1,0:T(8,128)(2,1)}, u32[]{:S(2)}) copy-start(bf16[2,8,32,512]{3,2,1,0:T(8,128)(2,1)} %param.2) | copy-start | bytes 1572868
  0.0 14.2 %copy-start.4 = (s32[8,4]{0,1:T(4,128)S(1)}, s32[8,4]{0,1:T(4,128)}, u32[]{:S(2)}) copy-start(s32[8,4]{0,1:T(4,128)} %param.3) | copy-start | bytes 388
  1.6 13.2 %collective-permute-start = (bf16[2,8,8,512]{3,2,1,0:T(8,128)(2,1)S(1)}, bf16[2,8,8,512]{3,2,1,0:T(8,128)(2,1)S(1)}, u32[]{:S(2)}, u32[]{:S(2)}) collective-permute-start(bf16[2,8,8,512]{3,2,1,0:T(8,128)(2,1)S(1)} %get-tuple-element.17), channel_id=1, source_target_pairs={{0,3},{1,0},{2,1},{3,2},{4,7},{5,4},{6,5},{7,6},{8,11},{9,8},{10,9... | collective-permute-start | bytes 393224 | tf_op jit(solution)/shard_map/ppermute | solution.py:85
  10.1 6.6 %collective-permute-start.1 = (bf16[2,8,8,512]{3,2,1,0:T(8,128)(2,1)S(1)}, bf16[2,8,8,512]{3,2,1,0:T(8,128)(2,1)S(1)}, u32[]{:S(2)}, u32[]{:S(2)}) collective-permute-start(bf16[2,8,8,512]{3,2,1,0:T(8,128)(2,1)S(1)} %get-tuple-element.20), channel_id=1, source_target_pairs={{0,2},{1,3},{2,0},{3,1},{4,6},{5,7},{6,4},{7,5},{8,10},{9,11},{10,... | collective-permute-start | bytes 393224 | tf_op jit(solution)/shard_map/ppermute | solution.py:85
  12.0 9.2 %collective-permute-start.2 = (bf16[2,8,8,512]{3,2,1,0:T(8,128)(2,1)S(1)}, bf16[2,8,8,512]{3,2,1,0:T(8,128)(2,1)S(1)}, u32[]{:S(2)}, u32[]{:S(2)}) collective-permute-start(bf16[2,8,8,512]{3,2,1,0:T(8,128)(2,1)S(1)} %get-tuple-element.19), channel_id=1, source_target_pairs={{0,1},{1,2},{2,3},{3,0},{4,5},{5,6},{6,7},{7,4},{8,9},{9,10},{10,1... | collective-permute-start | bytes 393224 | tf_op jit(solution)/shard_map/ppermute | solution.py:85
  22.3 4.9 %collective-permute-start.3 = (bf16[256,512]{1,0:T(8,128)(2,1)S(1)}, bf16[256,512]{1,0:T(8,128)(2,1)S(1)}, u32[]{:S(2)}, u32[]{:S(2)}) collective-permute-start(bf16[256,512]{1,0:T(8,128)(2,1)S(1)} %bitcast.54), channel_id=1, source_target_pairs={{0,4},{4,0},{1,5},{5,1},{2,6},{6,2},{3,7},{7,3},{8,12},{12,8},{9,1... | collective-permute-start | bytes 786440 | tf_op jit(solution)/shard_map/ppermute | solution.py:59
  61.2 64.3 %all-to-all-start.1 = ((bf16[512,4,512]{2,1,0:T(4,128)(2,1)}), bf16[512,4,512]{2,1,0:T(4,128)(2,1)S(1)}, u32[]{:S(2)}, u32[]{:S(2)}) async-start(bf16[512,4,512]{2,1,0:T(4,128)(2,1)} %broadcast_in_dim.2), calls=%async_computation.1 | async-start | bytes 4194304 | tf_op jit(solution)/shard_map/all_to_all | solution.py:65
  127.5 1.0 copy-start.2
  127.5 1.2 copy-start.3
  128.7 6.7 %copy-start.1 = (f32[512,512]{1,0:T(8,128)S(1)}, f32[512,512]{1,0:T(8,128)}, u32[]{:S(2)}) copy-start(f32[512,512]{1,0:T(8,128)} %get-tuple-element.22) | copy-start | bytes 3145732

commit v14 on v11

--- a/solution.py
+++ b/solution.py
@@ -61,10 +61,17 @@
         mine = lax.all_to_all(part, rest, 0, 0).sum(axis=0, dtype=value.dtype)
     else:
         mine = lax.all_to_all(chunks, chan_axes, 0, 0).sum(axis=0, dtype=value.dtype)
-    spread = jnp.broadcast_to(mine[None], (count * segs, rows, freqs))
-    got = lax.all_to_all(spread, chan_axes + (seg_axis,), 0, 0)
     if chan_axes == CHAN_AXES:
-        got = got.reshape(count // pair, pair, segs, rows, freqs).transpose(1, 0, 2, 3, 4)
+        far = lax.axis_index("zh") == 1
+        other = lax.ppermute(mine, "zh", [(0, 1), (1, 0)])
+        both = jnp.stack([jnp.where(far, other, mine), jnp.where(far, mine, other)])
+        near = ("x", "y", "c", seg_axis)
+        spread = jnp.broadcast_to(both[None], (count * segs // 2,) + both.shape)
+        got = lax.all_to_all(spread, near, 0, 0)
+        got = got.reshape(4, 8, pair, segs, 2, rows, freqs).transpose(2, 0, 4, 1, 3, 5, 6)
+    else:
+        spread = jnp.broadcast_to(mine[None], (count * segs, rows, freqs))
+        got = lax.all_to_all(spread, chan_axes + (seg_axis,), 0, 0)
     split = local_segs // rows
     got = got.reshape(parts, sources, split, segs, rows, freqs).transpose(0, 3, 2, 4, 1, 5)
     return got.reshape(parts, segs * local_segs, sources, freqs)

time: 129 us -> 140 us (1.085)
  waiting for transfers between devices: 41.9 us -> 49.1 us
  starting transfers between devices: 31.1 us -> 33.4 us
    ppermute x0 -> x1, waiting for transfers between devices: none -> 6.18 us  [gather_sources(): other = lax.ppermute(mine, 'zh', [(0, 1), (1, 0)])]
    ppermute x0 -> x1, starting transfers between devices: none -> 2.13 us  [gather_sources(): other = lax.ppermute(mine, 'zh', [(0, 1), (1, 0)])]
  transfers between devices with their start and end apart: 5 -> 6, of which waited for: 3 -> 4; matrix products, arithmetic and copies ran while one was open for 7% -> 6% of each run, Pallas kernels for 0% -> 0%
where the time goes in v14:
time: 140 us; the launch traced here: 139 us
  waiting for transfers between devices  49.1 us (35%)
  starting transfers between devices  33.4 us (24%)
  blocking collectives  29 us (21%)
  other arithmetic  18.3 us (13%)
  local copies, waits for them, and re-layouts  6.01 us (4%)
  matrix products  3.14 us (2%)
    ppermute x3, waiting for transfers between devices, regroup_receivers(): blocks.append(lax.ppermute(group((me + shift) % segs), seg_axis, pairs))  41.7 us
    all_to_all x1, blocking collectives, gather_sources(): mine = lax.all_to_all(part, rest, 0, 0).sum(axis=0, dtype=value.dtype)  29 us
    all_to_all x1, starting transfers between devices, gather_sources(): got = lax.all_to_all(spread, near, 0, 0)  12.8 us
    ppermute x3, starting transfers between devices, regroup_receivers(): blocks.append(lax.ppermute(group((me + shift) % segs), seg_axis, pairs))  9.65 us
    ppermute x1, starting transfers between devices, gather_sources(): half = keep + lax.ppermute(send, 'c', [(0, 1), (1, 0)])  8.79 us
    reduce_sum x1, other arithmetic, correlate(): real_part = jnp.sum(a * c + b * d, axis=0)  6.72 us
    ppermute x1, waiting for transfers between devices, gather_sources(): other = lax.ppermute(mine, 'zh', [(0, 1), (1, 0)])  6.18 us
    cos x1, other arithmetic, lag_matrix(): return jnp.concatenate([jnp.cos(angles), -jnp.sin(angles)], axis=0)  5.41 us
  transfers between devices with their start and end apart: 6, of which 4 were waited for; matrix products, arithmetic and copies ran while one was open for 6% of the time, Pallas kernels for 0%

profile of v14, /device:TPU:1, one launch (start us, length us, event | category | flops | bytes accessed | tf_op | source)
XLA Modules:
  0.0 139.1 jit_solution(17641056579225838669)
XLA Ops:
  0.0 0.7 broadcast_subtract_fusion
  0.9 1.2 convert_element_type.58
  2.8 8.8 %collective-permute-start = (bf16[256,512]{1,0:T(8,128)(2,1)S(1)}, bf16[256,512]{1,0:T(8,128)(2,1)S(1)}, u32[]{:S(2)}, u32[]{:S(2)}) collective-permute-start(bf16[256,512]{1,0:T(8,128)(2,1)S(1)} %bitcast.62), channel_id=1, source_target_pairs={{0,4},{4,0},{1,5},{5,1},{2,6},{6,2},{3,7},{7,3},{8,12},{12,8},{9,1... | collective-permute-start | bytes 786440 | tf_op jit(solution)/shard_map/ppermute | solution.py:59
  11.6 1.1 collective-permute-done
  13.0 29.0 %all_to_all.10 = bf16[64,4,512]{2,1,0:T(4,128)(2,1)S(1)} all-to-all(bf16[64,4,512]{2,1,0:T(4,128)(2,1)S(1)} %reshape.79), channel_id=1, replica_groups=mesh['x'=4,'zh'=2,'y'=8,'c'=2,'seg'=4] {'x','zh','y'}, dimensions={0} | all-to-all | bytes 524288 | tf_op jit(solution)/shard_map/all_to_all | solution.py:61
  42.1 2.1 %collective-permute-start.1 = (bf16[4,512]{1,0:T(4,128)(2,1)S(1)}, bf16[4,512]{1,0:T(4,128)(2,1)S(1)}, u32[]{:S(2)}, u32[]{:S(2)}) collective-permute-start(bf16[4,512]{1,0:T(4,128)(2,1)S(1)} %reduce_sum.37), channel_id=1, source_target_pairs={{0,64},{64,0},{1,65},{65,1},{2,66},{66,2},{3,67},{67,3},{4,68},{68... | collective-permute-start | bytes 12296 | tf_op jit(solution)/shard_map/ppermute | solution.py:66
  44.3 6.2 %collective-permute-done.1 = bf16[4,512]{1,0:T(4,128)(2,1)S(1)} collective-permute-done((bf16[4,512]{1,0:T(4,128)(2,1)S(1)}, bf16[4,512]{1,0:T(4,128)(2,1)S(1)}, u32[]{:S(2)}, u32[]{:S(2)}) %collective-permute-start.1) | collective-permute-done | bytes 4128 | tf_op jit(solution)/shard_map/ppermute | solution.py:66
  50.5 1.9 %broadcast_in_dim.2 = bf16[256,2,4,512]{3,2,1,0:T(4,128)(2,1)} broadcast(bf16[2,4,512]{2,1,0:T(4,128)(2,1)S(1)} %pad_maximum_fusion.1), dimensions={1,2,3} | broadcast | bytes 2105344 | tf_op jit(solution)/shard_map/broadcast_in_dim | solution.py:69
  52.4 12.8 %all-to-all-start.1 = ((bf16[256,2,4,512]{3,2,1,0:T(4,128)(2,1)}), bf16[256,2,4,512]{3,2,1,0:T(4,128)(2,1)S(1)}, u32[]{:S(2)}, u32[]{:S(2)}) async-start(bf16[256,2,4,512]{3,2,1,0:T(4,128)(2,1)} %broadcast_in_dim.2), calls=%async_computation.1 | async-start | bytes 4194304 | tf_op jit(solution)/shard_map/all_to_all | solution.py:70
  65.4 0.7 dynamic-slice_bitcast_fusion.3
  66.1 5.1 %collective-permute-start.2 = (bf16[2,8,8,512]{3,2,1,0:T(8,128)(2,1)}, bf16[2,8,8,512]{3,2,1,0:T(8,128)(2,1)}, u32[]{:S(2)}, u32[]{:S(2)}) collective-permute-start(bf16[2,8,8,512]{3,2,1,0:T(8,128)(2,1)} %get-tuple-element.13), channel_id=1, source_target_pairs={{0,3},{1,0},{2,1},{3,2},{4,7},{5,4},{6,5},{7,6},{8,11},{9,8},{10,9... | collective-permute-start | bytes 393224 | tf_op jit(solution)/shard_map/ppermute | solution.py:92
  71.2 1.9 %collective-permute-start.3 = (bf16[2,8,8,512]{3,2,1,0:T(8,128)(2,1)S(1)}, bf16[2,8,8,512]{3,2,1,0:T(8,128)(2,1)}, u32[]{:S(2)}, u32[]{:S(2)}) collective-permute-start(bf16[2,8,8,512]{3,2,1,0:T(8,128)(2,1)S(1)} %get-tuple-element.16), channel_id=1, source_target_pairs={{0,2},{1,3},{2,0},{3,1},{4,6},{5,7},{6,4},{7,5},{8,10},{9,11},{10,... | collective-permute-start | bytes 393224 | tf_op jit(solution)/shard_map/ppermute | solution.py:92
  73.1 2.6 %collective-permute-start.4 = (bf16[2,8,8,512]{3,2,1,0:T(8,128)(2,1)S(1)}, bf16[2,8,8,512]{3,2,1,0:T(8,128)(2,1)}, u32[]{:S(2)}, u32[]{:S(2)}) collective-permute-start(bf16[2,8,8,512]{3,2,1,0:T(8,128)(2,1)S(1)} %get-tuple-element.15), channel_id=1, source_target_pairs={{0,1},{1,2},{2,3},{3,0},{4,5},{5,6},{6,7},{7,4},{8,9},{9,10},{10,1... | collective-permute-start | bytes 393224 | tf_op jit(solution)/shard_map/ppermute | solution.py:92
  75.8 5.4 %fusion.24 = (f32[512,512]{1,0:T(8,128)S(1)}, f32[512,512]{1,0:T(8,128)}) fusion(s32[512]{0:T(512)S(1)} %iota_add_fusion), kind=kLoop, calls=%fused_computation.36 | loop fusion | flops 3932160 | bytes 2099200 | tf_op jit(solution)/shard_map/cos | solution.py:26
  81.2 7.6 %collective-permute-done.2 = bf16[2,8,8,512]{3,2,1,0:T(8,128)(2,1)} collective-permute-done((bf16[2,8,8,512]{3,2,1,0:T(8,128)(2,1)}, bf16[2,8,8,512]{3,2,1,0:T(8,128)(2,1)}, u32[]{:S(2)}, u32[]{:S(2)}) %collective-permute-start.2) | collective-permute-done | bytes 131104 | tf_op jit(solution)/shard_map/ppermute | solution.py:92
  88.8 34.2 %collective-permute-done.3 = bf16[2,8,8,512]{3,2,1,0:T(8,128)(2,1)} collective-permute-done((bf16[2,8,8,512]{3,2,1,0:T(8,128)(2,1)S(1)}, bf16[2,8,8,512]{3,2,1,0:T(8,128)(2,1)}, u32[]{:S(2)}, u32[]{:S(2)}) %collective-permute-start.3) | collective-permute-done | bytes 131104 | tf_op jit(solution)/shard_map/ppermute | solution.py:92
  122.9 1.1 pad_maximum_fusion
  124.0 1.1 fusion.27
  125.2 1.3 copy.16
  126.4 1.2 copy.17
  127.6 0.8 fusion
  128.4 0.6 fusion.16
  129.6 6.7 %add_reduce_fusion = (f32[32,8,512]{2,1,0:T(8,128)S(1)}, f32[32,8,512]{2,1,0:T(8,128)S(1)}) fusion(f32[32,8,512]{2,1,0:T(8,128)S(1)} %copy-done.3, f32[32,32,512]{2,1,0:T(8,128)S(1)} %get-tuple-element.8, f32[32,8,512]{2,1,0:T(8,128)S(1)} %copy-done.2, f32[32,32,512]{2,1,0:T(8,128)S(1)} %get-tuple-element.7), kind=kLoop, calls=%fused_computation.1 | loop fusion | flops 33292288 | bytes 6291456 | tf_op jit(solution)/shard_map/reduce_sum | solution.py:36
  136.3 2.8 %fusion.9 = f32[32,8,512]{2,1,0:T(8,128)} fusion(f32[512,512]{1,0:T(8,128)S(1)} %copy-done.1, f32[512,512]{1,0:T(8,128)S(1)} %get-tuple-element.19, f32[256,512]{1,0:T(8,128)S(1)} %bitcast.61, f32[256,512]{1,0:T(8,128)S(1)} %bitcast.60), kind=kOutput, calls=%fused_computation.15 | convolution fusion | flops 1611792384 | bytes 3670016 | tf_op jit(solution)/shard_map/dot_general | solution.py:40
  (24 shorter events, 2.1 us)
Async XLA Ops:
  0.0 2.2 %copy-start = (bf16[2,8,32,512]{3,2,1,0:T(8,128)(2,1)S(1)}, bf16[2,8,32,512]{3,2,1,0:T(8,128)(2,1)}, u32[]{:S(2)}) copy-start(bf16[2,8,32,512]{3,2,1,0:T(8,128)(2,1)} %param.2) | copy-start | bytes 1572868
  2.8 9.9 %collective-permute-start = (bf16[256,512]{1,0:T(8,128)(2,1)S(1)}, bf16[256,512]{1,0:T(8,128)(2,1)S(1)}, u32[]{:S(2)}, u32[]{:S(2)}) collective-permute-start(bf16[256,512]{1,0:T(8,128)(2,1)S(1)} %bitcast.62), channel_id=1, source_target_pairs={{0,4},{4,0},{1,5},{5,1},{2,6},{6,2},{3,7},{7,3},{8,12},{12,8},{9,1... | collective-permute-start | bytes 786440 | tf_op jit(solution)/shard_map/ppermute | solution.py:59
  42.1 8.3 %collective-permute-start.1 = (bf16[4,512]{1,0:T(4,128)(2,1)S(1)}, bf16[4,512]{1,0:T(4,128)(2,1)S(1)}, u32[]{:S(2)}, u32[]{:S(2)}) collective-permute-start(bf16[4,512]{1,0:T(4,128)(2,1)S(1)} %reduce_sum.37), channel_id=1, source_target_pairs={{0,64},{64,0},{1,65},{65,1},{2,66},{66,2},{3,67},{67,3},{4,68},{68... | collective-permute-start | bytes 12296 | tf_op jit(solution)/shard_map/ppermute | solution.py:66
  52.4 72.8 %all-to-all-start.1 = ((bf16[256,2,4,512]{3,2,1,0:T(4,128)(2,1)}), bf16[256,2,4,512]{3,2,1,0:T(4,128)(2,1)S(1)}, u32[]{:S(2)}, u32[]{:S(2)}) async-start(bf16[256,2,4,512]{3,2,1,0:T(4,128)(2,1)} %broadcast_in_dim.2), calls=%async_computation.1 | async-start | bytes 4194304 | tf_op jit(solution)/shard_map/all_to_all | solution.py:70
  66.1 22.6 %collective-permute-start.2 = (bf16[2,8,8,512]{3,2,1,0:T(8,128)(2,1)}, bf16[2,8,8,512]{3,2,1,0:T(8,128)(2,1)}, u32[]{:S(2)}, u32[]{:S(2)}) collective-permute-start(bf16[2,8,8,512]{3,2,1,0:T(8,128)(2,1)} %get-tuple-element.13), channel_id=1, source_target_pairs={{0,3},{1,0},{2,1},{3,2},{4,7},{5,4},{6,5},{7,6},{8,11},{9,8},{10,9... | collective-permute-start | bytes 393224 | tf_op jit(solution)/shard_map/ppermute | solution.py:92
  71.2 51.7 %collective-permute-start.3 = (bf16[2,8,8,512]{3,2,1,0:T(8,128)(2,1)S(1)}, bf16[2,8,8,512]{3,2,1,0:T(8,128)(2,1)}, u32[]{:S(2)}, u32[]{:S(2)}) collective-permute-start(bf16[2,8,8,512]{3,2,1,0:T(8,128)(2,1)S(1)} %get-tuple-element.16), channel_id=1, source_target_pairs={{0,2},{1,3},{2,0},{3,1},{4,6},{5,7},{6,4},{7,5},{8,10},{9,11},{10,... | collective-permute-start | bytes 393224 | tf_op jit(solution)/shard_map/ppermute | solution.py:92
  73.1 49.8 %collective-permute-start.4 = (bf16[2,8,8,512]{3,2,1,0:T(8,128)(2,1)S(1)}, bf16[2,8,8,512]{3,2,1,0:T(8,128)(2,1)}, u32[]{:S(2)}, u32[]{:S(2)}) collective-permute-start(bf16[2,8,8,512]{3,2,1,0:T(8,128)(2,1)S(1)} %get-tuple-element.15), channel_id=1, source_target_pairs={{0,1},{1,2},{2,3},{3,0},{4,5},{5,6},{6,7},{7,4},{8,9},{9,10},{10,1... | collective-permute-start | bytes 393224 | tf_op jit(solution)/shard_map/ppermute | solution.py:92
  128.4 1.0 copy-start.2
  128.4 1.2 copy-start.3
  129.6 6.7 %copy-start.1 = (f32[512,512]{1,0:T(8,128)S(1)}, f32[512,512]{1,0:T(8,128)}, u32[]{:S(2)}) copy-start(f32[512,512]{1,0:T(8,128)} %get-tuple-element.20) | copy-start | bytes 3145732

commit v15 on v11

--- a/solution.py
+++ b/solution.py
@@ -61,10 +61,14 @@
         mine = lax.all_to_all(part, rest, 0, 0).sum(axis=0, dtype=value.dtype)
     else:
         mine = lax.all_to_all(chunks, chan_axes, 0, 0).sum(axis=0, dtype=value.dtype)
-    spread = jnp.broadcast_to(mine[None], (count * segs, rows, freqs))
-    got = lax.all_to_all(spread, chan_axes + (seg_axis,), 0, 0)
     if chan_axes == CHAN_AXES:
-        got = got.reshape(count // pair, pair, segs, rows, freqs).transpose(1, 0, 2, 3, 4)
+        spread = jnp.broadcast_to(mine[None], (count * segs // pair, rows, freqs))
+        half_got = lax.all_to_all(spread, rest + (seg_axis,), 0, 0)
+        sibling = lax.ppermute(half_got, "c", [(0, 1), (1, 0)])
+        got = jnp.stack([jnp.where(upper, sibling, half_got), jnp.where(upper, half_got, sibling)])
+    else:
+        spread = jnp.broadcast_to(mine[None], (count * segs, rows, freqs))
+        got = lax.all_to_all(spread, chan_axes + (seg_axis,), 0, 0)
     split = local_segs // rows
     got = got.reshape(parts, sources, split, segs, rows, freqs).transpose(0, 3, 2, 4, 1, 5)
     return got.reshape(parts, segs * local_segs, sources, freqs)

time: 129 us -> 124 us (0.961)
  waiting for transfers between devices: 41.9 us -> 33.9 us
  starting transfers between devices: 31.1 us -> 34.6 us
    ppermute x3, waiting for transfers between devices: 40.8 us -> 3.92 us  [regroup_receivers(): blocks.append(lax.ppermute(group((me + shift) % segs), seg_axis, pairs))]
    all_to_all x1, waiting for transfers between devices: 0.01 us -> 28.8 us  [gather_sources(): half_got = lax.all_to_all(spread, rest + (seg_axis,), 0, 0)]
    ppermute x0 -> x1, starting transfers between devices: none -> 5.64 us  [gather_sources(): sibling = lax.ppermute(half_got, 'c', [(0, 1), (1, 0)])]
    ppermute x3, starting transfers between devices: 10.8 us -> 8.26 us  [regroup_receivers(): blocks.append(lax.ppermute(group((me + shift) % segs), seg_axis, pairs))]
    transpose x0 -> x1, other arithmetic: none -> 1.48 us  [gather_sources(): got.reshape(parts, sources, split, segs, rows, freqs)]
    select_n x0 -> x1, other arithmetic: none -> 1.37 us  [gather_sources(): jnp.where(upper, sibling, half_got)]
  transfers between devices with their start and end apart: 5 -> 6, of which waited for: 3 -> 3; matrix products, arithmetic and copies ran while one was open for 7% -> 5% of each run, Pallas kernels for 0% -> 0%
where the time goes in v15:
time: 124 us; the launch traced here: 123 us
  starting transfers between devices  34.6 us (28%)
  waiting for transfers between devices  33.9 us (27%)
  blocking collectives  29 us (23%)
  other arithmetic  19.1 us (15%)
  local copies, waits for them, and re-layouts  3.49 us (3%)
  matrix products  3.14 us (3%)
    all_to_all x1, blocking collectives, gather_sources(): mine = lax.all_to_all(part, rest, 0, 0).sum(axis=0, dtype=value.dtype)  29 us
    all_to_all x1, waiting for transfers between devices, gather_sources(): half_got = lax.all_to_all(spread, rest + (seg_axis,), 0, 0)  28.8 us
    all_to_all x1, starting transfers between devices, gather_sources(): half_got = lax.all_to_all(spread, rest + (seg_axis,), 0, 0)  11.9 us
    ppermute x1, starting transfers between devices, gather_sources(): half = keep + lax.ppermute(send, 'c', [(0, 1), (1, 0)])  8.79 us
    ppermute x3, starting transfers between devices, regroup_receivers(): blocks.append(lax.ppermute(group((me + shift) % segs), seg_axis, pairs))  8.26 us
    reduce_sum x1, other arithmetic, correlate(): real_part = jnp.sum(a * c + b * d, axis=0)  6.94 us
    ppermute x1, starting transfers between devices, gather_sources(): sibling = lax.ppermute(half_got, 'c', [(0, 1), (1, 0)])  5.64 us
    cos x1, other arithmetic, lag_matrix(): return jnp.concatenate([jnp.cos(angles), -jnp.sin(angles)], axis=0)  4.12 us
  transfers between devices with their start and end apart: 6, of which 3 were waited for; matrix products, arithmetic and copies ran while one was open for 5% of the time, Pallas kernels for 0%

profile of v15, /device:TPU:1, one launch (start us, length us, event | category | flops | bytes accessed | tf_op | source)
XLA Modules:
  0.0 123.4 jit_solution(14515507211433373375)
XLA Ops:
  0.0 0.7 broadcast_subtract_fusion
  0.9 1.2 convert_element_type.58
  2.3 0.4 fusion.5
  2.8 8.8 %collective-permute-start = (bf16[256,512]{1,0:T(8,128)(2,1)S(1)}, bf16[256,512]{1,0:T(8,128)(2,1)S(1)}, u32[]{:S(2)}, u32[]{:S(2)}) collective-permute-start(bf16[256,512]{1,0:T(8,128)(2,1)S(1)} %bitcast.61), channel_id=1, source_target_pairs={{0,4},{4,0},{1,5},{5,1},{2,6},{6,2},{3,7},{7,3},{8,12},{12,8},{9,1... | collective-permute-start | bytes 786440 | tf_op jit(solution)/shard_map/ppermute | solution.py:59
  11.6 1.1 collective-permute-done
  13.0 29.0 %all_to_all.10 = bf16[64,4,512]{2,1,0:T(4,128)(2,1)S(1)} all-to-all(bf16[64,4,512]{2,1,0:T(4,128)(2,1)S(1)} %reshape.78), channel_id=1, replica_groups=mesh['x'=4,'zh'=2,'y'=8,'c'=2,'seg'=4] {'x','zh','y'}, dimensions={0} | all-to-all | bytes 524288 | tf_op jit(solution)/shard_map/all_to_all | solution.py:61
  42.1 1.2 %broadcast_in_dim.2 = bf16[256,4,512]{2,1,0:T(4,128)(2,1)} broadcast(bf16[4,512]{1,0:T(4,128)(2,1)S(1)} %reduce_sum.37), dimensions={1,2} | broadcast | bytes 1052672 | tf_op jit(solution)/shard_map/broadcast_in_dim | solution.py:65
  43.4 11.9 %all-to-all-start.1 = ((bf16[256,4,512]{2,1,0:T(4,128)(2,1)}), bf16[256,4,512]{2,1,0:T(4,128)(2,1)S(1)}, u32[]{:S(2)}, u32[]{:S(2)}) async-start(bf16[256,4,512]{2,1,0:T(4,128)(2,1)} %broadcast_in_dim.2), calls=%async_computation.1 | async-start | bytes 2097152 | tf_op jit(solution)/shard_map/all_to_all | solution.py:66
  55.4 28.8 %all-to-all-done.1 = bf16[256,4,512]{2,1,0:T(4,128)(2,1)S(1)} async-done(((bf16[256,4,512]{2,1,0:T(4,128)(2,1)}), bf16[256,4,512]{2,1,0:T(4,128)(2,1)S(1)}, u32[]{:S(2)}, u32[]{:S(2)}) %all-to-all-start.1) | async-done | bytes 1048608 | tf_op jit(solution)/shard_map/all_to_all | solution.py:66
  84.2 5.6 %collective-permute-start.1 = (bf16[256,4,512]{2,1,0:T(4,128)(2,1)S(1)}, bf16[256,4,512]{2,1,0:T(4,128)(2,1)}, u32[]{:S(2)}, u32[]{:S(2)}) collective-permute-start(bf16[256,4,512]{2,1,0:T(4,128)(2,1)S(1)} %all-to-all-done.1), channel_id=1, source_target_pairs={{0,4},{4,0},{1,5},{5,1},{2,6},{6,2},{3,7},{7,3},{8,12},{12,8},{9,1... | collective-permute-start | bytes 3145736 | tf_op jit(solution)/shard_map/ppermute | solution.py:67
  90.0 0.7 dynamic-slice_bitcast_fusion.3
  90.7 2.7 %collective-permute-start.2 = (bf16[2,8,8,512]{3,2,1,0:T(8,128)(2,1)}, bf16[2,8,8,512]{3,2,1,0:T(8,128)(2,1)}, u32[]{:S(2)}, u32[]{:S(2)}) collective-permute-start(bf16[2,8,8,512]{3,2,1,0:T(8,128)(2,1)} %get-tuple-element.15), channel_id=1, source_target_pairs={{0,3},{1,0},{2,1},{3,2},{4,7},{5,4},{6,5},{7,6},{8,11},{9,8},{10,9... | collective-permute-start | bytes 393224 | tf_op jit(solution)/shard_map/ppermute | solution.py:89
  93.5 2.6 %collective-permute-start.3 = (bf16[2,8,8,512]{3,2,1,0:T(8,128)(2,1)S(1)}, bf16[2,8,8,512]{3,2,1,0:T(8,128)(2,1)}, u32[]{:S(2)}, u32[]{:S(2)}) collective-permute-start(bf16[2,8,8,512]{3,2,1,0:T(8,128)(2,1)S(1)} %get-tuple-element.18), channel_id=1, source_target_pairs={{0,2},{1,3},{2,0},{3,1},{4,6},{5,7},{6,4},{7,5},{8,10},{9,11},{10,... | collective-permute-start | bytes 393224 | tf_op jit(solution)/shard_map/ppermute | solution.py:89
  96.0 3.0 %collective-permute-start.4 = (bf16[2,8,8,512]{3,2,1,0:T(8,128)(2,1)S(1)}, bf16[2,8,8,512]{3,2,1,0:T(8,128)(2,1)}, u32[]{:S(2)}, u32[]{:S(2)}) collective-permute-start(bf16[2,8,8,512]{3,2,1,0:T(8,128)(2,1)S(1)} %get-tuple-element.17), channel_id=1, source_target_pairs={{0,1},{1,2},{2,3},{3,0},{4,5},{5,6},{6,7},{7,4},{8,9},{9,10},{10,1... | collective-permute-start | bytes 393224 | tf_op jit(solution)/shard_map/ppermute | solution.py:89
  99.0 4.1 %fusion.24 = (f32[512,512]{1,0:T(8,128)S(1)}, f32[512,512]{1,0:T(8,128)S(1)}) fusion(s32[512]{0:T(512)S(1)} %iota_add_fusion), kind=kLoop, calls=%fused_computation.39 | loop fusion | flops 3932160 | bytes 2099200 | tf_op jit(solution)/shard_map/cos | solution.py:26
  103.2 3.9 %collective-permute-done.3 = bf16[2,8,8,512]{3,2,1,0:T(8,128)(2,1)} collective-permute-done((bf16[2,8,8,512]{3,2,1,0:T(8,128)(2,1)S(1)}, bf16[2,8,8,512]{3,2,1,0:T(8,128)(2,1)}, u32[]{:S(2)}, u32[]{:S(2)}) %collective-permute-start.3) | collective-permute-done | bytes 131104 | tf_op jit(solution)/shard_map/ppermute | solution.py:89
  107.1 1.1 pad_maximum_fusion
  108.3 1.4 %broadcast_select_fusion.1 = (bf16[128,8,512]{2,1,0:T(8,128)(2,1)S(1)}, bf16[128,8,512]{2,1,0:T(8,128)(2,1)S(1)}) fusion(bf16[128,8,512]{2,1,0:T(8,128)(2,1)} %bitcast.51, bf16[128,8,512]{2,1,0:T(8,128)(2,1)S(1)} %bitcast.56, pred[]{:T(512)S(6)} %eq.23), kind=kLoop, calls=%fused_computation.33 | loop fusion | flops 1048576 | bytes 4194305 | tf_op jit(solution)/shard_map/jit(_where)/select_n | solution.py:68
  109.7 1.5 %maximum_bitcast_fusion = bf16[2,4,2,4,32,512]{5,3,1,2,4,0:T(4,128)(2,1)S(1)} fusion(bf16[1,32,2,4,4,512]{5,4,3,2,1,0:T(4,128)(2,1)S(1)} %bitcast.58, bf16[1,32,2,4,4,512]{5,4,3,2,1,0:T(4,128)(2,1)S(1)} %bitcast.57), kind=kLoop, calls=%fused_computation.5 | loop fusion | flops 1048576 | bytes 4194304 | tf_op jit(solution)/shard_map/transpose | solution.py:73
  111.2 1.2 copy.14
  112.3 0.8 fusion
  113.2 0.6 fusion.16
  113.7 6.9 %add_reduce_fusion = (f32[32,8,512]{2,1,0:T(8,128)S(1)}, f32[32,8,512]{2,1,0:T(8,128)S(1)}) fusion(f32[32,8,512]{2,1,0:T(8,128)S(1)} %get-tuple-element.12, f32[32,32,512]{2,1,0:T(8,128)S(1)} %get-tuple-element.8, f32[32,8,512]{2,1,0:T(8,128)S(1)} %get-tuple-element.11, f32[32,32,512]{2,1,0:T(8,128)S(1)} %get-tuple-element.7), kind=kLoop, calls=%fused_computation.1 | loop fusion | flops 33292288 | bytes 6291456 | tf_op jit(solution)/shard_map/reduce_sum | solution.py:36
  120.7 2.8 %fusion.9 = f32[32,8,512]{2,1,0:T(8,128)} fusion(f32[512,512]{1,0:T(8,128)S(1)} %get-tuple-element.20, f32[512,512]{1,0:T(8,128)S(1)} %get-tuple-element.19, f32[256,512]{1,0:T(8,128)S(1)} %bitcast.60, f32[256,512]{1,0:T(8,128)S(1)} %bitcast.59), kind=kOutput, calls=%fused_computation.16 | convolution fusion | flops 1611792384 | bytes 3670016 | tf_op jit(solution)/shard_map/dot_general | solution.py:40
  (17 shorter events, 1.2 us)
Async XLA Ops:
  0.0 2.2 %copy-start = (bf16[2,8,32,512]{3,2,1,0:T(8,128)(2,1)S(1)}, bf16[2,8,32,512]{3,2,1,0:T(8,128)(2,1)}, u32[]{:S(2)}) copy-start(bf16[2,8,32,512]{3,2,1,0:T(8,128)(2,1)} %param.2) | copy-start | bytes 1572868
  2.8 9.9 %collective-permute-start = (bf16[256,512]{1,0:T(8,128)(2,1)S(1)}, bf16[256,512]{1,0:T(8,128)(2,1)S(1)}, u32[]{:S(2)}, u32[]{:S(2)}) collective-permute-start(bf16[256,512]{1,0:T(8,128)(2,1)S(1)} %bitcast.61), channel_id=1, source_target_pairs={{0,4},{4,0},{1,5},{5,1},{2,6},{6,2},{3,7},{7,3},{8,12},{12,8},{9,1... | collective-permute-start | bytes 786440 | tf_op jit(solution)/shard_map/ppermute | solution.py:59
  43.4 40.8 %all-to-all-start.1 = ((bf16[256,4,512]{2,1,0:T(4,128)(2,1)}), bf16[256,4,512]{2,1,0:T(4,128)(2,1)S(1)}, u32[]{:S(2)}, u32[]{:S(2)}) async-start(bf16[256,4,512]{2,1,0:T(4,128)(2,1)} %broadcast_in_dim.2), calls=%async_computation.1 | async-start | bytes 2097152 | tf_op jit(solution)/shard_map/all_to_all | solution.py:66
  84.2 24.1 %collective-permute-start.1 = (bf16[256,4,512]{2,1,0:T(4,128)(2,1)S(1)}, bf16[256,4,512]{2,1,0:T(4,128)(2,1)}, u32[]{:S(2)}, u32[]{:S(2)}) collective-permute-start(bf16[256,4,512]{2,1,0:T(4,128)(2,1)S(1)} %all-to-all-done.1), channel_id=1, source_target_pairs={{0,4},{4,0},{1,5},{5,1},{2,6},{6,2},{3,7},{7,3},{8,12},{12,8},{9,1... | collective-permute-start | bytes 3145736 | tf_op jit(solution)/shard_map/ppermute | solution.py:67
  90.7 12.4 %collective-permute-start.2 = (bf16[2,8,8,512]{3,2,1,0:T(8,128)(2,1)}, bf16[2,8,8,512]{3,2,1,0:T(8,128)(2,1)}, u32[]{:S(2)}, u32[]{:S(2)}) collective-permute-start(bf16[2,8,8,512]{3,2,1,0:T(8,128)(2,1)} %get-tuple-element.15), channel_id=1, source_target_pairs={{0,3},{1,0},{2,1},{3,2},{4,7},{5,4},{6,5},{7,6},{8,11},{9,8},{10,9... | collective-permute-start | bytes 393224 | tf_op jit(solution)/shard_map/ppermute | solution.py:89
  93.5 13.6 %collective-permute-start.3 = (bf16[2,8,8,512]{3,2,1,0:T(8,128)(2,1)S(1)}, bf16[2,8,8,512]{3,2,1,0:T(8,128)(2,1)}, u32[]{:S(2)}, u32[]{:S(2)}) collective-permute-start(bf16[2,8,8,512]{3,2,1,0:T(8,128)(2,1)S(1)} %get-tuple-element.18), channel_id=1, source_target_pairs={{0,2},{1,3},{2,0},{3,1},{4,6},{5,7},{6,4},{7,5},{8,10},{9,11},{10,... | collective-permute-start | bytes 393224 | tf_op jit(solution)/shard_map/ppermute | solution.py:89
  96.0 11.0 %collective-permute-start.4 = (bf16[2,8,8,512]{3,2,1,0:T(8,128)(2,1)S(1)}, bf16[2,8,8,512]{3,2,1,0:T(8,128)(2,1)}, u32[]{:S(2)}, u32[]{:S(2)}) collective-permute-start(bf16[2,8,8,512]{3,2,1,0:T(8,128)(2,1)S(1)} %get-tuple-element.17), channel_id=1, source_target_pairs={{0,1},{1,2},{2,3},{3,0},{4,5},{5,6},{6,7},{7,4},{8,9},{9,10},{10,1... | collective-permute-start | bytes 393224 | tf_op jit(solution)/shard_map/ppermute | solution.py:89

commit v16 on v15

--- a/solution.py
+++ b/solution.py
@@ -43,7 +43,7 @@
     return result.reshape(stacked.shape[0], stacked.shape[1], -1)
 
 
-def gather_sources(value, chan_axes, seg_axis):
+def gather_sources(value, chan_axes, seg_axis, companion):
     parts, sources, local_segs, freqs = value.shape
     count = lax.psum(1, chan_axes)
     segs = lax.psum(1, seg_axis)
@@ -59,6 +59,7 @@
         half = keep + lax.ppermute(send, "c", [(0, 1), (1, 0)])
         part = half.reshape(count // pair, rows, freqs)
         mine = lax.all_to_all(part, rest, 0, 0).sum(axis=0, dtype=value.dtype)
+        mine, companion = lax.optimization_barrier((mine, companion))
     else:
         mine = lax.all_to_all(chunks, chan_axes, 0, 0).sum(axis=0, dtype=value.dtype)
     if chan_axes == CHAN_AXES:
@@ -71,7 +72,7 @@
         got = lax.all_to_all(spread, chan_axes + (seg_axis,), 0, 0)
     split = local_segs // rows
     got = got.reshape(parts, sources, split, segs, rows, freqs).transpose(0, 3, 2, 4, 1, 5)
-    return got.reshape(parts, segs * local_segs, sources, freqs)
+    return got.reshape(parts, segs * local_segs, sources, freqs), companion
 
 
 def regroup_receivers(whitened, seg_axis):
@@ -113,7 +114,8 @@
         local_spec = jnp.einsum(
             "pc,xscf->xpsf", onehot, whitened, preferred_element_type=jnp.float32
         ).astype(jnp.bfloat16)
-        source_spec = rotate_segments(gather_sources(local_spec, chan_axes, "seg"), "seg")
+        source_spec, regrouped = gather_sources(local_spec, chan_axes, "seg", regrouped)
+        source_spec = rotate_segments(source_spec, "seg")
         return correlate(source_spec, regrouped, lag_table)
 
     return shards

time: 124 us -> 118 us (0.952)
  waiting for transfers between devices: 33.9 us -> 12.9 us
  blocking collectives: 29 us -> 46.2 us
  other arithmetic: 19.1 us -> 16.1 us
  starting transfers between devices: 34.6 us -> 36.3 us
    all_to_all x1, waiting for transfers between devices: 28.8 us -> 0.01 us  [gather_sources(): mine = lax.all_to_all(part, rest, 0, 0).sum(axis=0, dtype=value.dtype)]
    all_to_all x1, blocking collectives: 29 us -> 46.2 us  [gather_sources(): half_got = lax.all_to_all(spread, rest + (seg_axis,), 0, 0)]
    ppermute x3, waiting for transfers between devices: 3.92 us -> 11.8 us  [regroup_receivers(): blocks.append(lax.ppermute(group((me + shift) % segs), seg_axis, pairs))]
    all_to_all x1, starting transfers between devices: 11.9 us -> 13.4 us  [gather_sources(): mine = lax.all_to_all(part, rest, 0, 0).sum(axis=0, dtype=value.dtype)]
  transfers between devices with their start and end apart: 6 -> 6, of which waited for: 3 -> 3; matrix products, arithmetic and copies ran while one was open for 5% -> 4% of each run, Pallas kernels for 0% -> 0%
where the time goes in v16:
time: 118 us
  blocking collectives  46.2 us (39%)
  starting transfers between devices  36.3 us (31%)
  other arithmetic  16.1 us (14%)
  waiting for transfers between devices  12.9 us (11%)
  matrix products  3.14 us (3%)
  local copies, waits for them, and re-layouts  2.57 us (2%)
    all_to_all x1, blocking collectives, gather_sources(): half_got = lax.all_to_all(spread, rest + (seg_axis,), 0, 0)  46.2 us
    all_to_all x1, starting transfers between devices, gather_sources(): mine = lax.all_to_all(part, rest, 0, 0).sum(axis=0, dtype=value.dtype)  13.4 us
    ppermute x3, waiting for transfers between devices, regroup_receivers(): blocks.append(lax.ppermute(group((me + shift) % segs), seg_axis, pairs))  11.8 us
    ppermute x3, starting transfers between devices, regroup_receivers(): blocks.append(lax.ppermute(group((me + shift) % segs), seg_axis, pairs))  9.29 us
    ppermute x1, starting transfers between devices, gather_sources(): half = keep + lax.ppermute(send, 'c', [(0, 1), (1, 0)])  8.79 us
    reduce_sum x1, other arithmetic, correlate(): real_part = jnp.sum(a * c + b * d, axis=0)  6.94 us
    ppermute x1, starting transfers between devices, gather_sources(): sibling = lax.ppermute(half_got, 'c', [(0, 1), (1, 0)])  4.89 us
    cos x1, other arithmetic, lag_matrix(): return jnp.concatenate([jnp.cos(angles), -jnp.sin(angles)], axis=0)  4.12 us
  transfers between devices with their start and end apart: 6, of which 3 were waited for; matrix products, arithmetic and copies ran while one was open for 4% of the time, Pallas kernels for 0%

profile of v16, /device:TPU:1, one launch (start us, length us, event | category | flops | bytes accessed | tf_op | source)
XLA Modules:
  0.0 117.6 jit_solution(7728179588775985770)
XLA Ops:
  0.0 1.2 %convert_element_type.58 = f32[2,8,32,512]{3,2,1,0:T(8,128)S(1)} convert(bf16[2,8,32,512]{3,2,1,0:T(8,128)(2,1)} %param.2) | non-fusion elementwise | flops 262144 | bytes 1572864 | tf_op jit(solution)/shard_map/convert_element_type | solution.py:14
  1.6 0.4 fusion.5
  2.0 0.2 copy.18
  2.2 8.8 %collective-permute-start = (bf16[256,512]{1,0:T(8,128)(2,1)S(1)}, bf16[256,512]{1,0:T(8,128)(2,1)S(1)}, u32[]{:S(2)}, u32[]{:S(2)}) collective-permute-start(bf16[256,512]{1,0:T(8,128)(2,1)S(1)} %bitcast.58), channel_id=1, source_target_pairs={{0,4},{4,0},{1,5},{5,1},{2,6},{6,2},{3,7},{7,3},{8,12},{12,8},{9,1... | collective-permute-start | bytes 786440 | tf_op jit(solution)/shard_map/ppermute | solution.py:59
  11.0 1.1 collective-permute-done
  12.1 0.2 bitcast_add_fusion
  12.3 0.8 reshape.78
  13.1 13.4 %all-to-all-start = ((bf16[64,4,512]{2,1,0:T(4,128)(2,1)}), bf16[64,4,512]{2,1,0:T(4,128)(2,1)S(1)}, u32[]{:S(2)}, u32[]{:S(2)}) async-start(bf16[64,4,512]{2,1,0:T(4,128)(2,1)} %reshape.78), calls=%async_computation | async-start | bytes 524288 | tf_op jit(solution)/shard_map/all_to_all | solution.py:61
  26.4 0.2 fusion.26
  26.7 4.9 %collective-permute-start.1 = (bf16[2,8,8,512]{3,2,1,0:T(8,128)(2,1)S(1)}, bf16[2,8,8,512]{3,2,1,0:T(8,128)(2,1)S(1)}, u32[]{:S(2)}, u32[]{:S(2)}) collective-permute-start(bf16[2,8,8,512]{3,2,1,0:T(8,128)(2,1)S(1)} %get-tuple-element.17), channel_id=1, source_target_pairs={{0,3},{1,0},{2,1},{3,2},{4,7},{5,4},{6,5},{7,6},{8,11},{9,8},{10,9... | collective-permute-start | bytes 393224 | tf_op jit(solution)/shard_map/ppermute | solution.py:90
  31.6 1.9 %collective-permute-start.2 = (bf16[2,8,8,512]{3,2,1,0:T(8,128)(2,1)S(1)}, bf16[2,8,8,512]{3,2,1,0:T(8,128)(2,1)S(1)}, u32[]{:S(2)}, u32[]{:S(2)}) collective-permute-start(bf16[2,8,8,512]{3,2,1,0:T(8,128)(2,1)S(1)} %get-tuple-element.20), channel_id=1, source_target_pairs={{0,2},{1,3},{2,0},{3,1},{4,6},{5,7},{6,4},{7,5},{8,10},{9,11},{10,... | collective-permute-start | bytes 393224 | tf_op jit(solution)/shard_map/ppermute | solution.py:90
  33.5 2.5 %collective-permute-start.3 = (bf16[2,8,8,512]{3,2,1,0:T(8,128)(2,1)S(1)}, bf16[2,8,8,512]{3,2,1,0:T(8,128)(2,1)S(1)}, u32[]{:S(2)}, u32[]{:S(2)}) collective-permute-start(bf16[2,8,8,512]{3,2,1,0:T(8,128)(2,1)S(1)} %get-tuple-element.19), channel_id=1, source_target_pairs={{0,1},{1,2},{2,3},{3,0},{4,5},{5,6},{6,7},{7,4},{8,9},{9,10},{10,1... | collective-permute-start | bytes 393224 | tf_op jit(solution)/shard_map/ppermute | solution.py:90
  36.0 2.4 %collective-permute-done.1 = bf16[2,8,8,512]{3,2,1,0:T(8,128)(2,1)S(1)} collective-permute-done((bf16[2,8,8,512]{3,2,1,0:T(8,128)(2,1)S(1)}, bf16[2,8,8,512]{3,2,1,0:T(8,128)(2,1)S(1)}, u32[]{:S(2)}, u32[]{:S(2)}) %collective-permute-start.1) | collective-permute-done | bytes 131104 | tf_op jit(solution)/shard_map/ppermute | solution.py:90
  38.3 9.4 %collective-permute-done.2 = bf16[2,8,8,512]{3,2,1,0:T(8,128)(2,1)S(1)} collective-permute-done((bf16[2,8,8,512]{3,2,1,0:T(8,128)(2,1)S(1)}, bf16[2,8,8,512]{3,2,1,0:T(8,128)(2,1)S(1)}, u32[]{:S(2)}, u32[]{:S(2)}) %collective-permute-start.2) | collective-permute-done | bytes 131104 | tf_op jit(solution)/shard_map/ppermute | solution.py:90
  48.0 0.3 broadcast_in_dim.2
  48.3 46.2 %all_to_all.10 = bf16[256,4,512]{2,1,0:T(4,128)(2,1)S(1)} all-to-all(bf16[256,4,512]{2,1,0:T(4,128)(2,1)S(1)} %broadcast_in_dim.2), channel_id=1, replica_groups=mesh['x'=4,'zh'=2,'y'=8,'c'=2,'seg'=4] {'x','zh','y','seg'}, dimensions={0} | all-to-all | bytes 2097152 | tf_op jit(solution)/shard_map/all_to_all | solution.py:67
  94.5 4.9 %collective-permute-start.4 = (bf16[256,4,512]{2,1,0:T(4,128)(2,1)S(1)}, bf16[256,4,512]{2,1,0:T(4,128)(2,1)S(1)}, u32[]{:S(2)}, u32[]{:S(2)}) collective-permute-start(bf16[256,4,512]{2,1,0:T(4,128)(2,1)S(1)} %all_to_all.10), channel_id=1, source_target_pairs={{0,4},{4,0},{1,5},{5,1},{2,6},{6,2},{3,7},{7,3},{8,12},{12,8},{9,1... | collective-permute-start | bytes 3145736 | tf_op jit(solution)/shard_map/ppermute | solution.py:68
  99.4 4.1 %fusion.24 = (f32[512,512]{1,0:T(8,128)S(1)}, f32[512,512]{1,0:T(8,128)S(1)}) fusion(s32[512]{0:T(512)S(1)} %iota_add_fusion), kind=kLoop, calls=%fused_computation.39 | loop fusion | flops 3932160 | bytes 2099200 | tf_op jit(solution)/shard_map/cos | solution.py:26
  103.8 1.5 %maximum_bitcast_fusion = bf16[2,4,2,4,32,512]{5,3,1,2,4,0:T(4,128)(2,1)S(1)} fusion(bf16[1,32,2,4,4,512]{5,4,3,2,1,0:T(4,128)(2,1)S(1)} %bitcast.54, bf16[1,32,2,4,4,512]{5,4,3,2,1,0:T(4,128)(2,1)S(1)} %bitcast.53), kind=kLoop, calls=%fused_computation.5 | loop fusion | flops 1048576 | bytes 4194304 | tf_op jit(solution)/shard_map/transpose | solution.py:74
  105.3 1.2 copy.14
  106.5 0.8 fusion
  107.3 0.6 fusion.16
  107.9 6.9 %add_reduce_fusion = (f32[32,8,512]{2,1,0:T(8,128)S(1)}, f32[32,8,512]{2,1,0:T(8,128)S(1)}) fusion(f32[32,8,512]{2,1,0:T(8,128)S(1)} %get-tuple-element.16, f32[32,32,512]{2,1,0:T(8,128)S(1)} %get-tuple-element.12, f32[32,8,512]{2,1,0:T(8,128)S(1)} %get-tuple-element.15, f32[32,32,512]{2,1,0:T(8,128)S(1)} %get-tuple-element.11), kind=kLoop, calls=%fused_computation.1 | loop fusion | flops 33292288 | bytes 6291456 | tf_op jit(solution)/shard_map/reduce_sum | solution.py:36
  114.8 2.8 %fusion.9 = f32[32,8,512]{2,1,0:T(8,128)} fusion(f32[512,512]{1,0:T(8,128)S(1)} %get-tuple-element.24, f32[512,512]{1,0:T(8,128)S(1)} %get-tuple-element.23, f32[256,512]{1,0:T(8,128)S(1)} %bitcast.56, f32[256,512]{1,0:T(8,128)S(1)} %bitcast.55), kind=kOutput, calls=%fused_computation.16 | convolution fusion | flops 1611792384 | bytes 3670016 | tf_op jit(solution)/shard_map/dot_general | solution.py:40
  (19 shorter events, 0.9 us)
Async XLA Ops:
  0.0 1.6 %copy-start = (bf16[2,8,32,512]{3,2,1,0:T(8,128)(2,1)S(1)}, bf16[2,8,32,512]{3,2,1,0:T(8,128)(2,1)}, u32[]{:S(2)}) copy-start(bf16[2,8,32,512]{3,2,1,0:T(8,128)(2,1)} %param.2) | copy-start | bytes 1572868
  0.0 1.4 %copy-start.1 = (s32[8,4]{0,1:T(4,128)S(1)}, s32[8,4]{0,1:T(4,128)}, u32[]{:S(2)}) copy-start(s32[8,4]{0,1:T(4,128)} %param.3) | copy-start | bytes 388
  2.2 9.9 %collective-permute-start = (bf16[256,512]{1,0:T(8,128)(2,1)S(1)}, bf16[256,512]{1,0:T(8,128)(2,1)S(1)}, u32[]{:S(2)}, u32[]{:S(2)}) collective-permute-start(bf16[256,512]{1,0:T(8,128)(2,1)S(1)} %bitcast.58), channel_id=1, source_target_pairs={{0,4},{4,0},{1,5},{5,1},{2,6},{6,2},{3,7},{7,3},{8,12},{12,8},{9,1... | collective-permute-start | bytes 786440 | tf_op jit(solution)/shard_map/ppermute | solution.py:59
  13.1 34.8 %all-to-all-start = ((bf16[64,4,512]{2,1,0:T(4,128)(2,1)}), bf16[64,4,512]{2,1,0:T(4,128)(2,1)S(1)}, u32[]{:S(2)}, u32[]{:S(2)}) async-start(bf16[64,4,512]{2,1,0:T(4,128)(2,1)} %reshape.78), calls=%async_computation | async-start | bytes 524288 | tf_op jit(solution)/shard_map/all_to_all | solution.py:61
  26.7 11.7 %collective-permute-start.1 = (bf16[2,8,8,512]{3,2,1,0:T(8,128)(2,1)S(1)}, bf16[2,8,8,512]{3,2,1,0:T(8,128)(2,1)S(1)}, u32[]{:S(2)}, u32[]{:S(2)}) collective-permute-start(bf16[2,8,8,512]{3,2,1,0:T(8,128)(2,1)S(1)} %get-tuple-element.17), channel_id=1, source_target_pairs={{0,3},{1,0},{2,1},{3,2},{4,7},{5,4},{6,5},{7,6},{8,11},{9,8},{10,9... | collective-permute-start | bytes 393224 | tf_op jit(solution)/shard_map/ppermute | solution.py:90
  31.6 16.2 %collective-permute-start.2 = (bf16[2,8,8,512]{3,2,1,0:T(8,128)(2,1)S(1)}, bf16[2,8,8,512]{3,2,1,0:T(8,128)(2,1)S(1)}, u32[]{:S(2)}, u32[]{:S(2)}) collective-permute-start(bf16[2,8,8,512]{3,2,1,0:T(8,128)(2,1)S(1)} %get-tuple-element.20), channel_id=1, source_target_pairs={{0,2},{1,3},{2,0},{3,1},{4,6},{5,7},{6,4},{7,5},{8,10},{9,11},{10,... | collective-permute-start | bytes 393224 | tf_op jit(solution)/shard_map/ppermute | solution.py:90
  33.5 14.3 %collective-permute-start.3 = (bf16[2,8,8,512]{3,2,1,0:T(8,128)(2,1)S(1)}, bf16[2,8,8,512]{3,2,1,0:T(8,128)(2,1)S(1)}, u32[]{:S(2)}, u32[]{:S(2)}) collective-permute-start(bf16[2,8,8,512]{3,2,1,0:T(8,128)(2,1)S(1)} %get-tuple-element.19), channel_id=1, source_target_pairs={{0,1},{1,2},{2,3},{3,0},{4,5},{5,6},{6,7},{7,4},{8,9},{9,10},{10,1... | collective-permute-start | bytes 393224 | tf_op jit(solution)/shard_map/ppermute | solution.py:90
  94.5 9.2 %collective-permute-start.4 = (bf16[256,4,512]{2,1,0:T(4,128)(2,1)S(1)}, bf16[256,4,512]{2,1,0:T(4,128)(2,1)S(1)}, u32[]{:S(2)}, u32[]{:S(2)}) collective-permute-start(bf16[256,4,512]{2,1,0:T(4,128)(2,1)S(1)} %all_to_all.10), channel_id=1, source_target_pairs={{0,4},{4,0},{1,5},{5,1},{2,6},{6,2},{3,7},{7,3},{8,12},{12,8},{9,1... | collective-permute-start | bytes 3145736 | tf_op jit(solution)/shard_map/ppermute | solution.py:68

commit v17 on v16

--- a/solution.py
+++ b/solution.py
@@ -114,7 +114,9 @@
         local_spec = jnp.einsum(
             "pc,xscf->xpsf", onehot, whitened, preferred_element_type=jnp.float32
         ).astype(jnp.bfloat16)
-        source_spec, regrouped = gather_sources(local_spec, chan_axes, "seg", regrouped)
+        source_spec, (regrouped, lag_table) = gather_sources(
+            local_spec, chan_axes, "seg", (regrouped, lag_table)
+        )
         source_spec = rotate_segments(source_spec, "seg")
         return correlate(source_spec, regrouped, lag_table)
 

time: 118 us -> 115 us (0.975)
  blocking collectives: 46.2 us -> 40.3 us
  other arithmetic: 16.1 us -> 19.1 us
  waiting for transfers between devices: 12.9 us -> 11.2 us
  starting transfers between devices: 36.3 us -> 37.5 us
    ppermute x3, waiting for transfers between devices: 11.8 us -> 0.01 us  [regroup_receivers(): blocks.append(lax.ppermute(group((me + shift) % segs), seg_axis, pairs))]
    all_to_all x1, waiting for transfers between devices: 0.01 us -> 10.1 us  [gather_sources(): mine = lax.all_to_all(part, rest, 0, 0).sum(axis=0, dtype=value.dtype)]
    all_to_all x1, blocking collectives: 46.2 us -> 40.3 us  [gather_sources(): half_got = lax.all_to_all(spread, rest + (seg_axis,), 0, 0)]
    ppermute x3, starting transfers between devices: 9.29 us -> 7.2 us  [regroup_receivers(): blocks.append(lax.ppermute(group((me + shift) % segs), seg_axis, pairs))]
    all_to_all x1, starting transfers between devices: 13.4 us -> 15.5 us  [gather_sources(): mine = lax.all_to_all(part, rest, 0, 0).sum(axis=0, dtype=value.dtype)]
    select_n x1, other arithmetic: 0.14 us -> 1.36 us  [gather_sources(): jnp.where(upper, sibling, half_got)]
  transfers between devices with their start and end apart: 6 -> 6, of which waited for: 3 -> 2; matrix products, arithmetic and copies ran while one was open for 4% -> 7% of each run, Pallas kernels for 0% -> 0%
where the time goes in v17:
time: 115 us; the launch traced here: 114 us
  blocking collectives  40.3 us (35%)
  starting transfers between devices  37.5 us (33%)
  other arithmetic  19.1 us (17%)
  waiting for transfers between devices  11.2 us (10%)
  matrix products  3.14 us (3%)
  local copies, waits for them, and re-layouts  2.56 us (2%)
    all_to_all x1, blocking collectives, gather_sources(): half_got = lax.all_to_all(spread, rest + (seg_axis,), 0, 0)  40.3 us
    all_to_all x1, starting transfers between devices, gather_sources(): mine = lax.all_to_all(part, rest, 0, 0).sum(axis=0, dtype=value.dtype)  15.5 us
    all_to_all x1, waiting for transfers between devices, gather_sources(): mine = lax.all_to_all(part, rest, 0, 0).sum(axis=0, dtype=value.dtype)  10.1 us
    ppermute x1, starting transfers between devices, gather_sources(): half = keep + lax.ppermute(send, 'c', [(0, 1), (1, 0)])  8.79 us
    ppermute x3, starting transfers between devices, regroup_receivers(): blocks.append(lax.ppermute(group((me + shift) % segs), seg_axis, pairs))  7.2 us
    reduce_sum x1, other arithmetic, correlate(): real_part = jnp.sum(a * c + b * d, axis=0)  6.72 us
    ppermute x1, starting transfers between devices, gather_sources(): sibling = lax.ppermute(half_got, 'c', [(0, 1), (1, 0)])  6.03 us
    cos x1, other arithmetic, lag_matrix(): return jnp.concatenate([jnp.cos(angles), -jnp.sin(angles)], axis=0)  4.12 us
  transfers between devices with their start and end apart: 6, of which 2 were waited for; matrix products, arithmetic and copies ran while one was open for 7% of the time, Pallas kernels for 0%

profile of v17, /device:TPU:1, one launch (start us, length us, event | category | flops | bytes accessed | tf_op | source)
XLA Modules:
  0.0 114.1 jit_solution(241115005495580184)
XLA Ops:
  0.0 1.2 %convert_element_type.58 = f32[2,8,32,512]{3,2,1,0:T(8,128)S(1)} convert(bf16[2,8,32,512]{3,2,1,0:T(8,128)(2,1)} %param.2) | non-fusion elementwise | flops 262144 | bytes 1572864 | tf_op jit(solution)/shard_map/convert_element_type | solution.py:14
  1.6 0.4 fusion.2
  2.2 8.8 %collective-permute-start = (bf16[256,512]{1,0:T(8,128)(2,1)S(1)}, bf16[256,512]{1,0:T(8,128)(2,1)S(1)}, u32[]{:S(2)}, u32[]{:S(2)}) collective-permute-start(bf16[256,512]{1,0:T(8,128)(2,1)S(1)} %bitcast.58), channel_id=1, source_target_pairs={{0,4},{4,0},{1,5},{5,1},{2,6},{6,2},{3,7},{7,3},{8,12},{12,8},{9,1... | collective-permute-start | bytes 786440 | tf_op jit(solution)/shard_map/ppermute | solution.py:59
  11.3 2.2 %collective-permute-start.1 = (bf16[2,8,8,512]{3,2,1,0:T(8,128)(2,1)S(1)}, bf16[2,8,8,512]{3,2,1,0:T(8,128)(2,1)S(1)}, u32[]{:S(2)}, u32[]{:S(2)}) collective-permute-start(bf16[2,8,8,512]{3,2,1,0:T(8,128)(2,1)S(1)} %get-tuple-element.19), channel_id=1, source_target_pairs={{0,3},{1,0},{2,1},{3,2},{4,7},{5,4},{6,5},{7,6},{8,11},{9,8},{10,9... | collective-permute-start | bytes 393224 | tf_op jit(solution)/shard_map/ppermute | solution.py:90
  13.5 1.9 %collective-permute-start.2 = (bf16[2,8,8,512]{3,2,1,0:T(8,128)(2,1)S(1)}, bf16[2,8,8,512]{3,2,1,0:T(8,128)(2,1)S(1)}, u32[]{:S(2)}, u32[]{:S(2)}) collective-permute-start(bf16[2,8,8,512]{3,2,1,0:T(8,128)(2,1)S(1)} %get-tuple-element.22), channel_id=1, source_target_pairs={{0,2},{1,3},{2,0},{3,1},{4,6},{5,7},{6,4},{7,5},{8,10},{9,11},{10,... | collective-permute-start | bytes 393224 | tf_op jit(solution)/shard_map/ppermute | solution.py:90
  15.4 3.0 %collective-permute-start.3 = (bf16[2,8,8,512]{3,2,1,0:T(8,128)(2,1)S(1)}, bf16[2,8,8,512]{3,2,1,0:T(8,128)(2,1)S(1)}, u32[]{:S(2)}, u32[]{:S(2)}) collective-permute-start(bf16[2,8,8,512]{3,2,1,0:T(8,128)(2,1)S(1)} %get-tuple-element.21), channel_id=1, source_target_pairs={{0,1},{1,2},{2,3},{3,0},{4,5},{5,6},{6,7},{7,4},{8,9},{9,10},{10,1... | collective-permute-start | bytes 393224 | tf_op jit(solution)/shard_map/ppermute | solution.py:90
  18.7 0.8 reshape.78
  19.4 15.5 %all-to-all-start = ((bf16[64,4,512]{2,1,0:T(4,128)(2,1)}), bf16[64,4,512]{2,1,0:T(4,128)(2,1)S(1)}, u32[]{:S(2)}, u32[]{:S(2)}) async-start(bf16[64,4,512]{2,1,0:T(4,128)(2,1)} %reshape.78), calls=%async_computation | async-start | bytes 524288 | tf_op jit(solution)/shard_map/all_to_all | solution.py:61
  34.9 4.1 %fusion.16 = (f32[512,512]{1,0:T(8,128)S(1)}, f32[512,512]{1,0:T(8,128)S(1)}) fusion(s32[512]{0:T(512)S(1)} %iota_add_fusion), kind=kLoop, calls=%fused_computation.37 | loop fusion | flops 3932160 | bytes 2099200 | tf_op jit(solution)/shard_map/cos | solution.py:26
  39.0 0.2 pad_maximum_fusion
  39.2 0.9 pad_maximum_fusion.1
  40.1 10.1 %all-to-all-done = bf16[64,4,512]{2,1,0:T(4,128)(2,1)S(1)} async-done(((bf16[64,4,512]{2,1,0:T(4,128)(2,1)}), bf16[64,4,512]{2,1,0:T(4,128)(2,1)S(1)}, u32[]{:S(2)}, u32[]{:S(2)}) %all-to-all-start) | async-done | bytes 262176 | tf_op jit(solution)/shard_map/all_to_all | solution.py:61
  50.4 0.3 broadcast_in_dim.2
  50.6 40.3 %all_to_all.10 = bf16[256,4,512]{2,1,0:T(4,128)(2,1)S(1)} all-to-all(bf16[256,4,512]{2,1,0:T(4,128)(2,1)S(1)} %broadcast_in_dim.2), channel_id=1, replica_groups=mesh['x'=4,'zh'=2,'y'=8,'c'=2,'seg'=4] {'x','zh','y','seg'}, dimensions={0} | all-to-all | bytes 2097152 | tf_op jit(solution)/shard_map/all_to_all | solution.py:67
  91.0 6.0 %collective-permute-start.4 = (bf16[256,4,512]{2,1,0:T(4,128)(2,1)S(1)}, bf16[256,4,512]{2,1,0:T(4,128)(2,1)}, u32[]{:S(2)}, u32[]{:S(2)}) collective-permute-start(bf16[256,4,512]{2,1,0:T(4,128)(2,1)S(1)} %all_to_all.10), channel_id=1, source_target_pairs={{0,4},{4,0},{1,5},{5,1},{2,6},{6,2},{3,7},{7,3},{8,12},{12,8},{9,1... | collective-permute-start | bytes 3145736 | tf_op jit(solution)/shard_map/ppermute | solution.py:68
  97.0 1.2 %bitcast_convert_fusion.1 = (f32[32,8,512]{2,1,0:T(8,128)S(1)}, f32[32,8,512]{2,1,0:T(8,128)S(1)}) fusion(bf16[2,32,8,512]{3,2,1,0:T(8,128)(2,1)} %pad_maximum_fusion.1), kind=kLoop, calls=%fused_computation.39 | loop fusion | flops 262144 | bytes 1572864 | tf_op jit(solution)/shard_map/convert_element_type | solution.py:34
  98.2 1.0 collective-permute-done.4
  99.2 1.4 %broadcast_select_fusion.1 = (bf16[128,8,512]{2,1,0:T(8,128)(2,1)S(1)}, bf16[128,8,512]{2,1,0:T(8,128)(2,1)S(1)}) fusion(bf16[128,8,512]{2,1,0:T(8,128)(2,1)} %bitcast.48, bf16[128,8,512]{2,1,0:T(8,128)(2,1)S(1)} %bitcast.53, pred[]{:T(512)S(6)} %eq.23), kind=kLoop, calls=%fused_computation.30 | loop fusion | flops 1048576 | bytes 4194305 | tf_op jit(solution)/shard_map/jit(_where)/select_n | solution.py:69
  100.6 1.5 %maximum_bitcast_fusion = bf16[2,4,2,4,32,512]{5,3,1,2,4,0:T(4,128)(2,1)S(1)} fusion(bf16[1,32,2,4,4,512]{5,4,3,2,1,0:T(4,128)(2,1)S(1)} %bitcast.55, bf16[1,32,2,4,4,512]{5,4,3,2,1,0:T(4,128)(2,1)S(1)} %bitcast.54), kind=kLoop, calls=%fused_computation.6 | loop fusion | flops 1048576 | bytes 4194304 | tf_op jit(solution)/shard_map/transpose | solution.py:74
  102.1 1.2 %copy.14 = bf16[2,4,2,4,32,512]{5,4,3,2,1,0:T(8,128)(2,1)S(1)} copy(bf16[2,4,2,4,32,512]{5,3,1,2,4,0:T(4,128)(2,1)S(1)} %maximum_bitcast_fusion) | data formatting | bytes 4194304 | tf_op jit(solution)/shard_map/transpose | solution.py:74
  103.3 0.8 fusion
  104.1 0.6 fusion.7
  104.6 6.7 %add_reduce_fusion = (f32[32,8,512]{2,1,0:T(8,128)S(1)}, f32[32,8,512]{2,1,0:T(8,128)S(1)}) fusion(f32[32,8,512]{2,1,0:T(8,128)S(1)} %get-tuple-element.18, f32[32,32,512]{2,1,0:T(8,128)S(1)} %get-tuple-element.14, f32[32,8,512]{2,1,0:T(8,128)S(1)} %get-tuple-element.17, f32[32,32,512]{2,1,0:T(8,128)S(1)} %get-tuple-element.13), kind=kLoop, calls=%fused_computation.1 | loop fusion | flops 33292288 | bytes 6291456 | tf_op jit(solution)/shard_map/reduce_sum | solution.py:36
  111.4 2.8 %fusion.1 = f32[32,8,512]{2,1,0:T(8,128)} fusion(f32[1024,512]{1,0:T(8,128)S(1)} %pad_maximum_fusion, f32[256,512]{1,0:T(8,128)S(1)} %bitcast.57, f32[256,512]{1,0:T(8,128)S(1)} %bitcast.56), kind=kOutput, calls=%fused_computation.12 | convolution fusion | flops 1611268096 | bytes 3670016 | tf_op jit(solution)/shard_map/dot_general | solution.py:40
  (20 shorter events, 1.0 us)
Async XLA Ops:
  0.0 1.6 %copy-start = (bf16[2,8,32,512]{3,2,1,0:T(8,128)(2,1)S(1)}, bf16[2,8,32,512]{3,2,1,0:T(8,128)(2,1)}, u32[]{:S(2)}) copy-start(bf16[2,8,32,512]{3,2,1,0:T(8,128)(2,1)} %param.2) | copy-start | bytes 1572868
  0.0 1.4 %copy-start.1 = (s32[8,4]{0,1:T(4,128)S(1)}, s32[8,4]{0,1:T(4,128)}, u32[]{:S(2)}) copy-start(s32[8,4]{0,1:T(4,128)} %param.3) | copy-start | bytes 388
  2.2 16.3 %collective-permute-start = (bf16[256,512]{1,0:T(8,128)(2,1)S(1)}, bf16[256,512]{1,0:T(8,128)(2,1)S(1)}, u32[]{:S(2)}, u32[]{:S(2)}) collective-permute-start(bf16[256,512]{1,0:T(8,128)(2,1)S(1)} %bitcast.58), channel_id=1, source_target_pairs={{0,4},{4,0},{1,5},{5,1},{2,6},{6,2},{3,7},{7,3},{8,12},{12,8},{9,1... | collective-permute-start | bytes 786440 | tf_op jit(solution)/shard_map/ppermute | solution.py:59
  11.3 27.9 %collective-permute-start.1 = (bf16[2,8,8,512]{3,2,1,0:T(8,128)(2,1)S(1)}, bf16[2,8,8,512]{3,2,1,0:T(8,128)(2,1)S(1)}, u32[]{:S(2)}, u32[]{:S(2)}) collective-permute-start(bf16[2,8,8,512]{3,2,1,0:T(8,128)(2,1)S(1)} %get-tuple-element.19), channel_id=1, source_target_pairs={{0,3},{1,0},{2,1},{3,2},{4,7},{5,4},{6,5},{7,6},{8,11},{9,8},{10,9... | collective-permute-start | bytes 393224 | tf_op jit(solution)/shard_map/ppermute | solution.py:90
  13.5 25.7 %collective-permute-start.2 = (bf16[2,8,8,512]{3,2,1,0:T(8,128)(2,1)S(1)}, bf16[2,8,8,512]{3,2,1,0:T(8,128)(2,1)S(1)}, u32[]{:S(2)}, u32[]{:S(2)}) collective-permute-start(bf16[2,8,8,512]{3,2,1,0:T(8,128)(2,1)S(1)} %get-tuple-element.22), channel_id=1, source_target_pairs={{0,2},{1,3},{2,0},{3,1},{4,6},{5,7},{6,4},{7,5},{8,10},{9,11},{10,... | collective-permute-start | bytes 393224 | tf_op jit(solution)/shard_map/ppermute | solution.py:90
  15.4 23.8 %collective-permute-start.3 = (bf16[2,8,8,512]{3,2,1,0:T(8,128)(2,1)S(1)}, bf16[2,8,8,512]{3,2,1,0:T(8,128)(2,1)S(1)}, u32[]{:S(2)}, u32[]{:S(2)}) collective-permute-start(bf16[2,8,8,512]{3,2,1,0:T(8,128)(2,1)S(1)} %get-tuple-element.21), channel_id=1, source_target_pairs={{0,1},{1,2},{2,3},{3,0},{4,5},{5,6},{6,7},{7,4},{8,9},{9,10},{10,1... | collective-permute-start | bytes 393224 | tf_op jit(solution)/shard_map/ppermute | solution.py:90
  19.4 30.8 %all-to-all-start = ((bf16[64,4,512]{2,1,0:T(4,128)(2,1)}), bf16[64,4,512]{2,1,0:T(4,128)(2,1)S(1)}, u32[]{:S(2)}, u32[]{:S(2)}) async-start(bf16[64,4,512]{2,1,0:T(4,128)(2,1)} %reshape.78), calls=%async_computation | async-start | bytes 524288 | tf_op jit(solution)/shard_map/all_to_all | solution.py:61
  91.0 8.2 %collective-permute-start.4 = (bf16[256,4,512]{2,1,0:T(4,128)(2,1)S(1)}, bf16[256,4,512]{2,1,0:T(4,128)(2,1)}, u32[]{:S(2)}, u32[]{:S(2)}) collective-permute-start(bf16[256,4,512]{2,1,0:T(4,128)(2,1)S(1)} %all_to_all.10), channel_id=1, source_target_pairs={{0,4},{4,0},{1,5},{5,1},{2,6},{6,2},{3,7},{7,3},{8,12},{12,8},{9,1... | collective-permute-start | bytes 3145736 | tf_op jit(solution)/shard_map/ppermute | solution.py:68

commit v18 on v17

--- a/solution.py
+++ b/solution.py
@@ -63,8 +63,16 @@
     else:
         mine = lax.all_to_all(chunks, chan_axes, 0, 0).sum(axis=0, dtype=value.dtype)
     if chan_axes == CHAN_AXES:
-        spread = jnp.broadcast_to(mine[None], (count * segs // pair, rows, freqs))
-        half_got = lax.all_to_all(spread, rest + (seg_axis,), 0, 0)
+        me = lax.axis_index(seg_axis)
+        came = [mine]
+        for shift in range(1, segs):
+            pairs = [(i, (i + shift) % segs) for i in range(segs)]
+            came.append(lax.ppermute(mine, seg_axis, pairs))
+        ring = jnp.stack(came[::-1] * 2)
+        start = (segs - (me + 1) % segs) % segs
+        ordered = lax.dynamic_slice_in_dim(ring, start, segs, axis=0)
+        spread = jnp.broadcast_to(ordered[None], (count // pair,) + ordered.shape)
+        half_got = lax.all_to_all(spread, rest, 0, 0).reshape(count * segs // pair, rows, freqs)
         sibling = lax.ppermute(half_got, "c", [(0, 1), (1, 0)])
         got = jnp.stack([jnp.where(upper, sibling, half_got), jnp.where(upper, half_got, sibling)])
     else:

time: 115 us -> 124 us (1.078)
  starting transfers between devices: 37.5 us -> 48.7 us
  blocking collectives: 40.3 us -> 33.3 us
  waiting for transfers between devices: 11.2 us -> 15.2 us
    ppermute x0 -> x3, starting transfers between devices: none -> 9.19 us  [gather_sources(): came.append(lax.ppermute(mine, seg_axis, pairs))]
    all_to_all x1, blocking collectives: 40.3 us -> 33.3 us  [gather_sources(): lax.all_to_all(spread, rest, 0, 0)]
    ppermute x0 -> x3, waiting for transfers between devices: none -> 4 us  [gather_sources(): came.append(lax.ppermute(mine, seg_axis, pairs))]
    ppermute x1, starting transfers between devices: 6.03 us -> 8.09 us  [gather_sources(): sibling = lax.ppermute(half_got, 'c', [(0, 1), (1, 0)])]
  transfers between devices with their start and end apart: 6 -> 9, of which waited for: 2 -> 4; matrix products, arithmetic and copies ran while one was open for 7% -> 6% of each run, Pallas kernels for 0% -> 0%
where the time goes in v18:
time: 124 us
  starting transfers between devices  48.7 us (39%)
  blocking collectives  33.3 us (27%)
  other arithmetic  19.9 us (16%)
  waiting for transfers between devices  15.2 us (12%)
  matrix products  3.14 us (3%)
  local copies, waits for them, and re-layouts  2.88 us (2%)
    all_to_all x1, blocking collectives, gather_sources(): lax.all_to_all(spread, rest, 0, 0)  33.3 us
    all_to_all x1, starting transfers between devices, gather_sources(): mine = lax.all_to_all(part, rest, 0, 0).sum(axis=0, dtype=value.dtype)  15.5 us
    all_to_all x1, waiting for transfers between devices, gather_sources(): mine = lax.all_to_all(part, rest, 0, 0).sum(axis=0, dtype=value.dtype)  10.1 us
    ppermute x3, starting transfers between devices, gather_sources(): came.append(lax.ppermute(mine, seg_axis, pairs))  9.19 us
    ppermute x1, starting transfers between devices, gather_sources(): half = keep + lax.ppermute(send, 'c', [(0, 1), (1, 0)])  8.79 us
    ppermute x1, starting transfers between devices, gather_sources(): sibling = lax.ppermute(half_got, 'c', [(0, 1), (1, 0)])  8.09 us
    ppermute x3, starting transfers between devices, regroup_receivers(): blocks.append(lax.ppermute(group((me + shift) % segs), seg_axis, pairs))  7.2 us
    reduce_sum x1, other arithmetic, correlate(): real_part = jnp.sum(a * c + b * d, axis=0)  6.72 us
  transfers between devices with their start and end apart: 9, of which 4 were waited for; matrix products, arithmetic and copies ran while one was open for 6% of the time, Pallas kernels for 0%

profile of v18, /device:TPU:1, one launch (start us, length us, event | category | flops | bytes accessed | tf_op | source)
XLA Modules:
  0.0 123.5 jit_solution(3790546865607757169)
XLA Ops:
  0.0 1.2 convert_element_type.58
  2.2 8.8 %collective-permute-start = (bf16[256,512]{1,0:T(8,128)(2,1)S(1)}, bf16[256,512]{1,0:T(8,128)(2,1)S(1)}, u32[]{:S(2)}, u32[]{:S(2)}) collective-permute-start(bf16[256,512]{1,0:T(8,128)(2,1)S(1)} %bitcast.69), channel_id=1, source_target_pairs={{0,4},{4,0},{1,5},{5,1},{2,6},{6,2},{3,7},{7,3},{8,12},{12,8},{9,1... | collective-permute-start | bytes 786440 | tf_op jit(solution)/shard_map/ppermute | solution.py:59
  11.3 2.2 %collective-permute-start.1 = (bf16[2,8,8,512]{3,2,1,0:T(8,128)(2,1)S(1)}, bf16[2,8,8,512]{3,2,1,0:T(8,128)(2,1)S(1)}, u32[]{:S(2)}, u32[]{:S(2)}) collective-permute-start(bf16[2,8,8,512]{3,2,1,0:T(8,128)(2,1)S(1)} %get-tuple-element.19), channel_id=1, source_target_pairs={{0,3},{1,0},{2,1},{3,2},{4,7},{5,4},{6,5},{7,6},{8,11},{9,8},{10,9... | collective-permute-start | bytes 393224 | tf_op jit(solution)/shard_map/ppermute | solution.py:98
  13.5 1.9 %collective-permute-start.2 = (bf16[2,8,8,512]{3,2,1,0:T(8,128)(2,1)S(1)}, bf16[2,8,8,512]{3,2,1,0:T(8,128)(2,1)S(1)}, u32[]{:S(2)}, u32[]{:S(2)}) collective-permute-start(bf16[2,8,8,512]{3,2,1,0:T(8,128)(2,1)S(1)} %get-tuple-element.22), channel_id=1, source_target_pairs={{0,2},{1,3},{2,0},{3,1},{4,6},{5,7},{6,4},{7,5},{8,10},{9,11},{10,... | collective-permute-start | bytes 393224 | tf_op jit(solution)/shard_map/ppermute | solution.py:98
  15.4 3.0 %collective-permute-start.3 = (bf16[2,8,8,512]{3,2,1,0:T(8,128)(2,1)S(1)}, bf16[2,8,8,512]{3,2,1,0:T(8,128)(2,1)S(1)}, u32[]{:S(2)}, u32[]{:S(2)}) collective-permute-start(bf16[2,8,8,512]{3,2,1,0:T(8,128)(2,1)S(1)} %get-tuple-element.21), channel_id=1, source_target_pairs={{0,1},{1,2},{2,3},{3,0},{4,5},{5,6},{6,7},{7,4},{8,9},{9,10},{10,1... | collective-permute-start | bytes 393224 | tf_op jit(solution)/shard_map/ppermute | solution.py:98
  19.4 15.5 %all-to-all-start = ((bf16[64,4,512]{2,1,0:T(4,128)(2,1)}), bf16[64,4,512]{2,1,0:T(4,128)(2,1)S(1)}, u32[]{:S(2)}, u32[]{:S(2)}) async-start(bf16[64,4,512]{2,1,0:T(4,128)(2,1)} %reshape.81), calls=%async_computation | async-start | bytes 524288 | tf_op jit(solution)/shard_map/all_to_all | solution.py:61
  34.9 4.1 %fusion.16 = (f32[512,512]{1,0:T(8,128)S(1)}, f32[512,512]{1,0:T(8,128)S(1)}) fusion(s32[512]{0:T(512)S(1)} %iota_add_fusion), kind=kLoop, calls=%fused_computation.37 | loop fusion | flops 3932160 | bytes 2099200 | tf_op jit(solution)/shard_map/cos | solution.py:26
  39.2 0.9 pad_maximum_fusion.1
  40.1 10.1 %all-to-all-done = bf16[64,4,512]{2,1,0:T(4,128)(2,1)S(1)} async-done(((bf16[64,4,512]{2,1,0:T(4,128)(2,1)}), bf16[64,4,512]{2,1,0:T(4,128)(2,1)S(1)}, u32[]{:S(2)}, u32[]{:S(2)}) %all-to-all-start) | async-done | bytes 262176 | tf_op jit(solution)/shard_map/all_to_all | solution.py:61
  50.4 4.8 %collective-permute-start.4 = (bf16[4,512]{1,0:T(4,128)(2,1)S(1)}, bf16[4,512]{1,0:T(4,128)(2,1)S(1)}, u32[]{:S(2)}, u32[]{:S(2)}) collective-permute-start(bf16[4,512]{1,0:T(4,128)(2,1)S(1)} %reduce_sum.37), channel_id=1, source_target_pairs={{0,3},{1,0},{2,1},{3,2},{4,7},{5,4},{6,5},{7,6},{8,11},{9,8},{10,9... | collective-permute-start | bytes 12296 | tf_op jit(solution)/shard_map/ppermute | solution.py:70
  55.2 2.3 %collective-permute-start.5 = (bf16[4,512]{1,0:T(4,128)(2,1)S(1)}, bf16[4,512]{1,0:T(4,128)(2,1)S(1)}, u32[]{:S(2)}, u32[]{:S(2)}) collective-permute-start(bf16[4,512]{1,0:T(4,128)(2,1)S(1)} %reduce_sum.37), channel_id=1, source_target_pairs={{0,2},{1,3},{2,0},{3,1},{4,6},{5,7},{6,4},{7,5},{8,10},{9,11},{10,... | collective-permute-start | bytes 12296 | tf_op jit(solution)/shard_map/ppermute | solution.py:70
  57.5 2.1 %collective-permute-start.6 = (bf16[4,512]{1,0:T(4,128)(2,1)S(1)}, bf16[4,512]{1,0:T(4,128)(2,1)S(1)}, u32[]{:S(2)}, u32[]{:S(2)}) collective-permute-start(bf16[4,512]{1,0:T(4,128)(2,1)S(1)} %reduce_sum.37), channel_id=1, source_target_pairs={{0,1},{1,2},{2,3},{3,0},{4,5},{5,6},{6,7},{7,4},{8,9},{9,10},{10,1... | collective-permute-start | bytes 12296 | tf_op jit(solution)/shard_map/ppermute | solution.py:70
  59.6 0.8 collective-permute-done.5
  60.5 3.2 %collective-permute-done.6 = bf16[4,512]{1,0:T(4,128)(2,1)S(1)} collective-permute-done((bf16[4,512]{1,0:T(4,128)(2,1)S(1)}, bf16[4,512]{1,0:T(4,128)(2,1)S(1)}, u32[]{:S(2)}, u32[]{:S(2)}) %collective-permute-start.6) | collective-permute-done | bytes 4128 | tf_op jit(solution)/shard_map/ppermute | solution.py:70
  64.2 33.3 %all_to_all.10 = bf16[64,4,4,512]{3,2,1,0:T(4,128)(2,1)S(1)} all-to-all(bf16[64,4,4,512]{3,2,1,0:T(4,128)(2,1)S(1)} %broadcast_in_dim.2), channel_id=1, replica_groups=mesh['x'=4,'zh'=2,'y'=8,'c'=2,'seg'=4] {'x','zh','y'}, dimensions={0} | all-to-all | bytes 2097152 | tf_op jit(solution)/shard_map/all_to_all | solution.py:75
  97.5 8.1 %collective-permute-start.7 = (bf16[256,4,512]{2,1,0:T(4,128)(2,1)S(1)}, bf16[256,4,512]{2,1,0:T(4,128)(2,1)}, u32[]{:S(2)}, u32[]{:S(2)}) collective-permute-start(bf16[256,4,512]{2,1,0:T(4,128)(2,1)S(1)} %bitcast.64), channel_id=1, source_target_pairs={{0,4},{4,0},{1,5},{5,1},{2,6},{6,2},{3,7},{7,3},{8,12},{12,8},{9,1... | collective-permute-start | bytes 3145736 | tf_op jit(solution)/shard_map/ppermute | solution.py:76
  105.7 1.2 bitcast_convert_fusion.1
  106.8 1.0 collective-permute-done.7
  107.9 2.1 %broadcast_select_fusion.1 = (bf16[256,4,512]{2,1,0:T(4,128)(2,1)S(1)}, bf16[256,4,512]{2,1,0:T(4,128)(2,1)S(1)}) fusion(bf16[256,4,512]{2,1,0:T(4,128)(2,1)} %collective-permute-done.7, pred[]{:T(512)S(6)} %eq.25, bf16[64,4,4,512]{3,2,1,0:T(4,128)(2,1)S(1)} %all_to_all.10), kind=kLoop, calls=%fused_computation.30 | loop fusion | flops 1048576 | bytes 4194305 | tf_op jit(solution)/shard_map/jit(_where)/select_n | solution.py:77
  110.0 1.5 %maximum_bitcast_fusion = bf16[2,4,2,4,32,512]{5,3,1,2,4,0:T(4,128)(2,1)S(1)} fusion(bf16[1,32,2,4,4,512]{5,4,3,2,1,0:T(4,128)(2,1)S(1)} %bitcast.66, bf16[1,32,2,4,4,512]{5,4,3,2,1,0:T(4,128)(2,1)S(1)} %bitcast.65), kind=kLoop, calls=%fused_computation.6 | loop fusion | flops 1048576 | bytes 4194304 | tf_op jit(solution)/shard_map/transpose | solution.py:82
  111.5 1.2 copy.14
  112.6 0.8 fusion
  114.0 6.7 %add_reduce_fusion = (f32[32,8,512]{2,1,0:T(8,128)S(1)}, f32[32,8,512]{2,1,0:T(8,128)S(1)}) fusion(f32[32,8,512]{2,1,0:T(8,128)S(1)} %get-tuple-element.18, f32[32,32,512]{2,1,0:T(8,128)S(1)} %get-tuple-element.14, f32[32,8,512]{2,1,0:T(8,128)S(1)} %get-tuple-element.17, f32[32,32,512]{2,1,0:T(8,128)S(1)} %get-tuple-element.13), kind=kLoop, calls=%fused_computation.1 | loop fusion | flops 33292288 | bytes 6291456 | tf_op jit(solution)/shard_map/reduce_sum | solution.py:36
  120.7 2.8 %fusion.1 = f32[32,8,512]{2,1,0:T(8,128)} fusion(f32[1024,512]{1,0:T(8,128)S(1)} %pad_maximum_fusion, f32[256,512]{1,0:T(8,128)S(1)} %bitcast.68, f32[256,512]{1,0:T(8,128)S(1)} %bitcast.67), kind=kOutput, calls=%fused_computation.12 | convolution fusion | flops 1611268096 | bytes 3670016 | tf_op jit(solution)/shard_map/dot_general | solution.py:40
  (35 shorter events, 3.5 us)
Async XLA Ops:
  0.0 1.6 %copy-start = (bf16[2,8,32,512]{3,2,1,0:T(8,128)(2,1)S(1)}, bf16[2,8,32,512]{3,2,1,0:T(8,128)(2,1)}, u32[]{:S(2)}) copy-start(bf16[2,8,32,512]{3,2,1,0:T(8,128)(2,1)} %param.2) | copy-start | bytes 1572868
  0.0 1.4 %copy-start.1 = (s32[8,4]{0,1:T(4,128)S(1)}, s32[8,4]{0,1:T(4,128)}, u32[]{:S(2)}) copy-start(s32[8,4]{0,1:T(4,128)} %param.3) | copy-start | bytes 388
  2.2 16.3 %collective-permute-start = (bf16[256,512]{1,0:T(8,128)(2,1)S(1)}, bf16[256,512]{1,0:T(8,128)(2,1)S(1)}, u32[]{:S(2)}, u32[]{:S(2)}) collective-permute-start(bf16[256,512]{1,0:T(8,128)(2,1)S(1)} %bitcast.69), channel_id=1, source_target_pairs={{0,4},{4,0},{1,5},{5,1},{2,6},{6,2},{3,7},{7,3},{8,12},{12,8},{9,1... | collective-permute-start | bytes 786440 | tf_op jit(solution)/shard_map/ppermute | solution.py:59
  11.3 27.9 %collective-permute-start.1 = (bf16[2,8,8,512]{3,2,1,0:T(8,128)(2,1)S(1)}, bf16[2,8,8,512]{3,2,1,0:T(8,128)(2,1)S(1)}, u32[]{:S(2)}, u32[]{:S(2)}) collective-permute-start(bf16[2,8,8,512]{3,2,1,0:T(8,128)(2,1)S(1)} %get-tuple-element.19), channel_id=1, source_target_pairs={{0,3},{1,0},{2,1},{3,2},{4,7},{5,4},{6,5},{7,6},{8,11},{9,8},{10,9... | collective-permute-start | bytes 393224 | tf_op jit(solution)/shard_map/ppermute | solution.py:98
  13.5 25.7 %collective-permute-start.2 = (bf16[2,8,8,512]{3,2,1,0:T(8,128)(2,1)S(1)}, bf16[2,8,8,512]{3,2,1,0:T(8,128)(2,1)S(1)}, u32[]{:S(2)}, u32[]{:S(2)}) collective-permute-start(bf16[2,8,8,512]{3,2,1,0:T(8,128)(2,1)S(1)} %get-tuple-element.22), channel_id=1, source_target_pairs={{0,2},{1,3},{2,0},{3,1},{4,6},{5,7},{6,4},{7,5},{8,10},{9,11},{10,... | collective-permute-start | bytes 393224 | tf_op jit(solution)/shard_map/ppermute | solution.py:98
  15.4 23.8 %collective-permute-start.3 = (bf16[2,8,8,512]{3,2,1,0:T(8,128)(2,1)S(1)}, bf16[2,8,8,512]{3,2,1,0:T(8,128)(2,1)S(1)}, u32[]{:S(2)}, u32[]{:S(2)}) collective-permute-start(bf16[2,8,8,512]{3,2,1,0:T(8,128)(2,1)S(1)} %get-tuple-element.21), channel_id=1, source_target_pairs={{0,1},{1,2},{2,3},{3,0},{4,5},{5,6},{6,7},{7,4},{8,9},{9,10},{10,1... | collective-permute-start | bytes 393224 | tf_op jit(solution)/shard_map/ppermute | solution.py:98
  19.4 30.8 %all-to-all-start = ((bf16[64,4,512]{2,1,0:T(4,128)(2,1)}), bf16[64,4,512]{2,1,0:T(4,128)(2,1)S(1)}, u32[]{:S(2)}, u32[]{:S(2)}) async-start(bf16[64,4,512]{2,1,0:T(4,128)(2,1)} %reshape.81), calls=%async_computation | async-start | bytes 524288 | tf_op jit(solution)/shard_map/all_to_all | solution.py:61
  50.4 9.2 %collective-permute-start.4 = (bf16[4,512]{1,0:T(4,128)(2,1)S(1)}, bf16[4,512]{1,0:T(4,128)(2,1)S(1)}, u32[]{:S(2)}, u32[]{:S(2)}) collective-permute-start(bf16[4,512]{1,0:T(4,128)(2,1)S(1)} %reduce_sum.37), channel_id=1, source_target_pairs={{0,3},{1,0},{2,1},{3,2},{4,7},{5,4},{6,5},{7,6},{8,11},{9,8},{10,9... | collective-permute-start | bytes 12296 | tf_op jit(solution)/shard_map/ppermute | solution.py:70
  55.2 5.3 %collective-permute-start.5 = (bf16[4,512]{1,0:T(4,128)(2,1)S(1)}, bf16[4,512]{1,0:T(4,128)(2,1)S(1)}, u32[]{:S(2)}, u32[]{:S(2)}) collective-permute-start(bf16[4,512]{1,0:T(4,128)(2,1)S(1)} %reduce_sum.37), channel_id=1, source_target_pairs={{0,2},{1,3},{2,0},{3,1},{4,6},{5,7},{6,4},{7,5},{8,10},{9,11},{10,... | collective-permute-start | bytes 12296 | tf_op jit(solution)/shard_map/ppermute | solution.py:70
  57.5 6.1 %collective-permute-start.6 = (bf16[4,512]{1,0:T(4,128)(2,1)S(1)}, bf16[4,512]{1,0:T(4,128)(2,1)S(1)}, u32[]{:S(2)}, u32[]{:S(2)}) collective-permute-start(bf16[4,512]{1,0:T(4,128)(2,1)S(1)} %reduce_sum.37), channel_id=1, source_target_pairs={{0,1},{1,2},{2,3},{3,0},{4,5},{5,6},{6,7},{7,4},{8,9},{9,10},{10,1... | collective-permute-start | bytes 12296 | tf_op jit(solution)/shard_map/ppermute | solution.py:70
  97.5 10.3 %collective-permute-start.7 = (bf16[256,4,512]{2,1,0:T(4,128)(2,1)S(1)}, bf16[256,4,512]{2,1,0:T(4,128)(2,1)}, u32[]{:S(2)}, u32[]{:S(2)}) collective-permute-start(bf16[256,4,512]{2,1,0:T(4,128)(2,1)S(1)} %bitcast.64), channel_id=1, source_target_pairs={{0,4},{4,0},{1,5},{5,1},{2,6},{6,2},{3,7},{7,3},{8,12},{12,8},{9,1... | collective-permute-start | bytes 3145736 | tf_op jit(solution)/shard_map/ppermute | solution.py:76

commit v19 on v17

--- a/solution.py
+++ b/solution.py
@@ -26,15 +26,18 @@
     return jnp.concatenate([jnp.cos(angles), -jnp.sin(angles)], axis=0)
 
 
-def correlate(source_spec, receiver_spec, lag_table):
+def correlate(source_spec, receiver_spec, lag_table, swapped):
     segs = receiver_spec.shape[1]
     freqs = receiver_spec.shape[3]
     a = source_spec[0].astype(jnp.float32)[:, :, None, :]
     b = source_spec[1].astype(jnp.float32)[:, :, None, :]
-    c = receiver_spec[0].astype(jnp.float32)[:, None, :, :]
-    d = receiver_spec[1].astype(jnp.float32)[:, None, :, :]
+    first = jnp.where(swapped, receiver_spec[1], receiver_spec[0])
+    second = jnp.where(swapped, receiver_spec[0], receiver_spec[1])
+    c = first.astype(jnp.float32)[:, None, :, :]
+    d = second.astype(jnp.float32)[:, None, :, :]
+    sign = jnp.where(swapped, -1.0, 1.0).astype(jnp.float32)
     real_part = jnp.sum(a * c + b * d, axis=0)
-    imag_part = jnp.sum(a * d - b * c, axis=0)
+    imag_part = jnp.sum(a * d - b * c, axis=0) * sign
     stacked = jnp.concatenate([real_part, imag_part], axis=-1) * (1.0 / math.sqrt(segs))
     flat = stacked.reshape(-1, 2 * freqs)
     result = jnp.dot(
@@ -66,7 +69,7 @@
         spread = jnp.broadcast_to(mine[None], (count * segs // pair, rows, freqs))
         half_got = lax.all_to_all(spread, rest + (seg_axis,), 0, 0)
         sibling = lax.ppermute(half_got, "c", [(0, 1), (1, 0)])
-        got = jnp.stack([jnp.where(upper, sibling, half_got), jnp.where(upper, half_got, sibling)])
+        got = jnp.stack([half_got, sibling])
     else:
         spread = jnp.broadcast_to(mine[None], (count * segs, rows, freqs))
         got = lax.all_to_all(spread, chan_axes + (seg_axis,), 0, 0)
@@ -88,15 +91,10 @@
     for shift in range(1, segs):
         pairs = [(i, (i + shift) % segs) for i in range(segs)]
         blocks.append(lax.ppermute(group((me + shift) % segs), seg_axis, pairs))
-    return jnp.concatenate(blocks[::-1], axis=1)
-
-
-def rotate_segments(source_spec, seg_axis):
-    segs = lax.psum(1, seg_axis)
-    me = lax.axis_index(seg_axis)
-    parts, all_segs, sources, freqs = source_spec.shape
-    doubled = jnp.concatenate([source_spec, source_spec], axis=1)
-    return lax.dynamic_slice_in_dim(doubled, ((me + 1) % segs) * (all_segs // segs), all_segs, axis=1)
+    rotated = jnp.concatenate(blocks[::-1], axis=1)
+    doubled = jnp.concatenate([rotated, rotated], axis=1)
+    start = ((segs - (me + 1) % segs) % segs) * local_segs
+    return lax.dynamic_slice_in_dim(doubled, start, segs * local_segs, axis=1)
 
 
 def make_shards(chan_axes):
@@ -117,8 +115,8 @@
         source_spec, (regrouped, lag_table) = gather_sources(
             local_spec, chan_axes, "seg", (regrouped, lag_table)
         )
-        source_spec = rotate_segments(source_spec, "seg")
-        return correlate(source_spec, regrouped, lag_table)
+        swapped = lax.axis_index("c") == 1 if chan_axes == CHAN_AXES else False
+        return correlate(source_spec, regrouped, lag_table, swapped)
 
     return shards
 

time: 115 us -> 121 us (1.052)
  local copies, waits for them, and re-layouts: 2.56 us -> 11.8 us
  other arithmetic: 19.1 us -> 15 us
  waiting for transfers between devices: 11.2 us -> 12.6 us
    ppermute x3, starting transfers between devices: 7.2 us -> 12.5 us  [regroup_receivers(): blocks.append(lax.ppermute(group((me + shift) % segs), seg_axis, pairs))]
    ppermute x1, starting transfers between devices: 8.79 us -> 3.98 us  [gather_sources(): half = keep + lax.ppermute(send, 'c', [(0, 1), (1, 0)])]
    unnamed x4 -> x16, local copies, waits for them, and re-layouts: 0.01 us -> 3.85 us
    all_to_all x1, waiting for transfers between devices: 10.1 us -> 12.6 us  [gather_sources(): mine = lax.all_to_all(part, rest, 0, 0).sum(axis=0, dtype=value.dtype)]
    another operation x0 -> x2, local copies, waits for them, and re-layouts: none -> 2.38 us  [gather_sources(): got = jnp.stack([half_got, sibling])]
    dynamic_slice x0 -> x2, local copies, waits for them, and re-layouts: none -> 1.93 us  [the longest x1 1.88 us: regroup_receivers(): return lax.dynamic_slice_in_dim(doubled, start, segs * local_segs, axis=1)]
    concatenate x2 -> x0, other arithmetic: 1.66 us -> none  [the longest x1 0.86 us: regroup_receivers(): return jnp.concatenate(blocks[::-1], axis=1)]
    select_n x1 -> x0, other arithmetic: 1.36 us -> none  [gather_sources(): jnp.where(upper, sibling, half_got)]
  transfers between devices with their start and end apart: 6 -> 6, of which waited for: 2 -> 1; matrix products, arithmetic and copies ran while one was open for 7% -> 11% of each run, Pallas kernels for 0% -> 0%
where the time goes in v19:
time: 121 us; the launch traced here: 120 us
  blocking collectives  39.7 us (33%)
  starting transfers between devices  37.9 us (31%)
  other arithmetic  15 us (12%)
  waiting for transfers between devices  12.6 us (10%)
  local copies, waits for them, and re-layouts  11.8 us (10%)
  matrix products  3.15 us (3%)
    all_to_all x1, blocking collectives, gather_sources(): half_got = lax.all_to_all(spread, rest + (seg_axis,), 0, 0)  39.7 us
    all_to_all x1, starting transfers between devices, gather_sources(): mine = lax.all_to_all(part, rest, 0, 0).sum(axis=0, dtype=value.dtype)  15.7 us
    all_to_all x1, waiting for transfers between devices, gather_sources(): mine = lax.all_to_all(part, rest, 0, 0).sum(axis=0, dtype=value.dtype)  12.6 us
    ppermute x3, starting transfers between devices, regroup_receivers(): blocks.append(lax.ppermute(group((me + shift) % segs), seg_axis, pairs))  12.5 us
    reduce_sum x1, other arithmetic, correlate(): real_part = jnp.sum(a * c + b * d, axis=0)  6.72 us
    ppermute x1, starting transfers between devices, gather_sources(): sibling = lax.ppermute(half_got, 'c', [(0, 1), (1, 0)])  5.65 us
    cos x1, other arithmetic, lag_matrix(): return jnp.concatenate([jnp.cos(angles), -jnp.sin(angles)], axis=0)  4.12 us
    ppermute x1, starting transfers between devices, gather_sources(): half = keep + lax.ppermute(send, 'c', [(0, 1), (1, 0)])  3.98 us
  transfers between devices with their start and end apart: 6, of which 1 were waited for; matrix products, arithmetic and copies ran while one was open for 11% of the time, Pallas kernels for 0%

profile of v19, /device:TPU:1, one launch (start us, length us, event | category | flops | bytes accessed | tf_op | source)
XLA Modules:
  0.0 120.4 jit_solution(1839632526892588515)
XLA Ops:
  0.0 1.2 %convert_element_type.58 = f32[2,8,32,512]{3,2,1,0:T(8,128)S(1)} convert(bf16[2,8,32,512]{3,2,1,0:T(8,128)(2,1)} %param.2) | non-fusion elementwise | flops 262144 | bytes 1572864 | tf_op jit(solution)/shard_map/convert_element_type | solution.py:14
  1.7 8.4 %collective-permute-start.1 = (bf16[2,8,8,512]{3,1,2,0:T(8,128)(2,1)S(1)}, bf16[2,8,8,512]{3,1,2,0:T(8,128)(2,1)S(1)}, u32[]{:S(2)}, u32[]{:S(2)}) collective-permute-start(bf16[2,8,8,512]{3,1,2,0:T(8,128)(2,1)S(1)} %bitcast.53), channel_id=1, source_target_pairs={{0,3},{1,0},{2,1},{3,2},{4,7},{5,4},{6,5},{7,6},{8,11},{9,8},{10,9... | collective-permute-start | bytes 393224 | tf_op jit(solution)/shard_map/ppermute | solution.py:93
  10.2 0.7 copy.69
  10.8 1.9 %collective-permute-start.2 = (bf16[2,8,8,512]{3,1,2,0:T(8,128)(2,1)}, bf16[2,8,8,512]{3,1,2,0:T(8,128)(2,1)S(1)}, u32[]{:S(2)}, u32[]{:S(2)}) collective-permute-start(bf16[2,8,8,512]{3,1,2,0:T(8,128)(2,1)} %bitcast.49), channel_id=1, source_target_pairs={{0,2},{1,3},{2,0},{3,1},{4,6},{5,7},{6,4},{7,5},{8,10},{9,11},{10,... | collective-permute-start | bytes 393224 | tf_op jit(solution)/shard_map/ppermute | solution.py:93
  12.8 0.7 copy.68
  13.5 2.2 %collective-permute-start.3 = (bf16[2,8,8,512]{3,1,2,0:T(8,128)(2,1)}, bf16[2,8,8,512]{3,1,2,0:T(8,128)(2,1)S(1)}, u32[]{:S(2)}, u32[]{:S(2)}) collective-permute-start(bf16[2,8,8,512]{3,1,2,0:T(8,128)(2,1)} %bitcast.48), channel_id=1, source_target_pairs={{0,1},{1,2},{2,3},{3,0},{4,5},{5,6},{6,7},{7,4},{8,9},{9,10},{10,1... | collective-permute-start | bytes 393224 | tf_op jit(solution)/shard_map/ppermute | solution.py:93
  16.3 0.9 copy.67
  17.1 4.0 %collective-permute-start = (bf16[256,512]{1,0:T(8,128)(2,1)}, bf16[256,512]{1,0:T(8,128)(2,1)S(1)}, u32[]{:S(2)}, u32[]{:S(2)}) collective-permute-start(bf16[256,512]{1,0:T(8,128)(2,1)} %bitcast.47), channel_id=1, source_target_pairs={{0,4},{4,0},{1,5},{5,1},{2,6},{6,2},{3,7},{7,3},{8,12},{12,8},{9,1... | collective-permute-start | bytes 786440 | tf_op jit(solution)/shard_map/ppermute | solution.py:62
  21.1 4.1 %fusion.13 = (f32[512,512]{1,0:T(8,128)S(1)}, f32[512,512]{1,0:T(8,128)S(1)}) fusion(s32[512]{0:T(512)S(1)} %iota_add_fusion), kind=kLoop, calls=%fused_computation.30 | loop fusion | flops 3932160 | bytes 2099200 | tf_op jit(solution)/shard_map/cos | solution.py:26
  25.6 1.0 copy-done.1
  26.8 0.8 reshape.97
  27.5 15.7 %all-to-all-start = ((bf16[64,4,512]{2,1,0:T(4,128)(2,1)}), bf16[64,4,512]{2,1,0:T(4,128)(2,1)S(1)}, u32[]{:S(2)}, u32[]{:S(2)}) async-start(bf16[64,4,512]{2,1,0:T(4,128)(2,1)} %reshape.97), calls=%async_computation | async-start | bytes 524288 | tf_op jit(solution)/shard_map/all_to_all | solution.py:64
  43.3 0.7 constant_dynamic-update-slice_fusion.1
  44.0 0.7 constant_dynamic-update-slice_fusion
  44.6 0.7 fusion.16
  45.3 1.9 %constant_dynamic-slice_fusion = bf16[2,32,8,512]{3,1,2,0:T(8,128)(2,1)} fusion(bf16[2,64,8,512]{3,1,2,0:T(8,128)(2,1)} %fusion.16, s32[]{:T(128)S(6)} %select_n.100), kind=kLoop, calls=%fused_computation.55 | loop fusion | bytes 1048580 | tf_op jit(solution)/shard_map/dynamic_slice | solution.py:97
  47.2 12.6 %all-to-all-done = bf16[64,4,512]{2,1,0:T(4,128)(2,1)S(1)} async-done(((bf16[64,4,512]{2,1,0:T(4,128)(2,1)}), bf16[64,4,512]{2,1,0:T(4,128)(2,1)S(1)}, u32[]{:S(2)}, u32[]{:S(2)}) %all-to-all-start) | async-done | bytes 262176 | tf_op jit(solution)/shard_map/all_to_all | solution.py:64
  60.2 39.7 %all_to_all.10 = bf16[256,4,512]{2,1,0:T(4,128)(2,1)S(1)} all-to-all(bf16[256,4,512]{2,1,0:T(4,128)(2,1)S(1)} %broadcast_in_dim.2), channel_id=1, replica_groups=mesh['x'=4,'zh'=2,'y'=8,'c'=2,'seg'=4] {'x','zh','y','seg'}, dimensions={0} | all-to-all | bytes 2097152 | tf_op jit(solution)/shard_map/all_to_all | solution.py:70
  99.9 5.6 %collective-permute-start.4 = (bf16[256,4,512]{2,1,0:T(4,128)(2,1)S(1)}, bf16[256,4,512]{2,1,0:T(4,128)(2,1)}, u32[]{:S(2)}, u32[]{:S(2)}) collective-permute-start(bf16[256,4,512]{2,1,0:T(4,128)(2,1)S(1)} %all_to_all.10), channel_id=1, source_target_pairs={{0,4},{4,0},{1,5},{5,1},{2,6},{6,2},{3,7},{7,3},{8,12},{12,8},{9,1... | collective-permute-start | bytes 3145736 | tf_op jit(solution)/shard_map/ppermute | solution.py:71
  105.6 1.1 bitcast_convert_fusion.3
  107.9 1.8 %copy.49 = bf16[1,32,2,4,4,512]{5,1,4,2,3,0:T(8,128)(2,1)S(1)} copy(bf16[1,32,2,4,4,512]{5,4,3,2,1,0:T(4,128)(2,1)} %bitcast.11) | data formatting | bytes 2097152 | tf_op jit(solution)/shard_map/stack | solution.py:72
  110.1 0.7 bitcast_convert_fusion
  110.9 6.7 %add_reduce_fusion = (f32[32,8,512]{2,1,0:T(8,128)S(1)}, f32[32,8,512]{2,1,0:T(8,128)S(1)}) fusion(f32[32,8,512]{2,1,0:T(8,128)S(1)} %copy.51, f32[32,32,512]{2,1,0:T(8,128)S(1)} %get-tuple-element.25, f32[32,8,512]{2,1,0:T(8,128)S(1)} %copy.50, f32[32,32,512]{2,1,0:T(8,128)S(1)} %get-tuple-element.26), kind=kLoop, calls=%fused_computation.1 | loop fusion | flops 33292288 | bytes 6291456 | tf_op jit(solution)/shard_map/reduce_sum | solution.py:39
  117.6 2.8 %fusion = f32[32,8,512]{2,1,0:T(8,128)} fusion(f32[1024,512]{1,0:T(8,128)S(1)} %pad_maximum_fusion, f32[256,512]{1,0:T(8,128)S(1)} %multiply_bitcast_fusion, f32[256,512]{1,0:T(8,128)S(1)} %bitcast.52), kind=kOutput, calls=%fused_computation.9 | convolution fusion | flops 1611268096 | bytes 3670016 | tf_op jit(solution)/shard_map/dot_general | solution.py:43
  (36 shorter events, 3.5 us)
Async XLA Ops:
  0.0 1.4 %copy-start = (bf16[2,8,32,512]{3,2,1,0:T(8,128)(2,1)S(1)}, bf16[2,8,32,512]{3,2,1,0:T(8,128)(2,1)}, u32[]{:S(2)}) copy-start(bf16[2,8,32,512]{3,2,1,0:T(8,128)(2,1)} %param.2) | copy-start | bytes 1572868
  1.2 14.4 %copy-start.2 = (s32[8,4]{0,1:T(4,128)S(1)}, s32[8,4]{0,1:T(4,128)}, u32[]{:S(2)}) copy-start(s32[8,4]{0,1:T(4,128)} %param.3) | copy-start | bytes 388
  1.7 23.8 %collective-permute-start.1 = (bf16[2,8,8,512]{3,1,2,0:T(8,128)(2,1)S(1)}, bf16[2,8,8,512]{3,1,2,0:T(8,128)(2,1)S(1)}, u32[]{:S(2)}, u32[]{:S(2)}) collective-permute-start(bf16[2,8,8,512]{3,1,2,0:T(8,128)(2,1)S(1)} %bitcast.53), channel_id=1, source_target_pairs={{0,3},{1,0},{2,1},{3,2},{4,7},{5,4},{6,5},{7,6},{8,11},{9,8},{10,9... | collective-permute-start | bytes 393224 | tf_op jit(solution)/shard_map/ppermute | solution.py:93
  10.8 14.6 %collective-permute-start.2 = (bf16[2,8,8,512]{3,1,2,0:T(8,128)(2,1)}, bf16[2,8,8,512]{3,1,2,0:T(8,128)(2,1)S(1)}, u32[]{:S(2)}, u32[]{:S(2)}) collective-permute-start(bf16[2,8,8,512]{3,1,2,0:T(8,128)(2,1)} %bitcast.49), channel_id=1, source_target_pairs={{0,2},{1,3},{2,0},{3,1},{4,6},{5,7},{6,4},{7,5},{8,10},{9,11},{10,... | collective-permute-start | bytes 393224 | tf_op jit(solution)/shard_map/ppermute | solution.py:93
  13.5 12.1 %collective-permute-start.3 = (bf16[2,8,8,512]{3,1,2,0:T(8,128)(2,1)}, bf16[2,8,8,512]{3,1,2,0:T(8,128)(2,1)S(1)}, u32[]{:S(2)}, u32[]{:S(2)}) collective-permute-start(bf16[2,8,8,512]{3,1,2,0:T(8,128)(2,1)} %bitcast.48), channel_id=1, source_target_pairs={{0,1},{1,2},{2,3},{3,0},{4,5},{5,6},{6,7},{7,4},{8,9},{9,10},{10,1... | collective-permute-start | bytes 393224 | tf_op jit(solution)/shard_map/ppermute | solution.py:93
  17.1 8.5 %collective-permute-start = (bf16[256,512]{1,0:T(8,128)(2,1)}, bf16[256,512]{1,0:T(8,128)(2,1)S(1)}, u32[]{:S(2)}, u32[]{:S(2)}) collective-permute-start(bf16[256,512]{1,0:T(8,128)(2,1)} %bitcast.47), channel_id=1, source_target_pairs={{0,4},{4,0},{1,5},{5,1},{2,6},{6,2},{3,7},{7,3},{8,12},{12,8},{9,1... | collective-permute-start | bytes 786440 | tf_op jit(solution)/shard_map/ppermute | solution.py:62
  25.6 1.0 copy-start.1
  27.5 32.3 %all-to-all-start = ((bf16[64,4,512]{2,1,0:T(4,128)(2,1)}), bf16[64,4,512]{2,1,0:T(4,128)(2,1)S(1)}, u32[]{:S(2)}, u32[]{:S(2)}) async-start(bf16[64,4,512]{2,1,0:T(4,128)(2,1)} %reshape.97), calls=%async_computation | async-start | bytes 524288 | tf_op jit(solution)/shard_map/all_to_all | solution.py:64
  99.9 8.0 %collective-permute-start.4 = (bf16[256,4,512]{2,1,0:T(4,128)(2,1)S(1)}, bf16[256,4,512]{2,1,0:T(4,128)(2,1)}, u32[]{:S(2)}, u32[]{:S(2)}) collective-permute-start(bf16[256,4,512]{2,1,0:T(4,128)(2,1)S(1)} %all_to_all.10), channel_id=1, source_target_pairs={{0,4},{4,0},{1,5},{5,1},{2,6},{6,2},{3,7},{7,3},{8,12},{12,8},{9,1... | collective-permute-start | bytes 3145736 | tf_op jit(solution)/shard_map/ppermute | solution.py:71

commit v20 on v19

--- a/solution.py
+++ b/solution.py
@@ -91,10 +91,15 @@
     for shift in range(1, segs):
         pairs = [(i, (i + shift) % segs) for i in range(segs)]
         blocks.append(lax.ppermute(group((me + shift) % segs), seg_axis, pairs))
-    rotated = jnp.concatenate(blocks[::-1], axis=1)
-    doubled = jnp.concatenate([rotated, rotated], axis=1)
-    start = ((segs - (me + 1) % segs) % segs) * local_segs
-    return lax.dynamic_slice_in_dim(doubled, start, segs * local_segs, axis=1)
+    return jnp.concatenate(blocks[::-1], axis=1)
+
+
+def rotate_segments(source_spec, seg_axis):
+    segs = lax.psum(1, seg_axis)
+    me = lax.axis_index(seg_axis)
+    parts, all_segs, sources, freqs = source_spec.shape
+    doubled = jnp.concatenate([source_spec, source_spec], axis=1)
+    return lax.dynamic_slice_in_dim(doubled, ((me + 1) % segs) * (all_segs // segs), all_segs, axis=1)
 
 
 def make_shards(chan_axes):
@@ -115,6 +120,7 @@
         source_spec, (regrouped, lag_table) = gather_sources(
             local_spec, chan_axes, "seg", (regrouped, lag_table)
         )
+        source_spec = rotate_segments(source_spec, "seg")
         swapped = lax.axis_index("c") == 1 if chan_axes == CHAN_AXES else False
         return correlate(source_spec, regrouped, lag_table, swapped)
 

time: 121 us -> 115 us (0.950)
  local copies, waits for them, and re-layouts: 11.8 us -> 3.35 us
  other arithmetic: 15 us -> 19.1 us
  waiting for transfers between devices: 12.6 us -> 10.6 us
    ppermute x3, starting transfers between devices: 12.5 us -> 7.2 us  [regroup_receivers(): blocks.append(lax.ppermute(group((me + shift) % segs), seg_axis, pairs))]
    ppermute x1, starting transfers between devices: 3.98 us -> 8.79 us  [gather_sources(): half = keep + lax.ppermute(send, 'c', [(0, 1), (1, 0)])]
    unnamed x16 -> x8, local copies, waits for them, and re-layouts: 3.85 us -> 0.18 us
    transpose x1, other arithmetic: 0.19 us -> 2.79 us  [gather_sources(): got.reshape(parts, sources, split, segs, rows, freqs)]
    all_to_all x1, waiting for transfers between devices: 12.6 us -> 10.1 us  [gather_sources(): mine = lax.all_to_all(part, rest, 0, 0).sum(axis=0, dtype=value.dtype)]
    another operation x2 -> x0, local copies, waits for them, and re-layouts: 2.38 us -> none  [gather_sources(): got = jnp.stack([half_got, sibling])]
    dynamic_slice x1 -> x0, local copies, waits for them, and re-layouts: 1.88 us -> none  [regroup_receivers(): return lax.dynamic_slice_in_dim(doubled, start, segs * local_segs, axis=1)]
    concatenate x0 -> x2, other arithmetic: none -> 1.65 us  [the longest x1 0.85 us: regroup_receivers(): return jnp.concatenate(blocks[::-1], axis=1)]
  transfers between devices with their start and end apart: 6 -> 6, of which waited for: 1 -> 2; matrix products, arithmetic and copies ran while one was open for 11% -> 7% of each run, Pallas kernels for 0% -> 0%
where the time goes in v20:
time: 115 us; the launch traced here: 114 us
  blocking collectives  40.3 us (35%)
  starting transfers between devices  37.5 us (33%)
  other arithmetic  19.1 us (17%)
  waiting for transfers between devices  10.6 us (9%)
  local copies, waits for them, and re-layouts  3.35 us (3%)
  matrix products  3.14 us (3%)
    all_to_all x1, blocking collectives, gather_sources(): half_got = lax.all_to_all(spread, rest + (seg_axis,), 0, 0)  40.3 us
    all_to_all x1, starting transfers between devices, gather_sources(): mine = lax.all_to_all(part, rest, 0, 0).sum(axis=0, dtype=value.dtype)  15.5 us
    all_to_all x1, waiting for transfers between devices, gather_sources(): mine = lax.all_to_all(part, rest, 0, 0).sum(axis=0, dtype=value.dtype)  10.1 us
    ppermute x1, starting transfers between devices, gather_sources(): half = keep + lax.ppermute(send, 'c', [(0, 1), (1, 0)])  8.79 us
    ppermute x3, starting transfers between devices, regroup_receivers(): blocks.append(lax.ppermute(group((me + shift) % segs), seg_axis, pairs))  7.2 us
    reduce_sum x1, other arithmetic, correlate(): real_part = jnp.sum(a * c + b * d, axis=0)  6.72 us
    ppermute x1, starting transfers between devices, gather_sources(): sibling = lax.ppermute(half_got, 'c', [(0, 1), (1, 0)])  6.03 us
    cos x1, other arithmetic, lag_matrix(): return jnp.concatenate([jnp.cos(angles), -jnp.sin(angles)], axis=0)  4.12 us
  transfers between devices with their start and end apart: 6, of which 2 were waited for; matrix products, arithmetic and copies ran while one was open for 7% of the time, Pallas kernels for 0%

profile of v20, /device:TPU:1, one launch (start us, length us, event | category | flops | bytes accessed | tf_op | source)
XLA Modules:
  0.0 114.3 jit_solution(9121729971072604638)
XLA Ops:
  0.0 1.2 %convert_element_type.58 = f32[2,8,32,512]{3,2,1,0:T(8,128)S(1)} convert(bf16[2,8,32,512]{3,2,1,0:T(8,128)(2,1)} %param.2) | non-fusion elementwise | flops 262144 | bytes 1572864 | tf_op jit(solution)/shard_map/convert_element_type | solution.py:14
  1.6 0.4 fusion.2
  2.2 8.8 %collective-permute-start = (bf16[256,512]{1,0:T(8,128)(2,1)S(1)}, bf16[256,512]{1,0:T(8,128)(2,1)S(1)}, u32[]{:S(2)}, u32[]{:S(2)}) collective-permute-start(bf16[256,512]{1,0:T(8,128)(2,1)S(1)} %bitcast.57), channel_id=1, source_target_pairs={{0,4},{4,0},{1,5},{5,1},{2,6},{6,2},{3,7},{7,3},{8,12},{12,8},{9,1... | collective-permute-start | bytes 786440 | tf_op jit(solution)/shard_map/ppermute | solution.py:62
  11.3 2.2 %collective-permute-start.1 = (bf16[2,8,8,512]{3,1,2,0:T(8,128)(2,1)S(1)}, bf16[2,8,8,512]{3,1,2,0:T(8,128)(2,1)S(1)}, u32[]{:S(2)}, u32[]{:S(2)}) collective-permute-start(bf16[2,8,8,512]{3,1,2,0:T(8,128)(2,1)S(1)} %bitcast.58), channel_id=1, source_target_pairs={{0,3},{1,0},{2,1},{3,2},{4,7},{5,4},{6,5},{7,6},{8,11},{9,8},{10,9... | collective-permute-start | bytes 393224 | tf_op jit(solution)/shard_map/ppermute | solution.py:93
  13.6 1.9 %collective-permute-start.2 = (bf16[2,8,8,512]{3,1,2,0:T(8,128)(2,1)S(1)}, bf16[2,8,8,512]{3,1,2,0:T(8,128)(2,1)S(1)}, u32[]{:S(2)}, u32[]{:S(2)}) collective-permute-start(bf16[2,8,8,512]{3,1,2,0:T(8,128)(2,1)S(1)} %bitcast.59), channel_id=1, source_target_pairs={{0,2},{1,3},{2,0},{3,1},{4,6},{5,7},{6,4},{7,5},{8,10},{9,11},{10,... | collective-permute-start | bytes 393224 | tf_op jit(solution)/shard_map/ppermute | solution.py:93
  15.6 3.0 %collective-permute-start.3 = (bf16[2,8,8,512]{3,1,2,0:T(8,128)(2,1)S(1)}, bf16[2,8,8,512]{3,1,2,0:T(8,128)(2,1)S(1)}, u32[]{:S(2)}, u32[]{:S(2)}) collective-permute-start(bf16[2,8,8,512]{3,1,2,0:T(8,128)(2,1)S(1)} %bitcast.60), channel_id=1, source_target_pairs={{0,1},{1,2},{2,3},{3,0},{4,5},{5,6},{6,7},{7,4},{8,9},{9,10},{10,1... | collective-permute-start | bytes 393224 | tf_op jit(solution)/shard_map/ppermute | solution.py:93
  18.9 0.8 reshape.95
  19.6 15.5 %all-to-all-start = ((bf16[64,4,512]{2,1,0:T(4,128)(2,1)}), bf16[64,4,512]{2,1,0:T(4,128)(2,1)S(1)}, u32[]{:S(2)}, u32[]{:S(2)}) async-start(bf16[64,4,512]{2,1,0:T(4,128)(2,1)} %reshape.95), calls=%async_computation | async-start | bytes 524288 | tf_op jit(solution)/shard_map/all_to_all | solution.py:64
  35.1 4.1 %fusion.16 = (f32[512,512]{1,0:T(8,128)S(1)}, f32[512,512]{1,0:T(8,128)S(1)}) fusion(s32[512]{0:T(512)S(1)} %iota_add_fusion), kind=kLoop, calls=%fused_computation.36 | loop fusion | flops 3932160 | bytes 2099200 | tf_op jit(solution)/shard_map/cos | solution.py:26
  39.4 0.9 pad_maximum_fusion.1
  40.3 10.1 %all-to-all-done = bf16[64,4,512]{2,1,0:T(4,128)(2,1)S(1)} async-done(((bf16[64,4,512]{2,1,0:T(4,128)(2,1)}), bf16[64,4,512]{2,1,0:T(4,128)(2,1)S(1)}, u32[]{:S(2)}, u32[]{:S(2)}) %all-to-all-start) | async-done | bytes 262176 | tf_op jit(solution)/shard_map/all_to_all | solution.py:64
  50.6 0.3 broadcast_in_dim.2
  50.8 40.3 %all_to_all.10 = bf16[256,4,512]{2,1,0:T(4,128)(2,1)S(1)} all-to-all(bf16[256,4,512]{2,1,0:T(4,128)(2,1)S(1)} %broadcast_in_dim.2), channel_id=1, replica_groups=mesh['x'=4,'zh'=2,'y'=8,'c'=2,'seg'=4] {'x','zh','y','seg'}, dimensions={0} | all-to-all | bytes 2097152 | tf_op jit(solution)/shard_map/all_to_all | solution.py:70
  91.2 6.0 %collective-permute-start.4 = (bf16[256,4,512]{2,1,0:T(4,128)(2,1)S(1)}, bf16[256,4,512]{2,1,0:T(4,128)(2,1)}, u32[]{:S(2)}, u32[]{:S(2)}) collective-permute-start(bf16[256,4,512]{2,1,0:T(4,128)(2,1)S(1)} %all_to_all.10), channel_id=1, source_target_pairs={{0,4},{4,0},{1,5},{5,1},{2,6},{6,2},{3,7},{7,3},{8,12},{12,8},{9,1... | collective-permute-start | bytes 3145736 | tf_op jit(solution)/shard_map/ppermute | solution.py:71
  97.2 1.1 bitcast_convert_fusion.1
  98.3 0.3 copy.37
  98.7 0.3 copy.38
  99.0 0.5 collective-permute-done.4
  99.4 2.8 %maximum_bitcast_fusion = bf16[2,4,2,4,32,512]{5,3,1,2,4,0:T(4,128)(2,1)S(1)} fusion(bf16[1,32,2,4,4,512]{5,4,3,2,1,0:T(4,128)(2,1)} %bitcast.11, bf16[1,32,2,4,4,512]{5,4,3,2,1,0:T(4,128)(2,1)S(1)} %bitcast.54), kind=kLoop, calls=%fused_computation.6 | loop fusion | flops 1048576 | bytes 4194304 | tf_op jit(solution)/shard_map/transpose | solution.py:77
  102.2 1.2 %copy.36 = bf16[2,4,2,4,32,512]{5,4,3,2,1,0:T(8,128)(2,1)S(1)} copy(bf16[2,4,2,4,32,512]{5,3,1,2,4,0:T(4,128)(2,1)S(1)} %maximum_bitcast_fusion) | data formatting | bytes 4194304 | tf_op jit(solution)/shard_map/transpose | solution.py:77
  103.4 0.8 fusion
  104.2 0.6 fusion.7
  104.8 6.7 %add_reduce_fusion = (f32[32,8,512]{2,1,0:T(8,128)S(1)}, f32[32,8,512]{2,1,0:T(8,128)S(1)}) fusion(f32[32,8,512]{2,1,0:T(8,128)S(1)} %copy.38, f32[32,32,512]{2,1,0:T(8,128)S(1)} %get-tuple-element.14, f32[32,8,512]{2,1,0:T(8,128)S(1)} %copy.37, f32[32,32,512]{2,1,0:T(8,128)S(1)} %get-tuple-element.13), kind=kLoop, calls=%fused_computation.1 | loop fusion | flops 33292288 | bytes 6291456 | tf_op jit(solution)/shard_map/reduce_sum | solution.py:39
  111.6 2.8 %fusion.1 = f32[32,8,512]{2,1,0:T(8,128)} fusion(f32[1024,512]{1,0:T(8,128)S(1)} %pad_maximum_fusion, f32[256,512]{1,0:T(8,128)S(1)} %multiply_bitcast_fusion, f32[256,512]{1,0:T(8,128)S(1)} %bitcast.55), kind=kOutput, calls=%fused_computation.12 | convolution fusion | flops 1611268096 | bytes 3670016 | tf_op jit(solution)/shard_map/dot_general | solution.py:43
  (26 shorter events, 1.4 us)
Async XLA Ops:
  0.0 1.6 %copy-start = (bf16[2,8,32,512]{3,2,1,0:T(8,128)(2,1)S(1)}, bf16[2,8,32,512]{3,2,1,0:T(8,128)(2,1)}, u32[]{:S(2)}) copy-start(bf16[2,8,32,512]{3,2,1,0:T(8,128)(2,1)} %param.2) | copy-start | bytes 1572868
  0.0 1.4 %copy-start.1 = (s32[8,4]{0,1:T(4,128)S(1)}, s32[8,4]{0,1:T(4,128)}, u32[]{:S(2)}) copy-start(s32[8,4]{0,1:T(4,128)} %param.3) | copy-start | bytes 388
  2.2 16.5 %collective-permute-start = (bf16[256,512]{1,0:T(8,128)(2,1)S(1)}, bf16[256,512]{1,0:T(8,128)(2,1)S(1)}, u32[]{:S(2)}, u32[]{:S(2)}) collective-permute-start(bf16[256,512]{1,0:T(8,128)(2,1)S(1)} %bitcast.57), channel_id=1, source_target_pairs={{0,4},{4,0},{1,5},{5,1},{2,6},{6,2},{3,7},{7,3},{8,12},{12,8},{9,1... | collective-permute-start | bytes 786440 | tf_op jit(solution)/shard_map/ppermute | solution.py:62
  11.3 28.1 %collective-permute-start.1 = (bf16[2,8,8,512]{3,1,2,0:T(8,128)(2,1)S(1)}, bf16[2,8,8,512]{3,1,2,0:T(8,128)(2,1)S(1)}, u32[]{:S(2)}, u32[]{:S(2)}) collective-permute-start(bf16[2,8,8,512]{3,1,2,0:T(8,128)(2,1)S(1)} %bitcast.58), channel_id=1, source_target_pairs={{0,3},{1,0},{2,1},{3,2},{4,7},{5,4},{6,5},{7,6},{8,11},{9,8},{10,9... | collective-permute-start | bytes 393224 | tf_op jit(solution)/shard_map/ppermute | solution.py:93
  13.6 25.8 %collective-permute-start.2 = (bf16[2,8,8,512]{3,1,2,0:T(8,128)(2,1)S(1)}, bf16[2,8,8,512]{3,1,2,0:T(8,128)(2,1)S(1)}, u32[]{:S(2)}, u32[]{:S(2)}) collective-permute-start(bf16[2,8,8,512]{3,1,2,0:T(8,128)(2,1)S(1)} %bitcast.59), channel_id=1, source_target_pairs={{0,2},{1,3},{2,0},{3,1},{4,6},{5,7},{6,4},{7,5},{8,10},{9,11},{10,... | collective-permute-start | bytes 393224 | tf_op jit(solution)/shard_map/ppermute | solution.py:93
  15.6 23.8 %collective-permute-start.3 = (bf16[2,8,8,512]{3,1,2,0:T(8,128)(2,1)S(1)}, bf16[2,8,8,512]{3,1,2,0:T(8,128)(2,1)S(1)}, u32[]{:S(2)}, u32[]{:S(2)}) collective-permute-start(bf16[2,8,8,512]{3,1,2,0:T(8,128)(2,1)S(1)} %bitcast.60), channel_id=1, source_target_pairs={{0,1},{1,2},{2,3},{3,0},{4,5},{5,6},{6,7},{7,4},{8,9},{9,10},{10,1... | collective-permute-start | bytes 393224 | tf_op jit(solution)/shard_map/ppermute | solution.py:93
  19.6 30.8 %all-to-all-start = ((bf16[64,4,512]{2,1,0:T(4,128)(2,1)}), bf16[64,4,512]{2,1,0:T(4,128)(2,1)S(1)}, u32[]{:S(2)}, u32[]{:S(2)}) async-start(bf16[64,4,512]{2,1,0:T(4,128)(2,1)} %reshape.95), calls=%async_computation | async-start | bytes 524288 | tf_op jit(solution)/shard_map/all_to_all | solution.py:64
  91.2 8.2 %collective-permute-start.4 = (bf16[256,4,512]{2,1,0:T(4,128)(2,1)S(1)}, bf16[256,4,512]{2,1,0:T(4,128)(2,1)}, u32[]{:S(2)}, u32[]{:S(2)}) collective-permute-start(bf16[256,4,512]{2,1,0:T(4,128)(2,1)S(1)} %all_to_all.10), channel_id=1, source_target_pairs={{0,4},{4,0},{1,5},{5,1},{2,6},{6,2},{3,7},{7,3},{8,12},{12,8},{9,1... | collective-permute-start | bytes 3145736 | tf_op jit(solution)/shard_map/ppermute | solution.py:71

commit v21 on v20

--- a/solution.py
+++ b/solution.py
@@ -94,12 +94,13 @@
     return jnp.concatenate(blocks[::-1], axis=1)
 
 
-def rotate_segments(source_spec, seg_axis):
+def unrotate_segments(spec, seg_axis):
     segs = lax.psum(1, seg_axis)
     me = lax.axis_index(seg_axis)
-    parts, all_segs, sources, freqs = source_spec.shape
-    doubled = jnp.concatenate([source_spec, source_spec], axis=1)
-    return lax.dynamic_slice_in_dim(doubled, ((me + 1) % segs) * (all_segs // segs), all_segs, axis=1)
+    all_segs = spec.shape[1]
+    doubled = jnp.concatenate([spec, spec], axis=1)
+    start = ((segs - (me + 1) % segs) % segs) * (all_segs // segs)
+    return lax.dynamic_slice_in_dim(doubled, start, all_segs, axis=1)
 
 
 def make_shards(chan_axes):
@@ -120,7 +121,7 @@
         source_spec, (regrouped, lag_table) = gather_sources(
             local_spec, chan_axes, "seg", (regrouped, lag_table)
         )
-        source_spec = rotate_segments(source_spec, "seg")
+        regrouped = unrotate_segments(regrouped, "seg")
         swapped = lax.axis_index("c") == 1 if chan_axes == CHAN_AXES else False
         return correlate(source_spec, regrouped, lag_table, swapped)
 

time: 115 us -> 113 us (0.983)
  other arithmetic: 19.1 us -> 16.1 us
  local copies, waits for them, and re-layouts: 3.35 us -> 4.81 us
    transpose x1, other arithmetic: 2.79 us -> 0.19 us  [gather_sources(): got.reshape(parts, sources, split, segs, rows, freqs)]
    another operation x0 -> x2, local copies, waits for them, and re-layouts: none -> 2.38 us  [gather_sources(): got = jnp.stack([half_got, sibling])]
    transpose x1 -> x0, local copies, waits for them, and re-layouts: 1.16 us -> none  [gather_sources(): got.reshape(parts, sources, split, segs, rows, freqs)]
  transfers between devices with their start and end apart: 6 -> 6, of which waited for: 2 -> 1; matrix products, arithmetic and copies ran while one was open for 7% -> 8% of each run, Pallas kernels for 0% -> 0%
where the time goes in v21:
time: 113 us; the launch traced here: 112 us
  blocking collectives  40.3 us (36%)
  starting transfers between devices  37.5 us (33%)
  other arithmetic  16.1 us (14%)
  waiting for transfers between devices  10.2 us (9%)
  local copies, waits for them, and re-layouts  4.81 us (4%)
  matrix products  3.14 us (3%)
    all_to_all x1, blocking collectives, gather_sources(): half_got = lax.all_to_all(spread, rest + (seg_axis,), 0, 0)  40.3 us
    all_to_all x1, starting transfers between devices, gather_sources(): mine = lax.all_to_all(part, rest, 0, 0).sum(axis=0, dtype=value.dtype)  15.5 us
    all_to_all x1, waiting for transfers between devices, gather_sources(): mine = lax.all_to_all(part, rest, 0, 0).sum(axis=0, dtype=value.dtype)  10.1 us
    ppermute x1, starting transfers between devices, gather_sources(): half = keep + lax.ppermute(send, 'c', [(0, 1), (1, 0)])  8.79 us
    ppermute x3, starting transfers between devices, regroup_receivers(): blocks.append(lax.ppermute(group((me + shift) % segs), seg_axis, pairs))  7.2 us
    reduce_sum x1, other arithmetic, correlate(): real_part = jnp.sum(a * c + b * d, axis=0)  6.72 us
    ppermute x1, starting transfers between devices, gather_sources(): sibling = lax.ppermute(half_got, 'c', [(0, 1), (1, 0)])  6.03 us
    cos x1, other arithmetic, lag_matrix(): return jnp.concatenate([jnp.cos(angles), -jnp.sin(angles)], axis=0)  4.12 us
  transfers between devices with their start and end apart: 6, of which 1 were waited for; matrix products, arithmetic and copies ran while one was open for 8% of the time, Pallas kernels for 0%

profile of v21, /device:TPU:1, one launch (start us, length us, event | category | flops | bytes accessed | tf_op | source)
XLA Modules:
  0.0 112.4 jit_solution(13884164275463806130)
XLA Ops:
  0.0 1.2 %convert_element_type.58 = f32[2,8,32,512]{3,2,1,0:T(8,128)S(1)} convert(bf16[2,8,32,512]{3,2,1,0:T(8,128)(2,1)} %param.2) | non-fusion elementwise | flops 262144 | bytes 1572864 | tf_op jit(solution)/shard_map/convert_element_type | solution.py:14
  1.6 0.4 fusion.1
  2.2 8.8 %collective-permute-start = (bf16[256,512]{1,0:T(8,128)(2,1)S(1)}, bf16[256,512]{1,0:T(8,128)(2,1)S(1)}, u32[]{:S(2)}, u32[]{:S(2)}) collective-permute-start(bf16[256,512]{1,0:T(8,128)(2,1)S(1)} %bitcast.51), channel_id=1, source_target_pairs={{0,4},{4,0},{1,5},{5,1},{2,6},{6,2},{3,7},{7,3},{8,12},{12,8},{9,1... | collective-permute-start | bytes 786440 | tf_op jit(solution)/shard_map/ppermute | solution.py:62
  11.3 2.2 %collective-permute-start.1 = (bf16[2,8,8,512]{3,1,2,0:T(8,128)(2,1)S(1)}, bf16[2,8,8,512]{3,1,2,0:T(8,128)(2,1)S(1)}, u32[]{:S(2)}, u32[]{:S(2)}) collective-permute-start(bf16[2,8,8,512]{3,1,2,0:T(8,128)(2,1)S(1)} %bitcast.52), channel_id=1, source_target_pairs={{0,3},{1,0},{2,1},{3,2},{4,7},{5,4},{6,5},{7,6},{8,11},{9,8},{10,9... | collective-permute-start | bytes 393224 | tf_op jit(solution)/shard_map/ppermute | solution.py:93
  13.6 1.9 %collective-permute-start.2 = (bf16[2,8,8,512]{3,1,2,0:T(8,128)(2,1)S(1)}, bf16[2,8,8,512]{3,1,2,0:T(8,128)(2,1)S(1)}, u32[]{:S(2)}, u32[]{:S(2)}) collective-permute-start(bf16[2,8,8,512]{3,1,2,0:T(8,128)(2,1)S(1)} %bitcast.53), channel_id=1, source_target_pairs={{0,2},{1,3},{2,0},{3,1},{4,6},{5,7},{6,4},{7,5},{8,10},{9,11},{10,... | collective-permute-start | bytes 393224 | tf_op jit(solution)/shard_map/ppermute | solution.py:93
  15.6 3.0 %collective-permute-start.3 = (bf16[2,8,8,512]{3,1,2,0:T(8,128)(2,1)S(1)}, bf16[2,8,8,512]{3,1,2,0:T(8,128)(2,1)S(1)}, u32[]{:S(2)}, u32[]{:S(2)}) collective-permute-start(bf16[2,8,8,512]{3,1,2,0:T(8,128)(2,1)S(1)} %bitcast.54), channel_id=1, source_target_pairs={{0,1},{1,2},{2,3},{3,0},{4,5},{5,6},{6,7},{7,4},{8,9},{9,10},{10,1... | collective-permute-start | bytes 393224 | tf_op jit(solution)/shard_map/ppermute | solution.py:93
  18.9 0.8 reshape.97
  19.6 15.5 %all-to-all-start = ((bf16[64,4,512]{2,1,0:T(4,128)(2,1)}), bf16[64,4,512]{2,1,0:T(4,128)(2,1)S(1)}, u32[]{:S(2)}, u32[]{:S(2)}) async-start(bf16[64,4,512]{2,1,0:T(4,128)(2,1)} %reshape.97), calls=%async_computation | async-start | bytes 524288 | tf_op jit(solution)/shard_map/all_to_all | solution.py:64
  35.1 4.1 %fusion.14 = (f32[512,512]{1,0:T(8,128)S(1)}, f32[512,512]{1,0:T(8,128)S(1)}) fusion(s32[512]{0:T(512)S(1)} %iota_add_fusion), kind=kLoop, calls=%fused_computation.34 | loop fusion | flops 3932160 | bytes 2099200 | tf_op jit(solution)/shard_map/cos | solution.py:26
  39.4 0.9 pad_maximum_fusion.1
  40.3 10.1 %all-to-all-done = bf16[64,4,512]{2,1,0:T(4,128)(2,1)S(1)} async-done(((bf16[64,4,512]{2,1,0:T(4,128)(2,1)}), bf16[64,4,512]{2,1,0:T(4,128)(2,1)S(1)}, u32[]{:S(2)}, u32[]{:S(2)}) %all-to-all-start) | async-done | bytes 262176 | tf_op jit(solution)/shard_map/all_to_all | solution.py:64
  50.6 0.3 broadcast_in_dim.2
  50.8 40.3 %all_to_all.10 = bf16[256,4,512]{2,1,0:T(4,128)(2,1)S(1)} all-to-all(bf16[256,4,512]{2,1,0:T(4,128)(2,1)S(1)} %broadcast_in_dim.2), channel_id=1, replica_groups=mesh['x'=4,'zh'=2,'y'=8,'c'=2,'seg'=4] {'x','zh','y','seg'}, dimensions={0} | all-to-all | bytes 2097152 | tf_op jit(solution)/shard_map/all_to_all | solution.py:70
  91.2 6.0 %collective-permute-start.4 = (bf16[256,4,512]{2,1,0:T(4,128)(2,1)S(1)}, bf16[256,4,512]{2,1,0:T(4,128)(2,1)}, u32[]{:S(2)}, u32[]{:S(2)}) collective-permute-start(bf16[256,4,512]{2,1,0:T(4,128)(2,1)S(1)} %all_to_all.10), channel_id=1, source_target_pairs={{0,4},{4,0},{1,5},{5,1},{2,6},{6,2},{3,7},{7,3},{8,12},{12,8},{9,1... | collective-permute-start | bytes 3145736 | tf_op jit(solution)/shard_map/ppermute | solution.py:71
  97.2 1.3 %fusion.10 = bf16[2,32,8,512]{3,1,2,0:T(8,128)(2,1)S(1)} fusion(s32[]{:T(128)S(6)} %select_n.101, bf16[2,32,8,512]{3,1,2,0:T(8,128)(2,1)} %pad_maximum_fusion.1), kind=kLoop, calls=%fused_computation.26 | loop fusion | flops 1048576 | bytes 1048580 | tf_op jit(solution)/shard_map/concatenate | solution.py:101
  98.6 0.3 copy.50
  99.0 0.3 copy.51
  99.3 0.6 copy.48
  99.9 1.8 %copy.49 = bf16[1,32,2,4,4,512]{5,1,4,2,3,0:T(8,128)(2,1)S(1)} copy(bf16[1,32,2,4,4,512]{5,4,3,2,1,0:T(4,128)(2,1)} %bitcast.11) | data formatting | bytes 2097152 | tf_op jit(solution)/shard_map/stack | solution.py:72
  101.7 0.2 maximum_bitcast_fusion
  101.9 0.2 fusion.21
  102.1 0.7 bitcast_convert_fusion
  102.8 6.7 %add_reduce_fusion = (f32[32,8,512]{2,1,0:T(8,128)S(1)}, f32[32,8,512]{2,1,0:T(8,128)S(1)}) fusion(f32[32,8,512]{2,1,0:T(8,128)S(1)} %copy.51, f32[32,32,512]{2,1,0:T(8,128)S(1)} %get-tuple-element.25, f32[32,8,512]{2,1,0:T(8,128)S(1)} %copy.50, f32[32,32,512]{2,1,0:T(8,128)S(1)} %get-tuple-element.26), kind=kLoop, calls=%fused_computation.1 | loop fusion | flops 33292288 | bytes 6291456 | tf_op jit(solution)/shard_map/reduce_sum | solution.py:39
  109.6 2.8 %fusion = f32[32,8,512]{2,1,0:T(8,128)} fusion(f32[1024,512]{1,0:T(8,128)S(1)} %pad_maximum_fusion, f32[256,512]{1,0:T(8,128)S(1)} %multiply_bitcast_fusion, f32[256,512]{1,0:T(8,128)S(1)} %bitcast.49), kind=kOutput, calls=%fused_computation.9 | convolution fusion | flops 1611268096 | bytes 3670016 | tf_op jit(solution)/shard_map/dot_general | solution.py:43
  (28 shorter events, 1.5 us)
Async XLA Ops:
  0.0 1.6 %copy-start = (bf16[2,8,32,512]{3,2,1,0:T(8,128)(2,1)S(1)}, bf16[2,8,32,512]{3,2,1,0:T(8,128)(2,1)}, u32[]{:S(2)}) copy-start(bf16[2,8,32,512]{3,2,1,0:T(8,128)(2,1)} %param.2) | copy-start | bytes 1572868
  0.0 1.4 %copy-start.1 = (s32[8,4]{0,1:T(4,128)S(1)}, s32[8,4]{0,1:T(4,128)}, u32[]{:S(2)}) copy-start(s32[8,4]{0,1:T(4,128)} %param.3) | copy-start | bytes 388
  2.2 16.5 %collective-permute-start = (bf16[256,512]{1,0:T(8,128)(2,1)S(1)}, bf16[256,512]{1,0:T(8,128)(2,1)S(1)}, u32[]{:S(2)}, u32[]{:S(2)}) collective-permute-start(bf16[256,512]{1,0:T(8,128)(2,1)S(1)} %bitcast.51), channel_id=1, source_target_pairs={{0,4},{4,0},{1,5},{5,1},{2,6},{6,2},{3,7},{7,3},{8,12},{12,8},{9,1... | collective-permute-start | bytes 786440 | tf_op jit(solution)/shard_map/ppermute | solution.py:62
  11.3 28.1 %collective-permute-start.1 = (bf16[2,8,8,512]{3,1,2,0:T(8,128)(2,1)S(1)}, bf16[2,8,8,512]{3,1,2,0:T(8,128)(2,1)S(1)}, u32[]{:S(2)}, u32[]{:S(2)}) collective-permute-start(bf16[2,8,8,512]{3,1,2,0:T(8,128)(2,1)S(1)} %bitcast.52), channel_id=1, source_target_pairs={{0,3},{1,0},{2,1},{3,2},{4,7},{5,4},{6,5},{7,6},{8,11},{9,8},{10,9... | collective-permute-start | bytes 393224 | tf_op jit(solution)/shard_map/ppermute | solution.py:93
  13.6 25.8 %collective-permute-start.2 = (bf16[2,8,8,512]{3,1,2,0:T(8,128)(2,1)S(1)}, bf16[2,8,8,512]{3,1,2,0:T(8,128)(2,1)S(1)}, u32[]{:S(2)}, u32[]{:S(2)}) collective-permute-start(bf16[2,8,8,512]{3,1,2,0:T(8,128)(2,1)S(1)} %bitcast.53), channel_id=1, source_target_pairs={{0,2},{1,3},{2,0},{3,1},{4,6},{5,7},{6,4},{7,5},{8,10},{9,11},{10,... | collective-permute-start | bytes 393224 | tf_op jit(solution)/shard_map/ppermute | solution.py:93
  15.6 23.8 %collective-permute-start.3 = (bf16[2,8,8,512]{3,1,2,0:T(8,128)(2,1)S(1)}, bf16[2,8,8,512]{3,1,2,0:T(8,128)(2,1)S(1)}, u32[]{:S(2)}, u32[]{:S(2)}) collective-permute-start(bf16[2,8,8,512]{3,1,2,0:T(8,128)(2,1)S(1)} %bitcast.54), channel_id=1, source_target_pairs={{0,1},{1,2},{2,3},{3,0},{4,5},{5,6},{6,7},{7,4},{8,9},{9,10},{10,1... | collective-permute-start | bytes 393224 | tf_op jit(solution)/shard_map/ppermute | solution.py:93
  19.6 30.8 %all-to-all-start = ((bf16[64,4,512]{2,1,0:T(4,128)(2,1)}), bf16[64,4,512]{2,1,0:T(4,128)(2,1)S(1)}, u32[]{:S(2)}, u32[]{:S(2)}) async-start(bf16[64,4,512]{2,1,0:T(4,128)(2,1)} %reshape.97), calls=%async_computation | async-start | bytes 524288 | tf_op jit(solution)/shard_map/all_to_all | solution.py:64
  91.2 8.7 %collective-permute-start.4 = (bf16[256,4,512]{2,1,0:T(4,128)(2,1)S(1)}, bf16[256,4,512]{2,1,0:T(4,128)(2,1)}, u32[]{:S(2)}, u32[]{:S(2)}) collective-permute-start(bf16[256,4,512]{2,1,0:T(4,128)(2,1)S(1)} %all_to_all.10), channel_id=1, source_target_pairs={{0,4},{4,0},{1,5},{5,1},{2,6},{6,2},{3,7},{7,3},{8,12},{12,8},{9,1... | collective-permute-start | bytes 3145736 | tf_op jit(solution)/shard_map/ppermute | solution.py:71

commit v22 on v21

--- a/solution.py
+++ b/solution.py
@@ -33,11 +33,11 @@
     b = source_spec[1].astype(jnp.float32)[:, :, None, :]
     first = jnp.where(swapped, receiver_spec[1], receiver_spec[0])
     second = jnp.where(swapped, receiver_spec[0], receiver_spec[1])
-    c = first.astype(jnp.float32)[:, None, :, :]
-    d = second.astype(jnp.float32)[:, None, :, :]
+    c = first.astype(jnp.float32)[None]
+    d = second.astype(jnp.float32)[None]
     sign = jnp.where(swapped, -1.0, 1.0).astype(jnp.float32)
-    real_part = jnp.sum(a * c + b * d, axis=0)
-    imag_part = jnp.sum(a * d - b * c, axis=0) * sign
+    real_part = jnp.sum(a * c + b * d, axis=1)
+    imag_part = jnp.sum(a * d - b * c, axis=1) * sign
     stacked = jnp.concatenate([real_part, imag_part], axis=-1) * (1.0 / math.sqrt(segs))
     flat = stacked.reshape(-1, 2 * freqs)
     result = jnp.dot(
@@ -74,8 +74,14 @@
         spread = jnp.broadcast_to(mine[None], (count * segs, rows, freqs))
         got = lax.all_to_all(spread, chan_axes + (seg_axis,), 0, 0)
     split = local_segs // rows
-    got = got.reshape(parts, sources, split, segs, rows, freqs).transpose(0, 3, 2, 4, 1, 5)
-    return got.reshape(parts, segs * local_segs, sources, freqs), companion
+    return got.reshape(parts, sources, segs * local_segs, freqs), companion
+
+
+def slot_order(spec, segs, rows):
+    parts, all_segs, receivers, freqs = spec.shape
+    split = all_segs // (segs * rows)
+    spec = spec.reshape(parts, segs, split, rows, receivers, freqs).transpose(0, 2, 1, 3, 4, 5)
+    return spec.reshape(parts, all_segs, receivers, freqs)
 
 
 def regroup_receivers(whitened, seg_axis):
@@ -122,6 +128,8 @@
             local_spec, chan_axes, "seg", (regrouped, lag_table)
         )
         regrouped = unrotate_segments(regrouped, "seg")
+        rows = local_spec.size // (lax.psum(1, chan_axes) * freqs)
+        regrouped = slot_order(regrouped, lax.psum(1, "seg"), rows)
         swapped = lax.axis_index("c") == 1 if chan_axes == CHAN_AXES else False
         return correlate(source_spec, regrouped, lag_table, swapped)
 

time: 113 us -> 113 us (level)
    convert_element_type x2 -> x4, local copies, waits for them, and re-layouts: 0.62 us -> 4.39 us  [the longest x1 2.51 us: correlate(): b = source_spec[1].astype(jnp.float32)[:, :, None, :]]
    another operation x2 -> x0, local copies, waits for them, and re-layouts: 2.38 us -> none  [gather_sources(): got = jnp.stack([half_got, sibling])]
    concatenate x1, other arithmetic: 0.17 us -> 1.5 us  [lag_matrix(): return jnp.concatenate([jnp.cos(angles), -jnp.sin(angles)], axis=0)]
where the time goes in v22:
time: 113 us
  blocking collectives  40.3 us (36%)
  starting transfers between devices  37.6 us (33%)
  other arithmetic  16.1 us (14%)
  waiting for transfers between devices  9.63 us (9%)
  local copies, waits for them, and re-layouts  5.81 us (5%)
  matrix products  3.14 us (3%)
    all_to_all x1, blocking collectives, gather_sources(): half_got = lax.all_to_all(spread, rest + (seg_axis,), 0, 0)  40.3 us
    all_to_all x1, starting transfers between devices, gather_sources(): mine = lax.all_to_all(part, rest, 0, 0).sum(axis=0, dtype=value.dtype)  15.5 us
    all_to_all x1, waiting for transfers between devices, gather_sources(): mine = lax.all_to_all(part, rest, 0, 0).sum(axis=0, dtype=value.dtype)  9.62 us
    ppermute x1, starting transfers between devices, gather_sources(): half = keep + lax.ppermute(send, 'c', [(0, 1), (1, 0)])  8.79 us
    reduce_sum x1, other arithmetic, correlate(): real_part = jnp.sum(a * c + b * d, axis=1)  7.41 us
    ppermute x3, starting transfers between devices, regroup_receivers(): blocks.append(lax.ppermute(group((me + shift) % segs), seg_axis, pairs))  7.2 us
    ppermute x1, starting transfers between devices, gather_sources(): sibling = lax.ppermute(half_got, 'c', [(0, 1), (1, 0)])  6.13 us
    cos x1, other arithmetic, lag_matrix(): return jnp.concatenate([jnp.cos(angles), -jnp.sin(angles)], axis=0)  4.12 us
  transfers between devices with their start and end apart: 6, of which 1 were waited for; matrix products, arithmetic and copies ran while one was open for 8% of the time, Pallas kernels for 0%

profile of v22, /device:TPU:1, one launch (start us, length us, event | category | flops | bytes accessed | tf_op | source)
XLA Modules:
  0.0 112.9 jit_solution(15660209583373514004)
XLA Ops:
  0.0 0.7 broadcast_subtract_fusion
  0.9 1.2 %convert_element_type.58 = f32[2,8,32,512]{3,2,1,0:T(8,128)S(1)} convert(bf16[2,8,32,512]{3,2,1,0:T(8,128)(2,1)} %param.2) | non-fusion elementwise | flops 262144 | bytes 1572864 | tf_op jit(solution)/shard_map/convert_element_type | solution.py:14
  2.3 0.4 fusion.1
  2.8 8.8 %collective-permute-start = (bf16[256,512]{1,0:T(8,128)(2,1)S(1)}, bf16[256,512]{1,0:T(8,128)(2,1)S(1)}, u32[]{:S(2)}, u32[]{:S(2)}) collective-permute-start(bf16[256,512]{1,0:T(8,128)(2,1)S(1)} %bitcast.45), channel_id=1, source_target_pairs={{0,4},{4,0},{1,5},{5,1},{2,6},{6,2},{3,7},{7,3},{8,12},{12,8},{9,1... | collective-permute-start | bytes 786440 | tf_op jit(solution)/shard_map/ppermute | solution.py:62
  11.6 0.2 fusion.15
  11.9 2.2 %collective-permute-start.1 = (bf16[2,8,8,512]{3,2,1,0:T(8,128)(2,1)S(1)}, bf16[2,8,8,512]{3,2,1,0:T(8,128)(2,1)S(1)}, u32[]{:S(2)}, u32[]{:S(2)}) collective-permute-start(bf16[2,8,8,512]{3,2,1,0:T(8,128)(2,1)S(1)} %get-tuple-element.15), channel_id=1, source_target_pairs={{0,3},{1,0},{2,1},{3,2},{4,7},{5,4},{6,5},{7,6},{8,11},{9,8},{10,9... | collective-permute-start | bytes 393224 | tf_op jit(solution)/shard_map/ppermute | solution.py:99
  14.2 3.0 %collective-permute-start.3 = (bf16[2,8,8,512]{3,2,1,0:T(8,128)(2,1)S(1)}, bf16[2,8,8,512]{3,2,1,0:T(8,128)(2,1)S(1)}, u32[]{:S(2)}, u32[]{:S(2)}) collective-permute-start(bf16[2,8,8,512]{3,2,1,0:T(8,128)(2,1)S(1)} %get-tuple-element.16), channel_id=1, source_target_pairs={{0,1},{1,2},{2,3},{3,0},{4,5},{5,6},{6,7},{7,4},{8,9},{9,10},{10,1... | collective-permute-start | bytes 393224 | tf_op jit(solution)/shard_map/ppermute | solution.py:99
  17.2 1.9 %collective-permute-start.2 = (bf16[2,8,8,512]{3,2,1,0:T(8,128)(2,1)S(1)}, bf16[2,8,8,512]{3,2,1,0:T(8,128)(2,1)S(1)}, u32[]{:S(2)}, u32[]{:S(2)}) collective-permute-start(bf16[2,8,8,512]{3,2,1,0:T(8,128)(2,1)S(1)} %get-tuple-element.17), channel_id=1, source_target_pairs={{0,2},{1,3},{2,0},{3,1},{4,6},{5,7},{6,4},{7,5},{8,10},{9,11},{10,... | collective-permute-start | bytes 393224 | tf_op jit(solution)/shard_map/ppermute | solution.py:99
  19.1 0.2 bitcast_add_fusion
  19.3 0.8 reshape.102
  20.1 15.5 %all-to-all-start = ((bf16[64,4,512]{2,1,0:T(4,128)(2,1)}), bf16[64,4,512]{2,1,0:T(4,128)(2,1)S(1)}, u32[]{:S(2)}, u32[]{:S(2)}) async-start(bf16[64,4,512]{2,1,0:T(4,128)(2,1)} %reshape.102), calls=%async_computation | async-start | bytes 524288 | tf_op jit(solution)/shard_map/all_to_all | solution.py:64
  35.5 4.1 %fusion.14 = (f32[512,512]{1,0:T(8,128)S(1)}, f32[512,512]{1,0:T(8,128)S(1)}) fusion(s32[512]{0:T(512)S(1)} %iota_add_fusion), kind=kLoop, calls=%fused_computation.31 | loop fusion | flops 3932160 | bytes 2099200 | tf_op jit(solution)/shard_map/cos | solution.py:26
  39.7 1.5 %pad_maximum_fusion = f32[1024,512]{1,0:T(8,128)} fusion(f32[512,512]{1,0:T(8,128)S(1)} %get-tuple-element.22, f32[512,512]{1,0:T(8,128)S(1)} %get-tuple-element.21), kind=kLoop, calls=%fused_computation.2 | loop fusion | flops 524288 | bytes 4194304 | tf_op jit(solution)/shard_map/concatenate | solution.py:26
  41.3 9.6 %all-to-all-done = bf16[64,4,512]{2,1,0:T(4,128)(2,1)S(1)} async-done(((bf16[64,4,512]{2,1,0:T(4,128)(2,1)}), bf16[64,4,512]{2,1,0:T(4,128)(2,1)S(1)}, u32[]{:S(2)}, u32[]{:S(2)}) %all-to-all-start) | async-done | bytes 262176 | tf_op jit(solution)/shard_map/all_to_all | solution.py:64
  51.0 0.3 broadcast_in_dim.2
  51.3 40.3 %all_to_all.10 = bf16[256,4,512]{2,1,0:T(4,128)(2,1)S(1)} all-to-all(bf16[256,4,512]{2,1,0:T(4,128)(2,1)S(1)} %broadcast_in_dim.2), channel_id=1, replica_groups=mesh['x'=4,'zh'=2,'y'=8,'c'=2,'seg'=4] {'x','zh','y','seg'}, dimensions={0} | all-to-all | bytes 2097152 | tf_op jit(solution)/shard_map/all_to_all | solution.py:70
  91.7 6.1 %collective-permute-start.4 = (bf16[256,4,512]{2,1,0:T(4,128)(2,1)S(1)}, bf16[256,4,512]{2,1,0:T(4,128)(2,1)}, u32[]{:S(2)}, u32[]{:S(2)}) collective-permute-start(bf16[256,4,512]{2,1,0:T(4,128)(2,1)S(1)} %all_to_all.10), channel_id=1, source_target_pairs={{0,4},{4,0},{1,5},{5,1},{2,6},{6,2},{3,7},{7,3},{8,12},{12,8},{9,1... | collective-permute-start | bytes 3145736 | tf_op jit(solution)/shard_map/ppermute | solution.py:71
  97.8 0.3 fusion.10
  98.2 0.9 copy.23
  99.1 0.8 copy.24
  99.9 0.2 reshape.106
  100.1 2.5 %reshape.108 = f32[32,32,512]{2,1,0:T(8,128)} reshape(bf16[256,4,512]{2,1,0:T(4,128)(2,1)} %collective-permute-done.4) | data formatting | bytes 3145728 | tf_op jit(solution)/shard_map/convert_element_type | solution.py:33
  102.7 7.4 %add_reduce_fusion = (f32[32,8,512]{2,1,0:T(8,128)S(1)}, f32[32,8,512]{2,1,0:T(8,128)S(1)}) fusion(f32[32,8,512]{2,1,0:T(8,128)S(1)} %bitcast.43, f32[32,32,512]{2,1,0:T(8,128)} %reshape.108, f32[32,8,512]{2,1,0:T(8,128)S(1)} %bitcast.42, f32[32,32,512]{2,1,0:T(8,128)S(1)} %reshape.106), kind=kLoop, calls=%fused_computation.1 | loop fusion | flops 33292288 | bytes 6291456 | tf_op jit(solution)/shard_map/reduce_sum | solution.py:39
  110.1 2.8 %fusion = f32[32,8,512]{2,1,0:T(8,128)} fusion(f32[1024,512]{1,0:T(8,128)S(1)} %copy-done, f32[256,512]{1,0:T(8,128)S(1)} %multiply_bitcast_fusion, f32[256,512]{1,0:T(8,128)S(1)} %bitcast.41), kind=kOutput, calls=%fused_computation.8 | convolution fusion | flops 1611268096 | bytes 3670016 | tf_op jit(solution)/shard_map/dot_general | solution.py:43
  (25 shorter events, 0.9 us)
Async XLA Ops:
  0.0 2.2 %copy-start.1 = (bf16[2,8,32,512]{3,2,1,0:T(8,128)(2,1)S(1)}, bf16[2,8,32,512]{3,2,1,0:T(8,128)(2,1)}, u32[]{:S(2)}) copy-start(bf16[2,8,32,512]{3,2,1,0:T(8,128)(2,1)} %param.2) | copy-start | bytes 1572868
  2.8 16.3 %collective-permute-start = (bf16[256,512]{1,0:T(8,128)(2,1)S(1)}, bf16[256,512]{1,0:T(8,128)(2,1)S(1)}, u32[]{:S(2)}, u32[]{:S(2)}) collective-permute-start(bf16[256,512]{1,0:T(8,128)(2,1)S(1)} %bitcast.45), channel_id=1, source_target_pairs={{0,4},{4,0},{1,5},{5,1},{2,6},{6,2},{3,7},{7,3},{8,12},{12,8},{9,1... | collective-permute-start | bytes 786440 | tf_op jit(solution)/shard_map/ppermute | solution.py:62
  11.9 29.3 %collective-permute-start.1 = (bf16[2,8,8,512]{3,2,1,0:T(8,128)(2,1)S(1)}, bf16[2,8,8,512]{3,2,1,0:T(8,128)(2,1)S(1)}, u32[]{:S(2)}, u32[]{:S(2)}) collective-permute-start(bf16[2,8,8,512]{3,2,1,0:T(8,128)(2,1)S(1)} %get-tuple-element.15), channel_id=1, source_target_pairs={{0,3},{1,0},{2,1},{3,2},{4,7},{5,4},{6,5},{7,6},{8,11},{9,8},{10,9... | collective-permute-start | bytes 393224 | tf_op jit(solution)/shard_map/ppermute | solution.py:99
  14.2 27.0 %collective-permute-start.3 = (bf16[2,8,8,512]{3,2,1,0:T(8,128)(2,1)S(1)}, bf16[2,8,8,512]{3,2,1,0:T(8,128)(2,1)S(1)}, u32[]{:S(2)}, u32[]{:S(2)}) collective-permute-start(bf16[2,8,8,512]{3,2,1,0:T(8,128)(2,1)S(1)} %get-tuple-element.16), channel_id=1, source_target_pairs={{0,1},{1,2},{2,3},{3,0},{4,5},{5,6},{6,7},{7,4},{8,9},{9,10},{10,1... | collective-permute-start | bytes 393224 | tf_op jit(solution)/shard_map/ppermute | solution.py:99
  17.2 24.0 %collective-permute-start.2 = (bf16[2,8,8,512]{3,2,1,0:T(8,128)(2,1)S(1)}, bf16[2,8,8,512]{3,2,1,0:T(8,128)(2,1)S(1)}, u32[]{:S(2)}, u32[]{:S(2)}) collective-permute-start(bf16[2,8,8,512]{3,2,1,0:T(8,128)(2,1)S(1)} %get-tuple-element.17), channel_id=1, source_target_pairs={{0,2},{1,3},{2,0},{3,1},{4,6},{5,7},{6,4},{7,5},{8,10},{9,11},{10,... | collective-permute-start | bytes 393224 | tf_op jit(solution)/shard_map/ppermute | solution.py:99
  20.1 30.8 %all-to-all-start = ((bf16[64,4,512]{2,1,0:T(4,128)(2,1)}), bf16[64,4,512]{2,1,0:T(4,128)(2,1)S(1)}, u32[]{:S(2)}, u32[]{:S(2)}) async-start(bf16[64,4,512]{2,1,0:T(4,128)(2,1)} %reshape.102), calls=%async_computation | async-start | bytes 524288 | tf_op jit(solution)/shard_map/all_to_all | solution.py:64
  91.7 8.5 %collective-permute-start.4 = (bf16[256,4,512]{2,1,0:T(4,128)(2,1)S(1)}, bf16[256,4,512]{2,1,0:T(4,128)(2,1)}, u32[]{:S(2)}, u32[]{:S(2)}) collective-permute-start(bf16[256,4,512]{2,1,0:T(4,128)(2,1)S(1)} %all_to_all.10), channel_id=1, source_target_pairs={{0,4},{4,0},{1,5},{5,1},{2,6},{6,2},{3,7},{7,3},{8,12},{12,8},{9,1... | collective-permute-start | bytes 3145736 | tf_op jit(solution)/shard_map/ppermute | solution.py:71
  100.1 2.5 %copy-start.2 = (f32[1,2,4,4,8,512]{5,4,3,2,1,0:T(8,128)S(1)}, f32[1,2,4,4,8,512]{5,4,3,2,1,0:T(8,128)}, u32[]{:S(2)}) copy-start(f32[1,2,4,4,8,512]{5,4,3,2,1,0:T(8,128)} %copy.23) | copy-start | bytes 1572868
  100.1 2.5 %copy-start.3 = (f32[1,2,4,4,8,512]{5,4,3,2,1,0:T(8,128)S(1)}, f32[1,2,4,4,8,512]{5,4,3,2,1,0:T(8,128)}, u32[]{:S(2)}) copy-start(f32[1,2,4,4,8,512]{5,4,3,2,1,0:T(8,128)} %copy.24) | copy-start | bytes 1572868
  102.7 7.5 %copy-start = (f32[1024,512]{1,0:T(8,128)S(1)}, f32[1024,512]{1,0:T(8,128)}, u32[]{:S(2)}) copy-start(f32[1024,512]{1,0:T(8,128)} %pad_maximum_fusion) | copy-start | bytes 6291460

commit v23 on v21

--- a/solution.py
+++ b/solution.py
@@ -36,8 +36,8 @@
     c = first.astype(jnp.float32)[:, None, :, :]
     d = second.astype(jnp.float32)[:, None, :, :]
     sign = jnp.where(swapped, -1.0, 1.0).astype(jnp.float32)
-    real_part = jnp.sum(a * c + b * d, axis=0)
-    imag_part = jnp.sum(a * d - b * c, axis=0) * sign
+    real_part = jnp.sum(a * c, axis=0) + jnp.sum(b * d, axis=0)
+    imag_part = (jnp.sum(a * d, axis=0) - jnp.sum(b * c, axis=0)) * sign
     stacked = jnp.concatenate([real_part, imag_part], axis=-1) * (1.0 / math.sqrt(segs))
     flat = stacked.reshape(-1, 2 * freqs)
     result = jnp.dot(
@@ -69,13 +69,19 @@
         spread = jnp.broadcast_to(mine[None], (count * segs // pair, rows, freqs))
         half_got = lax.all_to_all(spread, rest + (seg_axis,), 0, 0)
         sibling = lax.ppermute(half_got, "c", [(0, 1), (1, 0)])
-        got = jnp.stack([half_got, sibling])
+        halves = [half_got, sibling]
     else:
         spread = jnp.broadcast_to(mine[None], (count * segs, rows, freqs))
         got = lax.all_to_all(spread, chan_axes + (seg_axis,), 0, 0)
+        halves = list(got.reshape(parts, -1, rows, freqs))
     split = local_segs // rows
-    got = got.reshape(parts, sources, split, segs, rows, freqs).transpose(0, 3, 2, 4, 1, 5)
-    return got.reshape(parts, segs * local_segs, sources, freqs), companion
+    halves = [
+        half.reshape(sources, split, segs, rows, freqs)
+        .transpose(2, 1, 3, 0, 4)
+        .reshape(segs * local_segs, sources, freqs)
+        for half in halves
+    ]
+    return halves, companion
 
 
 def regroup_receivers(whitened, seg_axis):

time: 113 us -> 114 us (level)
  blocking collectives: 40.3 us -> 37.1 us
  starting transfers between devices: 37.5 us -> 40.2 us
  other arithmetic: 16.1 us -> 18.1 us
    all_to_all x1, blocking collectives: 40.3 us -> 37.1 us  [gather_sources(): half_got = lax.all_to_all(spread, rest + (seg_axis,), 0, 0)]
    convert_element_type x0 -> x2, local copies, waits for them, and re-layouts: none -> 2.44 us  [the longest x1 1.22 us: correlate(): a = source_spec[0].astype(jnp.float32)[:, :, None, :]]
    another operation x2 -> x0, local copies, waits for them, and re-layouts: 2.38 us -> none  [gather_sources(): got = jnp.stack([half_got, sibling])]
    ppermute x3, starting transfers between devices: 7.2 us -> 9 us  [regroup_receivers(): blocks.append(lax.ppermute(group((me + shift) % segs), seg_axis, pairs))]
  transfers between devices with their start and end apart: 6 -> 6, of which waited for: 1 -> 1; matrix products, arithmetic and copies ran while one was open for 8% -> 9% of each run, Pallas kernels for 0% -> 0%
where the time goes in v23:
time: 114 us
  starting transfers between devices  40.2 us (35%)
  blocking collectives  37.1 us (33%)
  other arithmetic  18.1 us (16%)
  waiting for transfers between devices  10.2 us (9%)
  local copies, waits for them, and re-layouts  4.62 us (4%)
  matrix products  3.15 us (3%)
    all_to_all x1, blocking collectives, gather_sources(): half_got = lax.all_to_all(spread, rest + (seg_axis,), 0, 0)  37.1 us
    all_to_all x1, starting transfers between devices, gather_sources(): mine = lax.all_to_all(part, rest, 0, 0).sum(axis=0, dtype=value.dtype)  15.5 us
    all_to_all x1, waiting for transfers between devices, gather_sources(): mine = lax.all_to_all(part, rest, 0, 0).sum(axis=0, dtype=value.dtype)  10.1 us
    ppermute x3, starting transfers between devices, regroup_receivers(): blocks.append(lax.ppermute(group((me + shift) % segs), seg_axis, pairs))  9 us
    ppermute x1, starting transfers between devices, gather_sources(): half = keep + lax.ppermute(send, 'c', [(0, 1), (1, 0)])  8.79 us
    reduce_sum x1, other arithmetic, correlate(): real_part = jnp.sum(a * c, axis=0) + jnp.sum(b * d, axis=0)  6.94 us
    ppermute x1, starting transfers between devices, gather_sources(): sibling = lax.ppermute(half_got, 'c', [(0, 1), (1, 0)])  6.91 us
    cos x1, other arithmetic, lag_matrix(): return jnp.concatenate([jnp.cos(angles), -jnp.sin(angles)], axis=0)  4.12 us
  transfers between devices with their start and end apart: 6, of which 1 were waited for; matrix products, arithmetic and copies ran while one was open for 9% of the time, Pallas kernels for 0%

profile of v23, /device:TPU:1, one launch (start us, length us, event | category | flops | bytes accessed | tf_op | source)
XLA Modules:
  0.0 113.7 jit_solution(9406653264999158904)
XLA Ops:
  0.0 0.7 broadcast_subtract_fusion
  0.9 1.2 %convert_element_type.70 = f32[2,8,32,512]{3,2,1,0:T(8,128)S(1)} convert(bf16[2,8,32,512]{3,2,1,0:T(8,128)(2,1)} %param.2) | non-fusion elementwise | flops 262144 | bytes 1572864 | tf_op jit(solution)/shard_map/convert_element_type | solution.py:14
  2.3 0.4 fusion.1
  2.8 8.8 %collective-permute-start = (bf16[256,512]{1,0:T(8,128)(2,1)S(1)}, bf16[256,512]{1,0:T(8,128)(2,1)S(1)}, u32[]{:S(2)}, u32[]{:S(2)}) collective-permute-start(bf16[256,512]{1,0:T(8,128)(2,1)S(1)} %bitcast.53), channel_id=1, source_target_pairs={{0,4},{4,0},{1,5},{5,1},{2,6},{6,2},{3,7},{7,3},{8,12},{12,8},{9,1... | collective-permute-start | bytes 786440 | tf_op jit(solution)/shard_map/ppermute | solution.py:62
  12.0 1.9 %collective-permute-start.2 = (bf16[2,8,8,512]{3,1,2,0:T(8,128)(2,1)S(1)}, bf16[2,8,8,512]{3,1,2,0:T(8,128)(2,1)S(1)}, u32[]{:S(2)}, u32[]{:S(2)}) collective-permute-start(bf16[2,8,8,512]{3,1,2,0:T(8,128)(2,1)S(1)} %bitcast.54), channel_id=1, source_target_pairs={{0,2},{1,3},{2,0},{3,1},{4,6},{5,7},{6,4},{7,5},{8,10},{9,11},{10,... | collective-permute-start | bytes 393224 | tf_op jit(solution)/shard_map/ppermute | solution.py:99
  13.9 2.5 %collective-permute-start.3 = (bf16[2,8,8,512]{3,1,2,0:T(8,128)(2,1)S(1)}, bf16[2,8,8,512]{3,1,2,0:T(8,128)(2,1)S(1)}, u32[]{:S(2)}, u32[]{:S(2)}) collective-permute-start(bf16[2,8,8,512]{3,1,2,0:T(8,128)(2,1)S(1)} %bitcast.55), channel_id=1, source_target_pairs={{0,1},{1,2},{2,3},{3,0},{4,5},{5,6},{6,7},{7,4},{8,9},{9,10},{10,1... | collective-permute-start | bytes 393224 | tf_op jit(solution)/shard_map/ppermute | solution.py:99
  16.5 4.6 %collective-permute-start.1 = (bf16[2,8,8,512]{3,1,2,0:T(8,128)(2,1)S(1)}, bf16[2,8,8,512]{3,1,2,0:T(8,128)(2,1)S(1)}, u32[]{:S(2)}, u32[]{:S(2)}) collective-permute-start(bf16[2,8,8,512]{3,1,2,0:T(8,128)(2,1)S(1)} %bitcast.56), channel_id=1, source_target_pairs={{0,3},{1,0},{2,1},{3,2},{4,7},{5,4},{6,5},{7,6},{8,11},{9,8},{10,9... | collective-permute-start | bytes 393224 | tf_op jit(solution)/shard_map/ppermute | solution.py:99
  21.3 0.8 reshape.100
  22.1 15.5 %all-to-all-start = ((bf16[64,4,512]{2,1,0:T(4,128)(2,1)}), bf16[64,4,512]{2,1,0:T(4,128)(2,1)S(1)}, u32[]{:S(2)}, u32[]{:S(2)}) async-start(bf16[64,4,512]{2,1,0:T(4,128)(2,1)} %reshape.100), calls=%async_computation | async-start | bytes 524288 | tf_op jit(solution)/shard_map/all_to_all | solution.py:64
  37.5 4.1 %fusion.14 = (f32[512,512]{1,0:T(8,128)S(1)}, f32[512,512]{1,0:T(8,128)S(1)}) fusion(s32[512]{0:T(512)S(1)} %iota_add_fusion), kind=kLoop, calls=%fused_computation.36 | loop fusion | flops 3932160 | bytes 2099200 | tf_op jit(solution)/shard_map/cos | solution.py:26
  41.9 0.9 pad_maximum_fusion.1
  42.7 10.1 %all-to-all-done = bf16[64,4,512]{2,1,0:T(4,128)(2,1)S(1)} async-done(((bf16[64,4,512]{2,1,0:T(4,128)(2,1)}), bf16[64,4,512]{2,1,0:T(4,128)(2,1)S(1)}, u32[]{:S(2)}, u32[]{:S(2)}) %all-to-all-start) | async-done | bytes 262176 | tf_op jit(solution)/shard_map/all_to_all | solution.py:64
  53.0 0.3 broadcast_in_dim.2
  53.3 37.1 %all_to_all.10 = bf16[256,4,512]{2,1,0:T(4,128)(2,1)S(1)} all-to-all(bf16[256,4,512]{2,1,0:T(4,128)(2,1)S(1)} %broadcast_in_dim.2), channel_id=1, replica_groups=mesh['x'=4,'zh'=2,'y'=8,'c'=2,'seg'=4] {'x','zh','y','seg'}, dimensions={0} | all-to-all | bytes 2097152 | tf_op jit(solution)/shard_map/all_to_all | solution.py:70
  90.4 6.9 %collective-permute-start.4 = (bf16[256,4,512]{2,1,0:T(4,128)(2,1)S(1)}, bf16[256,4,512]{2,1,0:T(4,128)(2,1)}, u32[]{:S(2)}, u32[]{:S(2)}) collective-permute-start(bf16[256,4,512]{2,1,0:T(4,128)(2,1)S(1)} %all_to_all.10), channel_id=1, source_target_pairs={{0,4},{4,0},{1,5},{5,1},{2,6},{6,2},{3,7},{7,3},{8,12},{12,8},{9,1... | collective-permute-start | bytes 3145736 | tf_op jit(solution)/shard_map/ppermute | solution.py:71
  97.3 1.3 %fusion.10 = bf16[2,32,8,512]{3,1,2,0:T(8,128)(2,1)S(1)} fusion(s32[]{:T(128)S(6)} %select_n.101, bf16[2,32,8,512]{3,1,2,0:T(8,128)(2,1)} %pad_maximum_fusion.1), kind=kLoop, calls=%fused_computation.27 | loop fusion | flops 1048576 | bytes 1048580 | tf_op jit(solution)/shard_map/concatenate | solution.py:107
  98.7 0.3 copy.40
  99.0 0.3 copy.38
  99.4 0.3 convert_bitcast_fusion.1
  99.7 1.2 %copy.37 = f32[4,2,4,32,512]{4,3,2,1,0:T(8,128)S(1)} copy(f32[4,2,4,32,512]{4,2,0,1,3:T(4,128)S(1)} %convert_bitcast_fusion.1) | data formatting | bytes 4194304 | tf_op jit(solution)/shard_map/convert_element_type | solution.py:32
  100.9 1.6 %convert_bitcast_fusion = f32[4,2,4,32,512]{4,2,0,1,3:T(4,128)S(1)} fusion(bf16[32,2,4,4,512]{4,3,2,1,0:T(4,128)(2,1)} %bitcast.24), kind=kLoop, calls=%fused_computation.5 | loop fusion | flops 524288 | bytes 3145728 | tf_op jit(solution)/shard_map/convert_element_type | solution.py:33
  102.5 1.2 %copy.39 = f32[4,2,4,32,512]{4,3,2,1,0:T(8,128)S(1)} copy(f32[4,2,4,32,512]{4,2,0,1,3:T(4,128)S(1)} %convert_bitcast_fusion) | data formatting | bytes 4194304 | tf_op jit(solution)/shard_map/convert_element_type | solution.py:33
  103.7 6.9 %multiply_reduce_fusion.3 = (f32[32,8,512]{2,1,0:T(8,128)S(1)}, f32[32,8,512]{2,1,0:T(8,128)S(1)}, f32[32,8,512]{2,1,0:T(8,128)S(1)}, f32[32,8,512]{2,1,0:T(8,128)S(1)}) fusion(f32[32,8,512]{2,1,0:T(8,128)S(1)} %copy.38, f32[32,32,512]{2,1,0:T(8,128)S(1)} %bitcast.49, f32[32,8,512]{2,1,0:T(8,128)S(1)} %copy.40, f32[32,32,512]{2,1,0:T(8,128)S(1)} %bitcast.50), kind=kLoop, calls=%fused_computation.3 | loop fusion | flops 33030144 | bytes 7340032 | tf_op jit(solution)/shard_map/reduce_sum | solution.py:39
  110.9 2.8 %fusion = f32[32,8,512]{2,1,0:T(8,128)} fusion(f32[1024,512]{1,0:T(8,128)S(1)} %pad_maximum_fusion, f32[256,512]{1,0:T(8,128)S(1)} %get-tuple-element.27, f32[256,512]{1,0:T(8,128)S(1)} %get-tuple-element.28), kind=kOutput, calls=%fused_computation.12 | convolution fusion | flops 1611268096 | bytes 3670016 | tf_op jit(solution)/shard_map/dot_general | solution.py:43
  (25 shorter events, 1.7 us)
Async XLA Ops:
  0.0 2.2 %copy-start = (bf16[2,8,32,512]{3,2,1,0:T(8,128)(2,1)S(1)}, bf16[2,8,32,512]{3,2,1,0:T(8,128)(2,1)}, u32[]{:S(2)}) copy-start(bf16[2,8,32,512]{3,2,1,0:T(8,128)(2,1)} %param.2) | copy-start | bytes 1572868
  2.8 18.3 %collective-permute-start = (bf16[256,512]{1,0:T(8,128)(2,1)S(1)}, bf16[256,512]{1,0:T(8,128)(2,1)S(1)}, u32[]{:S(2)}, u32[]{:S(2)}) collective-permute-start(bf16[256,512]{1,0:T(8,128)(2,1)S(1)} %bitcast.53), channel_id=1, source_target_pairs={{0,4},{4,0},{1,5},{5,1},{2,6},{6,2},{3,7},{7,3},{8,12},{12,8},{9,1... | collective-permute-start | bytes 786440 | tf_op jit(solution)/shard_map/ppermute | solution.py:62
  12.0 29.9 %collective-permute-start.2 = (bf16[2,8,8,512]{3,1,2,0:T(8,128)(2,1)S(1)}, bf16[2,8,8,512]{3,1,2,0:T(8,128)(2,1)S(1)}, u32[]{:S(2)}, u32[]{:S(2)}) collective-permute-start(bf16[2,8,8,512]{3,1,2,0:T(8,128)(2,1)S(1)} %bitcast.54), channel_id=1, source_target_pairs={{0,2},{1,3},{2,0},{3,1},{4,6},{5,7},{6,4},{7,5},{8,10},{9,11},{10,... | collective-permute-start | bytes 393224 | tf_op jit(solution)/shard_map/ppermute | solution.py:99
  13.9 27.9 %collective-permute-start.3 = (bf16[2,8,8,512]{3,1,2,0:T(8,128)(2,1)S(1)}, bf16[2,8,8,512]{3,1,2,0:T(8,128)(2,1)S(1)}, u32[]{:S(2)}, u32[]{:S(2)}) collective-permute-start(bf16[2,8,8,512]{3,1,2,0:T(8,128)(2,1)S(1)} %bitcast.55), channel_id=1, source_target_pairs={{0,1},{1,2},{2,3},{3,0},{4,5},{5,6},{6,7},{7,4},{8,9},{9,10},{10,1... | collective-permute-start | bytes 393224 | tf_op jit(solution)/shard_map/ppermute | solution.py:99
  16.5 25.4 %collective-permute-start.1 = (bf16[2,8,8,512]{3,1,2,0:T(8,128)(2,1)S(1)}, bf16[2,8,8,512]{3,1,2,0:T(8,128)(2,1)S(1)}, u32[]{:S(2)}, u32[]{:S(2)}) collective-permute-start(bf16[2,8,8,512]{3,1,2,0:T(8,128)(2,1)S(1)} %bitcast.56), channel_id=1, source_target_pairs={{0,3},{1,0},{2,1},{3,2},{4,7},{5,4},{6,5},{7,6},{8,11},{9,8},{10,9... | collective-permute-start | bytes 393224 | tf_op jit(solution)/shard_map/ppermute | solution.py:99
  22.1 30.8 %all-to-all-start = ((bf16[64,4,512]{2,1,0:T(4,128)(2,1)}), bf16[64,4,512]{2,1,0:T(4,128)(2,1)S(1)}, u32[]{:S(2)}, u32[]{:S(2)}) async-start(bf16[64,4,512]{2,1,0:T(4,128)(2,1)} %reshape.100), calls=%async_computation | async-start | bytes 524288 | tf_op jit(solution)/shard_map/all_to_all | solution.py:64
  90.4 10.5 %collective-permute-start.4 = (bf16[256,4,512]{2,1,0:T(4,128)(2,1)S(1)}, bf16[256,4,512]{2,1,0:T(4,128)(2,1)}, u32[]{:S(2)}, u32[]{:S(2)}) collective-permute-start(bf16[256,4,512]{2,1,0:T(4,128)(2,1)S(1)} %all_to_all.10), channel_id=1, source_target_pairs={{0,4},{4,0},{1,5},{5,1},{2,6},{6,2},{3,7},{7,3},{8,12},{12,8},{9,1... | collective-permute-start | bytes 3145736 | tf_op jit(solution)/shard_map/ppermute | solution.py:71

commit v24 on v21

--- a/solution.py
+++ b/solution.py
@@ -56,12 +56,7 @@
         pair = lax.psum(1, "c")
         rest = ("x", "zh", "y")
         upper = lax.axis_index("c") == 1
-        flat = value.reshape(pair, -1, freqs)
-        keep = jnp.where(upper, flat[1], flat[0])
-        send = jnp.where(upper, flat[0], flat[1])
-        half = keep + lax.ppermute(send, "c", [(0, 1), (1, 0)])
-        part = half.reshape(count // pair, rows, freqs)
-        mine = lax.all_to_all(part, rest, 0, 0).sum(axis=0, dtype=value.dtype)
+        mine = lax.all_to_all(chunks, ("c",) + rest, 0, 0).sum(axis=0, dtype=value.dtype)
         mine, companion = lax.optimization_barrier((mine, companion))
     else:
         mine = lax.all_to_all(chunks, chan_axes, 0, 0).sum(axis=0, dtype=value.dtype)

time: 113 us -> 119 us (1.053)
  blocking collectives: 40.3 us -> 46.2 us
  waiting for transfers between devices: 10.2 us -> 13.2 us
  starting transfers between devices: 37.5 us -> 35 us
    ppermute x3, waiting for transfers between devices: 0.01 us -> 12.8 us  [regroup_receivers(): blocks.append(lax.ppermute(group((me + shift) % segs), seg_axis, pairs))]
    all_to_all x1, waiting for transfers between devices: 10.1 us -> 0.01 us  [gather_sources(): lax.all_to_all(chunks, ('c',) + rest, 0, 0).sum(axis=0, dtype=value.dtype)]
    ppermute x1 -> x0, starting transfers between devices: 8.79 us -> none  [gather_sources(): half = keep + lax.ppermute(send, 'c', [(0, 1), (1, 0)])]
    all_to_all x1, blocking collectives: 40.3 us -> 46.2 us  [gather_sources(): half_got = lax.all_to_all(spread, rest + (seg_axis,), 0, 0)]
    all_to_all x1, starting transfers between devices: 15.5 us -> 21.2 us  [gather_sources(): lax.all_to_all(chunks, ('c',) + rest, 0, 0).sum(axis=0, dtype=value.dtype)]
    ppermute x3, starting transfers between devices: 7.2 us -> 9.29 us  [regroup_receivers(): blocks.append(lax.ppermute(group((me + shift) % segs), seg_axis, pairs))]
    ppermute x1, starting transfers between devices: 6.03 us -> 4.54 us  [gather_sources(): sibling = lax.ppermute(half_got, 'c', [(0, 1), (1, 0)])]
  transfers between devices with their start and end apart: 6 -> 5, of which waited for: 1 -> 3; matrix products, arithmetic and copies ran while one was open for 8% -> 6% of each run, Pallas kernels for 0% -> 0%
where the time goes in v24:
time: 119 us; the launch traced here: 118 us
  blocking collectives  46.2 us (39%)
  starting transfers between devices  35 us (29%)
  other arithmetic  16 us (13%)
  waiting for transfers between devices  13.2 us (11%)
  local copies, waits for them, and re-layouts  4.33 us (4%)
  matrix products  3.14 us (3%)
    all_to_all x1, blocking collectives, gather_sources(): half_got = lax.all_to_all(spread, rest + (seg_axis,), 0, 0)  46.2 us
    all_to_all x1, starting transfers between devices, gather_sources(): lax.all_to_all(chunks, ('c',) + rest, 0, 0).sum(axis=0, dtype=value.dtype)  21.2 us
    ppermute x3, waiting for transfers between devices, regroup_receivers(): blocks.append(lax.ppermute(group((me + shift) % segs), seg_axis, pairs))  12.8 us
    ppermute x3, starting transfers between devices, regroup_receivers(): blocks.append(lax.ppermute(group((me + shift) % segs), seg_axis, pairs))  9.29 us
    reduce_sum x1, other arithmetic, correlate(): real_part = jnp.sum(a * c + b * d, axis=0)  6.72 us
    ppermute x1, starting transfers between devices, gather_sources(): sibling = lax.ppermute(half_got, 'c', [(0, 1), (1, 0)])  4.54 us
    cos x1, other arithmetic, lag_matrix(): return jnp.concatenate([jnp.cos(angles), -jnp.sin(angles)], axis=0)  4.12 us
    dot_general x1, matrix products, correlate(): jnp.dot(flat, lag_table, precision=lax.Precision.HIGHEST, preferred_eleme...  2.76 us
  transfers between devices with their start and end apart: 5, of which 3 were waited for; matrix products, arithmetic and copies ran while one was open for 6% of the time, Pallas kernels for 0%

profile of v24, /device:TPU:1, one launch (start us, length us, event | category | flops | bytes accessed | tf_op | source)
XLA Modules:
  0.0 118.2 jit_solution(11739358153872324898)
XLA Ops:
  0.0 1.2 %convert_element_type.58 = f32[2,8,32,512]{3,2,1,0:T(8,128)S(1)} convert(bf16[2,8,32,512]{3,2,1,0:T(8,128)(2,1)} %param.2) | non-fusion elementwise | flops 262144 | bytes 1572864 | tf_op jit(solution)/shard_map/convert_element_type | solution.py:14
  1.6 0.4 fusion.1
  2.0 0.3 copy.15
  2.3 0.9 reshape.88
  3.2 21.2 %all-to-all-start = ((bf16[128,4,512]{2,1,0:T(4,128)(2,1)}), bf16[128,4,512]{2,1,0:T(4,128)(2,1)S(1)}, u32[]{:S(2)}, u32[]{:S(2)}) async-start(bf16[128,4,512]{2,1,0:T(4,128)(2,1)} %reshape.88), calls=%async_computation | async-start | bytes 1048576 | tf_op jit(solution)/shard_map/all_to_all | solution.py:59
  24.7 4.9 %collective-permute-start = (bf16[2,8,8,512]{3,2,1,0:T(8,128)(2,1)S(1)}, bf16[2,8,8,512]{3,2,1,0:T(8,128)(2,1)S(1)}, u32[]{:S(2)}, u32[]{:S(2)}) collective-permute-start(bf16[2,8,8,512]{3,2,1,0:T(8,128)(2,1)S(1)} %get-tuple-element.17), channel_id=1, source_target_pairs={{0,3},{1,0},{2,1},{3,2},{4,7},{5,4},{6,5},{7,6},{8,11},{9,8},{10,9... | collective-permute-start | bytes 393224 | tf_op jit(solution)/shard_map/ppermute | solution.py:88
  29.6 1.9 %collective-permute-start.1 = (bf16[2,8,8,512]{3,2,1,0:T(8,128)(2,1)S(1)}, bf16[2,8,8,512]{3,2,1,0:T(8,128)(2,1)S(1)}, u32[]{:S(2)}, u32[]{:S(2)}) collective-permute-start(bf16[2,8,8,512]{3,2,1,0:T(8,128)(2,1)S(1)} %get-tuple-element.20), channel_id=1, source_target_pairs={{0,2},{1,3},{2,0},{3,1},{4,6},{5,7},{6,4},{7,5},{8,10},{9,11},{10,... | collective-permute-start | bytes 393224 | tf_op jit(solution)/shard_map/ppermute | solution.py:88
  31.5 2.5 %collective-permute-start.2 = (bf16[2,8,8,512]{3,2,1,0:T(8,128)(2,1)S(1)}, bf16[2,8,8,512]{3,2,1,0:T(8,128)(2,1)S(1)}, u32[]{:S(2)}, u32[]{:S(2)}) collective-permute-start(bf16[2,8,8,512]{3,2,1,0:T(8,128)(2,1)S(1)} %get-tuple-element.19), channel_id=1, source_target_pairs={{0,1},{1,2},{2,3},{3,0},{4,5},{5,6},{6,7},{7,4},{8,9},{9,10},{10,1... | collective-permute-start | bytes 393224 | tf_op jit(solution)/shard_map/ppermute | solution.py:88
  34.0 4.1 %fusion.14 = (f32[512,512]{1,0:T(8,128)S(1)}, f32[512,512]{1,0:T(8,128)S(1)}) fusion(s32[512]{0:T(512)S(1)} %iota_add_fusion), kind=kLoop, calls=%fused_computation.34 | loop fusion | flops 3932160 | bytes 2099200 | tf_op jit(solution)/shard_map/cos | solution.py:26
  38.3 2.5 %collective-permute-done = bf16[2,8,8,512]{3,2,1,0:T(8,128)(2,1)S(1)} collective-permute-done((bf16[2,8,8,512]{3,2,1,0:T(8,128)(2,1)S(1)}, bf16[2,8,8,512]{3,2,1,0:T(8,128)(2,1)S(1)}, u32[]{:S(2)}, u32[]{:S(2)}) %collective-permute-start) | collective-permute-done | bytes 131104 | tf_op jit(solution)/shard_map/ppermute | solution.py:88
  40.8 10.2 %collective-permute-done.1 = bf16[2,8,8,512]{3,2,1,0:T(8,128)(2,1)S(1)} collective-permute-done((bf16[2,8,8,512]{3,2,1,0:T(8,128)(2,1)S(1)}, bf16[2,8,8,512]{3,2,1,0:T(8,128)(2,1)S(1)}, u32[]{:S(2)}, u32[]{:S(2)}) %collective-permute-start.1) | collective-permute-done | bytes 131104 | tf_op jit(solution)/shard_map/ppermute | solution.py:88
  51.1 0.9 pad_maximum_fusion.1
  51.9 0.3 reduce_sum.37
  52.2 0.3 broadcast_in_dim.2
  52.5 46.2 %all_to_all.10 = bf16[256,4,512]{2,1,0:T(4,128)(2,1)S(1)} all-to-all(bf16[256,4,512]{2,1,0:T(4,128)(2,1)S(1)} %broadcast_in_dim.2), channel_id=1, replica_groups=mesh['x'=4,'zh'=2,'y'=8,'c'=2,'seg'=4] {'x','zh','y','seg'}, dimensions={0} | all-to-all | bytes 2097152 | tf_op jit(solution)/shard_map/all_to_all | solution.py:65
  98.7 4.5 %collective-permute-start.3 = (bf16[256,4,512]{2,1,0:T(4,128)(2,1)S(1)}, bf16[256,4,512]{2,1,0:T(4,128)(2,1)}, u32[]{:S(2)}, u32[]{:S(2)}) collective-permute-start(bf16[256,4,512]{2,1,0:T(4,128)(2,1)S(1)} %all_to_all.10), channel_id=1, source_target_pairs={{0,4},{4,0},{1,5},{5,1},{2,6},{6,2},{3,7},{7,3},{8,12},{12,8},{9,1... | collective-permute-start | bytes 3145736 | tf_op jit(solution)/shard_map/ppermute | solution.py:66
  103.3 1.3 %fusion.10 = bf16[2,32,8,512]{3,2,1,0:T(8,128)(2,1)S(1)} fusion(s32[]{:T(128)S(6)} %select_n.81, bf16[2,32,8,512]{3,2,1,0:T(8,128)(2,1)} %pad_maximum_fusion.1), kind=kLoop, calls=%fused_computation.26 | loop fusion | flops 262144 | bytes 1048580 | tf_op jit(solution)/shard_map/concatenate | solution.py:96
  104.7 0.6 copy.16
  105.3 0.4 collective-permute-done.3
  105.7 1.8 %copy.17 = bf16[1,32,2,4,4,512]{5,1,4,2,3,0:T(8,128)(2,1)S(1)} copy(bf16[1,32,2,4,4,512]{5,4,3,2,1,0:T(4,128)(2,1)} %bitcast.9) | data formatting | bytes 2097152 | tf_op jit(solution)/shard_map/stack | solution.py:67
  107.7 0.2 fusion.21
  107.9 0.7 bitcast_convert_fusion
  108.6 6.7 %add_reduce_fusion = (f32[32,8,512]{2,1,0:T(8,128)S(1)}, f32[32,8,512]{2,1,0:T(8,128)S(1)}) fusion(f32[32,8,512]{2,1,0:T(8,128)S(1)} %get-tuple-element.16, f32[32,32,512]{2,1,0:T(8,128)S(1)} %get-tuple-element.23, f32[32,8,512]{2,1,0:T(8,128)S(1)} %get-tuple-element.15, f32[32,32,512]{2,1,0:T(8,128)S(1)} %get-tuple-element.24), kind=kLoop, calls=%fused_computation.1 | loop fusion | flops 33292288 | bytes 6291456 | tf_op jit(solution)/shard_map/reduce_sum | solution.py:39
  115.4 2.8 %fusion = f32[32,8,512]{2,1,0:T(8,128)} fusion(f32[1024,512]{1,0:T(8,128)S(1)} %pad_maximum_fusion, f32[256,512]{1,0:T(8,128)S(1)} %multiply_bitcast_fusion, f32[256,512]{1,0:T(8,128)S(1)} %bitcast.42), kind=kOutput, calls=%fused_computation.9 | convolution fusion | flops 1611268096 | bytes 3670016 | tf_op jit(solution)/shard_map/dot_general | solution.py:43
  (18 shorter events, 1.0 us)
Async XLA Ops:
  0.0 1.6 %copy-start = (bf16[2,8,32,512]{3,2,1,0:T(8,128)(2,1)S(1)}, bf16[2,8,32,512]{3,2,1,0:T(8,128)(2,1)}, u32[]{:S(2)}) copy-start(bf16[2,8,32,512]{3,2,1,0:T(8,128)(2,1)} %param.2) | copy-start | bytes 1572868
  0.0 1.4 %copy-start.1 = (s32[8,4]{0,1:T(4,128)S(1)}, s32[8,4]{0,1:T(4,128)}, u32[]{:S(2)}) copy-start(s32[8,4]{0,1:T(4,128)} %param.3) | copy-start | bytes 388
  3.2 48.7 %all-to-all-start = ((bf16[128,4,512]{2,1,0:T(4,128)(2,1)}), bf16[128,4,512]{2,1,0:T(4,128)(2,1)S(1)}, u32[]{:S(2)}, u32[]{:S(2)}) async-start(bf16[128,4,512]{2,1,0:T(4,128)(2,1)} %reshape.88), calls=%async_computation | async-start | bytes 1048576 | tf_op jit(solution)/shard_map/all_to_all | solution.py:59
  24.7 16.2 %collective-permute-start = (bf16[2,8,8,512]{3,2,1,0:T(8,128)(2,1)S(1)}, bf16[2,8,8,512]{3,2,1,0:T(8,128)(2,1)S(1)}, u32[]{:S(2)}, u32[]{:S(2)}) collective-permute-start(bf16[2,8,8,512]{3,2,1,0:T(8,128)(2,1)S(1)} %get-tuple-element.17), channel_id=1, source_target_pairs={{0,3},{1,0},{2,1},{3,2},{4,7},{5,4},{6,5},{7,6},{8,11},{9,8},{10,9... | collective-permute-start | bytes 393224 | tf_op jit(solution)/shard_map/ppermute | solution.py:88
  29.6 21.5 %collective-permute-start.1 = (bf16[2,8,8,512]{3,2,1,0:T(8,128)(2,1)S(1)}, bf16[2,8,8,512]{3,2,1,0:T(8,128)(2,1)S(1)}, u32[]{:S(2)}, u32[]{:S(2)}) collective-permute-start(bf16[2,8,8,512]{3,2,1,0:T(8,128)(2,1)S(1)} %get-tuple-element.20), channel_id=1, source_target_pairs={{0,2},{1,3},{2,0},{3,1},{4,6},{5,7},{6,4},{7,5},{8,10},{9,11},{10,... | collective-permute-start | bytes 393224 | tf_op jit(solution)/shard_map/ppermute | solution.py:88
  31.5 19.6 %collective-permute-start.2 = (bf16[2,8,8,512]{3,2,1,0:T(8,128)(2,1)S(1)}, bf16[2,8,8,512]{3,2,1,0:T(8,128)(2,1)S(1)}, u32[]{:S(2)}, u32[]{:S(2)}) collective-permute-start(bf16[2,8,8,512]{3,2,1,0:T(8,128)(2,1)S(1)} %get-tuple-element.19), channel_id=1, source_target_pairs={{0,1},{1,2},{2,3},{3,0},{4,5},{5,6},{6,7},{7,4},{8,9},{9,10},{10,1... | collective-permute-start | bytes 393224 | tf_op jit(solution)/shard_map/ppermute | solution.py:88
  98.7 6.9 %collective-permute-start.3 = (bf16[256,4,512]{2,1,0:T(4,128)(2,1)S(1)}, bf16[256,4,512]{2,1,0:T(4,128)(2,1)}, u32[]{:S(2)}, u32[]{:S(2)}) collective-permute-start(bf16[256,4,512]{2,1,0:T(4,128)(2,1)S(1)} %all_to_all.10), channel_id=1, source_target_pairs={{0,4},{4,0},{1,5},{5,1},{2,6},{6,2},{3,7},{7,3},{8,12},{12,8},{9,1... | collective-permute-start | bytes 3145736 | tf_op jit(solution)/shard_map/ppermute | solution.py:66
